TPU v7x, 32 devices: a whole 2x2x4 slice. The times are simulated.
32 devices in a mesh: slot: 8 (over y, x, core), head: 4 (over z).
Axes of the slice: x: 2, y: 2, z: 4, core: 2. Of those that a mesh axis runs over, the one named last changes fastest.
Arguments:
- activations: bfloat16 [4096, 6144], P('slot'), may hold values from -6 to 6
- mod_table: bfloat16 [8, 3, 6144], replicated, may hold values from -3 to 3
- step_index: int32 [8], replicated, may hold values from 0 to 7
- block_mask: int32 [8, 4, 32], replicated, may hold values 0 or 1
- cache_index: int32 [8, 6], replicated, may hold values from 0 to 7, as said below
- w_qkv: bfloat16 [6144, 3, 1536], P(None, None, 'head'), may hold values from -0.078125 to 0.078125
- q_gain: float32 [1536], P('head')
- k_gain: float32 [1536], P('head')
- pool_kv: bfloat16 [8, 512, 2, 1536], P('slot', None, None, 'head')
- w_out: bfloat16 [1536, 6144], P('head'), may hold values from -0.15625 to 0.15625
Outputs:
- result: float32 [4096, 6144], P('slot', 'head')
Inputs may be any that keep to these rules, and one draw needn't show every extreme that they name: `cache_index`: the 6 entries of one row are distinct.
All inputs are finite; a program needn't handle non-finite values.
Results may differ from a plain program's by a relative error of at most 0.0065.
The roundings to bfloat16 on the way count: a program that leaves them out, or rounds other values in their place, can miss the bound.
Values may be sent and summed in bfloat16 or wider, within the bound.
No kernel may reach another device: no remote copies, remote signals or barrier semaphores. Data moves between devices by JAX's collectives and lax.ppermute only.
A program may use at most 128 MiB of HBM per device.

v0:
```python
import jax
import jax.numpy as jnp
from jax import lax
from jax.sharding import PartitionSpec as P

HD = 128
BLOCK = 128


def from_behind(shard, axis, by):
    length = lax.axis_size(axis)
    return lax.ppermute(shard, axis, [(i, (i + by) % length) for i in range(length)])


def head_norm(values, gain, heads):
    shaped = values.reshape(values.shape[0], heads, HD)
    scaled = shaped * lax.rsqrt(jnp.mean(shaped * shaped, axis=-1, keepdims=True) + 1e-06)
    return scaled * gain.reshape(heads, HD)


def attend(state, queries, span_kv, visible_blocks):
    highest, totals, accum = state
    heads = queries.shape[1]
    span_keys = span_kv[:, 0].reshape(span_kv.shape[0], heads, HD)
    span_values = span_kv[:, 1].reshape(span_kv.shape[0], heads, HD)
    visible = jnp.repeat(jnp.repeat(visible_blocks, BLOCK, axis=0), BLOCK, axis=1) > 0
    scores = jnp.einsum("qhd,khd->hqk", queries, span_keys, preferred_element_type=jnp.float32) * (
        1.0 / HD**0.5
    )
    scores = jnp.where(visible[None], scores, -1e30)
    new_high = jnp.maximum(highest, jnp.max(scores, axis=-1))
    factor = jnp.exp(highest - new_high)
    weights = jnp.where(visible[None], jnp.exp(scores - new_high[..., None]), 0.0)
    totals = totals * factor + jnp.sum(weights, axis=-1)
    accum = accum * factor[..., None] + jnp.einsum(
        "hqk,khd->hqd",
        weights.astype(jnp.bfloat16),
        span_values,
        preferred_element_type=jnp.float32,
    )
    return (new_high, totals, accum)


def local(
    activations,
    mod_table,
    step_index,
    block_mask,
    cache_index,
    w_qkv,
    q_gain,
    k_gain,
    pool_kv,
    w_out,
):
    slot = lax.axis_index("slot")
    span = activations.shape[0]
    heads = q_gain.shape[0] // HD
    blocks_q = span // BLOCK
    cache_len = cache_index.shape[1]
    onehot = (jnp.arange(mod_table.shape[0], dtype=jnp.int32) == step_index[slot]).astype(
        jnp.float32
    )
    modulation = jnp.einsum("n,nkd->kd", onehot, mod_table.astype(jnp.float32))
    inputs = activations.astype(jnp.float32)
    normed = inputs * lax.rsqrt(jnp.mean(inputs * inputs, axis=-1, keepdims=True) + 1e-06)
    hidden = (normed * (1.0 + modulation[1][None, :]) + modulation[0][None, :]).astype(jnp.bfloat16)
    qkv = jnp.einsum("td,dkh->tkh", hidden, w_qkv, preferred_element_type=jnp.float32)
    queries = head_norm(qkv[:, 0], q_gain, heads).astype(jnp.bfloat16)
    keys = head_norm(qkv[:, 1], k_gain, heads).astype(jnp.bfloat16)
    values = qkv[:, 2].astype(jnp.bfloat16)
    local_kv = jnp.stack([keys.reshape(span, heads * HD), values], axis=1)
    own_mask = lax.dynamic_index_in_dim(block_mask, slot, 0, keepdims=False)
    own_cache = lax.dynamic_index_in_dim(cache_index, slot, 0, keepdims=False)
    state = (
        jnp.full((heads, span), -1e30, jnp.float32),
        jnp.zeros((heads, span), jnp.float32),
        jnp.zeros((heads, span, HD), jnp.float32),
    )
    state = attend(state, queries, local_kv, jnp.ones((blocks_q, blocks_q), jnp.int32))
    before = from_behind(local_kv, "slot", 1)
    state = attend(state, queries, before, own_mask[:, :blocks_q])
    earlier = from_behind(local_kv, "slot", 2)
    state = attend(state, queries, earlier, own_mask[:, blocks_q : 2 * blocks_q])
    positions = jnp.arange(cache_len, dtype=jnp.int32)
    piece = lax.all_gather(pool_kv, "slot", axis=0, tiled=True)

    def turn(index, inner):
        span_kv = lax.dynamic_index_in_dim(piece, index, 0, keepdims=False)
        hits = own_cache == index
        place = jnp.sum(jnp.where(hits, positions, 0))
        visible_blocks = lax.dynamic_slice_in_dim(own_mask, (2 + place) * blocks_q, blocks_q, 1)
        return lax.cond(
            jnp.any(hits),
            lambda held: attend(held, queries, span_kv, visible_blocks),
            lambda held: held,
            inner,
        )

    state = lax.fori_loop(0, piece.shape[0], turn, state)
    highest, totals, accum = state
    mixed = (accum / totals[..., None]).astype(jnp.bfloat16)
    mixed = jnp.transpose(mixed, (1, 0, 2)).reshape(span, heads * HD)
    term = jnp.dot(mixed, w_out, preferred_element_type=jnp.float32)
    summed = lax.psum_scatter(
        term.astype(jnp.bfloat16), "head", scatter_dimension=1, tiled=True
    ).astype(jnp.float32)
    columns = summed.shape[1]
    offset = lax.axis_index("head") * columns
    input_cols = lax.dynamic_slice_in_dim(inputs, offset, columns, 1)
    gate_cols = lax.dynamic_slice_in_dim(modulation[2], offset, columns, 0)
    return input_cols + gate_cols[None, :] * summed


def solution(mesh):
    placed = (
        P("slot", None),
        P(),
        P(),
        P(),
        P(),
        P(None, None, "head"),
        P("head"),
        P("head"),
        P("slot", None, None, "head"),
        P("head", None),
    )
    return jax.shard_map(
        local, mesh=mesh, in_specs=placed, out_specs=P("slot", "head"), check_vma=False
    )
```

profile of v0, /device:TPU:9, one launch (start us, length us, event | category | flops | bytes accessed | tf_op | source)
XLA Modules:
  0.0 273.4 jit_solution(6089837296422354574)
XLA Ops:
  6.5 2.2 copy.64
  8.8 1.2 dynamic_slice.45
  10.9 4.1 %multiply_reduce_fusion = f32[512]{0:T(512)S(1)} fusion(bf16[512,6144]{1,0:T(8,128)(2,1)} %param.14), kind=kLoop, calls=%fused_computation.21 | loop fusion | flops 9436672 | bytes 6293504 | tf_op jit(solution)/shard_map/reduce_sum | solution.py:66
  15.1 19.6 %fusion.15 = f32[512,3,384]{0,2,1:T(8,128)} fusion(bf16[6144,3,384]{2,0,1:T(8,128)(2,1)} %param.19, f32[6144]{0:T(1024)S(1)} %bitcast.115, f32[6144]{0:T(1024)S(1)} %bitcast.116, f32[512]{0:T(512)S(1)} %add_rsqrt_fusion.2, bf16[512,6144]{1,0:T(8,128)(2,1)} %param.14), kind=kOutput, calls=%fused_computation.24 | convolution fusion | flops 7263485952 | bytes 22857728 | tf_op jit(solution)/shard_map/td,dkh->tkh/dot_general | solution.py:68
  34.7 1.3 slice.66
  36.0 1.6 slice.77
  39.0 2.0 collective-permute-start
  41.0 1.2 collective-permute-start.1
  45.8 23.4 %collective-permute-done = bf16[512,2,384]{0,2,1:T(8,128)(2,1)} collective-permute-done((bf16[512,2,384]{0,2,1:T(8,128)(2,1)}, bf16[512,2,384]{0,2,1:T(8,128)(2,1)}, u32[]{:S(2)}, u32[]{:S(2)}) %collective-permute-start) | collective-permute-done | bytes 786464 | tf_op jit(solution)/shard_map/ppermute | solution.py:12
  70.4 10.0 %collective-permute-done.1 = bf16[512,2,384]{0,2,1:T(8,128)(2,1)} collective-permute-done((bf16[512,2,384]{0,2,1:T(8,128)(2,1)}, bf16[512,2,384]{0,2,1:T(8,128)(2,1)}, u32[]{:S(2)}, u32[]{:S(2)}) %collective-permute-start.1) | collective-permute-done | bytes 786464 | tf_op jit(solution)/shard_map/ppermute | solution.py:12
  84.2 1.3 fusion.24
  85.5 1.5 fusion.42
  87.0 1.2 fusion.33
  88.2 1.3 fusion.51
  89.5 8.7 %copy.66 = bf16[8,512,2,384]{1,3,2,0:T(8,128)(2,1)} copy(bf16[8,512,2,384]{3,1,2,0:T(8,128)(2,1)} %all-gather.2.cloned.1.call-done) | data formatting | bytes 12582912
  98.2 46.2 %while.18 = (s32[]{:T(128)}, f32[3,512]{1,0:T(4,128)S(1)}, f32[3,512]{1,0:T(4,128)S(1)}, f32[3,512,128]{2,1,0:T(8,128)S(1)}, s32[6]{0:T(128)S(1)}, /*index=5*/s3...) while((s32[]{:T(128)}, f32[3,512]{1,0:T(4,128)S(1)}, ...), condition=%wide.region_16.17_spmd.clone, body=%wide.region_9.16_spmd.clone.sunk | while | flops 413273120 | bytes 16491011 | solution.py:100
  99.5 5.9 %conditional.3 = ((f32[3,512]{1,0:T(4,128)S(1)}, f32[3,512]{1,0:T(4,128)S(1)}, f32[3,512,128]{2,1,0:T(8,128)S(1)})) conditional(s32[]{:T(128)} %convert_element_type.110, (f32[3,512]{1,0:T(4,128)S(1)}, f32[3,512]{1,0:T(4,128)S(1)}, f32[3,512,128]{2,1,0:T(8,128)S(1)}) %tuple.86, (pred[6]{0:T(512)(128)(4,1)S(1)}, s32[6]{0:T(128)S(1)}, ...), branch_computations={%region_11.11_spmd, %region_12.15_spmd} | conditional | flops 413273120 | bytes 16490758 | solution.py:93
  104.0 1.5 fusion.8
  106.7 5.9 %conditional.3 = ((f32[3,512]{1,0:T(4,128)S(1)}, f32[3,512]{1,0:T(4,128)S(1)}, f32[3,512,128]{2,1,0:T(8,128)S(1)})) conditional(s32[]{:T(128)} %convert_element_type.110, (f32[3,512]{1,0:T(4,128)S(1)}, f32[3,512]{1,0:T(4,128)S(1)}, f32[3,512,128]{2,1,0:T(8,128)S(1)}) %tuple.86, (pred[6]{0:T(512)(128)(4,1)S(1)}, s32[6]{0:T(128)S(1)}, ...), branch_computations={%region_11.11_spmd, %region_12.15_spmd} | conditional | flops 413273120 | bytes 16490758 | solution.py:93
  111.2 1.5 fusion.8
  115.3 5.9 %conditional.3 = ((f32[3,512]{1,0:T(4,128)S(1)}, f32[3,512]{1,0:T(4,128)S(1)}, f32[3,512,128]{2,1,0:T(8,128)S(1)})) conditional(s32[]{:T(128)} %convert_element_type.110, (f32[3,512]{1,0:T(4,128)S(1)}, f32[3,512]{1,0:T(4,128)S(1)}, f32[3,512,128]{2,1,0:T(8,128)S(1)}) %tuple.86, (pred[6]{0:T(512)(128)(4,1)S(1)}, s32[6]{0:T(128)S(1)}, ...), branch_computations={%region_11.11_spmd, %region_12.15_spmd} | conditional | flops 413273120 | bytes 16490758 | solution.py:93
  119.8 1.5 fusion.8
  122.6 5.9 %conditional.3 = ((f32[3,512]{1,0:T(4,128)S(1)}, f32[3,512]{1,0:T(4,128)S(1)}, f32[3,512,128]{2,1,0:T(8,128)S(1)})) conditional(s32[]{:T(128)} %convert_element_type.110, (f32[3,512]{1,0:T(4,128)S(1)}, f32[3,512]{1,0:T(4,128)S(1)}, f32[3,512,128]{2,1,0:T(8,128)S(1)}) %tuple.86, (pred[6]{0:T(512)(128)(4,1)S(1)}, s32[6]{0:T(128)S(1)}, ...), branch_computations={%region_11.11_spmd, %region_12.15_spmd} | conditional | flops 413273120 | bytes 16490758 | solution.py:93
  127.1 1.5 fusion.8
  129.8 5.9 %conditional.3 = ((f32[3,512]{1,0:T(4,128)S(1)}, f32[3,512]{1,0:T(4,128)S(1)}, f32[3,512,128]{2,1,0:T(8,128)S(1)})) conditional(s32[]{:T(128)} %convert_element_type.110, (f32[3,512]{1,0:T(4,128)S(1)}, f32[3,512]{1,0:T(4,128)S(1)}, f32[3,512,128]{2,1,0:T(8,128)S(1)}) %tuple.86, (pred[6]{0:T(512)(128)(4,1)S(1)}, s32[6]{0:T(128)S(1)}, ...), branch_computations={%region_11.11_spmd, %region_12.15_spmd} | conditional | flops 413273120 | bytes 16490758 | solution.py:93
  134.3 1.5 fusion.8
  138.4 5.9 %conditional.3 = ((f32[3,512]{1,0:T(4,128)S(1)}, f32[3,512]{1,0:T(4,128)S(1)}, f32[3,512,128]{2,1,0:T(8,128)S(1)})) conditional(s32[]{:T(128)} %convert_element_type.110, (f32[3,512]{1,0:T(4,128)S(1)}, f32[3,512]{1,0:T(4,128)S(1)}, f32[3,512,128]{2,1,0:T(8,128)S(1)}) %tuple.86, (pred[6]{0:T(512)(128)(4,1)S(1)}, s32[6]{0:T(128)S(1)}, ...), branch_computations={%region_11.11_spmd, %region_12.15_spmd} | conditional | flops 413273120 | bytes 16490758 | solution.py:93
  142.9 1.5 fusion.8
  144.8 7.7 %convolution_convert_fusion = bf16[512,6144]{1,0:T(8,128)(2,1)} fusion(bf16[512,384]{0,1:T(8,128)(2,1)S(1)} %bitcast.108, bf16[384,6144]{1,0:T(8,128)(2,1)} %param.23), kind=kOutput, calls=%fused_computation.22 | convolution fusion | flops 2419064832 | bytes 11403264 | tf_op jit(solution)/shard_map/dot_general | solution.py:104
  152.5 9.7 %convert_element_type.56 = f32[512,6144]{1,0:T(8,128)} convert(bf16[512,6144]{1,0:T(8,128)(2,1)} %param.14) | non-fusion elementwise | flops 3145728 | bytes 18874368 | tf_op jit(solution)/shard_map/convert_element_type | solution.py:65
  162.2 99.8 %reduce-scatter.2.cloned.1.call-done = bf16[512,1536]{1,0:T(8,128)(2,1)} async-done(((bf16[512,6144]{1,0:T(8,128)(2,1)}), bf16[512,1536]{1,0:T(8,128)(2,1)}) %reduce-scatter.2.cloned.1.call-update) | async-done | bytes 1572880 | tf_op jit(solution)/shard_map/reduce_scatter | solution.py:105
  262.0 4.5 %multiply_add_fusion.1 = f32[512,1536]{1,0:T(8,128)} fusion(bf16[512,1536]{1,0:T(8,128)(2,1)} %reduce-scatter.2.cloned.1.call-done, f32[512,6144]{1,0:T(8,128)} %convert_element_type.56, s32[]{:T(128)S(6)} %select_n.72, f32[1536]{0:T(1024)S(1)} %dynamic-slice_reduce_fusion), kind=kLoop, calls=%fused_computation.29 | loop fusion | flops 2359296 | bytes 7870468 | tf_op jit(solution)/shard_map/add | solution.py:112
  (142 shorter events, 38.9 us)
Async XLA Ops:
  6.5 3.5 %copy-start = (bf16[8,3,6144]{2,0,1:T(8,128)(2,1)S(1)}, bf16[8,3,6144]{2,0,1:T(8,128)(2,1)}, u32[]{:S(2)}) copy-start(bf16[8,3,6144]{2,0,1:T(8,128)(2,1)} %param.15) | copy-start | bytes 884740
  6.5 83.0 %all-gather.2.cloned.1.call-start = ((), (), s32[]{:S(2)}) async-start(), calls=%async_computation.1 | async-start | bytes 7077888 | tf_op jit(solution)/shard_map/all_gather | solution.py:86
  8.7 253.3 %reduce-scatter.2.cloned.1.call-start = ((), (), s32[]{:S(2)}) async-start(), calls=%async_computation.2 | async-start | bytes 7864320 | tf_op jit(solution)/shard_map/reduce_scatter | solution.py:105
  34.7 3.1 %copy-start.2 = (f32[512,3,384]{0,2,1:T(8,128)S(1)}, f32[512,3,384]{0,2,1:T(8,128)}, u32[]{:S(2)}) copy-start(f32[512,3,384]{0,2,1:T(8,128)} %fusion.15) | copy-start | bytes 7077892
  34.7 3.1 %copy-start.3 = (f32[384]{0:T(512)S(1)}, f32[384]{0:T(512)}, u32[]{:S(2)}) copy-start(f32[384]{0:T(512)} %param.21) | copy-start | bytes 4612
  38.1 6.8 %copy-start.4 = (f32[384]{0:T(512)S(1)}, f32[384]{0:T(512)}, u32[]{:S(2)}) copy-start(f32[384]{0:T(512)} %param.20) | copy-start | bytes 4612
  39.0 30.2 %collective-permute-start = (bf16[512,2,384]{0,2,1:T(8,128)(2,1)}, bf16[512,2,384]{0,2,1:T(8,128)(2,1)}, u32[]{:S(2)}, u32[]{:S(2)}) collective-permute-start(bf16[512,2,384]{0,2,1:T(8,128)(2,1)} %pad_maximum_fusion), channel_id=1, source_target_pairs={{0,4},{4,8},{8,12},{12,16},{16,20},{20,24},{24,28},{28,0},{1,5},{5... | collective-permute-start | bytes 2359304 | tf_op jit(solution)/shard_map/ppermute | solution.py:12
  41.0 39.3 %collective-permute-start.1 = (bf16[512,2,384]{0,2,1:T(8,128)(2,1)}, bf16[512,2,384]{0,2,1:T(8,128)(2,1)}, u32[]{:S(2)}, u32[]{:S(2)}) collective-permute-start(bf16[512,2,384]{0,2,1:T(8,128)(2,1)} %pad_maximum_fusion), channel_id=1, source_target_pairs={{0,8},{4,12},{8,16},{12,20},{16,24},{20,28},{24,0},{28,4},{1,9},{5... | collective-permute-start | bytes 2359304 | tf_op jit(solution)/shard_map/ppermute | solution.py:12
  162.2 104.4 %copy-start.1 = (bf16[8,3,6144]{2,0,1:T(8,128)(2,1)S(1)}, bf16[8,3,6144]{2,0,1:T(8,128)(2,1)}, u32[]{:S(2)}) copy-start(bf16[8,3,6144]{2,0,1:T(8,128)(2,1)} %param.15) | copy-start | bytes 884740
Sparse Core Ops, SparseCore 0:
  9.2 57.6 all-gather.1
  152.6 109.3 reduce-scatter.1
where the time goes:
time: 276 us; the launch traced here: 273 us
  waiting for transfers between devices  133 us (48%)
  matrix products  48.3 us (18%)
  other arithmetic  36.4 us (13%)
  local copies, waits for them, and re-layouts  28.7 us (10%)
  between operations  13.6 us (5%)
  loops' own time  9.84 us (4%)
  starting transfers between devices  3.28 us (1%)
    reduce_scatter x1, waiting for transfers between devices, local(): lax.psum_scatter(term.astype(jnp.bfloat16), 'head', scatter_dimension=1,...  99.8 us
    ppermute x2, waiting for transfers between devices, from_behind(): lax.ppermute(shard, axis, [(i, (i + by) % length) for i in range(length)])  33.4 us
    dot_general x1, matrix products, local(): jnp.einsum('td,dkh->tkh', hidden, w_qkv, preferred_element_type=jnp.float32)  19.6 us
    dot_general x9, matrix products, attend(): jnp.einsum('hqk,khd->hqd', weights.astype(jnp.bfloat16), span_values, pre...  12.7 us
    unnamed x17, local copies, waits for them, and re-layouts  11.1 us
    convert_element_type x1, other arithmetic, local(): inputs = activations.astype(jnp.float32)  9.73 us
    dot_general x1, matrix products, local(): term = jnp.dot(mixed, w_out, preferred_element_type=jnp.float32)  7.69 us
    dot_general x9, matrix products, attend(): jnp.einsum('qhd,khd->hqk', queries, span_keys, preferred_element_type=jnp...  7.46 us
  transfers between devices with their start and end apart: 4, of which 3 were waited for; matrix products, arithmetic and copies ran while one was open for 20% of the time, Pallas kernels for 0%

commit v1 on v0

--- a/solution.py
+++ b/solution.py
@@ -41,6 +41,21 @@
     return (new_high, totals, accum)
 
 
+def fetch_out_weight(w_out, head, core):
+    groups = lax.axis_size("head")
+    columns = w_out.shape[1] // groups
+    half = columns // 2
+    mine = []
+    for shift in range(groups):
+        dest = (head + shift) % groups
+        block = lax.dynamic_slice_in_dim(w_out, dest * columns + core * half, half, 1)
+        if shift:
+            block = lax.ppermute(block, "head", [(i, (i + shift) % groups) for i in range(groups)])
+        mine.append(block)
+    own_full = lax.dynamic_slice_in_dim(w_out, head * columns, columns, 1)
+    return own_full, mine
+
+
 def local(
     activations,
     mod_table,
@@ -54,10 +69,17 @@
     w_out,
 ):
     slot = lax.axis_index("slot")
+    head = lax.axis_index("head")
+    core = slot % 2
+    groups = lax.axis_size("head")
     span = activations.shape[0]
     heads = q_gain.shape[0] // HD
     blocks_q = span // BLOCK
     cache_len = cache_index.shape[1]
+
+    own_full, mine = fetch_out_weight(w_out, head, core)
+    piece = lax.all_gather(pool_kv, "slot", axis=0, tiled=True)
+
     onehot = (jnp.arange(mod_table.shape[0], dtype=jnp.int32) == step_index[slot]).astype(
         jnp.float32
     )
@@ -77,39 +99,49 @@
         jnp.zeros((heads, span), jnp.float32),
         jnp.zeros((heads, span, HD), jnp.float32),
     )
+    before = from_behind(local_kv, "slot", 1)
+    earlier = from_behind(local_kv, "slot", 2)
     state = attend(state, queries, local_kv, jnp.ones((blocks_q, blocks_q), jnp.int32))
-    before = from_behind(local_kv, "slot", 1)
     state = attend(state, queries, before, own_mask[:, :blocks_q])
-    earlier = from_behind(local_kv, "slot", 2)
     state = attend(state, queries, earlier, own_mask[:, blocks_q : 2 * blocks_q])
-    positions = jnp.arange(cache_len, dtype=jnp.int32)
-    piece = lax.all_gather(pool_kv, "slot", axis=0, tiled=True)
+    state, mine = lax.optimization_barrier((state, mine))
 
-    def turn(index, inner):
-        span_kv = lax.dynamic_index_in_dim(piece, index, 0, keepdims=False)
-        hits = own_cache == index
-        place = jnp.sum(jnp.where(hits, positions, 0))
+    def turn(place, inner):
+        span_kv = lax.dynamic_index_in_dim(piece, own_cache[place], 0, keepdims=False)
         visible_blocks = lax.dynamic_slice_in_dim(own_mask, (2 + place) * blocks_q, blocks_q, 1)
-        return lax.cond(
-            jnp.any(hits),
-            lambda held: attend(held, queries, span_kv, visible_blocks),
-            lambda held: held,
-            inner,
-        )
+        return attend(inner, queries, span_kv, visible_blocks)
 
-    state = lax.fori_loop(0, piece.shape[0], turn, state)
+    state = lax.fori_loop(0, cache_len, turn, state)
+    slots = lax.axis_size("slot")
+    sibling = lax.ppermute(
+        jnp.stack(mine[1:]), "slot", [(i, i ^ 1) for i in range(slots)]
+    )
     highest, totals, accum = state
     mixed = (accum / totals[..., None]).astype(jnp.bfloat16)
     mixed = jnp.transpose(mixed, (1, 0, 2)).reshape(span, heads * HD)
-    term = jnp.dot(mixed, w_out, preferred_element_type=jnp.float32)
-    summed = lax.psum_scatter(
-        term.astype(jnp.bfloat16), "head", scatter_dimension=1, tiled=True
-    ).astype(jnp.float32)
-    columns = summed.shape[1]
-    offset = lax.axis_index("head") * columns
+
+    gathered = lax.all_gather(mixed, "head", axis=0, tiled=False)
+    columns = own_full.shape[1]
+    half = columns // 2
+    attn = jnp.dot(mixed, own_full, preferred_element_type=jnp.float32).astype(jnp.bfloat16).astype(jnp.float32)
+    attn_mine = None
+    attn_sib = None
+    for shift in range(1, groups):
+        group_o = lax.dynamic_index_in_dim(gathered, (head - shift) % groups, 0, keepdims=False)
+        part = jnp.dot(group_o, mine[shift], preferred_element_type=jnp.float32)
+        part = part.astype(jnp.bfloat16).astype(jnp.float32)
+        attn_mine = part if attn_mine is None else attn_mine + part
+        part = jnp.dot(group_o, sibling[shift - 1], preferred_element_type=jnp.float32)
+        part = part.astype(jnp.bfloat16).astype(jnp.float32)
+        attn_sib = part if attn_sib is None else attn_sib + part
+    other = jnp.concatenate([attn_mine, attn_sib], axis=1)
+    swapped = jnp.concatenate([attn_sib, attn_mine], axis=1)
+    attn = attn + jnp.where(core == 0, other, swapped)
+
+    offset = head * columns
     input_cols = lax.dynamic_slice_in_dim(inputs, offset, columns, 1)
     gate_cols = lax.dynamic_slice_in_dim(modulation[2], offset, columns, 0)
-    return input_cols + gate_cols[None, :] * summed
+    return input_cols + gate_cols[None, :] * attn
 
 
 def solution(mesh):

time: 276 us -> 210 us (0.76)
  waiting for transfers between devices: 133 us -> 58.3 us
  other arithmetic: 36.4 us -> 25 us
  local copies, waits for them, and re-layouts: 28.7 us -> 36.8 us
  matrix products: 48.3 us -> 53.5 us
  starting transfers between devices: 3.28 us -> 7.26 us
    reduce_scatter x1 -> x0, waiting for transfers between devices: 99.8 us -> none  [local(): lax.psum_scatter(term.astype(jnp.bfloat16), 'head', scatter_dimension=1,...]
    all_gather x0 -> x1, waiting for transfers between devices: none -> 22.4 us  [local(): gathered = lax.all_gather(mixed, 'head', axis=0, tiled=False)]
    dynamic_slice x0 -> x31, local copies, waits for them, and re-layouts: none -> 16.7 us  [the longest x12 9.07 us: turn(): lax.dynamic_index_in_dim(piece, own_cache[place], 0, keepdims=False)]
    unnamed x17, local copies, waits for them, and re-layouts: 11.1 us -> 2.36 us
    ppermute x0 -> x4, waiting for transfers between devices: none -> 8.7 us  [the longest x3 8.7 us: fetch_out_weight(): lax.ppermute(block, 'head', [(i, (i + shift) % groups) for i in range(gro...]
    squeeze x6 -> x0, local copies, waits for them, and re-layouts: 7.13 us -> none  [turn(): span_kv = lax.dynamic_index_in_dim(piece, index, 0, keepdims=False)]
    while x1 -> x43, local copies, waits for them, and re-layouts: 0.26 us -> 7.13 us  [local(): state = lax.fori_loop(0, piece.shape[0], turn, state)]
    ppermute x2, waiting for transfers between devices: 33.4 us -> 27.2 us  [from_behind(): lax.ppermute(shard, axis, [(i, (i + by) % length) for i in range(length)])]
  transfers between devices with their start and end apart: 4 -> 8, of which waited for: 3 -> 5; matrix products, arithmetic and copies ran while one was open for 20% -> 31% of each run, Pallas kernels for 0% -> 0%
where the time goes in v1:
time: 210 us; the launch traced here: 206 us
  waiting for transfers between devices  58.3 us (28%)
  matrix products  53.5 us (25%)
  local copies, waits for them, and re-layouts  36.8 us (18%)
  other arithmetic  25 us (12%)
  between operations  13.7 us (7%)
  loops' own time  11.7 us (6%)
  starting transfers between devices  7.26 us (3%)
    ppermute x2, waiting for transfers between devices, from_behind(): lax.ppermute(shard, axis, [(i, (i + by) % length) for i in range(length)])  27.2 us
    all_gather x1, waiting for transfers between devices, local(): gathered = lax.all_gather(mixed, 'head', axis=0, tiled=False)  22.4 us
    dot_general x1, matrix products, local(): jnp.einsum('td,dkh->tkh', hidden, w_qkv, preferred_element_type=jnp.float32)  19.6 us
    dot_general x9, matrix products, attend(): jnp.einsum('hqk,khd->hqd', weights.astype(jnp.bfloat16), span_values, pre...  13.5 us
    another operation x1, loops' own time, local(): state = lax.fori_loop(0, cache_len, turn, state)  11.7 us
    dynamic_slice x12, local copies, waits for them, and re-layouts, turn(): lax.dynamic_index_in_dim(piece, own_cache[place], 0, keepdims=False)  9.07 us
    convert_element_type x1, other arithmetic, local(): inputs = activations.astype(jnp.float32)  9.01 us
    ppermute x3, waiting for transfers between devices, fetch_out_weight(): lax.ppermute(block, 'head', [(i, (i + shift) % groups) for i in range(gro...  8.7 us
  transfers between devices with their start and end apart: 8, of which 5 were waited for; matrix products, arithmetic and copies ran while one was open for 31% of the time, Pallas kernels for 0%

profile of v1, /device:TPU:9, one launch (start us, length us, event | category | flops | bytes accessed | tf_op | source)
XLA Modules:
  0.0 206.2 jit_solution(4798826463239611198)
XLA Ops:
  6.5 2.2 %copy.64 = bf16[1,512,2,384]{3,1,2,0:T(8,128)(2,1)} copy(bf16[1,512,2,384]{3,2,1,0:T(2,128)(2,1)} %param.20) | data formatting | bytes 1572864 | tf_op args[8]
  8.8 1.2 dynamic_slice.63
  10.9 4.1 %multiply_reduce_fusion = f32[512]{0:T(512)S(1)} fusion(bf16[512,6144]{1,0:T(8,128)(2,1)} %param.12), kind=kLoop, calls=%fused_computation.19 | loop fusion | flops 9436672 | bytes 6293504 | tf_op jit(solution)/shard_map/reduce_sum | solution.py:88
  15.1 19.6 %fusion.13 = f32[512,3,384]{0,2,1:T(8,128)} fusion(bf16[6144,3,384]{2,0,1:T(8,128)(2,1)} %param.17, f32[6144]{0:T(1024)S(1)} %bitcast.174, f32[6144]{0:T(1024)S(1)} %bitcast.175, f32[512]{0:T(512)S(1)} %add_rsqrt_fusion.2, bf16[512,6144]{1,0:T(8,128)(2,1)} %param.12), kind=kOutput, calls=%fused_computation.21 | convolution fusion | flops 7263485952 | bytes 22857728 | tf_op jit(solution)/shard_map/td,dkh->tkh/dot_general | solution.py:90
  34.7 1.3 slice.80
  36.0 1.6 slice.100
  39.0 2.0 collective-permute-start
  42.3 2.7 %constant_dynamic-slice_fusion.3 = (bf16[384,768]{1,0:T(8,128)(2,1)}, bf16[384,768]{1,0:T(8,128)(2,1)}, bf16[384,768]{1,0:T(8,128)(2,1)}) fusion(bf16[384,6144]{1,0:T(8,128)(2,1)} %param.21, s32[]{:T(128)S(6)} %select_n.134, s32[]{:T(128)S(6)} %select_n.132, s32[]{:T(128)S(6)} %select_n.130), kind=kLoop, calls=%fused_computation.116 | loop fusion | bytes 3538956 | tf_op jit(solution)/shard_map/dynamic_slice | solution.py:51
  45.0 1.2 collective-permute-start.2
  47.3 1.4 collective-permute-start.4
  52.0 17.2 %collective-permute-done = bf16[512,2,384]{0,2,1:T(8,128)(2,1)} collective-permute-done((bf16[512,2,384]{0,2,1:T(8,128)(2,1)}, bf16[512,2,384]{0,2,1:T(8,128)(2,1)}, u32[]{:S(2)}, u32[]{:S(2)}) %collective-permute-start) | collective-permute-done | bytes 786464 | tf_op jit(solution)/shard_map/ppermute | solution.py:12
  70.4 10.0 %collective-permute-done.1 = bf16[512,2,384]{0,2,1:T(8,128)(2,1)} collective-permute-done((bf16[512,2,384]{0,2,1:T(8,128)(2,1)}, bf16[512,2,384]{0,2,1:T(8,128)(2,1)}, u32[]{:S(2)}, u32[]{:S(2)}) %collective-permute-start.1) | collective-permute-done | bytes 786464 | tf_op jit(solution)/shard_map/ppermute | solution.py:12
  84.2 1.3 fusion.25
  86.7 1.5 fusion.43
  88.2 2.2 %fusion.52 = f32[3,512,128]{2,1,0:T(8,128)} fusion(f32[3,512,128]{2,1,0:T(8,128)S(1)} %fusion.34, f32[3,512,128]{2,1,0:T(8,128)S(1)} %fusion.43, bf16[512,3,128]{0,2,1:T(8,128)(2,1)S(1)} %bitcast.170, f32[3,512,512]{1,2,0:T(8,128)S(1)} %get-tuple-element.229, f32[3,512]{1,0:T(4,128)S(1)} %get-tuple-element.205, pred[512,512]{0,1:T(8,128)(4,1)S(1)} %bitcast.162, ...), kind=kOutput, calls=%fused_computation.65 | convolution fusion | flops 205848576 | bytes 6172672 | tf_op jit(solution)/shard_map/hqk,khd->hqd/dot_general | solution.py:35
  90.4 6.9 %collective-permute-done.3 = bf16[384,768]{1,0:T(8,128)(2,1)} collective-permute-done((bf16[384,768]{1,0:T(8,128)(2,1)}, bf16[384,768]{1,0:T(8,128)(2,1)}, u32[]{:S(2)}, u32[]{:S(2)}) %collective-permute-start.3) | collective-permute-done | bytes 589856 | tf_op jit(solution)/shard_map/ppermute | solution.py:53
  97.3 1.8 collective-permute-done.4
  99.1 51.1 %while.17 = (s32[]{:T(128)}, f32[3,512]{1,0:T(4,128)S(1)}, f32[3,512]{1,0:T(4,128)S(1)}, f32[3,512,128]{2,1,0:T(8,128)}, s32[4,32]{1,0:T(4,128)S(1)}, /*index=5*...) while((s32[]{:T(128)}, f32[3,512]{1,0:T(4,128)S(1)}, ...), condition=%wide.region_12.13_spmd, body=%wide.region_9.12_spmd.sunk | while | flops 413273120 | bytes 24355468 | solution.py:114
  105.3 1.5 fusion.133
  113.8 1.5 fusion.133
  122.3 1.4 fusion.133
  130.8 1.5 fusion.133
  139.3 1.5 fusion.133
  147.8 1.4 fusion.133
  150.2 1.4 copy.67
  152.6 2.8 %pad_maximum_fusion = bf16[3,384,768]{2,1,0:T(8,128)(2,1)} fusion(bf16[1,384,768]{2,1,0:T(8,128)(2,1)} %bitcast.34, bf16[1,384,768]{2,1,0:T(8,128)(2,1)} %bitcast.33, bf16[1,384,768]{2,1,0:T(8,128)(2,1)} %bitcast.32), kind=kLoop, calls=%fused_computation.45 | loop fusion | flops 1769472 | bytes 3538944 | tf_op jit(solution)/shard_map/stack | solution.py:117
  155.8 9.0 %convert_element_type.86 = f32[512,6144]{1,0:T(8,128)} convert(bf16[512,6144]{1,0:T(8,128)(2,1)} %param.12) | non-fusion elementwise | flops 3145728 | bytes 18874368 | tf_op jit(solution)/shard_map/convert_element_type | solution.py:87
  164.9 22.4 %all-gather.5.cloned.1.call-done = bf16[4,512,384]{2,1,0:T(8,128)(2,1)} async-done(((bf16[1,512,384]{2,1,0:T(8,128)(2,1)}), bf16[4,512,384]{2,1,0:T(8,128)(2,1)}) %all-gather.5.cloned.1.call-update) | async-done | bytes 1572880 | tf_op jit(solution)/shard_map/all_gather | solution.py:123
  187.2 1.9 convolution_convert_fusion.6
  189.1 1.8 convolution_convert_fusion.5
  192.0 1.6 convert_add_fusion.1
  194.3 5.1 %fusion.21 = f32[512,1536]{1,0:T(8,128)} fusion(f32[512,768]{1,0:T(8,128)S(1)} %convert_add_fusion, f32[512,768]{1,0:T(8,128)S(1)} %convert_add_fusion.1, f32[512,6144]{1,0:T(8,128)} %convert_element_type.86, s32[]{:T(128)S(6)} %select_n.122, bf16[512,384]{0,1:T(8,128)(2,1)S(1)} %bitcast.169, f32[1536]{0:T(1024)S(1)} %dynamic-slice_reduce_fusion, ...), kind=kOutput, calls=%fused_computation.29 | convolution fusion | flops 610271232 | bytes 11017728 | tf_op jit(solution)/shard_map/dot_general | solution.py:126
  (176 shorter events, 47.9 us)
Async XLA Ops:
  6.5 3.5 %copy-start = (bf16[8,3,6144]{2,0,1:T(8,128)(2,1)S(1)}, bf16[8,3,6144]{2,0,1:T(8,128)(2,1)}, u32[]{:S(2)}) copy-start(bf16[8,3,6144]{2,0,1:T(8,128)(2,1)} %param.13) | copy-start | bytes 884740
  6.5 92.6 %all-gather.3.cloned.1.call-start = ((), (), s32[]{:S(2)}) async-start(), calls=%async_computation | async-start | bytes 7077888 | tf_op jit(solution)/shard_map/all_gather | solution.py:81
  8.7 178.5 %all-gather.5.cloned.1.call-start = ((), (), s32[]{:S(2)}) async-start(), calls=%async_computation.1 | async-start | bytes 1966080 | tf_op jit(solution)/shard_map/all_gather | solution.py:123
  34.7 3.1 %copy-start.3 = (f32[512,3,384]{0,2,1:T(8,128)S(1)}, f32[512,3,384]{0,2,1:T(8,128)}, u32[]{:S(2)}) copy-start(f32[512,3,384]{0,2,1:T(8,128)} %fusion.13) | copy-start | bytes 7077892
  34.7 3.1 %copy-start.6 = (f32[384]{0:T(512)S(1)}, f32[384]{0:T(512)}, u32[]{:S(2)}) copy-start(f32[384]{0:T(512)} %param.19) | copy-start | bytes 4612
  39.0 30.2 %collective-permute-start = (bf16[512,2,384]{0,2,1:T(8,128)(2,1)}, bf16[512,2,384]{0,2,1:T(8,128)(2,1)}, u32[]{:S(2)}, u32[]{:S(2)}) collective-permute-start(bf16[512,2,384]{0,2,1:T(8,128)(2,1)} %pad_maximum_fusion.1), channel_id=1, source_target_pairs={{0,4},{4,8},{8,12},{12,16},{16,20},{20,24},{24,28},{28,0},{1,5},{5... | collective-permute-start | bytes 2359304 | tf_op jit(solution)/shard_map/ppermute | solution.py:12
  41.0 39.3 %collective-permute-start.1 = (bf16[512,2,384]{0,2,1:T(8,128)(2,1)}, bf16[512,2,384]{0,2,1:T(8,128)(2,1)}, u32[]{:S(2)}, u32[]{:S(2)}) collective-permute-start(bf16[512,2,384]{0,2,1:T(8,128)(2,1)} %pad_maximum_fusion.1), channel_id=1, source_target_pairs={{0,8},{4,12},{8,16},{12,20},{16,24},{20,28},{24,0},{28,4},{1,9},{5... | collective-permute-start | bytes 2359304 | tf_op jit(solution)/shard_map/ppermute | solution.py:12
  42.3 8.9 %copy-start.7 = (f32[384]{0:T(512)S(1)}, f32[384]{0:T(512)}, u32[]{:S(2)}) copy-start(f32[384]{0:T(512)} %param.18) | copy-start | bytes 4612
  45.0 45.4 %collective-permute-start.2 = (bf16[384,768]{1,0:T(8,128)(2,1)}, bf16[384,768]{1,0:T(8,128)(2,1)}, u32[]{:S(2)}, u32[]{:S(2)}) collective-permute-start(bf16[384,768]{1,0:T(8,128)(2,1)} %get-tuple-element.212), channel_id=1, source_target_pairs={{0,1},{1,2},{2,3},{3,0},{4,5},{5,6},{6,7},{7,4},{8,9},{9,10},{10,1... | collective-permute-start | bytes 1769480 | tf_op jit(solution)/shard_map/ppermute | solution.py:53
  46.2 51.1 %collective-permute-start.3 = (bf16[384,768]{1,0:T(8,128)(2,1)}, bf16[384,768]{1,0:T(8,128)(2,1)}, u32[]{:S(2)}, u32[]{:S(2)}) collective-permute-start(bf16[384,768]{1,0:T(8,128)(2,1)} %get-tuple-element.211), channel_id=1, source_target_pairs={{0,2},{1,3},{2,0},{3,1},{4,6},{5,7},{6,4},{7,5},{8,10},{9,11},{10,... | collective-permute-start | bytes 1769480 | tf_op jit(solution)/shard_map/ppermute | solution.py:53
  47.3 51.8 %collective-permute-start.4 = (bf16[384,768]{1,0:T(8,128)(2,1)}, bf16[384,768]{1,0:T(8,128)(2,1)}, u32[]{:S(2)}, u32[]{:S(2)}) collective-permute-start(bf16[384,768]{1,0:T(8,128)(2,1)} %get-tuple-element.210), channel_id=1, source_target_pairs={{0,3},{1,0},{2,1},{3,2},{4,7},{5,4},{6,5},{7,6},{8,11},{9,8},{10,9... | collective-permute-start | bytes 1769480 | tf_op jit(solution)/shard_map/ppermute | solution.py:53
  103.5 1.7 copy-start.4
  106.7 0.9 copy-start.5
  112.0 1.7 copy-start.4
  115.2 0.9 copy-start.5
  120.6 1.7 copy-start.4
  123.7 0.9 copy-start.5
  129.1 1.7 copy-start.4
  132.3 0.9 copy-start.5
  137.6 1.7 copy-start.4
  140.8 0.9 copy-start.5
  146.1 1.7 copy-start.4
  149.3 0.9 copy-start.5
  155.4 35.5 %collective-permute-start.5 = (bf16[3,384,768]{2,1,0:T(8,128)(2,1)}, bf16[3,384,768]{2,1,0:T(8,128)(2,1)S(1)}, u32[]{:S(2)}, u32[]{:S(2)}) collective-permute-start(bf16[3,384,768]{2,1,0:T(8,128)(2,1)} %pad_maximum_fusion), channel_id=1, source_target_pairs={{0,4},{4,0},{8,12},{12,8},{16,20},{20,16},{24,28},{28,24},{1,5},{5... | collective-permute-start | bytes 5308424 | tf_op jit(solution)/shard_map/ppermute | solution.py:116
  187.2 3.6 %copy-start.2 = (bf16[4,512,384]{2,1,0:T(8,128)(2,1)S(1)}, bf16[4,512,384]{2,1,0:T(8,128)(2,1)}, u32[]{:S(2)}) copy-start(bf16[4,512,384]{2,1,0:T(8,128)(2,1)} %all-gather.5.cloned.1.call-done) | copy-start | bytes 4718596
  194.3 5.1 %copy-start.1 = (bf16[8,3,6144]{2,0,1:T(8,128)(2,1)S(1)}, bf16[8,3,6144]{2,0,1:T(8,128)(2,1)}, u32[]{:S(2)}) copy-start(bf16[8,3,6144]{2,0,1:T(8,128)(2,1)} %param.13) | copy-start | bytes 884740
Sparse Core Ops, SparseCore 0:
  9.2 57.6 all-gather.2
  152.7 34.4 all-gather.4

commit v2 on v1

--- a/solution.py
+++ b/solution.py
@@ -120,14 +120,17 @@
     mixed = (accum / totals[..., None]).astype(jnp.bfloat16)
     mixed = jnp.transpose(mixed, (1, 0, 2)).reshape(span, heads * HD)
 
-    gathered = lax.all_gather(mixed, "head", axis=0, tiled=False)
+    received = [
+        lax.ppermute(mixed, "head", [(i, (i + shift) % groups) for i in range(groups)])
+        for shift in range(1, groups)
+    ]
     columns = own_full.shape[1]
     half = columns // 2
     attn = jnp.dot(mixed, own_full, preferred_element_type=jnp.float32).astype(jnp.bfloat16).astype(jnp.float32)
     attn_mine = None
     attn_sib = None
     for shift in range(1, groups):
-        group_o = lax.dynamic_index_in_dim(gathered, (head - shift) % groups, 0, keepdims=False)
+        group_o = received[shift - 1]
         part = jnp.dot(group_o, mine[shift], preferred_element_type=jnp.float32)
         part = part.astype(jnp.bfloat16).astype(jnp.float32)
         attn_mine = part if attn_mine is None else attn_mine + part
@@ -139,7 +142,7 @@
     attn = attn + jnp.where(core == 0, other, swapped)
 
     offset = head * columns
-    input_cols = lax.dynamic_slice_in_dim(inputs, offset, columns, 1)
+    input_cols = lax.dynamic_slice_in_dim(activations, offset, columns, 1).astype(jnp.float32)
     gate_cols = lax.dynamic_slice_in_dim(modulation[2], offset, columns, 0)
     return input_cols + gate_cols[None, :] * attn
 

time: 210 us -> 208 us (level); the launches traced: 206 us -> 206 us
  other arithmetic: 25 us -> 16.1 us
  waiting for transfers between devices: 58.3 us -> 65.2 us
  starting transfers between devices: 7.26 us -> 9.97 us
  matrix products: 53.5 us -> 56.1 us
  local copies, waits for them, and re-layouts: 36.8 us -> 34.5 us
    ppermute x0 -> x3, waiting for transfers between devices: none -> 29.6 us  [local(): lax.ppermute(mixed, 'head', [(i, (i + shift) % groups) for i in range(gro...]
    all_gather x1 -> x0, waiting for transfers between devices: 22.4 us -> none  [local(): gathered = lax.all_gather(mixed, 'head', axis=0, tiled=False)]
    convert_element_type x1 -> x0, other arithmetic: 9.01 us -> none  [local(): inputs = activations.astype(jnp.float32)]
    dot_general x3, matrix products: 1.69 us -> 5.02 us  [local(): jnp.dot(group_o, sibling[shift - 1], preferred_element_type=jnp.float32)]
    ppermute x0 -> x3, starting transfers between devices: none -> 2.65 us  [local(): lax.ppermute(mixed, 'head', [(i, (i + shift) % groups) for i in range(gro...]
  transfers between devices with their start and end apart: 8 -> 10, of which waited for: 5 -> 6; matrix products, arithmetic and copies ran while one was open for 31% -> 44% of each run, Pallas kernels for 0% -> 0%
where the time goes in v2:
time: 208 us; the launch traced here: 206 us
  waiting for transfers between devices  65.2 us (31%)
  matrix products  56.1 us (27%)
  local copies, waits for them, and re-layouts  34.5 us (17%)
  other arithmetic  16.1 us (8%)
  between operations  13.7 us (7%)
  loops' own time  10.8 us (5%)
  starting transfers between devices  9.97 us (5%)
    ppermute x3, waiting for transfers between devices, local(): lax.ppermute(mixed, 'head', [(i, (i + shift) % groups) for i in range(gro...  29.6 us
    ppermute x2, waiting for transfers between devices, from_behind(): lax.ppermute(shard, axis, [(i, (i + by) % length) for i in range(length)])  27.9 us
    dot_general x1, matrix products, local(): jnp.einsum('td,dkh->tkh', hidden, w_qkv, preferred_element_type=jnp.float32)  19.6 us
    dot_general x9, matrix products, attend(): jnp.einsum('hqk,khd->hqd', weights.astype(jnp.bfloat16), span_values, pre...  13.6 us
    another operation x1, loops' own time, local(): state = lax.fori_loop(0, cache_len, turn, state)  10.8 us
    dynamic_slice x12, local copies, waits for them, and re-layouts, turn(): lax.dynamic_index_in_dim(piece, own_cache[place], 0, keepdims=False)  9.07 us
    ppermute x3, waiting for transfers between devices, fetch_out_weight(): lax.ppermute(block, 'head', [(i, (i + shift) % groups) for i in range(gro...  7.66 us
    dot_general x9, matrix products, attend(): jnp.einsum('qhd,khd->hqk', queries, span_keys, preferred_element_type=jnp...  7.44 us
  transfers between devices with their start and end apart: 10, of which 6 were waited for; matrix products, arithmetic and copies ran while one was open for 44% of the time, Pallas kernels for 0%

profile of v2, /device:TPU:9, one launch (start us, length us, event | category | flops | bytes accessed | tf_op | source)
XLA Modules:
  0.0 206.4 jit_solution(2108882084600631301)
XLA Ops:
  6.5 2.2 %copy.64 = bf16[1,512,2,384]{3,1,2,0:T(8,128)(2,1)} copy(bf16[1,512,2,384]{3,2,1,0:T(2,128)(2,1)} %param.20) | data formatting | bytes 1572864 | tf_op args[8]
  8.7 4.1 %fusion.12 = f32[512]{0:T(512)S(1)} fusion(bf16[512,6144]{1,0:T(8,128)(2,1)} %param.12), kind=kLoop, calls=%fused_computation.20 | loop fusion | flops 9436672 | bytes 6293504 | tf_op jit(solution)/shard_map/reduce_sum | solution.py:88
  14.4 19.6 %fusion.17 = f32[512,3,384]{0,2,1:T(8,128)} fusion(bf16[6144,3,384]{2,0,1:T(8,128)(2,1)} %param.17, bf16[512,6144]{1,0:T(8,128)(2,1)} %param.12, f32[6144]{0:T(1024)S(1)} %bitcast.165, f32[6144]{0:T(1024)S(1)} %bitcast.166, f32[512]{0:T(512)S(1)} %add_rsqrt_fusion.2), kind=kOutput, calls=%fused_computation.25 | convolution fusion | flops 7263485952 | bytes 22857728 | tf_op jit(solution)/shard_map/td,dkh->tkh/dot_general | solution.py:90
  35.3 1.4 slice.100
  38.2 1.8 collective-permute-start
  41.2 2.8 %constant_dynamic-slice_fusion.3 = (bf16[384,768]{1,0:T(8,128)(2,1)}, bf16[384,768]{1,0:T(8,128)(2,1)}, bf16[384,768]{1,0:T(8,128)(2,1)}) fusion(bf16[384,6144]{1,0:T(8,128)(2,1)} %param.21, s32[]{:T(128)S(6)} %select_n.112, s32[]{:T(128)S(6)} %select_n.110, s32[]{:T(128)S(6)} %select_n.108), kind=kLoop, calls=%fused_computation.105 | loop fusion | bytes 3538956 | tf_op jit(solution)/shard_map/dynamic_slice | solution.py:51
  46.4 1.5 collective-permute-start.4
  51.3 17.9 %collective-permute-done = bf16[512,2,384]{0,2,1:T(8,128)(2,1)} collective-permute-done((bf16[512,2,384]{0,2,1:T(8,128)(2,1)}, bf16[512,2,384]{0,2,1:T(8,128)(2,1)}, u32[]{:S(2)}, u32[]{:S(2)}) %collective-permute-start) | collective-permute-done | bytes 786464 | tf_op jit(solution)/shard_map/ppermute | solution.py:12
  70.4 10.0 %collective-permute-done.1 = bf16[512,2,384]{0,2,1:T(8,128)(2,1)} collective-permute-done((bf16[512,2,384]{0,2,1:T(8,128)(2,1)}, bf16[512,2,384]{0,2,1:T(8,128)(2,1)}, u32[]{:S(2)}, u32[]{:S(2)}) %collective-permute-start.1) | collective-permute-done | bytes 786464 | tf_op jit(solution)/shard_map/ppermute | solution.py:12
  86.7 1.5 fusion.46
  88.2 2.2 %fusion.55 = f32[3,512,128]{2,1,0:T(8,128)} fusion(f32[3,512,128]{2,1,0:T(8,128)S(1)} %fusion.37, f32[3,512,128]{2,1,0:T(8,128)S(1)} %fusion.46, bf16[512,3,128]{0,2,1:T(8,128)(2,1)S(1)} %bitcast.161, f32[3,512,512]{1,2,0:T(8,128)S(1)} %get-tuple-element.229, f32[3,512]{1,0:T(4,128)S(1)} %get-tuple-element.205, pred[512,512]{0,1:T(8,128)(4,1)S(1)} %bitcast.151, ...), kind=kOutput, calls=%fused_computation.68 | convolution fusion | flops 205848576 | bytes 6172672 | tf_op jit(solution)/shard_map/hqk,khd->hqd/dot_general | solution.py:35
  90.4 5.9 %collective-permute-done.3 = bf16[384,768]{1,0:T(8,128)(2,1)} collective-permute-done((bf16[384,768]{1,0:T(8,128)(2,1)}, bf16[384,768]{1,0:T(8,128)(2,1)}, u32[]{:S(2)}, u32[]{:S(2)}) %collective-permute-start.3) | collective-permute-done | bytes 589856 | tf_op jit(solution)/shard_map/ppermute | solution.py:53
  96.3 1.7 collective-permute-done.4
  98.1 2.8 %pad_maximum_fusion = bf16[3,384,768]{2,1,0:T(8,128)(2,1)} fusion(bf16[1,384,768]{2,1,0:T(8,128)(2,1)} %bitcast.31, bf16[1,384,768]{2,1,0:T(8,128)(2,1)} %bitcast.30, bf16[1,384,768]{2,1,0:T(8,128)(2,1)} %bitcast.29), kind=kLoop, calls=%fused_computation.48 | loop fusion | flops 1769472 | bytes 3538944 | tf_op jit(solution)/shard_map/stack | solution.py:117
  101.3 49.7 %while.17 = (s32[]{:T(128)}, f32[3,512]{1,0:T(4,128)S(1)}, f32[3,512]{1,0:T(4,128)S(1)}, f32[3,512,128]{2,1,0:T(8,128)}, s32[4,32]{1,0:T(4,128)S(1)}, /*index=5*...) while((s32[]{:T(128)}, f32[3,512]{1,0:T(4,128)S(1)}, ...), condition=%wide.region_12.13_spmd, body=%wide.region_9.12_spmd.sunk | while | flops 413273120 | bytes 24355468 | solution.py:114
  107.2 1.5 fusion.123
  115.5 1.5 fusion.123
  123.8 1.5 fusion.123
  132.1 1.5 fusion.123
  140.4 1.5 fusion.123
  148.7 1.5 fusion.123
  151.0 1.4 copy.67
  153.8 1.4 collective-permute-start.7
  155.2 7.9 %collective-permute-done.5 = bf16[512,384]{0,1:T(8,128)(2,1)S(1)} collective-permute-done((bf16[512,384]{0,1:T(8,128)(2,1)S(1)}, bf16[512,384]{0,1:T(8,128)(2,1)S(1)}, u32[]{:S(2)}, u32[]{:S(2)}) %collective-permute-start.5) | collective-permute-done | bytes 393248 | tf_op jit(solution)/shard_map/ppermute | solution.py:124
  163.1 1.7 convolution_convert_fusion.6
  164.8 21.7 %collective-permute-done.6 = bf16[512,384]{0,1:T(8,128)(2,1)S(1)} collective-permute-done((bf16[512,384]{0,1:T(8,128)(2,1)S(1)}, bf16[512,384]{0,1:T(8,128)(2,1)S(1)}, u32[]{:S(2)}, u32[]{:S(2)}) %collective-permute-start.6) | collective-permute-done | bytes 393248 | tf_op jit(solution)/shard_map/ppermute | solution.py:124
  186.5 1.7 convolution_convert_fusion.5
  188.2 1.7 convolution_convert_fusion.3
  189.8 1.7 convolution_convert_fusion.2
  191.5 1.7 convert_add_fusion.1
  193.2 1.7 convert_add_fusion
  194.9 4.6 %fusion.24 = f32[512,1536]{1,0:T(8,128)} fusion(f32[512,768]{1,0:T(8,128)S(1)} %convert_add_fusion, f32[512,768]{1,0:T(8,128)S(1)} %convert_add_fusion.1, bf16[512,384]{0,1:T(8,128)(2,1)S(1)} %bitcast.160, f32[1536]{0:T(1024)S(1)} %dynamic-slice_reduce_fusion, bf16[512,6144]{1,0:T(8,128)(2,1)} %param.12, s32[]{:T(128)S(6)} %select_n.100, pred[]{:T(512)S(6)} %eq.17, ...), kind=kOutput, calls=%fused_computation.32 | convolution fusion | flops 611057664 | bytes 9444864 | tf_op jit(solution)/shard_map/dot_general | solution.py:129
  (177 shorter events, 50.7 us)
Async XLA Ops:
  6.5 6.9 %copy-start = (bf16[8,3,6144]{2,0,1:T(8,128)(2,1)S(1)}, bf16[8,3,6144]{2,0,1:T(8,128)(2,1)}, u32[]{:S(2)}) copy-start(bf16[8,3,6144]{2,0,1:T(8,128)(2,1)} %param.13) | copy-start | bytes 884740
  6.5 94.7 %all-gather.2.cloned.1.call-start = ((), (), s32[]{:S(2)}) async-start(), calls=%async_computation | async-start | bytes 7077888 | tf_op jit(solution)/shard_map/all_gather | solution.py:81
  8.7 4.1 %copy-start.7 = (s32[8]{0:T(128)S(1)}, s32[8]{0:T(128)}, u32[]{:S(2)}) copy-start(s32[8]{0:T(128)} %param.14) | copy-start | bytes 100
  34.0 3.0 %copy-start.2 = (f32[512,3,384]{0,2,1:T(8,128)S(1)}, f32[512,3,384]{0,2,1:T(8,128)}, u32[]{:S(2)}) copy-start(f32[512,3,384]{0,2,1:T(8,128)} %fusion.17) | copy-start | bytes 7077892
  34.0 3.0 %copy-start.5 = (f32[384]{0:T(512)S(1)}, f32[384]{0:T(512)}, u32[]{:S(2)}) copy-start(f32[384]{0:T(512)} %param.19) | copy-start | bytes 4612
  38.2 31.0 %collective-permute-start = (bf16[512,2,384]{0,2,1:T(8,128)(2,1)}, bf16[512,2,384]{0,2,1:T(8,128)(2,1)}, u32[]{:S(2)}, u32[]{:S(2)}) collective-permute-start(bf16[512,2,384]{0,2,1:T(8,128)(2,1)} %pad_maximum_fusion.1), channel_id=1, source_target_pairs={{0,4},{4,8},{8,12},{12,16},{16,20},{20,24},{24,28},{28,0},{1,5},{5... | collective-permute-start | bytes 2359304 | tf_op jit(solution)/shard_map/ppermute | solution.py:12
  39.9 40.4 %collective-permute-start.1 = (bf16[512,2,384]{0,2,1:T(8,128)(2,1)}, bf16[512,2,384]{0,2,1:T(8,128)(2,1)}, u32[]{:S(2)}, u32[]{:S(2)}) collective-permute-start(bf16[512,2,384]{0,2,1:T(8,128)(2,1)} %pad_maximum_fusion.1), channel_id=1, source_target_pairs={{0,8},{4,12},{8,16},{12,20},{16,24},{20,28},{24,0},{28,4},{1,9},{5... | collective-permute-start | bytes 2359304 | tf_op jit(solution)/shard_map/ppermute | solution.py:12
  41.2 9.2 %copy-start.6 = (f32[384]{0:T(512)S(1)}, f32[384]{0:T(512)}, u32[]{:S(2)}) copy-start(f32[384]{0:T(512)} %param.18) | copy-start | bytes 4612
  44.0 46.5 %collective-permute-start.2 = (bf16[384,768]{1,0:T(8,128)(2,1)}, bf16[384,768]{1,0:T(8,128)(2,1)}, u32[]{:S(2)}, u32[]{:S(2)}) collective-permute-start(bf16[384,768]{1,0:T(8,128)(2,1)} %get-tuple-element.212), channel_id=1, source_target_pairs={{0,1},{1,2},{2,3},{3,0},{4,5},{5,6},{6,7},{7,4},{8,9},{9,10},{10,1... | collective-permute-start | bytes 1769480 | tf_op jit(solution)/shard_map/ppermute | solution.py:53
  45.3 51.1 %collective-permute-start.3 = (bf16[384,768]{1,0:T(8,128)(2,1)}, bf16[384,768]{1,0:T(8,128)(2,1)}, u32[]{:S(2)}, u32[]{:S(2)}) collective-permute-start(bf16[384,768]{1,0:T(8,128)(2,1)} %get-tuple-element.211), channel_id=1, source_target_pairs={{0,2},{1,3},{2,0},{3,1},{4,6},{5,7},{6,4},{7,5},{8,10},{9,11},{10,... | collective-permute-start | bytes 1769480 | tf_op jit(solution)/shard_map/ppermute | solution.py:53
  46.4 51.6 %collective-permute-start.4 = (bf16[384,768]{1,0:T(8,128)(2,1)}, bf16[384,768]{1,0:T(8,128)(2,1)}, u32[]{:S(2)}, u32[]{:S(2)}) collective-permute-start(bf16[384,768]{1,0:T(8,128)(2,1)} %get-tuple-element.210), channel_id=1, source_target_pairs={{0,3},{1,0},{2,1},{3,2},{4,7},{5,4},{6,5},{7,6},{8,11},{9,8},{10,9... | collective-permute-start | bytes 1769480 | tf_op jit(solution)/shard_map/ppermute | solution.py:53
  100.9 87.3 %collective-permute-start.8 = (bf16[3,384,768]{2,1,0:T(8,128)(2,1)}, bf16[3,384,768]{2,1,0:T(8,128)(2,1)}, u32[]{:S(2)}, u32[]{:S(2)}) collective-permute-start(bf16[3,384,768]{2,1,0:T(8,128)(2,1)} %pad_maximum_fusion), channel_id=1, source_target_pairs={{0,4},{4,0},{8,12},{12,8},{16,20},{20,16},{24,28},{28,24},{1,5},{5... | collective-permute-start | bytes 5308424 | tf_op jit(solution)/shard_map/ppermute | solution.py:116
  105.5 1.7 copy-start.3
  108.7 0.9 copy-start.4
  113.8 1.7 copy-start.3
  117.0 0.9 copy-start.4
  122.1 1.7 copy-start.3
  125.3 0.9 copy-start.4
  130.3 1.7 copy-start.3
  133.6 0.9 copy-start.4
  138.6 1.7 copy-start.3
  141.8 0.9 copy-start.4
  146.9 1.7 copy-start.3
  150.1 0.9 copy-start.4
  152.5 10.6 %collective-permute-start.5 = (bf16[512,384]{0,1:T(8,128)(2,1)S(1)}, bf16[512,384]{0,1:T(8,128)(2,1)S(1)}, u32[]{:S(2)}, u32[]{:S(2)}) collective-permute-start(bf16[512,384]{0,1:T(8,128)(2,1)S(1)} %bitcast.157), channel_id=1, source_target_pairs={{0,1},{1,2},{2,3},{3,0},{4,5},{5,6},{6,7},{7,4},{8,9},{9,10},{10,1... | collective-permute-start | bytes 1179656 | tf_op jit(solution)/shard_map/ppermute | solution.py:124
  152.6 33.9 %collective-permute-start.6 = (bf16[512,384]{0,1:T(8,128)(2,1)S(1)}, bf16[512,384]{0,1:T(8,128)(2,1)S(1)}, u32[]{:S(2)}, u32[]{:S(2)}) collective-permute-start(bf16[512,384]{0,1:T(8,128)(2,1)S(1)} %bitcast.158), channel_id=1, source_target_pairs={{0,2},{1,3},{2,0},{3,1},{4,6},{5,7},{6,4},{7,5},{8,10},{9,11},{10,... | collective-permute-start | bytes 1179656 | tf_op jit(solution)/shard_map/ppermute | solution.py:124
  153.8 37.7 %collective-permute-start.7 = (bf16[512,384]{0,1:T(8,128)(2,1)S(1)}, bf16[512,384]{0,1:T(8,128)(2,1)S(1)}, u32[]{:S(2)}, u32[]{:S(2)}) collective-permute-start(bf16[512,384]{0,1:T(8,128)(2,1)S(1)} %bitcast.159), channel_id=1, source_target_pairs={{0,3},{1,0},{2,1},{3,2},{4,7},{5,4},{6,5},{7,6},{8,11},{9,8},{10,9... | collective-permute-start | bytes 1179656 | tf_op jit(solution)/shard_map/ppermute | solution.py:124
  193.2 6.4 %copy-start.1 = (bf16[8,3,6144]{2,0,1:T(8,128)(2,1)S(1)}, bf16[8,3,6144]{2,0,1:T(8,128)(2,1)}, u32[]{:S(2)}) copy-start(bf16[8,3,6144]{2,0,1:T(8,128)(2,1)} %param.13) | copy-start | bytes 884740
Sparse Core Ops, SparseCore 0:
  9.2 58.7 all-gather.1

commit v3 on v2

--- a/solution.py
+++ b/solution.py
@@ -2,6 +2,8 @@
 import jax.numpy as jnp
 from jax import lax
 from jax.sharding import PartitionSpec as P
+from jax.experimental import pallas as pl
+from jax.experimental.pallas import tpu as pltpu
 
 HD = 128
 BLOCK = 128
@@ -39,6 +41,96 @@
         preferred_element_type=jnp.float32,
     )
     return (new_high, totals, accum)
+
+
+def flash_kernel(chosen, q_ref, lk_ref, lv_ref, pk_ref, pv_ref, bias_ref, o_ref, m_sc, l_sc, acc_sc, *, heads, n_local):
+    step = pl.program_id(0)
+    span = q_ref.shape[0]
+    blocks = bias_ref.shape[0]
+
+    @pl.when(step == 0)
+    def _():
+        m_sc[...] = jnp.full(m_sc.shape, -1e30, jnp.float32)
+        l_sc[...] = jnp.zeros(l_sc.shape, jnp.float32)
+        acc_sc[...] = jnp.zeros(acc_sc.shape, jnp.float32)
+
+    def body(k_ref, v_ref):
+        bias = bias_ref[...][:, None, :]
+        for h in range(heads):
+            cols = slice(h * HD, (h + 1) * HD)
+            q = q_ref[:, cols]
+            k = k_ref[:, cols]
+            s = lax.dot_general(q, k, (((1,), (1,)), ((), ())), preferred_element_type=jnp.float32)
+            s = (s * (1.0 / HD**0.5)).reshape(blocks, span // blocks, s.shape[1]) + bias
+            s = s.reshape(span, -1)
+            m_prev = m_sc[h]
+            m_new = jnp.maximum(m_prev, jnp.max(s, axis=1, keepdims=True))
+            factor = jnp.exp(m_prev - m_new)
+            p = jnp.exp(s - m_new)
+            l_sc[h] = l_sc[h] * factor + jnp.sum(p, axis=1, keepdims=True)
+            acc_sc[h] = acc_sc[h] * factor + jnp.dot(
+                p.astype(jnp.bfloat16), v_ref[:, cols], preferred_element_type=jnp.float32
+            )
+            m_sc[h] = m_new
+
+    @pl.when(step < n_local)
+    def _():
+        body(lk_ref, lv_ref)
+
+    @pl.when(step >= n_local)
+    def _():
+        body(pk_ref, pv_ref)
+
+    @pl.when(step == pl.num_programs(0) - 1)
+    def _():
+        for h in range(heads):
+            cols = slice(h * HD, (h + 1) * HD)
+            o_ref[:, cols] = (acc_sc[h] / l_sc[h]).astype(o_ref.dtype)
+
+
+def flash(queries, local_stack, piece, bias, chosen, heads):
+    span, width = queries.shape
+    n_local = local_stack.shape[0]
+    steps = n_local + chosen.shape[0]
+    blocks = bias.shape[1]
+
+    def local_map(kv):
+        return lambda j, c: (jnp.minimum(j, n_local - 1), 0, kv)
+
+    def pool_map(kv):
+        return lambda j, c: (c[jnp.maximum(j - n_local, 0)], 0, kv)
+
+    kv_block = (None, span, width)
+    grid_spec = pltpu.PrefetchScalarGridSpec(
+        num_scalar_prefetch=1,
+        grid=(steps,),
+        in_specs=[
+            pl.BlockSpec((span, width), lambda j, c: (0, 0)),
+            pl.BlockSpec(kv_block, local_map(0)),
+            pl.BlockSpec(kv_block, local_map(1)),
+            pl.BlockSpec(kv_block, pool_map(0)),
+            pl.BlockSpec(kv_block, pool_map(1)),
+            pl.BlockSpec((None, blocks, span), lambda j, c: (j, 0, 0)),
+        ],
+        out_specs=pl.BlockSpec((span, width), lambda j, c: (0, 0)),
+        scratch_shapes=[
+            pltpu.VMEM((heads, span, 1), jnp.float32),
+            pltpu.VMEM((heads, span, 1), jnp.float32),
+            pltpu.VMEM((heads, span, HD), jnp.float32),
+        ],
+    )
+    kernel = lambda *refs: flash_kernel(*refs, heads=heads, n_local=n_local)
+    return pl.pallas_call(
+        kernel,
+        grid_spec=grid_spec,
+        out_shape=jax.ShapeDtypeStruct((span, width), jnp.bfloat16),
+        compiler_params=pltpu.CompilerParams(dimension_semantics=("arbitrary",)),
+        cost_estimate=pl.CostEstimate(
+            flops=4 * steps * heads * span * span * HD,
+            transcendentals=steps * heads * span * span,
+            bytes_accessed=2 * steps * span * width * 2,
+        ),
+    )(chosen, queries, local_stack, local_stack, piece, piece, bias)
 
 
 def fetch_out_weight(w_out, head, core):
@@ -94,31 +186,21 @@
     local_kv = jnp.stack([keys.reshape(span, heads * HD), values], axis=1)
     own_mask = lax.dynamic_index_in_dim(block_mask, slot, 0, keepdims=False)
     own_cache = lax.dynamic_index_in_dim(cache_index, slot, 0, keepdims=False)
-    state = (
-        jnp.full((heads, span), -1e30, jnp.float32),
-        jnp.zeros((heads, span), jnp.float32),
-        jnp.zeros((heads, span, HD), jnp.float32),
-    )
     before = from_behind(local_kv, "slot", 1)
     earlier = from_behind(local_kv, "slot", 2)
-    state = attend(state, queries, local_kv, jnp.ones((blocks_q, blocks_q), jnp.int32))
-    state = attend(state, queries, before, own_mask[:, :blocks_q])
-    state = attend(state, queries, earlier, own_mask[:, blocks_q : 2 * blocks_q])
-    state, mine = lax.optimization_barrier((state, mine))
-
-    def turn(place, inner):
-        span_kv = lax.dynamic_index_in_dim(piece, own_cache[place], 0, keepdims=False)
-        visible_blocks = lax.dynamic_slice_in_dim(own_mask, (2 + place) * blocks_q, blocks_q, 1)
-        return attend(inner, queries, span_kv, visible_blocks)
-
-    state = lax.fori_loop(0, cache_len, turn, state)
+    width = heads * HD
+    local_stack = jnp.stack([local_kv, before, earlier]).reshape(3, span, 2 * width)
+    pool_flat = piece.reshape(piece.shape[0], span, 2 * width)
+    visible = jnp.concatenate([jnp.ones((blocks_q, blocks_q), jnp.int32), own_mask], axis=1)
+    visible = jnp.transpose(visible.reshape(blocks_q, 3 + cache_len, blocks_q), (1, 0, 2))
+    visible = jnp.repeat(visible, BLOCK, axis=2)
+    bias = jnp.where(visible > 0, 0.0, -1e30).astype(jnp.float32)
+    local_stack, mine = lax.optimization_barrier((local_stack, mine))
+    mixed = flash(queries.reshape(span, width), local_stack, pool_flat, bias, own_cache, heads)
     slots = lax.axis_size("slot")
     sibling = lax.ppermute(
         jnp.stack(mine[1:]), "slot", [(i, i ^ 1) for i in range(slots)]
     )
-    highest, totals, accum = state
-    mixed = (accum / totals[..., None]).astype(jnp.bfloat16)
-    mixed = jnp.transpose(mixed, (1, 0, 2)).reshape(span, heads * HD)
 
     received = [
         lax.ppermute(mixed, "head", [(i, (i + shift) % groups) for i in range(groups)])

time: 208 us -> 196 us (0.942)
  Pallas kernels: 0 us -> 36.4 us
  matrix products: 56.1 us -> 29.4 us
  local copies, waits for them, and re-layouts: 34.5 us -> 19.3 us
  loops' own time: 10.8 us -> 0 us
  waiting for transfers between devices: 65.2 us -> 72.6 us
  other arithmetic: 16.1 us -> 11 us
    pallas_call x0 -> x1, Pallas kernels: none -> 36.4 us  [flash(): pl.pallas_call(kernel, grid_spec=grid_spec, out_shape=jax.ShapeDtypeStruc...]
    dot_general x18 -> x0, matrix products: 21 us -> none  [the longest x9 13.6 us: attend(): jnp.einsum('hqk,khd->hqd', weights.astype(jnp.bfloat16), span_values, pre...]
    dynamic_slice x30 -> x0, local copies, waits for them, and re-layouts: 13.4 us -> none  [the longest x12 9.07 us: turn(): lax.dynamic_index_in_dim(piece, own_cache[place], 0, keepdims=False)]
    another operation x1 -> x0, loops' own time: 10.8 us -> none  [local(): state = lax.fori_loop(0, cache_len, turn, state)]
    while x43 -> x0, local copies, waits for them, and re-layouts: 7.09 us -> none
    reduce_sum x8 -> x0, other arithmetic: 7.08 us -> none  [attend(): totals = totals * factor + jnp.sum(weights, axis=-1)]
    reshape x0 -> x1, local copies, waits for them, and re-layouts: none -> 6.09 us  [local(): pool_flat = piece.reshape(piece.shape[0], span, 2 * width)]
    dot_general x1, matrix products: 19.6 us -> 13.9 us  [local(): jnp.einsum('td,dkh->tkh', hidden, w_qkv, preferred_element_type=jnp.float32)]
  transfers between devices with their start and end apart: 10 -> 10, of which waited for: 6 -> 6; matrix products, arithmetic and copies ran while one was open for 44% -> 25% of each run, Pallas kernels for 0% -> 19%
where the time goes in v3:
time: 196 us; the launch traced here: 194 us
  waiting for transfers between devices  72.6 us (37%)
  Pallas kernels  36.4 us (19%)
  matrix products  29.4 us (15%)
  local copies, waits for them, and re-layouts  19.3 us (10%)
  between operations  13.7 us (7%)
  starting transfers between devices  12 us (6%)
  other arithmetic  11 us (6%)
    pallas_call x1, Pallas kernels, flash(): pl.pallas_call(kernel, grid_spec=grid_spec, out_shape=jax.ShapeDtypeStruc...  36.4 us
    ppermute x3, waiting for transfers between devices, local(): lax.ppermute(mixed, 'head', [(i, (i + shift) % groups) for i in range(gro...  30.9 us
    ppermute x2, waiting for transfers between devices, from_behind(): lax.ppermute(shard, axis, [(i, (i + by) % length) for i in range(length)])  29 us
    dot_general x1, matrix products, local(): jnp.einsum('td,dkh->tkh', hidden, w_qkv, preferred_element_type=jnp.float32)  13.9 us
    ppermute x3, waiting for transfers between devices, fetch_out_weight(): lax.ppermute(block, 'head', [(i, (i + shift) % groups) for i in range(gro...  12.8 us
    reshape x1, local copies, waits for them, and re-layouts, local(): pool_flat = piece.reshape(piece.shape[0], span, 2 * width)  6.09 us
    dot_general x3, matrix products, local(): jnp.dot(group_o, sibling[shift - 1], preferred_element_type=jnp.float32)  4.95 us
    dot_general x3, matrix products, local(): part = jnp.dot(group_o, mine[shift], preferred_element_type=jnp.float32)  4.89 us
  transfers between devices with their start and end apart: 10, of which 6 were waited for; matrix products, arithmetic and copies ran while one was open for 25% of the time, Pallas kernels for 19%

profile of v3, /device:TPU:9, one launch (start us, length us, event | category | flops | bytes accessed | tf_op | source)
XLA Modules:
  0.0 194.3 jit_solution(10833296415221846484)
XLA Ops:
  6.5 2.2 %copy.33 = bf16[1,512,2,384]{3,1,2,0:T(8,128)(2,1)} copy(bf16[1,512,2,384]{3,2,1,0:T(2,128)(2,1)} %param.18) | data formatting | bytes 1572864 | tf_op args[8]
  9.4 0.9 fusion.20
  10.3 4.1 %fusion = f32[512]{0:T(512)S(1)} fusion(bf16[512,6144]{1,0:T(8,128)(2,1)} %param.10), kind=kLoop, calls=%fused_computation.2 | loop fusion | flops 9436672 | bytes 6293504 | tf_op jit(solution)/shard_map/reduce_sum | solution.py:180
  14.4 13.9 %fusion.5 = f32[512,3,384]{0,2,1:T(8,128)S(1)} fusion(bf16[6144,3,384]{2,0,1:T(8,128)(2,1)} %param.15, bf16[512,6144]{1,0:T(8,128)(2,1)} %param.10, f32[6144]{0:T(1024)S(1)} %bitcast.72, f32[6144]{0:T(1024)S(1)} %bitcast.73, f32[512]{0:T(512)S(1)} %add_rsqrt_fusion.2), kind=kOutput, calls=%fused_computation.7 | convolution fusion | flops 7263485952 | bytes 22857728 | tf_op jit(solution)/shard_map/td,dkh->tkh/dot_general | solution.py:182
  29.4 1.1 fusion.15
  30.6 1.3 collective-permute-start.1
  31.9 2.2 %collective-permute-start = (bf16[512,2,384]{0,2,1:T(8,128)(2,1)S(1)}, bf16[512,2,384]{0,2,1:T(8,128)(2,1)}, u32[]{:S(2)}, u32[]{:S(2)}) collective-permute-start(bf16[512,2,384]{0,2,1:T(8,128)(2,1)S(1)} %pad_maximum_fusion.2), channel_id=1, source_target_pairs={{0,4},{4,8},{8,12},{12,16},{16,20},{20,24},{24,28},{28,0},{1,5},{5... | collective-permute-start | bytes 2359304 | tf_op jit(solution)/shard_map/ppermute | solution.py:14
  34.1 2.7 %constant_dynamic-slice_fusion = (bf16[384,768]{1,0:T(8,128)(2,1)}, bf16[384,768]{1,0:T(8,128)(2,1)}, bf16[384,768]{1,0:T(8,128)(2,1)}) fusion(bf16[384,6144]{1,0:T(8,128)(2,1)} %param.19, s32[]{:T(128)S(6)} %select_n.69, s32[]{:T(128)S(6)} %select_n.67, s32[]{:T(128)S(6)} %select_n.65), kind=kLoop, calls=%fused_computation.47 | loop fusion | bytes 3538956 | tf_op jit(solution)/shard_map/dynamic_slice | solution.py:143
  36.9 2.4 %collective-permute-start.3 = (bf16[384,768]{1,0:T(8,128)(2,1)}, bf16[384,768]{1,0:T(8,128)(2,1)}, u32[]{:S(2)}, u32[]{:S(2)}) collective-permute-start(bf16[384,768]{1,0:T(8,128)(2,1)} %get-tuple-element.14), channel_id=1, source_target_pairs={{0,2},{1,3},{2,0},{3,1},{4,6},{5,7},{6,4},{7,5},{8,10},{9,11},{10,... | collective-permute-start | bytes 1769480 | tf_op jit(solution)/shard_map/ppermute | solution.py:145
  39.3 2.2 %collective-permute-start.2 = (bf16[384,768]{1,0:T(8,128)(2,1)}, bf16[384,768]{1,0:T(8,128)(2,1)}, u32[]{:S(2)}, u32[]{:S(2)}) collective-permute-start(bf16[384,768]{1,0:T(8,128)(2,1)} %get-tuple-element.15), channel_id=1, source_target_pairs={{0,1},{1,2},{2,3},{3,0},{4,5},{5,6},{6,7},{7,4},{8,9},{9,10},{10,1... | collective-permute-start | bytes 1769480 | tf_op jit(solution)/shard_map/ppermute | solution.py:145
  44.1 17.0 %collective-permute-done.1 = bf16[512,2,384]{0,2,1:T(8,128)(2,1)} collective-permute-done((bf16[512,2,384]{0,2,1:T(8,128)(2,1)S(1)}, bf16[512,2,384]{0,2,1:T(8,128)(2,1)}, u32[]{:S(2)}, u32[]{:S(2)}) %collective-permute-start.1) | collective-permute-done | bytes 786464 | tf_op jit(solution)/shard_map/ppermute | solution.py:14
  61.1 1.4 copy.40
  62.5 12.0 %collective-permute-done = bf16[512,2,384]{0,2,1:T(8,128)(2,1)} collective-permute-done((bf16[512,2,384]{0,2,1:T(8,128)(2,1)S(1)}, bf16[512,2,384]{0,2,1:T(8,128)(2,1)}, u32[]{:S(2)}, u32[]{:S(2)}) %collective-permute-start) | collective-permute-done | bytes 786464 | tf_op jit(solution)/shard_map/ppermute | solution.py:14
  74.5 1.4 copy.39
  75.9 1.7 pad_maximum_fusion.refs_2_.refs_3_
  78.0 12.4 %collective-permute-done.2 = bf16[384,768]{1,0:T(8,128)(2,1)} collective-permute-done((bf16[384,768]{1,0:T(8,128)(2,1)}, bf16[384,768]{1,0:T(8,128)(2,1)}, u32[]{:S(2)}, u32[]{:S(2)}) %collective-permute-start.2) | collective-permute-done | bytes 589856 | tf_op jit(solution)/shard_map/ppermute | solution.py:145
  90.4 2.8 %pad_maximum_fusion.1 = bf16[3,384,768]{2,1,0:T(8,128)(2,1)} fusion(bf16[1,384,768]{2,1,0:T(8,128)(2,1)} %bitcast.19, bf16[1,384,768]{2,1,0:T(8,128)(2,1)} %bitcast.18, bf16[1,384,768]{2,1,0:T(8,128)(2,1)} %bitcast.17), kind=kLoop, calls=%fused_computation.17 | loop fusion | flops 1769472 | bytes 3538944 | tf_op jit(solution)/shard_map/stack | solution.py:202
  93.7 1.2 fusion.23.refs_0_
  94.9 0.8 fusion.17.refs_1_
  95.8 6.1 %copy.42 = bf16[8,2,64,8,384]{4,3,1,2,0:T(8,128)(2,1)} copy(bf16[8,2,64,8,384]{4,3,2,1,0:T(8,128)(2,1)} %bitcast.64) | data formatting | bytes 12582912 | tf_op jit(solution)/shard_map/reshape | solution.py:193
  101.9 36.4 %shard_map.100 = bf16[512,384]{1,0:T(8,128)(2,1)} custom-call(s32[6]{0:T(128)} %fusion.23.refs_0_, bf16[512,384]{1,0:T(8,128)(2,1)} %fusion.17.refs_1_, bf16[3,512,768]{2,1,0:T(8,128)(2,1)} %pad_maximum_fusion.refs_2_.refs_3_, bf16[3,512,768]{2,1,0:T(8,128)(2,1)} %pad_maximum_fusion.refs_2_.refs_3_, bf16[8,512,768]{2,1,0:T(8,128)(2,1)} %bitcast.62, ...), custom_call_target="tpu_custom_call" | custom-call | flops 3623878656 | bytes 7077888 | tf_op jit(solution)/shard_map/pallas_call | solution.py:123
  138.2 2.2 %collective-permute-start.5 = (bf16[512,384]{1,0:T(8,128)(2,1)}, bf16[512,384]{1,0:T(8,128)(2,1)S(1)}, u32[]{:S(2)}, u32[]{:S(2)}) collective-permute-start(bf16[512,384]{1,0:T(8,128)(2,1)} %shard_map.100), channel_id=1, source_target_pairs={{0,1},{1,2},{2,3},{3,0},{4,5},{5,6},{6,7},{7,4},{8,9},{9,10},{10,1... | collective-permute-start | bytes 1179656 | tf_op jit(solution)/shard_map/ppermute | solution.py:206
  140.6 1.3 collective-permute-start.7
  141.9 23.9 %collective-permute-done.5 = bf16[512,384]{1,0:T(8,128)(2,1)S(1)} collective-permute-done((bf16[512,384]{1,0:T(8,128)(2,1)}, bf16[512,384]{1,0:T(8,128)(2,1)S(1)}, u32[]{:S(2)}, u32[]{:S(2)}) %collective-permute-start.5) | collective-permute-done | bytes 393248 | tf_op jit(solution)/shard_map/ppermute | solution.py:206
  165.8 1.6 convolution_convert_fusion.6
  167.5 6.9 %collective-permute-done.6 = bf16[512,384]{1,0:T(8,128)(2,1)S(1)} collective-permute-done((bf16[512,384]{1,0:T(8,128)(2,1)}, bf16[512,384]{1,0:T(8,128)(2,1)S(1)}, u32[]{:S(2)}, u32[]{:S(2)}) %collective-permute-start.6) | collective-permute-done | bytes 393248 | tf_op jit(solution)/shard_map/ppermute | solution.py:206
  174.4 1.6 convolution_convert_fusion.5
  176.1 1.6 convolution_convert_fusion.2
  177.7 1.6 convolution_convert_fusion.3
  179.3 1.6 convert_add_fusion.1
  181.0 1.7 convert_add_fusion
  182.7 4.8 %fusion.12 = f32[512,1536]{1,0:T(8,128)} fusion(f32[512,768]{1,0:T(8,128)S(1)} %convert_add_fusion, f32[512,768]{1,0:T(8,128)S(1)} %convert_add_fusion.1, bf16[512,384]{1,0:T(8,128)(2,1)S(1)} %copy-done.4, f32[1536]{0:T(1024)S(1)} %dynamic-slice_reduce_fusion, bf16[512,6144]{1,0:T(8,128)(2,1)} %param.10, s32[]{:T(128)S(6)} %select_n.61, pred[]{:T(512)S(6)} %eq.17, ...), kind=kOutput, calls=%fused_computation.14 | convolution fusion | flops 611057664 | bytes 9444864 | tf_op jit(solution)/shard_map/dot_general | solution.py:211
  (51 shorter events, 5.6 us)
Async XLA Ops:
  6.5 2.8 %copy-start = (bf16[8,3,6144]{2,0,1:T(8,128)(2,1)S(1)}, bf16[8,3,6144]{2,0,1:T(8,128)(2,1)}, u32[]{:S(2)}) copy-start(bf16[8,3,6144]{2,0,1:T(8,128)(2,1)} %param.11) | copy-start | bytes 884740
  6.5 2.2 %copy-start.7 = (s32[8]{0:T(128)S(1)}, s32[8]{0:T(128)}, u32[]{:S(2)}) copy-start(s32[8]{0:T(128)} %param.12) | copy-start | bytes 100
  6.5 89.2 %all-gather.2.cloned.1.call-start = ((), (), s32[]{:S(2)}) async-start(), calls=%async_computation | async-start | bytes 7077888 | tf_op jit(solution)/shard_map/all_gather | solution.py:173
  28.3 1.1 copy-start.5
  29.3 1.2 copy-start.3
  30.6 12.6 %copy-start.2 = (f32[512,1,384]{0,2,1:T(8,128)S(1)}, f32[512,1,384]{0,2,1:T(8,128)}, u32[]{:S(2)}) copy-start(f32[512,1,384]{0,2,1:T(8,128)} %get-tuple-element.17) | copy-start | bytes 2359300
  30.6 30.5 %collective-permute-start.1 = (bf16[512,2,384]{0,2,1:T(8,128)(2,1)S(1)}, bf16[512,2,384]{0,2,1:T(8,128)(2,1)}, u32[]{:S(2)}, u32[]{:S(2)}) collective-permute-start(bf16[512,2,384]{0,2,1:T(8,128)(2,1)S(1)} %pad_maximum_fusion.2), channel_id=1, source_target_pairs={{0,8},{4,12},{8,16},{12,20},{16,24},{20,28},{24,0},{28,4},{1,9},{5... | collective-permute-start | bytes 2359304 | tf_op jit(solution)/shard_map/ppermute | solution.py:14
  31.9 42.6 %collective-permute-start = (bf16[512,2,384]{0,2,1:T(8,128)(2,1)S(1)}, bf16[512,2,384]{0,2,1:T(8,128)(2,1)}, u32[]{:S(2)}, u32[]{:S(2)}) collective-permute-start(bf16[512,2,384]{0,2,1:T(8,128)(2,1)S(1)} %pad_maximum_fusion.2), channel_id=1, source_target_pairs={{0,4},{4,8},{8,12},{12,16},{16,20},{20,24},{24,28},{28,0},{1,5},{5... | collective-permute-start | bytes 2359304 | tf_op jit(solution)/shard_map/ppermute | solution.py:14
  36.8 40.8 %collective-permute-start.4 = (bf16[384,768]{1,0:T(8,128)(2,1)}, bf16[384,768]{1,0:T(8,128)(2,1)}, u32[]{:S(2)}, u32[]{:S(2)}) collective-permute-start(bf16[384,768]{1,0:T(8,128)(2,1)} %get-tuple-element.13), channel_id=1, source_target_pairs={{0,3},{1,0},{2,1},{3,2},{4,7},{5,4},{6,5},{7,6},{8,11},{9,8},{10,9... | collective-permute-start | bytes 1769480 | tf_op jit(solution)/shard_map/ppermute | solution.py:145
  36.9 41.1 %collective-permute-start.3 = (bf16[384,768]{1,0:T(8,128)(2,1)}, bf16[384,768]{1,0:T(8,128)(2,1)}, u32[]{:S(2)}, u32[]{:S(2)}) collective-permute-start(bf16[384,768]{1,0:T(8,128)(2,1)} %get-tuple-element.14), channel_id=1, source_target_pairs={{0,2},{1,3},{2,0},{3,1},{4,6},{5,7},{6,4},{7,5},{8,10},{9,11},{10,... | collective-permute-start | bytes 1769480 | tf_op jit(solution)/shard_map/ppermute | solution.py:145
  39.3 51.1 %collective-permute-start.2 = (bf16[384,768]{1,0:T(8,128)(2,1)}, bf16[384,768]{1,0:T(8,128)(2,1)}, u32[]{:S(2)}, u32[]{:S(2)}) collective-permute-start(bf16[384,768]{1,0:T(8,128)(2,1)} %get-tuple-element.15), channel_id=1, source_target_pairs={{0,1},{1,2},{2,3},{3,0},{4,5},{5,6},{6,7},{7,4},{8,9},{9,10},{10,1... | collective-permute-start | bytes 1769480 | tf_op jit(solution)/shard_map/ppermute | solution.py:145
  90.4 4.6 %copy-start.6 = (f32[384]{0:T(512)S(1)}, f32[384]{0:T(512)}, u32[]{:S(2)}) copy-start(f32[384]{0:T(512)} %param.16) | copy-start | bytes 4612
  93.2 82.8 %collective-permute-start.8 = (bf16[3,384,768]{2,1,0:T(8,128)(2,1)}, bf16[3,384,768]{2,1,0:T(8,128)(2,1)}, u32[]{:S(2)}, u32[]{:S(2)}) collective-permute-start(bf16[3,384,768]{2,1,0:T(8,128)(2,1)} %pad_maximum_fusion.1), channel_id=1, source_target_pairs={{0,4},{4,0},{8,12},{12,8},{16,20},{20,16},{24,28},{28,24},{1,5},{5... | collective-permute-start | bytes 5308424 | tf_op jit(solution)/shard_map/ppermute | solution.py:201
  138.2 27.6 %collective-permute-start.5 = (bf16[512,384]{1,0:T(8,128)(2,1)}, bf16[512,384]{1,0:T(8,128)(2,1)S(1)}, u32[]{:S(2)}, u32[]{:S(2)}) collective-permute-start(bf16[512,384]{1,0:T(8,128)(2,1)} %shard_map.100), channel_id=1, source_target_pairs={{0,1},{1,2},{2,3},{3,0},{4,5},{5,6},{6,7},{7,4},{8,9},{9,10},{10,1... | collective-permute-start | bytes 1179656 | tf_op jit(solution)/shard_map/ppermute | solution.py:206
  140.4 34.0 %collective-permute-start.6 = (bf16[512,384]{1,0:T(8,128)(2,1)}, bf16[512,384]{1,0:T(8,128)(2,1)S(1)}, u32[]{:S(2)}, u32[]{:S(2)}) collective-permute-start(bf16[512,384]{1,0:T(8,128)(2,1)} %shard_map.100), channel_id=1, source_target_pairs={{0,2},{1,3},{2,0},{3,1},{4,6},{5,7},{6,4},{7,5},{8,10},{9,11},{10,... | collective-permute-start | bytes 1179656 | tf_op jit(solution)/shard_map/ppermute | solution.py:206
  140.6 38.7 %collective-permute-start.7 = (bf16[512,384]{1,0:T(8,128)(2,1)}, bf16[512,384]{1,0:T(8,128)(2,1)S(1)}, u32[]{:S(2)}, u32[]{:S(2)}) collective-permute-start(bf16[512,384]{1,0:T(8,128)(2,1)} %shard_map.100), channel_id=1, source_target_pairs={{0,3},{1,0},{2,1},{3,2},{4,7},{5,4},{6,5},{7,6},{8,11},{9,8},{10,9... | collective-permute-start | bytes 1179656 | tf_op jit(solution)/shard_map/ppermute | solution.py:206
  181.0 1.7 copy-start.4
  182.7 4.8 %copy-start.1 = (bf16[8,3,6144]{2,0,1:T(8,128)(2,1)S(1)}, bf16[8,3,6144]{2,0,1:T(8,128)(2,1)}, u32[]{:S(2)}) copy-start(bf16[8,3,6144]{2,0,1:T(8,128)(2,1)} %param.11) | copy-start | bytes 884740
Sparse Core Ops, SparseCore 0:
  9.2 63.5 all-gather.1

commit v4 on v3

--- a/solution.py
+++ b/solution.py
@@ -170,7 +170,9 @@
     cache_len = cache_index.shape[1]
 
     own_full, mine = fetch_out_weight(w_out, head, core)
-    piece = lax.all_gather(pool_kv, "slot", axis=0, tiled=True)
+    slots = lax.axis_size("slot")
+    same_core = [pool_kv] + [from_behind(pool_kv, "slot", 2 * k) for k in range(1, slots // 2)]
+    same_core = jnp.concatenate(same_core, axis=0)
 
     onehot = (jnp.arange(mod_table.shape[0], dtype=jnp.int32) == step_index[slot]).astype(
         jnp.float32
@@ -181,11 +183,20 @@
     hidden = (normed * (1.0 + modulation[1][None, :]) + modulation[0][None, :]).astype(jnp.bfloat16)
     qkv = jnp.einsum("td,dkh->tkh", hidden, w_qkv, preferred_element_type=jnp.float32)
     queries = head_norm(qkv[:, 0], q_gain, heads).astype(jnp.bfloat16)
+    queries, same_core = lax.optimization_barrier((queries, same_core))
+    other_core = lax.ppermute(same_core, "slot", [(i, i ^ 1) for i in range(slots)])
+    piece = jnp.concatenate([same_core, other_core], axis=0)
     keys = head_norm(qkv[:, 1], k_gain, heads).astype(jnp.bfloat16)
     values = qkv[:, 2].astype(jnp.bfloat16)
     local_kv = jnp.stack([keys.reshape(span, heads * HD), values], axis=1)
     own_mask = lax.dynamic_index_in_dim(block_mask, slot, 0, keepdims=False)
     own_cache = lax.dynamic_index_in_dim(cache_index, slot, 0, keepdims=False)
+    sibling_slot = jnp.bitwise_xor(slot, 1)
+    own_cache = jnp.where(
+        own_cache % 2 == core,
+        ((slot - own_cache) % slots) // 2,
+        slots // 2 + ((sibling_slot - own_cache) % slots) // 2,
+    ).astype(jnp.int32)
     before = from_behind(local_kv, "slot", 1)
     earlier = from_behind(local_kv, "slot", 2)
     width = heads * HD
@@ -197,7 +208,6 @@
     bias = jnp.where(visible > 0, 0.0, -1e30).astype(jnp.float32)
     local_stack, mine = lax.optimization_barrier((local_stack, mine))
     mixed = flash(queries.reshape(span, width), local_stack, pool_flat, bias, own_cache, heads)
-    slots = lax.axis_size("slot")
     sibling = lax.ppermute(
         jnp.stack(mine[1:]), "slot", [(i, i ^ 1) for i in range(slots)]
     )

time: 196 us -> 221 us (1.13)
  other arithmetic: 11 us -> 31 us
  local copies, waits for them, and re-layouts: 19.3 us -> 33.7 us
  between operations: 13.7 us -> 0.23 us
  waiting for transfers between devices: 72.6 us -> 76.6 us
    concatenate x0 -> x2, other arithmetic: none -> 17.2 us  [the longest x1 10.2 us: local(): piece = jnp.concatenate([same_core, other_core], axis=0)]
    ppermute x3, waiting for transfers between devices: 12.8 us -> 24.6 us  [fetch_out_weight(): lax.ppermute(block, 'head', [(i, (i + shift) % groups) for i in range(gro...]
    reshape x1, local copies, waits for them, and re-layouts: 6.09 us -> 14.6 us  [local(): pool_flat = piece.reshape(piece.shape[0], span, 2 * width)]
    ppermute x2 -> x5, waiting for transfers between devices: 29 us -> 23.1 us  [from_behind(): lax.ppermute(shard, axis, [(i, (i + by) % length) for i in range(length)])]
    another operation x3, local copies, waits for them, and re-layouts: 3.08 us -> 6.9 us  [local(): jnp.stack([local_kv, before, earlier]).reshape(3, span, 2 * width)]
    ppermute x2 -> x5, starting transfers between devices: 3.47 us -> 5.84 us  [from_behind(): lax.ppermute(shard, axis, [(i, (i + by) % length) for i in range(length)])]
    ppermute x3, starting transfers between devices: 4.72 us -> 2.48 us  [fetch_out_weight(): lax.ppermute(block, 'head', [(i, (i + shift) % groups) for i in range(gro...]
    select_n x3, local copies, waits for them, and re-layouts: 0.76 us -> 2.99 us  [local(): bias = jnp.where(visible > 0, 0.0, -1e+30).astype(jnp.float32)]
  transfers between devices with their start and end apart: 10 -> 13, of which waited for: 6 -> 7; matrix products, arithmetic and copies ran while one was open for 25% -> 35% of each run, Pallas kernels for 19% -> 17%
where the time goes in v4:
time: 221 us; the launch traced here: 219 us
  waiting for transfers between devices  76.6 us (35%)
  Pallas kernels  36.4 us (16%)
  local copies, waits for them, and re-layouts  33.7 us (15%)
  other arithmetic  31 us (14%)
  matrix products  28.9 us (13%)
  starting transfers between devices  12.5 us (6%)
    pallas_call x1, Pallas kernels, flash(): pl.pallas_call(kernel, grid_spec=grid_spec, out_shape=jax.ShapeDtypeStruc...  36.4 us
    ppermute x3, waiting for transfers between devices, local(): lax.ppermute(mixed, 'head', [(i, (i + shift) % groups) for i in range(gro...  28.8 us
    ppermute x3, waiting for transfers between devices, fetch_out_weight(): lax.ppermute(block, 'head', [(i, (i + shift) % groups) for i in range(gro...  24.6 us
    ppermute x5, waiting for transfers between devices, from_behind(): lax.ppermute(shard, axis, [(i, (i + by) % length) for i in range(length)])  23.1 us
    reshape x1, local copies, waits for them, and re-layouts, local(): pool_flat = piece.reshape(piece.shape[0], span, 2 * width)  14.6 us
    dot_general x1, matrix products, local(): jnp.einsum('td,dkh->tkh', hidden, w_qkv, preferred_element_type=jnp.float32)  13.5 us
    concatenate x1, other arithmetic, local(): piece = jnp.concatenate([same_core, other_core], axis=0)  10.2 us
    concatenate x1, other arithmetic, local(): same_core = jnp.concatenate(same_core, axis=0)  7 us
  transfers between devices with their start and end apart: 13, of which 7 were waited for; matrix products, arithmetic and copies ran while one was open for 35% of the time, Pallas kernels for 17%

profile of v4, /device:TPU:9, one launch (start us, length us, event | category | flops | bytes accessed | tf_op | source)
XLA Modules:
  0.0 219.3 jit_solution(166674073335496496)
XLA Ops:
  1.2 1.2 collective-permute-start.1
  6.4 4.1 %fusion = f32[512]{0:T(512)S(1)} fusion(bf16[512,6144]{1,0:T(8,128)(2,1)} %param.10), kind=kLoop, calls=%fused_computation.2 | loop fusion | flops 9436672 | bytes 6293504 | tf_op jit(solution)/shard_map/reduce_sum | solution.py:182
  10.5 13.5 %fusion.5 = f32[512,3,384]{0,2,1:T(8,128)S(1)} fusion(bf16[6144,3,384]{2,0,1:T(8,128)(2,1)} %param.15, bf16[512,6144]{1,0:T(8,128)(2,1)} %param.10, f32[6144]{0:T(1024)S(1)} %bitcast.64, f32[6144]{0:T(1024)S(1)} %bitcast.65, f32[512]{0:T(512)S(1)} %add_rsqrt_fusion.2), kind=kOutput, calls=%fused_computation.7 | convolution fusion | flops 7263485952 | bytes 22857728 | tf_op jit(solution)/shard_map/td,dkh->tkh/dot_general | solution.py:184
  25.7 11.8 %collective-permute-done.1 = bf16[1,512,2,384]{3,2,1,0:T(2,128)(2,1)} collective-permute-done((bf16[1,512,2,384]{3,2,1,0:T(2,128)(2,1)}, bf16[1,512,2,384]{3,2,1,0:T(2,128)(2,1)}, u32[]{:S(2)}, u32[]{:S(2)}) %collective-permute-start.1) | collective-permute-done | bytes 786464 | tf_op jit(solution)/shard_map/ppermute | solution.py:14
  37.5 7.0 %pad_maximum_fusion.1 = bf16[4,512,2,384]{3,2,1,0:T(2,128)(2,1)S(1)} fusion(bf16[1,512,2,384]{3,2,1,0:T(2,128)(2,1)} %collective-permute-done.2, bf16[1,512,2,384]{3,2,1,0:T(2,128)(2,1)} %collective-permute-done.1, bf16[1,512,2,384]{3,2,1,0:T(2,128)(2,1)} %collective-permute-done, bf16[1,512,2,384]{3,2,1,0:T(2,128)(2,1)S(1)} %copy-done.3), kind=kLoop, calls=%fused_computation.12 | loop fusion | flops 4718592 | bytes 6291456 | tf_op jit(solution)/shard_map/concatenate | solution.py:175
  47.3 1.3 collective-permute-start.3
  49.6 2.7 %constant_dynamic-slice_fusion = (bf16[384,768]{1,0:T(8,128)(2,1)}, bf16[384,768]{1,0:T(8,128)(2,1)}, bf16[384,768]{1,0:T(8,128)(2,1)}) fusion(bf16[384,6144]{1,0:T(8,128)(2,1)} %param.19, s32[]{:T(128)S(6)} %select_n.100, s32[]{:T(128)S(6)} %select_n.98, s32[]{:T(128)S(6)} %select_n.96), kind=kLoop, calls=%fused_computation.54 | loop fusion | bytes 3538956 | tf_op jit(solution)/shard_map/dynamic_slice | solution.py:143
  52.3 1.3 collective-permute-start.5
  54.6 10.7 %collective-permute-done.3 = bf16[512,2,384]{0,2,1:T(8,128)(2,1)} collective-permute-done((bf16[512,2,384]{0,2,1:T(8,128)(2,1)}, bf16[512,2,384]{0,2,1:T(8,128)(2,1)}, u32[]{:S(2)}, u32[]{:S(2)}) %collective-permute-start.3) | collective-permute-done | bytes 786464 | tf_op jit(solution)/shard_map/ppermute | solution.py:14
  65.4 2.3 %copy.26 = bf16[1,512,768]{2,1,0:T(8,128)(2,1)} copy(bf16[1,512,768]{1,2,0:T(8,128)(2,1)} %bitcast.12) | data formatting | bytes 1572864 | tf_op jit(solution)/shard_map/stack | solution.py:203
  70.7 1.5 select_n.104.refs_6_
  72.2 1.3 compare_select_fusion.6.refs_0_
  73.5 2.3 %copy.27 = bf16[1,512,768]{2,1,0:T(8,128)(2,1)} copy(bf16[1,512,768]{1,2,0:T(8,128)(2,1)} %bitcast.13) | data formatting | bytes 1572864 | tf_op jit(solution)/shard_map/stack | solution.py:203
  76.4 2.3 %copy.28 = bf16[1,512,768]{2,1,0:T(8,128)(2,1)} copy(bf16[1,512,768]{1,2,0:T(8,128)(2,1)} %bitcast.14) | data formatting | bytes 1572864 | tf_op jit(solution)/shard_map/stack | solution.py:203
  78.7 3.3 %pad_maximum_fusion.2.refs_2_.refs_3_ = bf16[3,512,768]{2,1,0:T(8,128)(2,1)} fusion(bf16[1,512,768]{2,1,0:T(8,128)(2,1)} %copy.28, bf16[1,512,768]{2,1,0:T(8,128)(2,1)} %copy.27, bf16[1,512,768]{2,1,0:T(8,128)(2,1)} %copy.26), kind=kLoop, calls=%fused_computation.18 | loop fusion | flops 2359296 | bytes 4718592 | tf_op jit(solution)/shard_map/stack | solution.py:203
  82.0 22.6 %collective-permute-done.6 = bf16[384,768]{1,0:T(8,128)(2,1)} collective-permute-done((bf16[384,768]{1,0:T(8,128)(2,1)}, bf16[384,768]{1,0:T(8,128)(2,1)}, u32[]{:S(2)}, u32[]{:S(2)}) %collective-permute-start.6) | collective-permute-done | bytes 589856 | tf_op jit(solution)/shard_map/ppermute | solution.py:145
  104.6 2.0 collective-permute-done.7
  107.6 2.8 %pad_maximum_fusion.3 = bf16[3,384,768]{2,1,0:T(8,128)(2,1)} fusion(bf16[1,384,768]{2,1,0:T(8,128)(2,1)} %bitcast.19, bf16[1,384,768]{2,1,0:T(8,128)(2,1)} %bitcast.18, bf16[1,384,768]{2,1,0:T(8,128)(2,1)} %bitcast.17), kind=kLoop, calls=%fused_computation.19 | loop fusion | flops 1769472 | bytes 3538944 | tf_op jit(solution)/shard_map/stack | solution.py:212
  110.9 10.2 %pad_maximum_fusion = bf16[8,512,2,384]{3,2,1,0:T(2,128)(2,1)} fusion(bf16[4,512,2,384]{3,2,1,0:T(2,128)(2,1)} %collective-permute-done.8, bf16[4,512,2,384]{3,2,1,0:T(2,128)(2,1)S(1)} %pad_maximum_fusion.1), kind=kLoop, calls=%fused_computation.8 | loop fusion | flops 3145728 | bytes 12582912 | tf_op jit(solution)/shard_map/concatenate | solution.py:188
  121.1 14.6 %reshape.60.refs_4_.refs_5_ = bf16[8,512,768]{2,1,0:T(8,128)(2,1)} reshape(bf16[8,512,2,384]{3,2,1,0:T(2,128)(2,1)} %pad_maximum_fusion) | data formatting | bytes 12582912 | tf_op jit(solution)/shard_map/reshape | solution.py:204
  135.7 36.4 %shard_map.100 = bf16[512,384]{1,0:T(8,128)(2,1)} custom-call(s32[6]{0:T(128)} %compare_select_fusion.6.refs_0_, bf16[512,384]{1,0:T(8,128)(2,1)} %copy.23.refs_1_, bf16[3,512,768]{2,1,0:T(8,128)(2,1)} %pad_maximum_fusion.2.refs_2_.refs_3_, bf16[3,512,768]{2,1,0:T(8,128)(2,1)} %pad_maximum_fusion.2.refs_2_.refs_3_, ...), custom_call_target="tpu_custom_call" | custom-call | flops 3623878656 | bytes 7077888 | tf_op jit(solution)/shard_map/pallas_call | solution.py:123
  172.1 1.4 collective-permute-start.10
  174.2 1.7 collective-permute-start.11
  175.9 7.1 %collective-permute-done.9 = bf16[512,384]{1,0:T(8,128)(2,1)S(1)} collective-permute-done((bf16[512,384]{1,0:T(8,128)(2,1)}, bf16[512,384]{1,0:T(8,128)(2,1)S(1)}, u32[]{:S(2)}, u32[]{:S(2)}) %collective-permute-start.9) | collective-permute-done | bytes 393248 | tf_op jit(solution)/shard_map/ppermute | solution.py:216
  183.0 1.6 convolution_convert_fusion.6
  184.6 21.8 %collective-permute-done.10 = bf16[512,384]{1,0:T(8,128)(2,1)S(1)} collective-permute-done((bf16[512,384]{1,0:T(8,128)(2,1)}, bf16[512,384]{1,0:T(8,128)(2,1)S(1)}, u32[]{:S(2)}, u32[]{:S(2)}) %collective-permute-start.10) | collective-permute-done | bytes 393248 | tf_op jit(solution)/shard_map/ppermute | solution.py:216
  206.4 1.6 convolution_convert_fusion.5
  208.0 1.6 convolution_convert_fusion.3
  209.7 1.6 convolution_convert_fusion.2
  211.3 1.7 convert_add_fusion.1
  213.0 1.7 convert_add_fusion
  214.7 4.6 %fusion.12 = f32[512,1536]{1,0:T(8,128)} fusion(f32[512,768]{1,0:T(8,128)S(1)} %convert_add_fusion, f32[512,768]{1,0:T(8,128)S(1)} %convert_add_fusion.1, bf16[512,384]{1,0:T(8,128)(2,1)S(1)} %copy-done.4, f32[1536]{0:T(1024)S(1)} %dynamic-slice_reduce_fusion, bf16[512,6144]{1,0:T(8,128)(2,1)} %param.10, s32[]{:T(128)S(6)} %select_n.86, pred[]{:T(512)S(6)} %eq.29, ...), kind=kOutput, calls=%fused_computation.16 | convolution fusion | flops 611057664 | bytes 9444864 | tf_op jit(solution)/shard_map/dot_general | solution.py:221
  (51 shorter events, 17.3 us)
Async XLA Ops:
  0.0 4.8 %copy-start = (bf16[8,3,6144]{2,0,1:T(8,128)(2,1)S(1)}, bf16[8,3,6144]{2,0,1:T(8,128)(2,1)}, u32[]{:S(2)}) copy-start(bf16[8,3,6144]{2,0,1:T(8,128)(2,1)} %param.11) | copy-start | bytes 884740
  0.0 25.7 %collective-permute-start = (bf16[1,512,2,384]{3,2,1,0:T(2,128)(2,1)}, bf16[1,512,2,384]{3,2,1,0:T(2,128)(2,1)}, u32[]{:S(2)}, u32[]{:S(2)}) collective-permute-start(bf16[1,512,2,384]{3,2,1,0:T(2,128)(2,1)} %param.18), channel_id=1, source_target_pairs={{0,8},{4,12},{8,16},{12,20},{16,24},{20,28},{24,0},{28,4},{1,9},{5... | collective-permute-start | bytes 2359304 | tf_op jit(solution)/shard_map/ppermute | solution.py:14
  1.2 36.3 %collective-permute-start.1 = (bf16[1,512,2,384]{3,2,1,0:T(2,128)(2,1)}, bf16[1,512,2,384]{3,2,1,0:T(2,128)(2,1)}, u32[]{:S(2)}, u32[]{:S(2)}) collective-permute-start(bf16[1,512,2,384]{3,2,1,0:T(2,128)(2,1)} %param.18), channel_id=1, source_target_pairs={{0,16},{4,20},{8,24},{12,28},{16,0},{20,4},{24,8},{28,12},{1,17},{... | collective-permute-start | bytes 2359304 | tf_op jit(solution)/shard_map/ppermute | solution.py:14
  2.5 35.1 %collective-permute-start.2 = (bf16[1,512,2,384]{3,2,1,0:T(2,128)(2,1)}, bf16[1,512,2,384]{3,2,1,0:T(2,128)(2,1)}, u32[]{:S(2)}, u32[]{:S(2)}) collective-permute-start(bf16[1,512,2,384]{3,2,1,0:T(2,128)(2,1)} %param.18), channel_id=1, source_target_pairs={{0,24},{4,28},{8,0},{12,4},{16,8},{20,12},{24,16},{28,20},{1,25},{... | collective-permute-start | bytes 2359304 | tf_op jit(solution)/shard_map/ppermute | solution.py:14
  24.0 1.4 copy-start.2
  24.1 0.7 copy-start.5
  24.1 1.4 copy-start.6
  24.2 13.3 %copy-start.3 = (bf16[1,512,2,384]{3,2,1,0:T(2,128)(2,1)S(1)}, bf16[1,512,2,384]{3,2,1,0:T(2,128)(2,1)}, u32[]{:S(2)}) copy-start(bf16[1,512,2,384]{3,2,1,0:T(2,128)(2,1)} %param.18) | copy-start | bytes 2359300
  44.5 66.3 %collective-permute-start.8 = (bf16[4,512,2,384]{3,2,1,0:T(2,128)(2,1)S(1)}, bf16[4,512,2,384]{3,2,1,0:T(2,128)(2,1)}, u32[]{:S(2)}, u32[]{:S(2)}) collective-permute-start(bf16[4,512,2,384]{3,2,1,0:T(2,128)(2,1)S(1)} %pad_maximum_fusion.1), channel_id=1, source_target_pairs={{0,4},{4,0},{8,12},{12,8},{16,20},{20,16},{24,28},{28,24},{1,5},{5... | collective-permute-start | bytes 9437192 | tf_op jit(solution)/shard_map/ppermute | solution.py:187
  47.3 17.9 %collective-permute-start.3 = (bf16[512,2,384]{0,2,1:T(8,128)(2,1)}, bf16[512,2,384]{0,2,1:T(8,128)(2,1)}, u32[]{:S(2)}, u32[]{:S(2)}) collective-permute-start(bf16[512,2,384]{0,2,1:T(8,128)(2,1)} %pad_maximum_fusion.4), channel_id=1, source_target_pairs={{0,4},{4,8},{8,12},{12,16},{16,20},{20,24},{24,28},{28,0},{1,5},{5... | collective-permute-start | bytes 2359304 | tf_op jit(solution)/shard_map/ppermute | solution.py:14
  48.7 27.8 %collective-permute-start.4 = (bf16[512,2,384]{0,2,1:T(8,128)(2,1)}, bf16[512,2,384]{0,2,1:T(8,128)(2,1)}, u32[]{:S(2)}, u32[]{:S(2)}) collective-permute-start(bf16[512,2,384]{0,2,1:T(8,128)(2,1)} %pad_maximum_fusion.4), channel_id=1, source_target_pairs={{0,8},{4,12},{8,16},{12,20},{16,24},{20,28},{24,0},{28,4},{1,9},{5... | collective-permute-start | bytes 2359304 | tf_op jit(solution)/shard_map/ppermute | solution.py:14
  52.3 29.7 %collective-permute-start.5 = (bf16[384,768]{1,0:T(8,128)(2,1)}, bf16[384,768]{1,0:T(8,128)(2,1)}, u32[]{:S(2)}, u32[]{:S(2)}) collective-permute-start(bf16[384,768]{1,0:T(8,128)(2,1)} %get-tuple-element.19), channel_id=1, source_target_pairs={{0,1},{1,2},{2,3},{3,0},{4,5},{5,6},{6,7},{7,4},{8,9},{9,10},{10,1... | collective-permute-start | bytes 1769480 | tf_op jit(solution)/shard_map/ppermute | solution.py:145
  53.6 51.0 %collective-permute-start.6 = (bf16[384,768]{1,0:T(8,128)(2,1)}, bf16[384,768]{1,0:T(8,128)(2,1)}, u32[]{:S(2)}, u32[]{:S(2)}) collective-permute-start(bf16[384,768]{1,0:T(8,128)(2,1)} %get-tuple-element.18), channel_id=1, source_target_pairs={{0,2},{1,3},{2,0},{3,1},{4,6},{5,7},{6,4},{7,5},{8,10},{9,11},{10,... | collective-permute-start | bytes 1769480 | tf_op jit(solution)/shard_map/ppermute | solution.py:145
  65.3 41.4 %collective-permute-start.7 = (bf16[384,768]{1,0:T(8,128)(2,1)}, bf16[384,768]{1,0:T(8,128)(2,1)}, u32[]{:S(2)}, u32[]{:S(2)}) collective-permute-start(bf16[384,768]{1,0:T(8,128)(2,1)} %get-tuple-element.17), channel_id=1, source_target_pairs={{0,3},{1,0},{2,1},{3,2},{4,7},{5,4},{6,5},{7,6},{8,11},{9,8},{10,9... | collective-permute-start | bytes 1769480 | tf_op jit(solution)/shard_map/ppermute | solution.py:145
  110.4 97.6 %collective-permute-start.12 = (bf16[3,384,768]{2,1,0:T(8,128)(2,1)}, bf16[3,384,768]{2,1,0:T(8,128)(2,1)}, u32[]{:S(2)}, u32[]{:S(2)}) collective-permute-start(bf16[3,384,768]{2,1,0:T(8,128)(2,1)} %pad_maximum_fusion.3), channel_id=1, source_target_pairs={{0,4},{4,0},{8,12},{12,8},{16,20},{20,16},{24,28},{28,24},{1,5},{5... | collective-permute-start | bytes 5308424 | tf_op jit(solution)/shard_map/ppermute | solution.py:211
  172.1 10.9 %collective-permute-start.9 = (bf16[512,384]{1,0:T(8,128)(2,1)}, bf16[512,384]{1,0:T(8,128)(2,1)S(1)}, u32[]{:S(2)}, u32[]{:S(2)}) collective-permute-start(bf16[512,384]{1,0:T(8,128)(2,1)} %shard_map.100), channel_id=1, source_target_pairs={{0,1},{1,2},{2,3},{3,0},{4,5},{5,6},{6,7},{7,4},{8,9},{9,10},{10,1... | collective-permute-start | bytes 1179656 | tf_op jit(solution)/shard_map/ppermute | solution.py:216
  172.1 34.3 %collective-permute-start.10 = (bf16[512,384]{1,0:T(8,128)(2,1)}, bf16[512,384]{1,0:T(8,128)(2,1)S(1)}, u32[]{:S(2)}, u32[]{:S(2)}) collective-permute-start(bf16[512,384]{1,0:T(8,128)(2,1)} %shard_map.100), channel_id=1, source_target_pairs={{0,2},{1,3},{2,0},{3,1},{4,6},{5,7},{6,4},{7,5},{8,10},{9,11},{10,... | collective-permute-start | bytes 1179656 | tf_op jit(solution)/shard_map/ppermute | solution.py:216
  174.2 37.1 %collective-permute-start.11 = (bf16[512,384]{1,0:T(8,128)(2,1)}, bf16[512,384]{1,0:T(8,128)(2,1)S(1)}, u32[]{:S(2)}, u32[]{:S(2)}) collective-permute-start(bf16[512,384]{1,0:T(8,128)(2,1)} %shard_map.100), channel_id=1, source_target_pairs={{0,3},{1,0},{2,1},{3,2},{4,7},{5,4},{6,5},{7,6},{8,11},{9,8},{10,9... | collective-permute-start | bytes 1179656 | tf_op jit(solution)/shard_map/ppermute | solution.py:216
  211.3 3.4 %copy-start.4 = (bf16[512,384]{1,0:T(8,128)(2,1)S(1)}, bf16[512,384]{1,0:T(8,128)(2,1)}, u32[]{:S(2)}) copy-start(bf16[512,384]{1,0:T(8,128)(2,1)} %shard_map.100) | copy-start | bytes 1179652
  213.0 6.3 %copy-start.1 = (bf16[8,3,6144]{2,0,1:T(8,128)(2,1)S(1)}, bf16[8,3,6144]{2,0,1:T(8,128)(2,1)}, u32[]{:S(2)}) copy-start(bf16[8,3,6144]{2,0,1:T(8,128)(2,1)} %param.11) | copy-start | bytes 884740

commit v5 on v4

--- a/solution.py
+++ b/solution.py
@@ -43,7 +43,7 @@
     return (new_high, totals, accum)
 
 
-def flash_kernel(chosen, q_ref, lk_ref, lv_ref, pk_ref, pv_ref, bias_ref, o_ref, m_sc, l_sc, acc_sc, *, heads, n_local):
+def flash_kernel(chosen, q_ref, lk_ref, lv_ref, ak_ref, av_ref, bk_ref, bv_ref, bias_ref, o_ref, m_sc, l_sc, acc_sc, *, heads, n_local, half):
     step = pl.program_id(0)
     span = q_ref.shape[0]
     blocks = bias_ref.shape[0]
@@ -77,9 +77,15 @@
     def _():
         body(lk_ref, lv_ref)
 
-    @pl.when(step >= n_local)
-    def _():
-        body(pk_ref, pv_ref)
+    pos = chosen[jnp.maximum(step - n_local, 0)]
+
+    @pl.when((step >= n_local) & (pos < half))
+    def _():
+        body(ak_ref, av_ref)
+
+    @pl.when((step >= n_local) & (pos >= half))
+    def _():
+        body(bk_ref, bv_ref)
 
     @pl.when(step == pl.num_programs(0) - 1)
     def _():
@@ -88,17 +94,23 @@
             o_ref[:, cols] = (acc_sc[h] / l_sc[h]).astype(o_ref.dtype)
 
 
-def flash(queries, local_stack, piece, bias, chosen, heads):
+def flash(queries, local_stack, same_core, other_core, bias, chosen, heads):
     span, width = queries.shape
     n_local = local_stack.shape[0]
+    half = same_core.shape[0]
     steps = n_local + chosen.shape[0]
     blocks = bias.shape[1]
 
     def local_map(kv):
         return lambda j, c: (jnp.minimum(j, n_local - 1), 0, kv)
 
-    def pool_map(kv):
-        return lambda j, c: (c[jnp.maximum(j - n_local, 0)], 0, kv)
+    def pool_map(kv, upper):
+        def index(j, c):
+            pos = c[jnp.maximum(j - n_local, 0)]
+            hit = (j >= n_local) & ((pos >= half) == upper)
+            return (jnp.where(hit, pos - upper * half, 0), 0, kv)
+
+        return index
 
     kv_block = (None, span, width)
     grid_spec = pltpu.PrefetchScalarGridSpec(
@@ -108,8 +120,10 @@
             pl.BlockSpec((span, width), lambda j, c: (0, 0)),
             pl.BlockSpec(kv_block, local_map(0)),
             pl.BlockSpec(kv_block, local_map(1)),
-            pl.BlockSpec(kv_block, pool_map(0)),
-            pl.BlockSpec(kv_block, pool_map(1)),
+            pl.BlockSpec(kv_block, pool_map(0, False)),
+            pl.BlockSpec(kv_block, pool_map(1, False)),
+            pl.BlockSpec(kv_block, pool_map(0, True)),
+            pl.BlockSpec(kv_block, pool_map(1, True)),
             pl.BlockSpec((None, blocks, span), lambda j, c: (j, 0, 0)),
         ],
         out_specs=pl.BlockSpec((span, width), lambda j, c: (0, 0)),
@@ -119,7 +133,7 @@
             pltpu.VMEM((heads, span, HD), jnp.float32),
         ],
     )
-    kernel = lambda *refs: flash_kernel(*refs, heads=heads, n_local=n_local)
+    kernel = lambda *refs: flash_kernel(*refs, heads=heads, n_local=n_local, half=half)
     return pl.pallas_call(
         kernel,
         grid_spec=grid_spec,
@@ -130,7 +144,7 @@
             transcendentals=steps * heads * span * span,
             bytes_accessed=2 * steps * span * width * 2,
         ),
-    )(chosen, queries, local_stack, local_stack, piece, piece, bias)
+    )(chosen, queries, local_stack, local_stack, same_core, same_core, other_core, other_core, bias)
 
 
 def fetch_out_weight(w_out, head, core):
@@ -171,7 +185,8 @@
 
     own_full, mine = fetch_out_weight(w_out, head, core)
     slots = lax.axis_size("slot")
-    same_core = [pool_kv] + [from_behind(pool_kv, "slot", 2 * k) for k in range(1, slots // 2)]
+    pool_flat = pool_kv.reshape(1, pool_kv.shape[1], -1)
+    same_core = [pool_flat] + [from_behind(pool_flat, "slot", 2 * k) for k in range(1, slots // 2)]
     same_core = jnp.concatenate(same_core, axis=0)
 
     onehot = (jnp.arange(mod_table.shape[0], dtype=jnp.int32) == step_index[slot]).astype(
@@ -185,10 +200,9 @@
     queries = head_norm(qkv[:, 0], q_gain, heads).astype(jnp.bfloat16)
     queries, same_core = lax.optimization_barrier((queries, same_core))
     other_core = lax.ppermute(same_core, "slot", [(i, i ^ 1) for i in range(slots)])
-    piece = jnp.concatenate([same_core, other_core], axis=0)
     keys = head_norm(qkv[:, 1], k_gain, heads).astype(jnp.bfloat16)
     values = qkv[:, 2].astype(jnp.bfloat16)
-    local_kv = jnp.stack([keys.reshape(span, heads * HD), values], axis=1)
+    local_kv = jnp.concatenate([keys.reshape(span, heads * HD), values], axis=1)
     own_mask = lax.dynamic_index_in_dim(block_mask, slot, 0, keepdims=False)
     own_cache = lax.dynamic_index_in_dim(cache_index, slot, 0, keepdims=False)
     sibling_slot = jnp.bitwise_xor(slot, 1)
@@ -201,13 +215,12 @@
     earlier = from_behind(local_kv, "slot", 2)
     width = heads * HD
     local_stack = jnp.stack([local_kv, before, earlier]).reshape(3, span, 2 * width)
-    pool_flat = piece.reshape(piece.shape[0], span, 2 * width)
     visible = jnp.concatenate([jnp.ones((blocks_q, blocks_q), jnp.int32), own_mask], axis=1)
     visible = jnp.transpose(visible.reshape(blocks_q, 3 + cache_len, blocks_q), (1, 0, 2))
     visible = jnp.repeat(visible, BLOCK, axis=2)
     bias = jnp.where(visible > 0, 0.0, -1e30).astype(jnp.float32)
     local_stack, mine = lax.optimization_barrier((local_stack, mine))
-    mixed = flash(queries.reshape(span, width), local_stack, pool_flat, bias, own_cache, heads)
+    mixed = flash(queries.reshape(span, width), local_stack, same_core, other_core, bias, own_cache, heads)
     sibling = lax.ppermute(
         jnp.stack(mine[1:]), "slot", [(i, i ^ 1) for i in range(slots)]
     )

time: 221 us -> 211 us (0.955)
  other arithmetic: 31 us -> 20.8 us
  local copies, waits for them, and re-layouts: 33.7 us -> 24.4 us
  waiting for transfers between devices: 76.6 us -> 81.9 us
    reshape x1, local copies, waits for them, and re-layouts: 14.6 us -> 2.49 us  [local(): pool_flat = pool_kv.reshape(1, pool_kv.shape[1], -1)]
    concatenate x1 -> x0, other arithmetic: 10.2 us -> none  [local(): piece = jnp.concatenate([same_core, other_core], axis=0)]
    another operation x3 -> x0, local copies, waits for them, and re-layouts: 6.9 us -> none  [local(): jnp.stack([local_kv, before, earlier]).reshape(3, span, 2 * width)]
    dot_general x1, matrix products: 13.5 us -> 18.8 us  [local(): jnp.einsum('td,dkh->tkh', hidden, w_qkv, preferred_element_type=jnp.float32)]
    concatenate x1, other arithmetic: 7 us -> 1.81 us  [local(): same_core = jnp.concatenate(same_core, axis=0)]
    ppermute x5, waiting for transfers between devices: 23.1 us -> 27 us  [from_behind(): lax.ppermute(shard, axis, [(i, (i + by) % length) for i in range(length)])]
    dot_general x3, matrix products: 4.94 us -> 1.7 us  [local(): part = jnp.dot(group_o, mine[shift], preferred_element_type=jnp.float32)]
    mul x1 -> x2, local copies, waits for them, and re-layouts: 0.08 us -> 3.28 us  [head_norm(): shaped * lax.rsqrt(jnp.mean(shaped * shaped, axis=-1, keepdims=True) + 1e...]
  transfers between devices with their start and end apart: 13 -> 13, of which waited for: 7 -> 7; matrix products, arithmetic and copies ran while one was open for 35% -> 31% of each run, Pallas kernels for 17% -> 18%
where the time goes in v5:
time: 211 us; the launch traced here: 209 us
  waiting for transfers between devices  81.9 us (39%)
  Pallas kernels  37.5 us (18%)
  matrix products  31 us (15%)
  local copies, waits for them, and re-layouts  24.4 us (12%)
  other arithmetic  20.8 us (10%)
  starting transfers between devices  13.6 us (6%)
    pallas_call x1, Pallas kernels, flash(): pl.pallas_call(kernel, grid_spec=grid_spec, out_shape=jax.ShapeDtypeStruc...  37.5 us
    ppermute x3, waiting for transfers between devices, local(): lax.ppermute(mixed, 'head', [(i, (i + shift) % groups) for i in range(gro...  29 us
    ppermute x5, waiting for transfers between devices, from_behind(): lax.ppermute(shard, axis, [(i, (i + by) % length) for i in range(length)])  27 us
    ppermute x3, waiting for transfers between devices, fetch_out_weight(): lax.ppermute(block, 'head', [(i, (i + shift) % groups) for i in range(gro...  25.8 us
    dot_general x1, matrix products, local(): jnp.einsum('td,dkh->tkh', hidden, w_qkv, preferred_element_type=jnp.float32)  18.8 us
    ppermute x5, starting transfers between devices, from_behind(): lax.ppermute(shard, axis, [(i, (i + by) % length) for i in range(length)])  6.04 us
    another operation x2, other arithmetic, local(): jnp.stack([local_kv, before, earlier]).reshape(3, span, 2 * width)  5.35 us
    dot_general x3, matrix products, local(): jnp.dot(group_o, sibling[shift - 1], preferred_element_type=jnp.float32)  4.95 us
  transfers between devices with their start and end apart: 13, of which 7 were waited for; matrix products, arithmetic and copies ran while one was open for 31% of the time, Pallas kernels for 18%

profile of v5, /device:TPU:9, one launch (start us, length us, event | category | flops | bytes accessed | tf_op | source)
XLA Modules:
  0.0 209.5 jit_solution(9836005937487349825)
XLA Ops:
  0.0 2.5 %reshape.53 = bf16[1,512,768]{2,1,0:T(8,128)(2,1)S(1)} reshape(bf16[1,512,2,384]{3,2,1,0:T(2,128)(2,1)} %param.18) | data formatting | bytes 1572864 | tf_op jit(solution)/shard_map/reshape | solution.py:188
  9.0 4.1 %fusion = f32[512]{0:T(512)S(1)} fusion(bf16[512,6144]{1,0:T(8,128)(2,1)} %param.10), kind=kLoop, calls=%fused_computation.2 | loop fusion | flops 9436672 | bytes 6293504 | tf_op jit(solution)/shard_map/reduce_sum | solution.py:197
  13.1 18.8 %fusion.5 = f32[512,3,384]{0,2,1:T(8,128)} fusion(bf16[6144,3,384]{2,0,1:T(8,128)(2,1)} %param.15, bf16[512,6144]{1,0:T(8,128)(2,1)} %param.10, f32[6144]{0:T(1024)S(1)} %bitcast.72, f32[6144]{0:T(1024)S(1)} %bitcast.73, f32[512]{0:T(512)S(1)} %add_rsqrt_fusion.2), kind=kOutput, calls=%fused_computation.7 | convolution fusion | flops 7263485952 | bytes 22857728 | tf_op jit(solution)/shard_map/td,dkh->tkh/dot_general | solution.py:199
  31.9 2.4 %fusion.28 = (f32[512,1,384]{0,2,1:T(8,128)}, f32[512,1,384]{0,2,1:T(8,128)S(1)}) fusion(f32[512,3,384]{0,2,1:T(8,128)} %fusion.5), kind=kLoop, calls=%fused_computation.80 | loop fusion | bytes 3145728 | tf_op jit(solution)/shard_map/slice | solution.py:203
  35.4 4.5 %collective-permute-done.1 = bf16[1,512,768]{2,1,0:T(8,128)(2,1)} collective-permute-done((bf16[1,512,768]{2,1,0:T(8,128)(2,1)S(1)}, bf16[1,512,768]{2,1,0:T(8,128)(2,1)}, u32[]{:S(2)}, u32[]{:S(2)}) %collective-permute-start.1) | collective-permute-done | bytes 786464 | tf_op jit(solution)/shard_map/ppermute | solution.py:14
  39.9 1.8 pad_maximum_fusion.refs_4_.refs_5_
  42.4 1.6 slice.42
  44.0 2.3 %copy.25 = f32[512,1,384]{2,0,1:T(8,128)} copy(f32[512,1,384]{0,2,1:T(8,128)} %get-tuple-element.20) | data formatting | bytes 1572864
  46.3 2.3 %mul.121 = f32[512,1,384]{2,0,1:T(8,128)} multiply(f32[512,1,384]{2,0,1:T(8,128)} %copy.25, f32[512,1,384]{2,0,1:T(8,128)} %copy.25) | non-fusion elementwise | flops 196608 | bytes 2359296 | tf_op jit(solution)/shard_map/mul | solution.py:19
  48.6 2.3 %copy.18 = f32[512,1,384]{0,2,1:T(8,128)} copy(f32[512,1,384]{2,0,1:T(8,128)} %mul.121) | data formatting | bytes 1572864 | tf_op jit(solution)/shard_map/mul | solution.py:19
  53.2 2.3 %copy.19 = f32[512,384]{1,0:T(8,128)} copy(f32[512,384]{0,1:T(8,128)} %bitcast.64) | data formatting | bytes 1572864 | tf_op jit(solution)/shard_map/mul | solution.py:19
  56.4 1.5 fusion.15
  57.8 2.3 %fusion.27 = (bf16[1,512,768]{2,1,0:T(8,128)(2,1)}, bf16[512,768]{1,0:T(8,128)(2,1)}) fusion(bf16[512,384]{1,0:T(8,128)(2,1)} %bitcast.68, bf16[512,384]{1,0:T(8,128)(2,1)S(1)} %fusion.15), kind=kLoop, calls=%fused_computation.79 | loop fusion | flops 1572864 | bytes 2359296 | tf_op jit(solution)/shard_map/stack | solution.py:217
  60.1 1.5 collective-permute-start.3
  62.5 1.6 constant_dynamic-slice_fusion
  64.1 1.3 collective-permute-start.5
  66.6 12.2 %collective-permute-done.3 = bf16[512,768]{1,0:T(8,128)(2,1)} collective-permute-done((bf16[512,768]{1,0:T(8,128)(2,1)}, bf16[512,768]{1,0:T(8,128)(2,1)}, u32[]{:S(2)}, u32[]{:S(2)}) %collective-permute-start.3) | collective-permute-done | bytes 786464 | tf_op jit(solution)/shard_map/ppermute | solution.py:14
  78.9 10.4 %collective-permute-done.4 = bf16[512,768]{1,0:T(8,128)(2,1)} collective-permute-done((bf16[512,768]{1,0:T(8,128)(2,1)}, bf16[512,768]{1,0:T(8,128)(2,1)}, u32[]{:S(2)}, u32[]{:S(2)}) %collective-permute-start.4) | collective-permute-done | bytes 786464 | tf_op jit(solution)/shard_map/ppermute | solution.py:14
  89.2 3.1 %pad_maximum_fusion.1.refs_2_.refs_3_ = bf16[3,512,768]{2,1,0:T(8,128)(2,1)} fusion(bf16[1,512,768]{2,1,0:T(8,128)(2,1)} %bitcast.16, bf16[1,512,768]{2,1,0:T(8,128)(2,1)} %bitcast.15, bf16[1,512,768]{2,1,0:T(8,128)(2,1)S(1)} %copy-done.5), kind=kLoop, calls=%fused_computation.17 | loop fusion | flops 2359296 | bytes 4718592 | tf_op jit(solution)/shard_map/stack | solution.py:217
  92.3 24.2 %collective-permute-done.6 = bf16[384,768]{1,0:T(8,128)(2,1)S(1)} collective-permute-done((bf16[384,768]{1,0:T(8,128)(2,1)S(1)}, bf16[384,768]{1,0:T(8,128)(2,1)S(1)}, u32[]{:S(2)}, u32[]{:S(2)}) %collective-permute-start.6) | collective-permute-done | bytes 589856 | tf_op jit(solution)/shard_map/ppermute | solution.py:159
  116.5 1.7 collective-permute-done.7
  118.2 1.5 pad_maximum_fusion.2
  123.1 1.5 select_n.104.refs_8_
  126.8 37.5 %shard_map.100 = bf16[512,384]{1,0:T(8,128)(2,1)} custom-call(s32[6]{0:T(128)} %compare_select_fusion.6.refs_0_, bf16[512,384]{1,0:T(8,128)(2,1)} %copy.22.refs_1_, bf16[3,512,768]{2,1,0:T(8,128)(2,1)} %pad_maximum_fusion.1.refs_2_.refs_3_, bf16[3,512,768]{2,1,0:T(8,128)(2,1)} %pad_maximum_fusion.1.refs_2_.refs_3_, bf16[4,512,768]{2,1,0:T(8,128)(2,1)} %copy-done.2, ...), custom_call_target="tpu_custom_call" | custom-call | flops 3623878656 | bytes 7077888 | tf_op jit(solution)/shard_map/pallas_call | solution.py:137
  164.3 2.3 %collective-permute-start.10 = (bf16[512,384]{1,0:T(8,128)(2,1)}, bf16[512,384]{1,0:T(8,128)(2,1)S(1)}, u32[]{:S(2)}, u32[]{:S(2)}) collective-permute-start(bf16[512,384]{1,0:T(8,128)(2,1)} %shard_map.100), channel_id=1, source_target_pairs={{0,2},{1,3},{2,0},{3,1},{4,6},{5,7},{6,4},{7,5},{8,10},{9,11},{10,... | collective-permute-start | bytes 1179656 | tf_op jit(solution)/shard_map/ppermute | solution.py:229
  167.3 1.7 collective-permute-start.11
  169.0 6.2 %collective-permute-done.9 = bf16[512,384]{1,0:T(8,128)(2,1)S(1)} collective-permute-done((bf16[512,384]{1,0:T(8,128)(2,1)}, bf16[512,384]{1,0:T(8,128)(2,1)S(1)}, u32[]{:S(2)}, u32[]{:S(2)}) %collective-permute-start.9) | collective-permute-done | bytes 393248 | tf_op jit(solution)/shard_map/ppermute | solution.py:229
  175.8 22.8 %collective-permute-done.10 = bf16[512,384]{1,0:T(8,128)(2,1)S(1)} collective-permute-done((bf16[512,384]{1,0:T(8,128)(2,1)}, bf16[512,384]{1,0:T(8,128)(2,1)S(1)}, u32[]{:S(2)}, u32[]{:S(2)}) %collective-permute-start.10) | collective-permute-done | bytes 393248 | tf_op jit(solution)/shard_map/ppermute | solution.py:229
  199.2 1.6 convolution_convert_fusion.3
  200.8 1.6 convolution_convert_fusion.2
  203.1 1.7 convert_add_fusion
  204.8 4.7 %fusion.12 = f32[512,1536]{1,0:T(8,128)} fusion(f32[512,768]{1,0:T(8,128)S(1)} %convert_add_fusion, f32[512,768]{1,0:T(8,128)S(1)} %convert_add_fusion.1, bf16[512,384]{1,0:T(8,128)(2,1)S(1)} %copy-done.14, f32[1536]{0:T(1024)S(1)} %dynamic-slice_reduce_fusion, bf16[512,6144]{1,0:T(8,128)(2,1)} %param.10, s32[]{:T(128)S(6)} %select_n.86, pred[]{:T(512)S(6)} %eq.29, ...), kind=kOutput, calls=%fused_computation.15 | convolution fusion | flops 611057664 | bytes 9444864 | tf_op jit(solution)/shard_map/dot_general | solution.py:234
  (72 shorter events, 21.5 us)
Async XLA Ops:
  0.0 7.4 %copy-start = (bf16[8,3,6144]{2,0,1:T(8,128)(2,1)S(1)}, bf16[8,3,6144]{2,0,1:T(8,128)(2,1)}, u32[]{:S(2)}) copy-start(bf16[8,3,6144]{2,0,1:T(8,128)(2,1)} %param.11) | copy-start | bytes 884740
  2.5 10.6 %copy-start.3 = (bf16[1,512,768]{2,1,0:T(8,128)(2,1)}, bf16[1,512,768]{2,1,0:T(8,128)(2,1)S(1)}, u32[]{:S(2)}) copy-start(bf16[1,512,768]{2,1,0:T(8,128)(2,1)S(1)} %reshape.53) | copy-start | bytes 2359300
  2.5 32.9 %collective-permute-start = (bf16[1,512,768]{2,1,0:T(8,128)(2,1)S(1)}, bf16[1,512,768]{2,1,0:T(8,128)(2,1)S(1)}, u32[]{:S(2)}, u32[]{:S(2)}) collective-permute-start(bf16[1,512,768]{2,1,0:T(8,128)(2,1)S(1)} %reshape.53), channel_id=1, source_target_pairs={{0,8},{4,12},{8,16},{12,20},{16,24},{20,28},{24,0},{28,4},{1,9},{5... | collective-permute-start | bytes 2359304 | tf_op jit(solution)/shard_map/ppermute | solution.py:14
  3.8 36.1 %collective-permute-start.1 = (bf16[1,512,768]{2,1,0:T(8,128)(2,1)S(1)}, bf16[1,512,768]{2,1,0:T(8,128)(2,1)}, u32[]{:S(2)}, u32[]{:S(2)}) collective-permute-start(bf16[1,512,768]{2,1,0:T(8,128)(2,1)S(1)} %reshape.53), channel_id=1, source_target_pairs={{0,16},{4,20},{8,24},{12,28},{16,0},{20,4},{24,8},{28,12},{1,17},{... | collective-permute-start | bytes 2359304 | tf_op jit(solution)/shard_map/ppermute | solution.py:14
  5.0 34.9 %collective-permute-start.2 = (bf16[1,512,768]{2,1,0:T(8,128)(2,1)S(1)}, bf16[1,512,768]{2,1,0:T(8,128)(2,1)}, u32[]{:S(2)}, u32[]{:S(2)}) collective-permute-start(bf16[1,512,768]{2,1,0:T(8,128)(2,1)S(1)} %reshape.53), channel_id=1, source_target_pairs={{0,24},{4,28},{8,0},{12,4},{16,8},{20,12},{24,16},{28,20},{1,25},{... | collective-permute-start | bytes 2359304 | tf_op jit(solution)/shard_map/ppermute | solution.py:14
  31.9 2.6 %copy-start.15 = (f32[384]{0:T(512)S(1)}, f32[384]{0:T(512)}, u32[]{:S(2)}) copy-start(f32[384]{0:T(512)} %param.16) | copy-start | bytes 4612
  31.9 8.0 %copy-start.4 = (bf16[1,512,768]{2,1,0:T(8,128)(2,1)S(1)}, bf16[1,512,768]{2,1,0:T(8,128)(2,1)}, u32[]{:S(2)}) copy-start(bf16[1,512,768]{2,1,0:T(8,128)(2,1)} %copy-done.3) | copy-start | bytes 2359300
  35.4 4.5 %copy-start.13 = (bf16[1,512,768]{2,1,0:T(8,128)(2,1)}, bf16[1,512,768]{2,1,0:T(8,128)(2,1)S(1)}, u32[]{:S(2)}) copy-start(bf16[1,512,768]{2,1,0:T(8,128)(2,1)S(1)} %collective-permute-done) | copy-start | bytes 2359300
  41.7 6.9 %copy-start.2 = (bf16[4,512,768]{2,1,0:T(8,128)(2,1)}, bf16[4,512,768]{2,1,0:T(8,128)(2,1)S(1)}, u32[]{:S(2)}) copy-start(bf16[4,512,768]{2,1,0:T(8,128)(2,1)S(1)} %pad_maximum_fusion.refs_4_.refs_5_) | copy-start | bytes 9437188
  41.7 85.1 %collective-permute-start.8 = (bf16[4,512,768]{2,1,0:T(8,128)(2,1)S(1)}, bf16[4,512,768]{2,1,0:T(8,128)(2,1)}, u32[]{:S(2)}, u32[]{:S(2)}) collective-permute-start(bf16[4,512,768]{2,1,0:T(8,128)(2,1)S(1)} %pad_maximum_fusion.refs_4_.refs_5_), channel_id=1, source_target_pairs={{0,4},{4,0},{8,12},{12,8},{16,20},{20,16},{24,28},{28,24},{1,5},{5... | collective-permute-start | bytes 9437192 | tf_op jit(solution)/shard_map/ppermute | solution.py:202
  50.9 5.4 %copy-start.16 = (f32[384]{0:T(512)S(1)}, f32[384]{0:T(512)}, u32[]{:S(2)}) copy-start(f32[384]{0:T(512)} %param.17) | copy-start | bytes 4612
  60.1 18.6 %collective-permute-start.3 = (bf16[512,768]{1,0:T(8,128)(2,1)}, bf16[512,768]{1,0:T(8,128)(2,1)}, u32[]{:S(2)}, u32[]{:S(2)}) collective-permute-start(bf16[512,768]{1,0:T(8,128)(2,1)} %get-tuple-element.23), channel_id=1, source_target_pairs={{0,4},{4,8},{8,12},{12,16},{16,20},{20,24},{24,28},{28,0},{1,5},{5... | collective-permute-start | bytes 2359304 | tf_op jit(solution)/shard_map/ppermute | solution.py:14
  61.6 27.7 %collective-permute-start.4 = (bf16[512,768]{1,0:T(8,128)(2,1)}, bf16[512,768]{1,0:T(8,128)(2,1)}, u32[]{:S(2)}, u32[]{:S(2)}) collective-permute-start(bf16[512,768]{1,0:T(8,128)(2,1)} %get-tuple-element.23), channel_id=1, source_target_pairs={{0,8},{4,12},{8,16},{12,20},{16,24},{20,28},{24,0},{28,4},{1,9},{5... | collective-permute-start | bytes 2359304 | tf_op jit(solution)/shard_map/ppermute | solution.py:14
  62.5 26.8 %copy-start.5 = (bf16[1,512,768]{2,1,0:T(8,128)(2,1)S(1)}, bf16[1,512,768]{2,1,0:T(8,128)(2,1)}, u32[]{:S(2)}) copy-start(bf16[1,512,768]{2,1,0:T(8,128)(2,1)} %get-tuple-element.22) | copy-start | bytes 2359300
  64.1 28.2 %collective-permute-start.5 = (bf16[384,768]{1,0:T(8,128)(2,1)S(1)}, bf16[384,768]{1,0:T(8,128)(2,1)S(1)}, u32[]{:S(2)}, u32[]{:S(2)}) collective-permute-start(bf16[384,768]{1,0:T(8,128)(2,1)S(1)} %get-tuple-element.19), channel_id=1, source_target_pairs={{0,1},{1,2},{2,3},{3,0},{4,5},{5,6},{6,7},{7,4},{8,9},{9,10},{10,1... | collective-permute-start | bytes 1769480 | tf_op jit(solution)/shard_map/ppermute | solution.py:159
  65.5 51.1 %collective-permute-start.6 = (bf16[384,768]{1,0:T(8,128)(2,1)S(1)}, bf16[384,768]{1,0:T(8,128)(2,1)S(1)}, u32[]{:S(2)}, u32[]{:S(2)}) collective-permute-start(bf16[384,768]{1,0:T(8,128)(2,1)S(1)} %get-tuple-element.18), channel_id=1, source_target_pairs={{0,2},{1,3},{2,0},{3,1},{4,6},{5,7},{6,4},{7,5},{8,10},{9,11},{10,... | collective-permute-start | bytes 1769480 | tf_op jit(solution)/shard_map/ppermute | solution.py:159
  78.7 39.5 %collective-permute-start.7 = (bf16[384,768]{1,0:T(8,128)(2,1)S(1)}, bf16[384,768]{1,0:T(8,128)(2,1)S(1)}, u32[]{:S(2)}, u32[]{:S(2)}) collective-permute-start(bf16[384,768]{1,0:T(8,128)(2,1)S(1)} %get-tuple-element.17), channel_id=1, source_target_pairs={{0,3},{1,0},{2,1},{3,2},{4,7},{5,4},{6,5},{7,6},{8,11},{9,8},{10,9... | collective-permute-start | bytes 1769480 | tf_op jit(solution)/shard_map/ppermute | solution.py:159
  92.3 33.6 %copy-start.12 = (bf16[512,3,128]{0,2,1:T(8,128)(2,1)S(1)}, bf16[512,3,128]{0,2,1:T(8,128)(2,1)}, u32[]{:S(2)}) copy-start(bf16[512,3,128]{0,2,1:T(8,128)(2,1)} %multiply_convert_fusion) | copy-start | bytes 1179652
  92.3 27.3 %copy-start.8 = (bf16[384,768]{1,0:T(8,128)(2,1)}, bf16[384,768]{1,0:T(8,128)(2,1)S(1)}, u32[]{:S(2)}) copy-start(bf16[384,768]{1,0:T(8,128)(2,1)S(1)} %collective-permute-done.5) | copy-start | bytes 1769476
  116.5 1.7 copy-start.6
  118.2 1.5 copy-start.10
  119.7 79.5 %collective-permute-start.12 = (bf16[3,384,768]{2,1,0:T(8,128)(2,1)}, bf16[3,384,768]{2,1,0:T(8,128)(2,1)}, u32[]{:S(2)}, u32[]{:S(2)}) collective-permute-start(bf16[3,384,768]{2,1,0:T(8,128)(2,1)} %pad_maximum_fusion.2), channel_id=1, source_target_pairs={{0,4},{4,0},{8,12},{12,8},{16,20},{20,16},{24,28},{28,24},{1,5},{5... | collective-permute-start | bytes 5308424 | tf_op jit(solution)/shard_map/ppermute | solution.py:224
  126.8 48.4 %copy-start.9 = (bf16[384,768]{1,0:T(8,128)(2,1)S(1)}, bf16[384,768]{1,0:T(8,128)(2,1)}, u32[]{:S(2)}) copy-start(bf16[384,768]{1,0:T(8,128)(2,1)} %copy-done.8) | copy-start | bytes 1769476
  126.8 71.8 %copy-start.7 = (bf16[384,768]{1,0:T(8,128)(2,1)S(1)}, bf16[384,768]{1,0:T(8,128)(2,1)}, u32[]{:S(2)}) copy-start(bf16[384,768]{1,0:T(8,128)(2,1)} %copy-done.6) | copy-start | bytes 1769476
  164.3 10.9 %collective-permute-start.9 = (bf16[512,384]{1,0:T(8,128)(2,1)}, bf16[512,384]{1,0:T(8,128)(2,1)S(1)}, u32[]{:S(2)}, u32[]{:S(2)}) collective-permute-start(bf16[512,384]{1,0:T(8,128)(2,1)} %shard_map.100), channel_id=1, source_target_pairs={{0,1},{1,2},{2,3},{3,0},{4,5},{5,6},{6,7},{7,4},{8,9},{9,10},{10,1... | collective-permute-start | bytes 1179656 | tf_op jit(solution)/shard_map/ppermute | solution.py:229
  164.3 34.3 %collective-permute-start.10 = (bf16[512,384]{1,0:T(8,128)(2,1)}, bf16[512,384]{1,0:T(8,128)(2,1)S(1)}, u32[]{:S(2)}, u32[]{:S(2)}) collective-permute-start(bf16[512,384]{1,0:T(8,128)(2,1)} %shard_map.100), channel_id=1, source_target_pairs={{0,2},{1,3},{2,0},{3,1},{4,6},{5,7},{6,4},{7,5},{8,10},{9,11},{10,... | collective-permute-start | bytes 1179656 | tf_op jit(solution)/shard_map/ppermute | solution.py:229
  167.3 35.2 %collective-permute-start.11 = (bf16[512,384]{1,0:T(8,128)(2,1)}, bf16[512,384]{1,0:T(8,128)(2,1)S(1)}, u32[]{:S(2)}, u32[]{:S(2)}) collective-permute-start(bf16[512,384]{1,0:T(8,128)(2,1)} %shard_map.100), channel_id=1, source_target_pairs={{0,3},{1,0},{2,1},{3,2},{4,7},{5,4},{6,5},{7,6},{8,11},{9,8},{10,9... | collective-permute-start | bytes 1179656 | tf_op jit(solution)/shard_map/ppermute | solution.py:229
  175.8 26.7 %copy-start.11 = (bf16[384,768]{1,0:T(8,128)(2,1)S(1)}, bf16[384,768]{1,0:T(8,128)(2,1)}, u32[]{:S(2)}) copy-start(bf16[384,768]{1,0:T(8,128)(2,1)} %copy-done.10) | copy-start | bytes 1769476
  203.1 1.7 copy-start.14
  204.8 4.7 %copy-start.1 = (bf16[8,3,6144]{2,0,1:T(8,128)(2,1)S(1)}, bf16[8,3,6144]{2,0,1:T(8,128)(2,1)}, u32[]{:S(2)}) copy-start(bf16[8,3,6144]{2,0,1:T(8,128)(2,1)} %param.11) | copy-start | bytes 884740

commit v6 on v5

--- a/solution.py
+++ b/solution.py
@@ -197,8 +197,8 @@
     normed = inputs * lax.rsqrt(jnp.mean(inputs * inputs, axis=-1, keepdims=True) + 1e-06)
     hidden = (normed * (1.0 + modulation[1][None, :]) + modulation[0][None, :]).astype(jnp.bfloat16)
     qkv = jnp.einsum("td,dkh->tkh", hidden, w_qkv, preferred_element_type=jnp.float32)
+    qkv, same_core, mine = lax.optimization_barrier((qkv, same_core, mine))
     queries = head_norm(qkv[:, 0], q_gain, heads).astype(jnp.bfloat16)
-    queries, same_core = lax.optimization_barrier((queries, same_core))
     other_core = lax.ppermute(same_core, "slot", [(i, i ^ 1) for i in range(slots)])
     keys = head_norm(qkv[:, 1], k_gain, heads).astype(jnp.bfloat16)
     values = qkv[:, 2].astype(jnp.bfloat16)
@@ -219,7 +219,6 @@
     visible = jnp.transpose(visible.reshape(blocks_q, 3 + cache_len, blocks_q), (1, 0, 2))
     visible = jnp.repeat(visible, BLOCK, axis=2)
     bias = jnp.where(visible > 0, 0.0, -1e30).astype(jnp.float32)
-    local_stack, mine = lax.optimization_barrier((local_stack, mine))
     mixed = flash(queries.reshape(span, width), local_stack, same_core, other_core, bias, own_cache, heads)
     sibling = lax.ppermute(
         jnp.stack(mine[1:]), "slot", [(i, i ^ 1) for i in range(slots)]

time: 211 us -> 195 us (0.924)
  waiting for transfers between devices: 81.9 us -> 76.2 us
  matrix products: 31 us -> 25.9 us
  local copies, waits for them, and re-layouts: 24.4 us -> 20.7 us
  starting transfers between devices: 13.6 us -> 11.4 us
    dot_general x1, matrix products: 18.8 us -> 11.6 us  [local(): jnp.einsum('td,dkh->tkh', hidden, w_qkv, preferred_element_type=jnp.float32)]
    ppermute x3, waiting for transfers between devices: 29 us -> 23.1 us  [local(): lax.ppermute(mixed, 'head', [(i, (i + shift) % groups) for i in range(gro...]
    ppermute x5, waiting for transfers between devices: 27 us -> 32.5 us  [from_behind(): lax.ppermute(shard, axis, [(i, (i + by) % length) for i in range(length)])]
    ppermute x3, waiting for transfers between devices: 25.8 us -> 20.6 us  [fetch_out_weight(): lax.ppermute(block, 'head', [(i, (i + shift) % groups) for i in range(gro...]
    slice x2 -> x0, local copies, waits for them, and re-layouts: 4.07 us -> none  [the longest x1 2.45 us: local(): keys = head_norm(qkv[:, 1], k_gain, heads).astype(jnp.bfloat16)]
    mul x2 -> x4, local copies, waits for them, and re-layouts: 3.28 us -> 6.57 us  [head_norm(): shaped * lax.rsqrt(jnp.mean(shaped * shaped, axis=-1, keepdims=True) + 1e...]
    unnamed x36 -> x30, local copies, waits for them, and re-layouts: 3.3 us -> 0.94 us
    mul x1 -> x2, local copies, waits for them, and re-layouts: 2.3 us -> 4.58 us  [head_norm(): shaped * shaped]
  transfers between devices with their start and end apart: 13 -> 13, of which waited for: 7 -> 8; matrix products, arithmetic and copies ran while one was open for 31% -> 30% of each run, Pallas kernels for 18% -> 19%
where the time goes in v6:
time: 195 us; the launch traced here: 193 us
  waiting for transfers between devices  76.2 us (39%)
  Pallas kernels  37.4 us (19%)
  matrix products  25.9 us (13%)
  other arithmetic  21.4 us (11%)
  local copies, waits for them, and re-layouts  20.7 us (11%)
  starting transfers between devices  11.4 us (6%)
    pallas_call x1, Pallas kernels, flash(): pl.pallas_call(kernel, grid_spec=grid_spec, out_shape=jax.ShapeDtypeStruc...  37.4 us
    ppermute x5, waiting for transfers between devices, from_behind(): lax.ppermute(shard, axis, [(i, (i + by) % length) for i in range(length)])  32.5 us
    ppermute x3, waiting for transfers between devices, local(): lax.ppermute(mixed, 'head', [(i, (i + shift) % groups) for i in range(gro...  23.1 us
    ppermute x3, waiting for transfers between devices, fetch_out_weight(): lax.ppermute(block, 'head', [(i, (i + shift) % groups) for i in range(gro...  20.6 us
    dot_general x1, matrix products, local(): jnp.einsum('td,dkh->tkh', hidden, w_qkv, preferred_element_type=jnp.float32)  11.6 us
    mul x4, local copies, waits for them, and re-layouts, head_norm(): shaped * lax.rsqrt(jnp.mean(shaped * shaped, axis=-1, keepdims=True) + 1e...  6.57 us
    ppermute x5, starting transfers between devices, from_behind(): lax.ppermute(shard, axis, [(i, (i + by) % length) for i in range(length)])  5.06 us
    dot_general x3, matrix products, local(): jnp.dot(group_o, sibling[shift - 1], preferred_element_type=jnp.float32)  4.95 us
  transfers between devices with their start and end apart: 13, of which 8 were waited for; matrix products, arithmetic and copies ran while one was open for 30% of the time, Pallas kernels for 19%

profile of v6, /device:TPU:9, one launch (start us, length us, event | category | flops | bytes accessed | tf_op | source)
XLA Modules:
  0.0 193.3 jit_solution(16942760398801755567)
XLA Ops:
  0.0 2.5 %reshape.56 = bf16[1,512,768]{2,1,0:T(8,128)(2,1)S(1)} reshape(bf16[1,512,2,384]{3,2,1,0:T(2,128)(2,1)} %param.18) | data formatting | bytes 1572864 | tf_op jit(solution)/shard_map/reshape | solution.py:188
  6.2 2.7 %constant_dynamic-slice_fusion = (bf16[384,768]{1,0:T(8,128)(2,1)}, bf16[384,768]{1,0:T(8,128)(2,1)}, bf16[384,768]{1,0:T(8,128)(2,1)}) fusion(bf16[384,6144]{1,0:T(8,128)(2,1)} %param.19, s32[]{:T(128)S(6)} %select_n.100, s32[]{:T(128)S(6)} %select_n.98, s32[]{:T(128)S(6)} %select_n.96), kind=kLoop, calls=%fused_computation.56 | loop fusion | bytes 3538956 | tf_op jit(solution)/shard_map/dynamic_slice | solution.py:157
  8.9 1.3 collective-permute-start.3
  12.7 4.2 %fusion = f32[512]{0:T(512)S(1)} fusion(bf16[512,6144]{1,0:T(8,128)(2,1)} %param.10), kind=kLoop, calls=%fused_computation.2 | loop fusion | flops 9436672 | bytes 6293504 | tf_op jit(solution)/shard_map/reduce_sum | solution.py:197
  17.1 4.9 %collective-permute-done = bf16[1,512,768]{2,1,0:T(8,128)(2,1)S(1)} collective-permute-done((bf16[1,512,768]{2,1,0:T(8,128)(2,1)S(1)}, bf16[1,512,768]{2,1,0:T(8,128)(2,1)S(1)}, u32[]{:S(2)}, u32[]{:S(2)}) %collective-permute-start) | collective-permute-done | bytes 786464 | tf_op jit(solution)/shard_map/ppermute | solution.py:14
  22.3 11.6 %fusion.5 = f32[512,3,384]{2,0,1:T(8,128)S(1)} fusion(bf16[6144,3,384]{2,0,1:T(8,128)(2,1)} %param.15, bf16[512,6144]{1,0:T(8,128)(2,1)S(1)} %copy-done.3, f32[6144]{0:T(1024)S(1)} %bitcast.72, f32[6144]{0:T(1024)S(1)} %bitcast.73, f32[512]{0:T(512)S(1)} %add_rsqrt_fusion.2), kind=kOutput, calls=%fused_computation.7 | convolution fusion | flops 7263485952 | bytes 22857728 | tf_op jit(solution)/shard_map/td,dkh->tkh/dot_general | solution.py:199
  33.9 6.0 %collective-permute-done.1 = bf16[1,512,768]{2,1,0:T(8,128)(2,1)S(1)} collective-permute-done((bf16[1,512,768]{2,1,0:T(8,128)(2,1)S(1)}, bf16[1,512,768]{2,1,0:T(8,128)(2,1)S(1)}, u32[]{:S(2)}, u32[]{:S(2)}) %collective-permute-start.1) | collective-permute-done | bytes 786464 | tf_op jit(solution)/shard_map/ppermute | solution.py:14
  40.8 1.8 pad_maximum_fusion.refs_4_.refs_5_
  42.6 16.9 %collective-permute-done.4 = bf16[384,768]{1,0:T(8,128)(2,1)} collective-permute-done((bf16[384,768]{1,0:T(8,128)(2,1)}, bf16[384,768]{1,0:T(8,128)(2,1)}, u32[]{:S(2)}, u32[]{:S(2)}) %collective-permute-start.4) | collective-permute-done | bytes 589856 | tf_op jit(solution)/shard_map/ppermute | solution.py:159
  59.6 3.6 %collective-permute-done.5 = bf16[384,768]{1,0:T(8,128)(2,1)S(1)} collective-permute-done((bf16[384,768]{1,0:T(8,128)(2,1)}, bf16[384,768]{1,0:T(8,128)(2,1)S(1)}, u32[]{:S(2)}, u32[]{:S(2)}) %collective-permute-start.5) | collective-permute-done | bytes 589856 | tf_op jit(solution)/shard_map/ppermute | solution.py:159
  63.7 1.3 slice_multiply_fusion
  65.0 2.3 %copy.12 = f32[512,1,384]{0,2,1:T(8,128)} copy(f32[512,1,384]{2,0,1:T(8,128)} %get-tuple-element.21) | data formatting | bytes 1572864 | tf_op jit(solution)/shard_map/mul | solution.py:19
  69.5 2.3 %copy.13 = f32[512,384]{1,0:T(8,128)} copy(f32[512,384]{0,1:T(8,128)} %bitcast.67) | data formatting | bytes 1572864 | tf_op jit(solution)/shard_map/mul | solution.py:19
  71.7 2.3 %copy.14 = f32[512,1,384]{0,2,1:T(8,128)} copy(f32[512,1,384]{2,0,1:T(8,128)} %get-tuple-element.20) | data formatting | bytes 1572864 | tf_op jit(solution)/shard_map/mul | solution.py:19
  76.3 2.3 %copy.15 = f32[512,384]{1,0:T(8,128)} copy(f32[512,384]{0,1:T(8,128)} %bitcast.68) | data formatting | bytes 1572864 | tf_op jit(solution)/shard_map/mul | solution.py:19
  79.8 2.8 %fusion.15 = (bf16[512,384]{1,0:T(8,128)(2,1)S(1)}, bf16[512,384]{1,0:T(8,128)(2,1)}) fusion(f32[512,384]{1,0:T(8,128)} %copy.15, f32[512,3,384]{2,0,1:T(8,128)} %copy-done.4, f32[384]{0:T(512)S(1)} %copy-done.12, f32[384]{0:T(512)S(1)} %copy-done.13, f32[512,384]{1,0:T(8,128)} %copy.13), kind=kLoop, calls=%fused_computation.32 | loop fusion | flops 1179648 | bytes 3935232 | tf_op jit(solution)/shard_map/convert_element_type | solution.py:203
  85.2 2.9 %pad_maximum_fusion.2 = bf16[3,384,768]{2,1,0:T(8,128)(2,1)} fusion(bf16[1,384,768]{2,1,0:T(8,128)(2,1)} %bitcast.69, bf16[1,384,768]{2,1,0:T(8,128)(2,1)} %bitcast.20, bf16[1,384,768]{2,1,0:T(8,128)(2,1)} %bitcast.19), kind=kLoop, calls=%fused_computation.18 | loop fusion | flops 1769472 | bytes 3538944 | tf_op jit(solution)/shard_map/stack | solution.py:224
  89.8 1.3 compare_select_fusion.6.refs_0_
  91.0 9.8 %collective-permute-done.6 = bf16[512,768]{1,0:T(8,128)(2,1)} collective-permute-done((bf16[512,768]{1,0:T(8,128)(2,1)}, bf16[512,768]{1,0:T(8,128)(2,1)}, u32[]{:S(2)}, u32[]{:S(2)}) %collective-permute-start.6) | collective-permute-done | bytes 786464 | tf_op jit(solution)/shard_map/ppermute | solution.py:14
  100.8 11.9 %collective-permute-done.7 = bf16[512,768]{1,0:T(8,128)(2,1)} collective-permute-done((bf16[512,768]{1,0:T(8,128)(2,1)}, bf16[512,768]{1,0:T(8,128)(2,1)}, u32[]{:S(2)}, u32[]{:S(2)}) %collective-permute-start.7) | collective-permute-done | bytes 786464 | tf_op jit(solution)/shard_map/ppermute | solution.py:14
  112.7 3.3 %pad_maximum_fusion.1.refs_2_.refs_3_ = bf16[3,512,768]{2,1,0:T(8,128)(2,1)} fusion(bf16[1,512,768]{2,1,0:T(8,128)(2,1)} %bitcast.16, bf16[1,512,768]{2,1,0:T(8,128)(2,1)} %bitcast.15, bf16[1,512,768]{2,1,0:T(8,128)(2,1)} %get-tuple-element.22), kind=kLoop, calls=%fused_computation.17 | loop fusion | flops 2359296 | bytes 4718592 | tf_op jit(solution)/shard_map/stack | solution.py:217
  116.0 37.4 %shard_map.100 = bf16[512,384]{1,0:T(8,128)(2,1)} custom-call(s32[6]{0:T(128)} %compare_select_fusion.6.refs_0_, bf16[512,384]{1,0:T(8,128)(2,1)} %get-tuple-element.19.refs_1_, bf16[3,512,768]{2,1,0:T(8,128)(2,1)} %pad_maximum_fusion.1.refs_2_.refs_3_, bf16[3,512,768]{2,1,0:T(8,128)(2,1)} %pad_maximum_fusion.1.refs_2_.refs_3_, ...), custom_call_target="tpu_custom_call" | custom-call | flops 3623878656 | bytes 7077888 | tf_op jit(solution)/shard_map/pallas_call | solution.py:137
  153.4 1.5 collective-permute-start.10
  154.9 1.7 collective-permute-start.11
  156.6 20.6 %collective-permute-done.9 = bf16[512,384]{1,0:T(8,128)(2,1)S(1)} collective-permute-done((bf16[512,384]{1,0:T(8,128)(2,1)}, bf16[512,384]{1,0:T(8,128)(2,1)S(1)}, u32[]{:S(2)}, u32[]{:S(2)}) %collective-permute-start.9) | collective-permute-done | bytes 393248 | tf_op jit(solution)/shard_map/ppermute | solution.py:228
  177.2 1.6 convolution_convert_fusion.6
  178.8 2.6 %collective-permute-done.10 = bf16[512,384]{1,0:T(8,128)(2,1)S(1)} collective-permute-done((bf16[512,384]{1,0:T(8,128)(2,1)}, bf16[512,384]{1,0:T(8,128)(2,1)S(1)}, u32[]{:S(2)}, u32[]{:S(2)}) %collective-permute-start.10) | collective-permute-done | bytes 393248 | tf_op jit(solution)/shard_map/ppermute | solution.py:228
  181.4 1.6 convolution_convert_fusion.5
  183.0 1.6 convolution_convert_fusion.3
  184.7 1.6 convolution_convert_fusion.2
  186.9 1.7 convert_add_fusion
  188.6 4.7 %fusion.12 = f32[512,1536]{1,0:T(8,128)} fusion(f32[512,768]{1,0:T(8,128)S(1)} %convert_add_fusion, f32[512,768]{1,0:T(8,128)S(1)} %convert_add_fusion.1, bf16[512,384]{1,0:T(8,128)(2,1)S(1)} %copy-done.11, f32[1536]{0:T(1024)S(1)} %dynamic-slice_reduce_fusion, bf16[512,6144]{1,0:T(8,128)(2,1)} %param.10, s32[]{:T(128)S(6)} %select_n.86, pred[]{:T(512)S(6)} %eq.29, ...), kind=kOutput, calls=%fused_computation.15 | convolution fusion | flops 611057664 | bytes 9444864 | tf_op jit(solution)/shard_map/dot_general | solution.py:233
  (66 shorter events, 18.5 us)
Async XLA Ops:
  0.0 11.8 %copy-start = (bf16[8,3,6144]{2,0,1:T(8,128)(2,1)S(1)}, bf16[8,3,6144]{2,0,1:T(8,128)(2,1)}, u32[]{:S(2)}) copy-start(bf16[8,3,6144]{2,0,1:T(8,128)(2,1)} %param.11) | copy-start | bytes 884740
  0.0 11.2 %copy-start.14 = (s32[8]{0:T(128)S(1)}, s32[8]{0:T(128)}, u32[]{:S(2)}) copy-start(s32[8]{0:T(128)} %param.12) | copy-start | bytes 100
  2.5 14.5 %copy-start.5 = (bf16[1,512,768]{2,1,0:T(8,128)(2,1)}, bf16[1,512,768]{2,1,0:T(8,128)(2,1)S(1)}, u32[]{:S(2)}) copy-start(bf16[1,512,768]{2,1,0:T(8,128)(2,1)S(1)} %reshape.56) | copy-start | bytes 2359300
  2.5 19.4 %collective-permute-start = (bf16[1,512,768]{2,1,0:T(8,128)(2,1)S(1)}, bf16[1,512,768]{2,1,0:T(8,128)(2,1)S(1)}, u32[]{:S(2)}, u32[]{:S(2)}) collective-permute-start(bf16[1,512,768]{2,1,0:T(8,128)(2,1)S(1)} %reshape.56), channel_id=1, source_target_pairs={{0,8},{4,12},{8,16},{12,20},{16,24},{20,28},{24,0},{28,4},{1,9},{5... | collective-permute-start | bytes 2359304 | tf_op jit(solution)/shard_map/ppermute | solution.py:14
  3.8 36.1 %collective-permute-start.1 = (bf16[1,512,768]{2,1,0:T(8,128)(2,1)S(1)}, bf16[1,512,768]{2,1,0:T(8,128)(2,1)S(1)}, u32[]{:S(2)}, u32[]{:S(2)}) collective-permute-start(bf16[1,512,768]{2,1,0:T(8,128)(2,1)S(1)} %reshape.56), channel_id=1, source_target_pairs={{0,16},{4,20},{8,24},{12,28},{16,0},{20,4},{24,8},{28,12},{1,17},{... | collective-permute-start | bytes 2359304 | tf_op jit(solution)/shard_map/ppermute | solution.py:14
  5.0 35.8 %collective-permute-start.2 = (bf16[1,512,768]{2,1,0:T(8,128)(2,1)S(1)}, bf16[1,512,768]{2,1,0:T(8,128)(2,1)}, u32[]{:S(2)}, u32[]{:S(2)}) collective-permute-start(bf16[1,512,768]{2,1,0:T(8,128)(2,1)S(1)} %reshape.56), channel_id=1, source_target_pairs={{0,24},{4,28},{8,0},{12,4},{16,8},{20,12},{24,16},{28,20},{1,25},{... | collective-permute-start | bytes 2359304 | tf_op jit(solution)/shard_map/ppermute | solution.py:14
  8.9 33.7 %collective-permute-start.3 = (bf16[384,768]{1,0:T(8,128)(2,1)}, bf16[384,768]{1,0:T(8,128)(2,1)}, u32[]{:S(2)}, u32[]{:S(2)}) collective-permute-start(bf16[384,768]{1,0:T(8,128)(2,1)} %get-tuple-element.17), channel_id=1, source_target_pairs={{0,1},{1,2},{2,3},{3,0},{4,5},{5,6},{6,7},{7,4},{8,9},{9,10},{10,1... | collective-permute-start | bytes 1769480 | tf_op jit(solution)/shard_map/ppermute | solution.py:159
  10.2 49.3 %collective-permute-start.4 = (bf16[384,768]{1,0:T(8,128)(2,1)}, bf16[384,768]{1,0:T(8,128)(2,1)}, u32[]{:S(2)}, u32[]{:S(2)}) collective-permute-start(bf16[384,768]{1,0:T(8,128)(2,1)} %get-tuple-element.16), channel_id=1, source_target_pairs={{0,2},{1,3},{2,0},{3,1},{4,6},{5,7},{6,4},{7,5},{8,10},{9,11},{10,... | collective-permute-start | bytes 1769480 | tf_op jit(solution)/shard_map/ppermute | solution.py:159
  12.7 9.6 %copy-start.3 = (bf16[512,6144]{1,0:T(8,128)(2,1)S(1)}, bf16[512,6144]{1,0:T(8,128)(2,1)}, u32[]{:S(2)}) copy-start(bf16[512,6144]{1,0:T(8,128)(2,1)} %param.10) | copy-start | bytes 18874372
  21.9 12.0 %copy-start.9 = (bf16[1,512,768]{2,1,0:T(8,128)(2,1)}, bf16[1,512,768]{2,1,0:T(8,128)(2,1)S(1)}, u32[]{:S(2)}) copy-start(bf16[1,512,768]{2,1,0:T(8,128)(2,1)S(1)} %collective-permute-done) | copy-start | bytes 2359300
  21.9 41.3 %collective-permute-start.5 = (bf16[384,768]{1,0:T(8,128)(2,1)}, bf16[384,768]{1,0:T(8,128)(2,1)S(1)}, u32[]{:S(2)}, u32[]{:S(2)}) collective-permute-start(bf16[384,768]{1,0:T(8,128)(2,1)} %get-tuple-element.15), channel_id=1, source_target_pairs={{0,3},{1,0},{2,1},{3,2},{4,7},{5,4},{6,5},{7,6},{8,11},{9,8},{10,9... | collective-permute-start | bytes 1769480 | tf_op jit(solution)/shard_map/ppermute | solution.py:159
  22.3 18.4 %copy-start.6 = (bf16[1,512,768]{2,1,0:T(8,128)(2,1)S(1)}, bf16[1,512,768]{2,1,0:T(8,128)(2,1)}, u32[]{:S(2)}) copy-start(bf16[1,512,768]{2,1,0:T(8,128)(2,1)} %copy-done.5) | copy-start | bytes 2359300
  33.9 29.8 %copy-start.4 = (f32[512,3,384]{2,0,1:T(8,128)}, f32[512,3,384]{2,0,1:T(8,128)S(1)}, u32[]{:S(2)}) copy-start(f32[512,3,384]{2,0,1:T(8,128)S(1)} %fusion.5) | copy-start | bytes 7077892
  39.9 0.9 copy-start.10
  42.6 24.7 %copy-start.2 = (bf16[4,512,768]{2,1,0:T(8,128)(2,1)}, bf16[4,512,768]{2,1,0:T(8,128)(2,1)S(1)}, u32[]{:S(2)}) copy-start(bf16[4,512,768]{2,1,0:T(8,128)(2,1)S(1)} %pad_maximum_fusion.refs_4_.refs_5_) | copy-start | bytes 9437188
  63.2 1.8 copy-start.7
  63.2 52.8 %collective-permute-start.8 = (bf16[4,512,768]{2,1,0:T(8,128)(2,1)S(1)}, bf16[4,512,768]{2,1,0:T(8,128)(2,1)}, u32[]{:S(2)}, u32[]{:S(2)}) collective-permute-start(bf16[4,512,768]{2,1,0:T(8,128)(2,1)S(1)} %pad_maximum_fusion.refs_4_.refs_5_), channel_id=1, source_target_pairs={{0,4},{4,0},{8,12},{12,8},{16,20},{20,16},{24,28},{28,24},{1,5},{5... | collective-permute-start | bytes 9437192 | tf_op jit(solution)/shard_map/ppermute | solution.py:202
  74.0 5.7 %copy-start.12 = (f32[384]{0:T(512)S(1)}, f32[384]{0:T(512)}, u32[]{:S(2)}) copy-start(f32[384]{0:T(512)} %param.17) | copy-start | bytes 4612
  74.0 5.7 %copy-start.13 = (f32[384]{0:T(512)S(1)}, f32[384]{0:T(512)}, u32[]{:S(2)}) copy-start(f32[384]{0:T(512)} %param.16) | copy-start | bytes 4612
  83.8 17.0 %collective-permute-start.6 = (bf16[512,768]{1,0:T(8,128)(2,1)}, bf16[512,768]{1,0:T(8,128)(2,1)}, u32[]{:S(2)}, u32[]{:S(2)}) collective-permute-start(bf16[512,768]{1,0:T(8,128)(2,1)} %get-tuple-element.23), channel_id=1, source_target_pairs={{0,4},{4,8},{8,12},{12,16},{16,20},{20,24},{24,28},{28,0},{1,5},{5... | collective-permute-start | bytes 2359304 | tf_op jit(solution)/shard_map/ppermute | solution.py:14
  84.1 28.6 %collective-permute-start.7 = (bf16[512,768]{1,0:T(8,128)(2,1)}, bf16[512,768]{1,0:T(8,128)(2,1)}, u32[]{:S(2)}, u32[]{:S(2)}) collective-permute-start(bf16[512,768]{1,0:T(8,128)(2,1)} %get-tuple-element.23), channel_id=1, source_target_pairs={{0,8},{4,12},{8,16},{12,20},{16,24},{20,28},{24,0},{28,4},{1,9},{5... | collective-permute-start | bytes 2359304 | tf_op jit(solution)/shard_map/ppermute | solution.py:14
  88.1 94.9 %collective-permute-start.12 = (bf16[3,384,768]{2,1,0:T(8,128)(2,1)}, bf16[3,384,768]{2,1,0:T(8,128)(2,1)}, u32[]{:S(2)}, u32[]{:S(2)}) collective-permute-start(bf16[3,384,768]{2,1,0:T(8,128)(2,1)} %pad_maximum_fusion.2), channel_id=1, source_target_pairs={{0,4},{4,0},{8,12},{12,8},{16,20},{20,16},{24,28},{28,24},{1,5},{5... | collective-permute-start | bytes 5308424 | tf_op jit(solution)/shard_map/ppermute | solution.py:223
  153.4 23.8 %collective-permute-start.9 = (bf16[512,384]{1,0:T(8,128)(2,1)}, bf16[512,384]{1,0:T(8,128)(2,1)S(1)}, u32[]{:S(2)}, u32[]{:S(2)}) collective-permute-start(bf16[512,384]{1,0:T(8,128)(2,1)} %shard_map.100), channel_id=1, source_target_pairs={{0,1},{1,2},{2,3},{3,0},{4,5},{5,6},{6,7},{7,4},{8,9},{9,10},{10,1... | collective-permute-start | bytes 1179656 | tf_op jit(solution)/shard_map/ppermute | solution.py:228
  153.4 28.0 %collective-permute-start.10 = (bf16[512,384]{1,0:T(8,128)(2,1)}, bf16[512,384]{1,0:T(8,128)(2,1)S(1)}, u32[]{:S(2)}, u32[]{:S(2)}) collective-permute-start(bf16[512,384]{1,0:T(8,128)(2,1)} %shard_map.100), channel_id=1, source_target_pairs={{0,2},{1,3},{2,0},{3,1},{4,6},{5,7},{6,4},{7,5},{8,10},{9,11},{10,... | collective-permute-start | bytes 1179656 | tf_op jit(solution)/shard_map/ppermute | solution.py:228
  154.9 31.4 %collective-permute-start.11 = (bf16[512,384]{1,0:T(8,128)(2,1)}, bf16[512,384]{1,0:T(8,128)(2,1)S(1)}, u32[]{:S(2)}, u32[]{:S(2)}) collective-permute-start(bf16[512,384]{1,0:T(8,128)(2,1)} %shard_map.100), channel_id=1, source_target_pairs={{0,3},{1,0},{2,1},{3,2},{4,7},{5,4},{6,5},{7,6},{8,11},{9,8},{10,9... | collective-permute-start | bytes 1179656 | tf_op jit(solution)/shard_map/ppermute | solution.py:228
  178.8 7.5 %copy-start.8 = (bf16[384,768]{1,0:T(8,128)(2,1)S(1)}, bf16[384,768]{1,0:T(8,128)(2,1)}, u32[]{:S(2)}) copy-start(bf16[384,768]{1,0:T(8,128)(2,1)} %copy-done.7) | copy-start | bytes 1769476
  186.9 1.7 copy-start.11
  188.6 4.7 %copy-start.1 = (bf16[8,3,6144]{2,0,1:T(8,128)(2,1)S(1)}, bf16[8,3,6144]{2,0,1:T(8,128)(2,1)}, u32[]{:S(2)}) copy-start(bf16[8,3,6144]{2,0,1:T(8,128)(2,1)} %param.11) | copy-start | bytes 884740

commit v7 on v6

--- a/solution.py
+++ b/solution.py
@@ -112,7 +112,8 @@
 
         return index
 
-    kv_block = (None, span, width)
+    keys_len = local_stack.shape[1]
+    kv_block = (None, keys_len, width)
     grid_spec = pltpu.PrefetchScalarGridSpec(
         num_scalar_prefetch=1,
         grid=(steps,),
@@ -124,7 +125,7 @@
             pl.BlockSpec(kv_block, pool_map(1, False)),
             pl.BlockSpec(kv_block, pool_map(0, True)),
             pl.BlockSpec(kv_block, pool_map(1, True)),
-            pl.BlockSpec((None, blocks, span), lambda j, c: (j, 0, 0)),
+            pl.BlockSpec((None, blocks, keys_len), lambda j, c: (j, 0, 0)),
         ],
         out_specs=pl.BlockSpec((span, width), lambda j, c: (0, 0)),
         scratch_shapes=[
@@ -197,12 +198,12 @@
     normed = inputs * lax.rsqrt(jnp.mean(inputs * inputs, axis=-1, keepdims=True) + 1e-06)
     hidden = (normed * (1.0 + modulation[1][None, :]) + modulation[0][None, :]).astype(jnp.bfloat16)
     qkv = jnp.einsum("td,dkh->tkh", hidden, w_qkv, preferred_element_type=jnp.float32)
-    qkv, same_core, mine = lax.optimization_barrier((qkv, same_core, mine))
     queries = head_norm(qkv[:, 0], q_gain, heads).astype(jnp.bfloat16)
-    other_core = lax.ppermute(same_core, "slot", [(i, i ^ 1) for i in range(slots)])
     keys = head_norm(qkv[:, 1], k_gain, heads).astype(jnp.bfloat16)
     values = qkv[:, 2].astype(jnp.bfloat16)
     local_kv = jnp.concatenate([keys.reshape(span, heads * HD), values], axis=1)
+    queries, local_kv, same_core, mine = lax.optimization_barrier((queries, local_kv, same_core, mine))
+    other_core = lax.ppermute(same_core, "slot", [(i, i ^ 1) for i in range(slots)])
     own_mask = lax.dynamic_index_in_dim(block_mask, slot, 0, keepdims=False)
     own_cache = lax.dynamic_index_in_dim(cache_index, slot, 0, keepdims=False)
     sibling_slot = jnp.bitwise_xor(slot, 1)
@@ -219,15 +220,26 @@
     visible = jnp.transpose(visible.reshape(blocks_q, 3 + cache_len, blocks_q), (1, 0, 2))
     visible = jnp.repeat(visible, BLOCK, axis=2)
     bias = jnp.where(visible > 0, 0.0, -1e30).astype(jnp.float32)
-    mixed = flash(queries.reshape(span, width), local_stack, same_core, other_core, bias, own_cache, heads)
+    rows = span // 2
+    parts = rows // BLOCK
+    queries = queries.reshape(span, width)
+    mixed_parts = [
+        flash(queries[p * rows : (p + 1) * rows], local_stack, same_core, other_core,
+              bias[:, p * parts : (p + 1) * parts], own_cache, heads)
+        for p in range(2)
+    ]
     sibling = lax.ppermute(
         jnp.stack(mine[1:]), "slot", [(i, i ^ 1) for i in range(slots)]
     )
 
     received = [
-        lax.ppermute(mixed, "head", [(i, (i + shift) % groups) for i in range(groups)])
+        jnp.concatenate([
+            lax.ppermute(part, "head", [(i, (i + shift) % groups) for i in range(groups)])
+            for part in mixed_parts
+        ], axis=0)
         for shift in range(1, groups)
     ]
+    mixed = jnp.concatenate(mixed_parts, axis=0)
     columns = own_full.shape[1]
     half = columns // 2
     attn = jnp.dot(mixed, own_full, preferred_element_type=jnp.float32).astype(jnp.bfloat16).astype(jnp.float32)

time: 195 us -> 171 us (0.88)
  waiting for transfers between devices: 76.2 us -> 43.1 us
  matrix products: 25.9 us -> 34.1 us
  starting transfers between devices: 11.4 us -> 18.5 us
  other arithmetic: 21.4 us -> 16.5 us
    ppermute x5, waiting for transfers between devices: 32.5 us -> 19 us  [from_behind(): lax.ppermute(shard, axis, [(i, (i + by) % length) for i in range(length)])]
    ppermute x3, waiting for transfers between devices: 20.6 us -> 9.15 us  [fetch_out_weight(): lax.ppermute(block, 'head', [(i, (i + shift) % groups) for i in range(gro...]
    slice x0 -> x6, local copies, waits for them, and re-layouts: none -> 8.36 us  [the longest x3 4.29 us: local(): queries[p * rows:(p + 1) * rows]]
    ppermute x3 -> x6, waiting for transfers between devices: 23.1 us -> 15 us  [local(): lax.ppermute(part, 'head', [(i, (i + shift) % groups) for i in range(grou...]
    dot_general x1, matrix products: 11.6 us -> 18.8 us  [local(): jnp.einsum('td,dkh->tkh', hidden, w_qkv, preferred_element_type=jnp.float32)]
    ppermute x3 -> x6, starting transfers between devices: 3.16 us -> 7.5 us  [local(): lax.ppermute(part, 'head', [(i, (i + shift) % groups) for i in range(grou...]
    mul x4 -> x2, local copies, waits for them, and re-layouts: 6.57 us -> 2.37 us  [head_norm(): shaped * lax.rsqrt(jnp.mean(shaped * shaped, axis=-1, keepdims=True) + 1e...]
    mul x2 -> x1, local copies, waits for them, and re-layouts: 4.58 us -> 1.39 us  [head_norm(): shaped * shaped]
  transfers between devices with their start and end apart: 13 -> 16, of which waited for: 8 -> 6; matrix products, arithmetic and copies ran while one was open for 30% -> 35% of each run, Pallas kernels for 19% -> 21%
where the time goes in v7:
time: 171 us; the launch traced here: 170 us
  waiting for transfers between devices  43.1 us (25%)
  Pallas kernels  35.7 us (21%)
  matrix products  34.1 us (20%)
  local copies, waits for them, and re-layouts  22.1 us (13%)
  starting transfers between devices  18.5 us (11%)
  other arithmetic  16.5 us (10%)
    pallas_call x2, Pallas kernels, flash(): pl.pallas_call(kernel, grid_spec=grid_spec, out_shape=jax.ShapeDtypeStruc...  35.7 us
    ppermute x5, waiting for transfers between devices, from_behind(): lax.ppermute(shard, axis, [(i, (i + by) % length) for i in range(length)])  19 us
    dot_general x1, matrix products, local(): jnp.einsum('td,dkh->tkh', hidden, w_qkv, preferred_element_type=jnp.float32)  18.8 us
    ppermute x6, waiting for transfers between devices, local(): lax.ppermute(part, 'head', [(i, (i + shift) % groups) for i in range(grou...  15 us
    ppermute x3, waiting for transfers between devices, fetch_out_weight(): lax.ppermute(block, 'head', [(i, (i + shift) % groups) for i in range(gro...  9.15 us
    ppermute x6, starting transfers between devices, local(): lax.ppermute(part, 'head', [(i, (i + shift) % groups) for i in range(grou...  7.5 us
    ppermute x5, starting transfers between devices, from_behind(): lax.ppermute(shard, axis, [(i, (i + by) % length) for i in range(length)])  4.95 us
    dot_general x3, matrix products, local(): jnp.dot(group_o, sibling[shift - 1], preferred_element_type=jnp.float32)  4.94 us
  transfers between devices with their start and end apart: 16, of which 6 were waited for; matrix products, arithmetic and copies ran while one was open for 35% of the time, Pallas kernels for 21%

profile of v7, /device:TPU:9, one launch (start us, length us, event | category | flops | bytes accessed | tf_op | source)
XLA Modules:
  0.0 170.4 jit_solution(12578589354897494370)
XLA Ops:
  0.0 2.5 %reshape.53 = bf16[1,512,768]{2,1,0:T(8,128)(2,1)S(1)} reshape(bf16[1,512,2,384]{3,2,1,0:T(2,128)(2,1)} %param.18) | data formatting | bytes 1572864 | tf_op jit(solution)/shard_map/reshape | solution.py:189
  6.2 2.7 %constant_dynamic-slice_fusion = (bf16[384,768]{1,0:T(8,128)(2,1)}, bf16[384,768]{1,0:T(8,128)(2,1)}, bf16[384,768]{1,0:T(8,128)(2,1)}) fusion(bf16[384,6144]{1,0:T(8,128)(2,1)} %param.19, s32[]{:T(128)S(6)} %select_n.104, s32[]{:T(128)S(6)} %select_n.102, s32[]{:T(128)S(6)} %select_n.100), kind=kLoop, calls=%fused_computation.61 | loop fusion | bytes 3538956 | tf_op jit(solution)/shard_map/dynamic_slice | solution.py:158
  12.8 4.1 %fusion = f32[512]{0:T(512)S(1)} fusion(bf16[512,6144]{1,0:T(8,128)(2,1)} %param.10), kind=kLoop, calls=%fused_computation.2 | loop fusion | flops 9436672 | bytes 6293504 | tf_op jit(solution)/shard_map/reduce_sum | solution.py:198
  16.9 18.8 %fusion.5 = f32[512,3,384]{0,2,1:T(8,128)} fusion(bf16[6144,3,384]{2,0,1:T(8,128)(2,1)} %param.15, bf16[512,6144]{1,0:T(8,128)(2,1)} %param.10, f32[6144]{0:T(1024)S(1)} %bitcast.69, f32[6144]{0:T(1024)S(1)} %bitcast.70, f32[512]{0:T(512)S(1)} %add_rsqrt_fusion.2), kind=kOutput, calls=%fused_computation.7 | convolution fusion | flops 7263485952 | bytes 22857728 | tf_op jit(solution)/shard_map/td,dkh->tkh/dot_general | solution.py:200
  35.6 1.5 fusion.31
  37.1 1.9 %slice.66 = bf16[512,1,384]{0,2,1:T(8,128)(2,1)} slice(f32[512,3,384]{0,2,1:T(8,128)} %fusion.5), slice={[0:512], [2:3], [0:384]} | slice | bytes 786432 | tf_op jit(solution)/shard_map/slice | solution.py:203
  40.3 1.4 copy.18
  44.2 1.9 %copy.27 = bf16[512,1,384]{2,0,1:T(8,128)(2,1)} copy(bf16[512,1,384]{0,2,1:T(8,128)(2,1)} %slice.66) | data formatting | bytes 786432
  47.1 1.5 collective-permute-start.5
  50.5 1.8 %pad_maximum_fusion.refs_4_.refs_5_ = bf16[4,512,768]{2,1,0:T(8,128)(2,1)S(1)} fusion(bf16[1,512,768]{2,1,0:T(8,128)(2,1)} %collective-permute-done.2, bf16[1,512,768]{2,1,0:T(8,128)(2,1)} %collective-permute-done.1, bf16[1,512,768]{2,1,0:T(8,128)(2,1)} %collective-permute-done, bf16[1,512,768]{2,1,0:T(8,128)(2,1)S(1)} %copy-done.4), kind=kLoop, calls=%fused_computation.11 | loop fusion | flops 4718592 | bytes 6291456 | tf_op jit(solution)/shard_map/concatenate | solution.py:191
  52.3 9.1 %collective-permute-done.5 = bf16[384,768]{1,0:T(8,128)(2,1)} collective-permute-done((bf16[384,768]{1,0:T(8,128)(2,1)S(1)}, bf16[384,768]{1,0:T(8,128)(2,1)}, u32[]{:S(2)}, u32[]{:S(2)}) %collective-permute-start.5) | collective-permute-done | bytes 589856 | tf_op jit(solution)/shard_map/ppermute | solution.py:160
  61.5 2.2 %collective-permute-start.8 = (bf16[4,512,768]{2,1,0:T(8,128)(2,1)S(1)}, bf16[4,512,768]{2,1,0:T(8,128)(2,1)}, u32[]{:S(2)}, u32[]{:S(2)}) collective-permute-start(bf16[4,512,768]{2,1,0:T(8,128)(2,1)S(1)} %pad_maximum_fusion.refs_4_.refs_5_), channel_id=1, source_target_pairs={{0,4},{4,0},{8,12},{12,8},{16,20},{20,16},{24,28},{28,24},{1,5},{5... | collective-permute-start | bytes 9437192 | tf_op jit(solution)/shard_map/ppermute | solution.py:206
  67.9 1.7 %fusion.32 = (bf16[256,3,128]{0,2,1:T(8,128)(2,1)S(1)}, bf16[256,3,128]{0,2,1:T(8,128)(2,1)}) fusion(bf16[512,3,128]{0,2,1:T(8,128)(2,1)} %multiply_convert_fusion), kind=kLoop, calls=%fused_computation.90 | loop fusion | bytes 786432 | tf_op jit(solution)/shard_map/slice | solution.py:227
  69.6 1.7 %copy.22.refs_1_ = bf16[256,384]{1,0:T(8,128)(2,1)} copy(bf16[256,384]{0,1:T(8,128)(2,1)} %bitcast.66) | data formatting | bytes 393216 | tf_op jit(solution)/shard_map/slice | solution.py:227
  71.4 2.8 %pad_maximum_fusion.2 = bf16[3,384,768]{2,1,0:T(8,128)(2,1)} fusion(bf16[1,384,768]{2,1,0:T(8,128)(2,1)} %bitcast.22, bf16[1,384,768]{2,1,0:T(8,128)(2,1)} %bitcast.21, bf16[1,384,768]{2,1,0:T(8,128)(2,1)} %bitcast.20), kind=kLoop, calls=%fused_computation.18 | loop fusion | flops 1769472 | bytes 3538944 | tf_op jit(solution)/shard_map/stack | solution.py:232
  74.2 7.0 %collective-permute-done.6 = bf16[512,768]{1,0:T(8,128)(2,1)} collective-permute-done((bf16[512,768]{1,0:T(8,128)(2,1)}, bf16[512,768]{1,0:T(8,128)(2,1)}, u32[]{:S(2)}, u32[]{:S(2)}) %collective-permute-start.6) | collective-permute-done | bytes 786464 | tf_op jit(solution)/shard_map/ppermute | solution.py:14
  81.2 12.0 %collective-permute-done.7 = bf16[512,768]{1,0:T(8,128)(2,1)} collective-permute-done((bf16[512,768]{1,0:T(8,128)(2,1)}, bf16[512,768]{1,0:T(8,128)(2,1)}, u32[]{:S(2)}, u32[]{:S(2)}) %collective-permute-start.7) | collective-permute-done | bytes 786464 | tf_op jit(solution)/shard_map/ppermute | solution.py:14
  93.2 3.3 %pad_maximum_fusion.1.refs_2_.refs_3_ = bf16[3,512,768]{2,1,0:T(8,128)(2,1)} fusion(bf16[1,512,768]{2,1,0:T(8,128)(2,1)} %bitcast.16, bf16[1,512,768]{2,1,0:T(8,128)(2,1)} %bitcast.15, bf16[1,512,768]{2,1,0:T(8,128)(2,1)} %bitcast.14), kind=kLoop, calls=%fused_computation.17 | loop fusion | flops 2359296 | bytes 4718592 | tf_op jit(solution)/shard_map/stack | solution.py:218
  96.5 17.8 %shard_map.100 = bf16[256,384]{1,0:T(8,128)(2,1)} custom-call(s32[6]{0:T(128)} %compare_select_fusion.6.refs_0_, bf16[256,384]{1,0:T(8,128)(2,1)} %copy.22.refs_1_, bf16[3,512,768]{2,1,0:T(8,128)(2,1)} %pad_maximum_fusion.1.refs_2_.refs_3_, bf16[3,512,768]{2,1,0:T(8,128)(2,1)} %pad_maximum_fusion.1.refs_2_.refs_3_, bf16[4,512,768]{2,1,0:T(8,128)(2,1)} %copy-done.2, ...), custom_call_target="tpu_custom_call" | custom-call | flops 905969664 | bytes 3538944 | tf_op jit(solution)/shard_map/pallas_call | solution.py:138
  115.2 3.3 %collective-permute-start.11 = (bf16[256,384]{1,0:T(8,128)(2,1)}, bf16[256,384]{1,0:T(8,128)(2,1)S(1)}, u32[]{:S(2)}, u32[]{:S(2)}) collective-permute-start(bf16[256,384]{1,0:T(8,128)(2,1)} %shard_map.100), channel_id=1, source_target_pairs={{0,2},{1,3},{2,0},{3,1},{4,6},{5,7},{6,4},{7,5},{8,10},{9,11},{10,... | collective-permute-start | bytes 589832 | tf_op jit(solution)/shard_map/ppermute | solution.py:237
  118.4 17.9 %shard_map.101 = bf16[256,384]{1,0:T(8,128)(2,1)} custom-call(s32[6]{0:T(128)} %compare_select_fusion.6.refs_0_, bf16[256,384]{1,0:T(8,128)(2,1)} %copy.23.refs_1_, bf16[3,512,768]{2,1,0:T(8,128)(2,1)} %pad_maximum_fusion.1.refs_2_.refs_3_, bf16[3,512,768]{2,1,0:T(8,128)(2,1)} %pad_maximum_fusion.1.refs_2_.refs_3_, bf16[4,512,768]{2,1,0:T(8,128)(2,1)} %copy-done.2, ...), custom_call_target="tpu_custom_call" | custom-call | flops 905969664 | bytes 3538944 | tf_op jit(solution)/shard_map/pallas_call | solution.py:138
  136.4 2.7 %collective-permute-start.12 = (bf16[256,384]{1,0:T(8,128)(2,1)}, bf16[256,384]{1,0:T(8,128)(2,1)S(1)}, u32[]{:S(2)}, u32[]{:S(2)}) collective-permute-start(bf16[256,384]{1,0:T(8,128)(2,1)} %shard_map.101), channel_id=1, source_target_pairs={{0,2},{1,3},{2,0},{3,1},{4,6},{5,7},{6,4},{7,5},{8,10},{9,11},{10,... | collective-permute-start | bytes 589832 | tf_op jit(solution)/shard_map/ppermute | solution.py:237
  139.2 1.5 collective-permute-start.14
  140.7 12.5 %collective-permute-done.13 = bf16[256,384]{1,0:T(8,128)(2,1)S(1)} collective-permute-done((bf16[256,384]{1,0:T(8,128)(2,1)S(1)}, bf16[256,384]{1,0:T(8,128)(2,1)S(1)}, u32[]{:S(2)}, u32[]{:S(2)}) %collective-permute-start.13) | collective-permute-done | bytes 196640 | tf_op jit(solution)/shard_map/ppermute | solution.py:237
  153.6 2.2 %collective-permute-done.14 = bf16[256,384]{1,0:T(8,128)(2,1)S(1)} collective-permute-done((bf16[256,384]{1,0:T(8,128)(2,1)}, bf16[256,384]{1,0:T(8,128)(2,1)S(1)}, u32[]{:S(2)}, u32[]{:S(2)}) %collective-permute-start.14) | collective-permute-done | bytes 196640 | tf_op jit(solution)/shard_map/ppermute | solution.py:237
  155.8 1.6 convolution_convert_fusion.6
  157.5 1.6 convolution_convert_fusion.5
  159.1 1.6 convert_add_fusion.1
  160.7 1.6 convolution_convert_fusion.3
  162.4 1.6 convolution_convert_fusion.2
  164.0 1.7 convert_add_fusion
  165.7 4.7 %fusion.12 = f32[512,1536]{1,0:T(8,128)} fusion(f32[512,768]{1,0:T(8,128)S(1)} %convert_add_fusion, f32[512,768]{1,0:T(8,128)S(1)} %convert_add_fusion.1, f32[1536]{0:T(1024)S(1)} %dynamic-slice_reduce_fusion, bf16[512,6144]{1,0:T(8,128)(2,1)} %param.10, s32[]{:T(128)S(6)} %select_n.90, pred[]{:T(512)S(6)} %eq.29, bf16[384,6144]{1,0:T(8,128)(2,1)} %param.19, ...), kind=kOutput, calls=%fused_computation.15 | convolution fusion | flops 611844096 | bytes 9444864 | tf_op jit(solution)/shard_map/dot_general | solution.py:245
  (78 shorter events, 19.6 us)
Async XLA Ops:
  0.0 11.8 %copy-start = (bf16[8,3,6144]{2,0,1:T(8,128)(2,1)S(1)}, bf16[8,3,6144]{2,0,1:T(8,128)(2,1)}, u32[]{:S(2)}) copy-start(bf16[8,3,6144]{2,0,1:T(8,128)(2,1)} %param.11) | copy-start | bytes 884740
  0.0 11.2 %copy-start.11 = (s32[8]{0:T(128)S(1)}, s32[8]{0:T(128)}, u32[]{:S(2)}) copy-start(s32[8]{0:T(128)} %param.12) | copy-start | bytes 100
  2.5 14.3 %copy-start.3 = (bf16[1,512,768]{2,1,0:T(8,128)(2,1)}, bf16[1,512,768]{2,1,0:T(8,128)(2,1)S(1)}, u32[]{:S(2)}) copy-start(bf16[1,512,768]{2,1,0:T(8,128)(2,1)S(1)} %reshape.53) | copy-start | bytes 2359300
  2.5 43.8 %collective-permute-start = (bf16[1,512,768]{2,1,0:T(8,128)(2,1)S(1)}, bf16[1,512,768]{2,1,0:T(8,128)(2,1)}, u32[]{:S(2)}, u32[]{:S(2)}) collective-permute-start(bf16[1,512,768]{2,1,0:T(8,128)(2,1)S(1)} %reshape.53), channel_id=1, source_target_pairs={{0,8},{4,12},{8,16},{12,20},{16,24},{20,28},{24,0},{28,4},{1,9},{5... | collective-permute-start | bytes 2359304 | tf_op jit(solution)/shard_map/ppermute | solution.py:14
  3.8 46.7 %collective-permute-start.1 = (bf16[1,512,768]{2,1,0:T(8,128)(2,1)S(1)}, bf16[1,512,768]{2,1,0:T(8,128)(2,1)}, u32[]{:S(2)}, u32[]{:S(2)}) collective-permute-start(bf16[1,512,768]{2,1,0:T(8,128)(2,1)S(1)} %reshape.53), channel_id=1, source_target_pairs={{0,16},{4,20},{8,24},{12,28},{16,0},{20,4},{24,8},{28,12},{1,17},{... | collective-permute-start | bytes 2359304 | tf_op jit(solution)/shard_map/ppermute | solution.py:14
  5.0 45.4 %collective-permute-start.2 = (bf16[1,512,768]{2,1,0:T(8,128)(2,1)S(1)}, bf16[1,512,768]{2,1,0:T(8,128)(2,1)}, u32[]{:S(2)}, u32[]{:S(2)}) collective-permute-start(bf16[1,512,768]{2,1,0:T(8,128)(2,1)S(1)} %reshape.53), channel_id=1, source_target_pairs={{0,24},{4,28},{8,0},{12,4},{16,8},{20,12},{24,16},{28,20},{1,25},{... | collective-permute-start | bytes 2359304 | tf_op jit(solution)/shard_map/ppermute | solution.py:14
  8.9 43.4 %collective-permute-start.3 = (bf16[384,768]{1,0:T(8,128)(2,1)}, bf16[384,768]{1,0:T(8,128)(2,1)}, u32[]{:S(2)}, u32[]{:S(2)}) collective-permute-start(bf16[384,768]{1,0:T(8,128)(2,1)} %get-tuple-element.19), channel_id=1, source_target_pairs={{0,1},{1,2},{2,3},{3,0},{4,5},{5,6},{6,7},{7,4},{8,9},{9,10},{10,1... | collective-permute-start | bytes 1769480 | tf_op jit(solution)/shard_map/ppermute | solution.py:160
  10.2 42.1 %collective-permute-start.4 = (bf16[384,768]{1,0:T(8,128)(2,1)}, bf16[384,768]{1,0:T(8,128)(2,1)}, u32[]{:S(2)}, u32[]{:S(2)}) collective-permute-start(bf16[384,768]{1,0:T(8,128)(2,1)} %get-tuple-element.18), channel_id=1, source_target_pairs={{0,2},{1,3},{2,0},{3,1},{4,6},{5,7},{6,4},{7,5},{8,10},{9,11},{10,... | collective-permute-start | bytes 1769480 | tf_op jit(solution)/shard_map/ppermute | solution.py:160
  41.7 4.5 %copy-start.9 = (f32[384]{0:T(512)S(1)}, f32[384]{0:T(512)}, u32[]{:S(2)}) copy-start(f32[384]{0:T(512)} %param.17) | copy-start | bytes 4612
  46.1 1.1 copy-start.6
  46.1 2.5 %copy-start.5 = (bf16[512,1,384]{2,0,1:T(8,128)(2,1)S(1)}, bf16[512,1,384]{2,0,1:T(8,128)(2,1)}, u32[]{:S(2)}) copy-start(bf16[512,1,384]{2,0,1:T(8,128)(2,1)} %copy.27) | copy-start | bytes 1179652
  46.1 3.5 %copy-start.10 = (f32[384]{0:T(512)S(1)}, f32[384]{0:T(512)}, u32[]{:S(2)}) copy-start(f32[384]{0:T(512)} %param.16) | copy-start | bytes 4612
  46.2 4.3 %copy-start.4 = (bf16[1,512,768]{2,1,0:T(8,128)(2,1)S(1)}, bf16[1,512,768]{2,1,0:T(8,128)(2,1)}, u32[]{:S(2)}) copy-start(bf16[1,512,768]{2,1,0:T(8,128)(2,1)} %copy-done.3) | copy-start | bytes 2359300
  47.1 14.3 %collective-permute-start.5 = (bf16[384,768]{1,0:T(8,128)(2,1)S(1)}, bf16[384,768]{1,0:T(8,128)(2,1)}, u32[]{:S(2)}, u32[]{:S(2)}) collective-permute-start(bf16[384,768]{1,0:T(8,128)(2,1)S(1)} %copy-done.6), channel_id=1, source_target_pairs={{0,3},{1,0},{2,1},{3,2},{4,7},{5,4},{6,5},{7,6},{8,11},{9,8},{10,9... | collective-permute-start | bytes 1769480 | tf_op jit(solution)/shard_map/ppermute | solution.py:160
  52.3 21.9 %copy-start.2 = (bf16[4,512,768]{2,1,0:T(8,128)(2,1)}, bf16[4,512,768]{2,1,0:T(8,128)(2,1)S(1)}, u32[]{:S(2)}) copy-start(bf16[4,512,768]{2,1,0:T(8,128)(2,1)S(1)} %pad_maximum_fusion.refs_4_.refs_5_) | copy-start | bytes 9437188
  61.5 35.0 %collective-permute-start.8 = (bf16[4,512,768]{2,1,0:T(8,128)(2,1)S(1)}, bf16[4,512,768]{2,1,0:T(8,128)(2,1)}, u32[]{:S(2)}, u32[]{:S(2)}) collective-permute-start(bf16[4,512,768]{2,1,0:T(8,128)(2,1)S(1)} %pad_maximum_fusion.refs_4_.refs_5_), channel_id=1, source_target_pairs={{0,4},{4,0},{8,12},{12,8},{16,20},{20,16},{24,28},{28,24},{1,5},{5... | collective-permute-start | bytes 9437192 | tf_op jit(solution)/shard_map/ppermute | solution.py:206
  64.4 16.8 %collective-permute-start.6 = (bf16[512,768]{1,0:T(8,128)(2,1)}, bf16[512,768]{1,0:T(8,128)(2,1)}, u32[]{:S(2)}, u32[]{:S(2)}) collective-permute-start(bf16[512,768]{1,0:T(8,128)(2,1)} %pad_maximum_fusion.3), channel_id=1, source_target_pairs={{0,4},{4,8},{8,12},{12,16},{16,20},{20,24},{24,28},{28,0},{1,5},{5... | collective-permute-start | bytes 2359304 | tf_op jit(solution)/shard_map/ppermute | solution.py:14
  64.6 28.6 %collective-permute-start.7 = (bf16[512,768]{1,0:T(8,128)(2,1)}, bf16[512,768]{1,0:T(8,128)(2,1)}, u32[]{:S(2)}, u32[]{:S(2)}) collective-permute-start(bf16[512,768]{1,0:T(8,128)(2,1)} %pad_maximum_fusion.3), channel_id=1, source_target_pairs={{0,8},{4,12},{8,16},{12,20},{16,24},{20,28},{24,0},{28,4},{1,9},{5... | collective-permute-start | bytes 2359304 | tf_op jit(solution)/shard_map/ppermute | solution.py:14
  74.2 86.5 %collective-permute-start.15 = (bf16[3,384,768]{2,1,0:T(8,128)(2,1)}, bf16[3,384,768]{2,1,0:T(8,128)(2,1)}, u32[]{:S(2)}, u32[]{:S(2)}) collective-permute-start(bf16[3,384,768]{2,1,0:T(8,128)(2,1)} %pad_maximum_fusion.2), channel_id=1, source_target_pairs={{0,4},{4,0},{8,12},{12,8},{16,20},{20,16},{24,28},{28,24},{1,5},{5... | collective-permute-start | bytes 5308424 | tf_op jit(solution)/shard_map/ppermute | solution.py:231
  114.3 24.8 %collective-permute-start.9 = (bf16[256,384]{1,0:T(8,128)(2,1)}, bf16[256,384]{1,0:T(8,128)(2,1)S(1)}, u32[]{:S(2)}, u32[]{:S(2)}) collective-permute-start(bf16[256,384]{1,0:T(8,128)(2,1)} %shard_map.100), channel_id=1, source_target_pairs={{0,1},{1,2},{2,3},{3,0},{4,5},{5,6},{6,7},{7,4},{8,9},{9,10},{10,1... | collective-permute-start | bytes 589832 | tf_op jit(solution)/shard_map/ppermute | solution.py:237
  115.2 24.0 %collective-permute-start.11 = (bf16[256,384]{1,0:T(8,128)(2,1)}, bf16[256,384]{1,0:T(8,128)(2,1)S(1)}, u32[]{:S(2)}, u32[]{:S(2)}) collective-permute-start(bf16[256,384]{1,0:T(8,128)(2,1)} %shard_map.100), channel_id=1, source_target_pairs={{0,2},{1,3},{2,0},{3,1},{4,6},{5,7},{6,4},{7,5},{8,10},{9,11},{10,... | collective-permute-start | bytes 589832 | tf_op jit(solution)/shard_map/ppermute | solution.py:237
  118.4 20.7 %copy-start.7 = (bf16[256,384]{1,0:T(8,128)(2,1)S(1)}, bf16[256,384]{1,0:T(8,128)(2,1)}, u32[]{:S(2)}) copy-start(bf16[256,384]{1,0:T(8,128)(2,1)} %shard_map.100) | copy-start | bytes 589828
  136.4 16.8 %collective-permute-start.10 = (bf16[256,384]{1,0:T(8,128)(2,1)}, bf16[256,384]{1,0:T(8,128)(2,1)S(1)}, u32[]{:S(2)}, u32[]{:S(2)}) collective-permute-start(bf16[256,384]{1,0:T(8,128)(2,1)} %shard_map.101), channel_id=1, source_target_pairs={{0,1},{1,2},{2,3},{3,0},{4,5},{5,6},{6,7},{7,4},{8,9},{9,10},{10,1... | collective-permute-start | bytes 589832 | tf_op jit(solution)/shard_map/ppermute | solution.py:237
  136.4 17.2 %collective-permute-start.12 = (bf16[256,384]{1,0:T(8,128)(2,1)}, bf16[256,384]{1,0:T(8,128)(2,1)S(1)}, u32[]{:S(2)}, u32[]{:S(2)}) collective-permute-start(bf16[256,384]{1,0:T(8,128)(2,1)} %shard_map.101), channel_id=1, source_target_pairs={{0,2},{1,3},{2,0},{3,1},{4,6},{5,7},{6,4},{7,5},{8,10},{9,11},{10,... | collective-permute-start | bytes 589832 | tf_op jit(solution)/shard_map/ppermute | solution.py:237
  139.1 14.1 %collective-permute-start.13 = (bf16[256,384]{1,0:T(8,128)(2,1)S(1)}, bf16[256,384]{1,0:T(8,128)(2,1)S(1)}, u32[]{:S(2)}, u32[]{:S(2)}) collective-permute-start(bf16[256,384]{1,0:T(8,128)(2,1)S(1)} %copy-done.7), channel_id=1, source_target_pairs={{0,3},{1,0},{2,1},{3,2},{4,7},{5,4},{6,5},{7,6},{8,11},{9,8},{10,9... | collective-permute-start | bytes 589832 | tf_op jit(solution)/shard_map/ppermute | solution.py:237
  139.2 16.6 %collective-permute-start.14 = (bf16[256,384]{1,0:T(8,128)(2,1)}, bf16[256,384]{1,0:T(8,128)(2,1)S(1)}, u32[]{:S(2)}, u32[]{:S(2)}) collective-permute-start(bf16[256,384]{1,0:T(8,128)(2,1)} %shard_map.101), channel_id=1, source_target_pairs={{0,3},{1,0},{2,1},{3,2},{4,7},{5,4},{6,5},{7,6},{8,11},{9,8},{10,9... | collective-permute-start | bytes 589832 | tf_op jit(solution)/shard_map/ppermute | solution.py:237
  164.0 1.7 copy-start.8
  165.7 4.7 %copy-start.1 = (bf16[8,3,6144]{2,0,1:T(8,128)(2,1)S(1)}, bf16[8,3,6144]{2,0,1:T(8,128)(2,1)}, u32[]{:S(2)}) copy-start(bf16[8,3,6144]{2,0,1:T(8,128)(2,1)} %param.11) | copy-start | bytes 884740

commit v8 on v7

--- a/solution.py
+++ b/solution.py
@@ -152,13 +152,14 @@
     groups = lax.axis_size("head")
     columns = w_out.shape[1] // groups
     half = columns // 2
-    mine = []
-    for shift in range(groups):
-        dest = (head + shift) % groups
-        block = lax.dynamic_slice_in_dim(w_out, dest * columns + core * half, half, 1)
-        if shift:
-            block = lax.ppermute(block, "head", [(i, (i + shift) % groups) for i in range(groups)])
-        mine.append(block)
+    blocks = lax.dynamic_slice_in_dim(
+        w_out.reshape(w_out.shape[0], groups, columns), core * half, half, 2
+    )
+    exchanged = lax.all_to_all(blocks, "head", 1, 1)
+    mine = [
+        lax.dynamic_index_in_dim(exchanged, (head - shift) % groups, 1, keepdims=False)
+        for shift in range(groups)
+    ]
     own_full = lax.dynamic_slice_in_dim(w_out, head * columns, columns, 1)
     return own_full, mine
 
@@ -202,7 +203,11 @@
     keys = head_norm(qkv[:, 1], k_gain, heads).astype(jnp.bfloat16)
     values = qkv[:, 2].astype(jnp.bfloat16)
     local_kv = jnp.concatenate([keys.reshape(span, heads * HD), values], axis=1)
-    queries, local_kv, same_core, mine = lax.optimization_barrier((queries, local_kv, same_core, mine))
+    before = from_behind(local_kv, "slot", 1)
+    earlier = from_behind(local_kv, "slot", 2)
+    queries, before, earlier, same_core, mine = lax.optimization_barrier(
+        (queries, before, earlier, same_core, mine)
+    )
     other_core = lax.ppermute(same_core, "slot", [(i, i ^ 1) for i in range(slots)])
     own_mask = lax.dynamic_index_in_dim(block_mask, slot, 0, keepdims=False)
     own_cache = lax.dynamic_index_in_dim(cache_index, slot, 0, keepdims=False)
@@ -212,8 +217,6 @@
         ((slot - own_cache) % slots) // 2,
         slots // 2 + ((sibling_slot - own_cache) % slots) // 2,
     ).astype(jnp.int32)
-    before = from_behind(local_kv, "slot", 1)
-    earlier = from_behind(local_kv, "slot", 2)
     width = heads * HD
     local_stack = jnp.stack([local_kv, before, earlier]).reshape(3, span, 2 * width)
     visible = jnp.concatenate([jnp.ones((blocks_q, blocks_q), jnp.int32), own_mask], axis=1)

time: 171 us -> 176 us (1.029)
  local copies, waits for them, and re-layouts: 22.1 us -> 35.2 us
  waiting for transfers between devices: 43.1 us -> 33.9 us
  matrix products: 34.1 us -> 30.9 us
  other arithmetic: 16.5 us -> 18.8 us
    ppermute x5, waiting for transfers between devices: 19 us -> 8.42 us  [from_behind(): lax.ppermute(shard, axis, [(i, (i + by) % length) for i in range(length)])]
    dynamic_slice x1 -> x5, local copies, waits for them, and re-layouts: 2.69 us -> 12.4 us  [the longest x4 9.05 us: fetch_out_weight(): lax.dynamic_index_in_dim(exchanged, (head - shift) % groups, 1, keepdims=...]
    ppermute x3 -> x0, waiting for transfers between devices: 9.15 us -> none  [fetch_out_weight(): lax.ppermute(block, 'head', [(i, (i + shift) % groups) for i in range(gro...]
    all_to_all x0 -> x1, waiting for transfers between devices: none -> 6.13 us  [fetch_out_weight(): exchanged = lax.all_to_all(blocks, 'head', 1, 1)]
    all_to_all x0 -> x1, starting transfers between devices: none -> 4.89 us  [fetch_out_weight(): exchanged = lax.all_to_all(blocks, 'head', 1, 1)]
    ppermute x6, waiting for transfers between devices: 15 us -> 19.4 us  [local(): lax.ppermute(part, 'head', [(i, (i + shift) % groups) for i in range(grou...]
    unnamed x29 -> x32, local copies, waits for them, and re-layouts: 3.13 us -> 7.21 us
    ppermute x3 -> x0, starting transfers between devices: 3.78 us -> none  [fetch_out_weight(): lax.ppermute(block, 'head', [(i, (i + shift) % groups) for i in range(gro...]
  transfers between devices with their start and end apart: 16 -> 14, of which waited for: 6 -> 5; matrix products, arithmetic and copies ran while one was open for 35% -> 42% of each run, Pallas kernels for 21% -> 20%
where the time goes in v8:
time: 176 us; the launch traced here: 175 us
  Pallas kernels  35.7 us (20%)
  local copies, waits for them, and re-layouts  35.2 us (20%)
  waiting for transfers between devices  33.9 us (19%)
  matrix products  30.9 us (18%)
  starting transfers between devices  19.7 us (11%)
  other arithmetic  18.8 us (11%)
    pallas_call x2, Pallas kernels, flash(): pl.pallas_call(kernel, grid_spec=grid_spec, out_shape=jax.ShapeDtypeStruc...  35.7 us
    ppermute x6, waiting for transfers between devices, local(): lax.ppermute(part, 'head', [(i, (i + shift) % groups) for i in range(grou...  19.4 us
    dot_general x1, matrix products, local(): jnp.einsum('td,dkh->tkh', hidden, w_qkv, preferred_element_type=jnp.float32)  18.8 us
    dynamic_slice x4, local copies, waits for them, and re-layouts, fetch_out_weight(): lax.dynamic_index_in_dim(exchanged, (head - shift) % groups, 1, keepdims=...  9.05 us
    ppermute x5, waiting for transfers between devices, from_behind(): lax.ppermute(shard, axis, [(i, (i + by) % length) for i in range(length)])  8.42 us
    ppermute x6, starting transfers between devices, local(): lax.ppermute(part, 'head', [(i, (i + shift) % groups) for i in range(grou...  7.43 us
    unnamed x32, local copies, waits for them, and re-layouts  7.21 us
    ppermute x5, starting transfers between devices, from_behind(): lax.ppermute(shard, axis, [(i, (i + by) % length) for i in range(length)])  6.83 us
  transfers between devices with their start and end apart: 14, of which 5 were waited for; matrix products, arithmetic and copies ran while one was open for 42% of the time, Pallas kernels for 20%

profile of v8, /device:TPU:9, one launch (start us, length us, event | category | flops | bytes accessed | tf_op | source)
XLA Modules:
  0.0 174.6 jit_solution(857289809874892130)
XLA Ops:
  0.0 2.5 %reshape.56 = bf16[1,512,768]{2,1,0:T(8,128)(2,1)S(1)} reshape(bf16[1,512,2,384]{3,2,1,0:T(2,128)(2,1)} %param.18) | data formatting | bytes 1572864 | tf_op jit(solution)/shard_map/reshape | solution.py:190
  2.5 2.2 %collective-permute-start.4 = (bf16[1,512,768]{2,1,0:T(8,128)(2,1)S(1)}, bf16[1,512,768]{2,1,0:T(8,128)(2,1)}, u32[]{:S(2)}, u32[]{:S(2)}) collective-permute-start(bf16[1,512,768]{2,1,0:T(8,128)(2,1)S(1)} %reshape.56), channel_id=1, source_target_pairs={{0,24},{4,28},{8,0},{12,4},{16,8},{20,12},{24,16},{28,20},{1,25},{... | collective-permute-start | bytes 2359304 | tf_op jit(solution)/shard_map/ppermute | solution.py:14
  5.3 6.6 %copy.29 = bf16[384,6144]{0,1:T(8,128)(2,1)} copy(bf16[384,6144]{1,0:T(8,128)(2,1)} %param.19) | data formatting | bytes 9437184 | tf_op args[9]
  11.9 3.3 %constant_dynamic-slice_fusion.4 = bf16[384,4,768]{0,2,1:T(8,128)(2,1)} fusion(bf16[384,4,1536]{0,2,1:T(8,128)(2,1)} %bitcast.65, s32[]{:T(128)S(6)} %select_n.103), kind=kLoop, calls=%fused_computation.56 | loop fusion | bytes 4718596 | tf_op jit(solution)/shard_map/dynamic_slice | solution.py:155
  15.2 4.9 %all-to-all-start = ((bf16[384,4,768]{0,2,1:T(8,128)(2,1)}), bf16[384,4,768]{0,2,1:T(8,128)(2,1)}, u32[]{:S(2)}, u32[]{:S(2)}) async-start(bf16[384,4,768]{0,2,1:T(8,128)(2,1)} %constant_dynamic-slice_fusion.4), calls=%async_computation | async-start | bytes 4718592 | tf_op jit(solution)/shard_map/all_to_all | solution.py:158
  21.7 4.1 %fusion = f32[512]{0:T(512)S(1)} fusion(bf16[512,6144]{1,0:T(8,128)(2,1)} %param.10), kind=kLoop, calls=%fused_computation.2 | loop fusion | flops 9436672 | bytes 6293504 | tf_op jit(solution)/shard_map/reduce_sum | solution.py:199
  25.8 18.8 %fusion.5 = f32[512,3,384]{0,2,1:T(8,128)} fusion(bf16[6144,3,384]{2,0,1:T(8,128)(2,1)} %param.15, bf16[512,6144]{1,0:T(8,128)(2,1)} %param.10, f32[6144]{0:T(1024)S(1)} %bitcast.81, f32[6144]{0:T(1024)S(1)} %bitcast.82, f32[512]{0:T(512)S(1)} %add_rsqrt_fusion.2), kind=kOutput, calls=%fused_computation.7 | convolution fusion | flops 7263485952 | bytes 22857728 | tf_op jit(solution)/shard_map/td,dkh->tkh/dot_general | solution.py:201
  44.6 1.5 fusion.33
  53.5 2.2 %fusion.32 = (bf16[1,512,768]{2,1,0:T(8,128)(2,1)}, bf16[512,768]{1,0:T(8,128)(2,1)}) fusion(bf16[512,384]{1,0:T(8,128)(2,1)S(1)} %bitcast.76, bf16[512,384]{1,0:T(8,128)(2,1)} %fusion.15), kind=kLoop, calls=%fused_computation.91 | loop fusion | flops 1572864 | bytes 2359296 | tf_op jit(solution)/shard_map/stack | solution.py:221
  55.8 4.1 %collective-permute-start = (bf16[512,768]{1,0:T(8,128)(2,1)}, bf16[512,768]{1,0:T(8,128)(2,1)}, u32[]{:S(2)}, u32[]{:S(2)}) collective-permute-start(bf16[512,768]{1,0:T(8,128)(2,1)} %get-tuple-element.25), channel_id=1, source_target_pairs={{0,4},{4,8},{8,12},{12,16},{16,20},{20,24},{24,28},{28,0},{1,5},{5... | collective-permute-start | bytes 2359304 | tf_op jit(solution)/shard_map/ppermute | solution.py:14
  61.0 2.0 %pad_maximum_fusion.refs_4_.refs_5_ = bf16[4,512,768]{2,1,0:T(8,128)(2,1)S(1)} fusion(bf16[1,512,768]{2,1,0:T(8,128)(2,1)} %collective-permute-done.4, bf16[1,512,768]{2,1,0:T(8,128)(2,1)} %collective-permute-done.3, bf16[1,512,768]{2,1,0:T(8,128)(2,1)} %collective-permute-done.2, bf16[1,512,768]{2,1,0:T(8,128)(2,1)} %copy-done.6), kind=kLoop, calls=%fused_computation.11 | loop fusion | flops 4718592 | bytes 6291456 | tf_op jit(solution)/shard_map/concatenate | solution.py:192
  63.1 6.1 %all-to-all-done = bf16[384,4,768]{0,2,1:T(8,128)(2,1)} async-done(((bf16[384,4,768]{0,2,1:T(8,128)(2,1)}), bf16[384,4,768]{0,2,1:T(8,128)(2,1)}, u32[]{:S(2)}, u32[]{:S(2)}) %all-to-all-start) | async-done | bytes 2359328 | tf_op jit(solution)/shard_map/all_to_all | solution.py:158
  69.2 2.7 %constant_dynamic-slice_fusion.1 = (bf16[384,1,768]{0,2,1:T(8,128)(2,1)}, bf16[384,1,768]{0,2,1:T(8,128)(2,1)}, bf16[384,1,768]{0,2,1:T(8,128)(2,1)}) fusion(bf16[384,4,768]{0,2,1:T(8,128)(2,1)} %all-to-all-done, s32[]{:T(128)S(6)} %select_n.109, s32[]{:T(128)S(6)} %select_n.107, s32[]{:T(128)S(6)} %select_n.105), kind=kLoop, calls=%fused_computation.53 | loop fusion | bytes 3538956 | tf_op jit(solution)/shard_map/jit(dynamic_index_in_dim)/dynamic_slice | solution.py:160
  71.9 2.1 %copy.30 = bf16[384,1,768]{2,0,1:T(8,128)(2,1)} copy(bf16[384,1,768]{0,2,1:T(8,128)(2,1)} %get-tuple-element.21) | data formatting | bytes 1179648 | tf_op jit(solution)/shard_map/jit(dynamic_index_in_dim)/dynamic_slice | solution.py:160
  74.0 2.1 %copy.31 = bf16[384,1,768]{2,0,1:T(8,128)(2,1)} copy(bf16[384,1,768]{0,2,1:T(8,128)(2,1)} %get-tuple-element.20) | data formatting | bytes 1179648 | tf_op jit(solution)/shard_map/jit(dynamic_index_in_dim)/dynamic_slice | solution.py:160
  76.1 2.1 %copy.32 = bf16[384,1,768]{2,0,1:T(8,128)(2,1)} copy(bf16[384,1,768]{0,2,1:T(8,128)(2,1)} %get-tuple-element.19) | data formatting | bytes 1179648 | tf_op jit(solution)/shard_map/jit(dynamic_index_in_dim)/dynamic_slice | solution.py:160
  78.2 8.4 %collective-permute-done.1 = bf16[512,768]{1,0:T(8,128)(2,1)} collective-permute-done((bf16[512,768]{1,0:T(8,128)(2,1)}, bf16[512,768]{1,0:T(8,128)(2,1)}, u32[]{:S(2)}, u32[]{:S(2)}) %collective-permute-start.1) | collective-permute-done | bytes 786464 | tf_op jit(solution)/shard_map/ppermute | solution.py:14
  89.6 1.7 fusion.34
  91.4 1.7 copy.34.refs_1_
  93.1 2.9 %pad_maximum_fusion.2 = bf16[3,384,768]{2,1,0:T(8,128)(2,1)} fusion(bf16[1,384,768]{2,1,0:T(8,128)(2,1)} %bitcast.72, bf16[1,384,768]{2,1,0:T(8,128)(2,1)} %bitcast.70, bf16[1,384,768]{2,1,0:T(8,128)(2,1)} %bitcast.68), kind=kLoop, calls=%fused_computation.18 | loop fusion | flops 1769472 | bytes 3538944 | tf_op jit(solution)/shard_map/stack | solution.py:235
  96.5 3.1 %pad_maximum_fusion.1.refs_2_.refs_3_ = bf16[3,512,768]{2,1,0:T(8,128)(2,1)} fusion(bf16[1,512,768]{2,1,0:T(8,128)(2,1)} %bitcast.20, bf16[1,512,768]{2,1,0:T(8,128)(2,1)} %bitcast.19, bf16[1,512,768]{2,1,0:T(8,128)(2,1)S(1)} %copy-done.7), kind=kLoop, calls=%fused_computation.17 | loop fusion | flops 2359296 | bytes 4718592 | tf_op jit(solution)/shard_map/stack | solution.py:221
  99.6 17.8 %shard_map.100 = bf16[256,384]{1,0:T(8,128)(2,1)} custom-call(s32[6]{0:T(128)} %compare_select_fusion.6.refs_0_, bf16[256,384]{1,0:T(8,128)(2,1)} %copy.34.refs_1_, bf16[3,512,768]{2,1,0:T(8,128)(2,1)} %pad_maximum_fusion.1.refs_2_.refs_3_, bf16[3,512,768]{2,1,0:T(8,128)(2,1)} %pad_maximum_fusion.1.refs_2_.refs_3_, bf16[4,512,768]{2,1,0:T(8,128)(2,1)} %copy-done.2, ...), custom_call_target="tpu_custom_call" | custom-call | flops 905969664 | bytes 3538944 | tf_op jit(solution)/shard_map/pallas_call | solution.py:138
  117.4 2.1 %collective-permute-start.8 = (bf16[256,384]{1,0:T(8,128)(2,1)}, bf16[256,384]{1,0:T(8,128)(2,1)S(1)}, u32[]{:S(2)}, u32[]{:S(2)}) collective-permute-start(bf16[256,384]{1,0:T(8,128)(2,1)} %shard_map.100), channel_id=1, source_target_pairs={{0,2},{1,3},{2,0},{3,1},{4,6},{5,7},{6,4},{7,5},{8,10},{9,11},{10,... | collective-permute-start | bytes 589832 | tf_op jit(solution)/shard_map/ppermute | solution.py:240
  120.4 17.9 %shard_map.101 = bf16[256,384]{1,0:T(8,128)(2,1)} custom-call(s32[6]{0:T(128)} %compare_select_fusion.6.refs_0_, bf16[256,384]{1,0:T(8,128)(2,1)} %copy.35.refs_1_, bf16[3,512,768]{2,1,0:T(8,128)(2,1)} %pad_maximum_fusion.1.refs_2_.refs_3_, bf16[3,512,768]{2,1,0:T(8,128)(2,1)} %pad_maximum_fusion.1.refs_2_.refs_3_, bf16[4,512,768]{2,1,0:T(8,128)(2,1)} %copy-done.2, ...), custom_call_target="tpu_custom_call" | custom-call | flops 905969664 | bytes 3538944 | tf_op jit(solution)/shard_map/pallas_call | solution.py:138
  138.3 2.4 %collective-permute-start.9 = (bf16[256,384]{1,0:T(8,128)(2,1)}, bf16[256,384]{1,0:T(8,128)(2,1)S(1)}, u32[]{:S(2)}, u32[]{:S(2)}) collective-permute-start(bf16[256,384]{1,0:T(8,128)(2,1)} %shard_map.101), channel_id=1, source_target_pairs={{0,2},{1,3},{2,0},{3,1},{4,6},{5,7},{6,4},{7,5},{8,10},{9,11},{10,... | collective-permute-start | bytes 589832 | tf_op jit(solution)/shard_map/ppermute | solution.py:240
  143.7 15.3 %collective-permute-done.10 = bf16[256,384]{1,0:T(8,128)(2,1)S(1)} collective-permute-done((bf16[256,384]{1,0:T(8,128)(2,1)S(1)}, bf16[256,384]{1,0:T(8,128)(2,1)S(1)}, u32[]{:S(2)}, u32[]{:S(2)}) %collective-permute-start.10) | collective-permute-done | bytes 196640 | tf_op jit(solution)/shard_map/ppermute | solution.py:240
  159.1 2.6 %collective-permute-done.7 = bf16[256,384]{1,0:T(8,128)(2,1)S(1)} collective-permute-done((bf16[256,384]{1,0:T(8,128)(2,1)}, bf16[256,384]{1,0:T(8,128)(2,1)S(1)}, u32[]{:S(2)}, u32[]{:S(2)}) %collective-permute-start.7) | collective-permute-done | bytes 196640 | tf_op jit(solution)/shard_map/ppermute | solution.py:240
  161.7 1.5 collective-permute-done.11
  165.0 1.6 convolution_convert_fusion.2
  166.6 1.6 convolution_convert_fusion.3
  168.3 1.7 convert_add_fusion
  170.0 4.7 %fusion.12 = f32[512,1536]{1,0:T(8,128)} fusion(f32[512,768]{1,0:T(8,128)S(1)} %convert_add_fusion, f32[512,768]{1,0:T(8,128)S(1)} %convert_add_fusion.1, f32[1536]{0:T(1024)S(1)} %dynamic-slice_reduce_fusion, bf16[512,6144]{1,0:T(8,128)(2,1)} %param.10, s32[]{:T(128)S(6)} %select_n.94, pred[]{:T(512)S(6)} %eq.29, bf16[384,6144]{1,0:T(8,128)(2,1)} %param.19, ...), kind=kOutput, calls=%fused_computation.15 | convolution fusion | flops 611844096 | bytes 9444864 | tf_op jit(solution)/shard_map/dot_general | solution.py:248
  (81 shorter events, 19.7 us)
Async XLA Ops:
  0.0 20.7 %copy-start = (bf16[8,3,6144]{2,0,1:T(8,128)(2,1)S(1)}, bf16[8,3,6144]{2,0,1:T(8,128)(2,1)}, u32[]{:S(2)}) copy-start(bf16[8,3,6144]{2,0,1:T(8,128)(2,1)} %param.11) | copy-start | bytes 884740
  2.5 9.4 %copy-start.6 = (bf16[1,512,768]{2,1,0:T(8,128)(2,1)}, bf16[1,512,768]{2,1,0:T(8,128)(2,1)S(1)}, u32[]{:S(2)}) copy-start(bf16[1,512,768]{2,1,0:T(8,128)(2,1)S(1)} %reshape.56) | copy-start | bytes 2359300
  2.5 58.5 %collective-permute-start.4 = (bf16[1,512,768]{2,1,0:T(8,128)(2,1)S(1)}, bf16[1,512,768]{2,1,0:T(8,128)(2,1)}, u32[]{:S(2)}, u32[]{:S(2)}) collective-permute-start(bf16[1,512,768]{2,1,0:T(8,128)(2,1)S(1)} %reshape.56), channel_id=1, source_target_pairs={{0,24},{4,28},{8,0},{12,4},{16,8},{20,12},{24,16},{28,20},{1,25},{... | collective-permute-start | bytes 2359304 | tf_op jit(solution)/shard_map/ppermute | solution.py:14
  4.7 56.3 %collective-permute-start.3 = (bf16[1,512,768]{2,1,0:T(8,128)(2,1)S(1)}, bf16[1,512,768]{2,1,0:T(8,128)(2,1)}, u32[]{:S(2)}, u32[]{:S(2)}) collective-permute-start(bf16[1,512,768]{2,1,0:T(8,128)(2,1)S(1)} %reshape.56), channel_id=1, source_target_pairs={{0,16},{4,20},{8,24},{12,28},{16,0},{20,4},{24,8},{28,12},{1,17},{... | collective-permute-start | bytes 2359304 | tf_op jit(solution)/shard_map/ppermute | solution.py:14
  5.0 56.0 %collective-permute-start.2 = (bf16[1,512,768]{2,1,0:T(8,128)(2,1)S(1)}, bf16[1,512,768]{2,1,0:T(8,128)(2,1)}, u32[]{:S(2)}, u32[]{:S(2)}) collective-permute-start(bf16[1,512,768]{2,1,0:T(8,128)(2,1)S(1)} %reshape.56), channel_id=1, source_target_pairs={{0,8},{4,12},{8,16},{12,20},{16,24},{20,28},{24,0},{28,4},{1,9},{5... | collective-permute-start | bytes 2359304 | tf_op jit(solution)/shard_map/ppermute | solution.py:14
  15.2 4.9 %copy-start.12 = (s32[8]{0:T(128)S(1)}, s32[8]{0:T(128)}, u32[]{:S(2)}) copy-start(s32[8]{0:T(128)} %param.12) | copy-start | bytes 100
  15.2 53.9 %all-to-all-start = ((bf16[384,4,768]{0,2,1:T(8,128)(2,1)}), bf16[384,4,768]{0,2,1:T(8,128)(2,1)}, u32[]{:S(2)}, u32[]{:S(2)}) async-start(bf16[384,4,768]{0,2,1:T(8,128)(2,1)} %constant_dynamic-slice_fusion.4), calls=%async_computation | async-start | bytes 4718592 | tf_op jit(solution)/shard_map/all_to_all | solution.py:158
  47.3 3.9 %copy-start.10 = (f32[384]{0:T(512)S(1)}, f32[384]{0:T(512)}, u32[]{:S(2)}) copy-start(f32[384]{0:T(512)} %param.17) | copy-start | bytes 4612
  52.1 7.9 %copy-start.11 = (f32[384]{0:T(512)S(1)}, f32[384]{0:T(512)}, u32[]{:S(2)}) copy-start(f32[384]{0:T(512)} %param.16) | copy-start | bytes 4612
  55.8 22.5 %collective-permute-start = (bf16[512,768]{1,0:T(8,128)(2,1)}, bf16[512,768]{1,0:T(8,128)(2,1)}, u32[]{:S(2)}, u32[]{:S(2)}) collective-permute-start(bf16[512,768]{1,0:T(8,128)(2,1)} %get-tuple-element.25), channel_id=1, source_target_pairs={{0,4},{4,8},{8,12},{12,16},{16,20},{20,24},{24,28},{28,0},{1,5},{5... | collective-permute-start | bytes 2359304 | tf_op jit(solution)/shard_map/ppermute | solution.py:14
  59.9 26.8 %collective-permute-start.1 = (bf16[512,768]{1,0:T(8,128)(2,1)}, bf16[512,768]{1,0:T(8,128)(2,1)}, u32[]{:S(2)}, u32[]{:S(2)}) collective-permute-start(bf16[512,768]{1,0:T(8,128)(2,1)} %get-tuple-element.25), channel_id=1, source_target_pairs={{0,8},{4,12},{8,16},{12,20},{16,24},{20,28},{24,0},{28,4},{1,9},{5... | collective-permute-start | bytes 2359304 | tf_op jit(solution)/shard_map/ppermute | solution.py:14
  63.0 23.6 %copy-start.2 = (bf16[4,512,768]{2,1,0:T(8,128)(2,1)}, bf16[4,512,768]{2,1,0:T(8,128)(2,1)S(1)}, u32[]{:S(2)}) copy-start(bf16[4,512,768]{2,1,0:T(8,128)(2,1)S(1)} %pad_maximum_fusion.refs_4_.refs_5_) | copy-start | bytes 9437188
  86.7 13.0 %collective-permute-start.5 = (bf16[4,512,768]{2,1,0:T(8,128)(2,1)S(1)}, bf16[4,512,768]{2,1,0:T(8,128)(2,1)}, u32[]{:S(2)}, u32[]{:S(2)}) collective-permute-start(bf16[4,512,768]{2,1,0:T(8,128)(2,1)S(1)} %pad_maximum_fusion.refs_4_.refs_5_), channel_id=1, source_target_pairs={{0,4},{4,0},{8,12},{12,8},{16,20},{20,16},{24,28},{28,24},{1,5},{5... | collective-permute-start | bytes 9437192 | tf_op jit(solution)/shard_map/ppermute | solution.py:211
  93.1 3.4 %copy-start.7 = (bf16[1,512,768]{2,1,0:T(8,128)(2,1)S(1)}, bf16[1,512,768]{2,1,0:T(8,128)(2,1)}, u32[]{:S(2)}) copy-start(bf16[1,512,768]{2,1,0:T(8,128)(2,1)} %get-tuple-element.24) | copy-start | bytes 2359300
  96.0 69.0 %collective-permute-start.12 = (bf16[3,384,768]{2,1,0:T(8,128)(2,1)}, bf16[3,384,768]{2,1,0:T(8,128)(2,1)}, u32[]{:S(2)}, u32[]{:S(2)}) collective-permute-start(bf16[3,384,768]{2,1,0:T(8,128)(2,1)} %pad_maximum_fusion.2), channel_id=1, source_target_pairs={{0,4},{4,0},{8,12},{12,8},{16,20},{20,16},{24,28},{28,24},{1,5},{5... | collective-permute-start | bytes 5308424 | tf_op jit(solution)/shard_map/ppermute | solution.py:234
  117.4 23.6 %collective-permute-start.8 = (bf16[256,384]{1,0:T(8,128)(2,1)}, bf16[256,384]{1,0:T(8,128)(2,1)S(1)}, u32[]{:S(2)}, u32[]{:S(2)}) collective-permute-start(bf16[256,384]{1,0:T(8,128)(2,1)} %shard_map.100), channel_id=1, source_target_pairs={{0,2},{1,3},{2,0},{3,1},{4,6},{5,7},{6,4},{7,5},{8,10},{9,11},{10,... | collective-permute-start | bytes 589832 | tf_op jit(solution)/shard_map/ppermute | solution.py:240
  120.3 21.9 %collective-permute-start.6 = (bf16[256,384]{1,0:T(8,128)(2,1)}, bf16[256,384]{1,0:T(8,128)(2,1)S(1)}, u32[]{:S(2)}, u32[]{:S(2)}) collective-permute-start(bf16[256,384]{1,0:T(8,128)(2,1)} %shard_map.100), channel_id=1, source_target_pairs={{0,1},{1,2},{2,3},{3,0},{4,5},{5,6},{6,7},{7,4},{8,9},{9,10},{10,1... | collective-permute-start | bytes 589832 | tf_op jit(solution)/shard_map/ppermute | solution.py:240
  120.4 20.7 %copy-start.8 = (bf16[256,384]{1,0:T(8,128)(2,1)S(1)}, bf16[256,384]{1,0:T(8,128)(2,1)}, u32[]{:S(2)}) copy-start(bf16[256,384]{1,0:T(8,128)(2,1)} %shard_map.100) | copy-start | bytes 589828
  138.3 24.9 %copy-start.4 = (bf16[384,1,768]{2,0,1:T(8,128)(2,1)S(1)}, bf16[384,1,768]{2,0,1:T(8,128)(2,1)}, u32[]{:S(2)}) copy-start(bf16[384,1,768]{2,0,1:T(8,128)(2,1)} %copy.31) | copy-start | bytes 1769476
  138.3 25.5 %copy-start.3 = (bf16[384,1,768]{2,0,1:T(8,128)(2,1)S(1)}, bf16[384,1,768]{2,0,1:T(8,128)(2,1)}, u32[]{:S(2)}) copy-start(bf16[384,1,768]{2,0,1:T(8,128)(2,1)} %copy.30) | copy-start | bytes 1769476
  138.3 20.7 %collective-permute-start.9 = (bf16[256,384]{1,0:T(8,128)(2,1)}, bf16[256,384]{1,0:T(8,128)(2,1)S(1)}, u32[]{:S(2)}, u32[]{:S(2)}) collective-permute-start(bf16[256,384]{1,0:T(8,128)(2,1)} %shard_map.101), channel_id=1, source_target_pairs={{0,2},{1,3},{2,0},{3,1},{4,6},{5,7},{6,4},{7,5},{8,10},{9,11},{10,... | collective-permute-start | bytes 589832 | tf_op jit(solution)/shard_map/ppermute | solution.py:240
  140.7 20.9 %collective-permute-start.7 = (bf16[256,384]{1,0:T(8,128)(2,1)}, bf16[256,384]{1,0:T(8,128)(2,1)S(1)}, u32[]{:S(2)}, u32[]{:S(2)}) collective-permute-start(bf16[256,384]{1,0:T(8,128)(2,1)} %shard_map.101), channel_id=1, source_target_pairs={{0,1},{1,2},{2,3},{3,0},{4,5},{5,6},{6,7},{7,4},{8,9},{9,10},{10,1... | collective-permute-start | bytes 589832 | tf_op jit(solution)/shard_map/ppermute | solution.py:240
  141.0 18.0 %collective-permute-start.10 = (bf16[256,384]{1,0:T(8,128)(2,1)S(1)}, bf16[256,384]{1,0:T(8,128)(2,1)S(1)}, u32[]{:S(2)}, u32[]{:S(2)}) collective-permute-start(bf16[256,384]{1,0:T(8,128)(2,1)S(1)} %copy-done.8), channel_id=1, source_target_pairs={{0,3},{1,0},{2,1},{3,2},{4,7},{5,4},{6,5},{7,6},{8,11},{9,8},{10,9... | collective-permute-start | bytes 589832 | tf_op jit(solution)/shard_map/ppermute | solution.py:240
  142.2 21.0 %collective-permute-start.11 = (bf16[256,384]{1,0:T(8,128)(2,1)}, bf16[256,384]{1,0:T(8,128)(2,1)S(1)}, u32[]{:S(2)}, u32[]{:S(2)}) collective-permute-start(bf16[256,384]{1,0:T(8,128)(2,1)} %shard_map.101), channel_id=1, source_target_pairs={{0,3},{1,0},{2,1},{3,2},{4,7},{5,4},{6,5},{7,6},{8,11},{9,8},{10,9... | collective-permute-start | bytes 589832 | tf_op jit(solution)/shard_map/ppermute | solution.py:240
  159.0 5.4 %copy-start.5 = (bf16[384,1,768]{2,0,1:T(8,128)(2,1)S(1)}, bf16[384,1,768]{2,0,1:T(8,128)(2,1)}, u32[]{:S(2)}) copy-start(bf16[384,1,768]{2,0,1:T(8,128)(2,1)} %copy.32) | copy-start | bytes 1769476
  168.3 1.7 copy-start.9
  170.0 4.7 %copy-start.1 = (bf16[8,3,6144]{2,0,1:T(8,128)(2,1)S(1)}, bf16[8,3,6144]{2,0,1:T(8,128)(2,1)}, u32[]{:S(2)}) copy-start(bf16[8,3,6144]{2,0,1:T(8,128)(2,1)} %param.11) | copy-start | bytes 884740

commit v9 on v8

--- a/solution.py
+++ b/solution.py
@@ -152,12 +152,13 @@
     groups = lax.axis_size("head")
     columns = w_out.shape[1] // groups
     half = columns // 2
-    blocks = lax.dynamic_slice_in_dim(
-        w_out.reshape(w_out.shape[0], groups, columns), core * half, half, 2
-    )
-    exchanged = lax.all_to_all(blocks, "head", 1, 1)
+    blocks = jnp.stack([
+        lax.dynamic_slice_in_dim(w_out, dest * columns + core * half, half, 1)
+        for dest in range(groups)
+    ])
+    exchanged = lax.all_to_all(blocks, "head", 0, 0)
     mine = [
-        lax.dynamic_index_in_dim(exchanged, (head - shift) % groups, 1, keepdims=False)
+        lax.dynamic_index_in_dim(exchanged, (head - shift) % groups, 0, keepdims=False)
         for shift in range(groups)
     ]
     own_full = lax.dynamic_slice_in_dim(w_out, head * columns, columns, 1)

time: 176 us -> 169 us (0.960)
  local copies, waits for them, and re-layouts: 35.2 us -> 20.7 us
  waiting for transfers between devices: 33.9 us -> 40.2 us
    dynamic_slice x5 -> x0, local copies, waits for them, and re-layouts: 12.4 us -> none  [the longest x4 9.05 us: fetch_out_weight(): lax.dynamic_index_in_dim(exchanged, (head - shift) % groups, 1, keepdims=...]
    unnamed x32 -> x31, local copies, waits for them, and re-layouts: 7.21 us -> 0.59 us
    ppermute x5, waiting for transfers between devices: 8.42 us -> 14.7 us  [from_behind(): lax.ppermute(shard, axis, [(i, (i + by) % length) for i in range(length)])]
    squeeze x0 -> x1, local copies, waits for them, and re-layouts: none -> 2.77 us  [fetch_out_weight(): lax.dynamic_index_in_dim(exchanged, (head - shift) % groups, 0, keepdims=...]
  transfers between devices with their start and end apart: 14 -> 14, of which waited for: 5 -> 6; matrix products, arithmetic and copies ran while one was open for 42% -> 36% of each run, Pallas kernels for 20% -> 21%
where the time goes in v9:
time: 169 us; the launch traced here: 168 us
  waiting for transfers between devices  40.2 us (24%)
  Pallas kernels  35.8 us (21%)
  matrix products  30.9 us (18%)
  local copies, waits for them, and re-layouts  20.7 us (12%)
  other arithmetic  20.4 us (12%)
  starting transfers between devices  19.7 us (12%)
    pallas_call x2, Pallas kernels, flash(): pl.pallas_call(kernel, grid_spec=grid_spec, out_shape=jax.ShapeDtypeStruc...  35.8 us
    ppermute x6, waiting for transfers between devices, local(): lax.ppermute(part, 'head', [(i, (i + shift) % groups) for i in range(grou...  19.4 us
    dot_general x1, matrix products, local(): jnp.einsum('td,dkh->tkh', hidden, w_qkv, preferred_element_type=jnp.float32)  18.8 us
    ppermute x5, waiting for transfers between devices, from_behind(): lax.ppermute(shard, axis, [(i, (i + by) % length) for i in range(length)])  14.7 us
    ppermute x6, starting transfers between devices, local(): lax.ppermute(part, 'head', [(i, (i + shift) % groups) for i in range(grou...  7.44 us
    ppermute x5, starting transfers between devices, from_behind(): lax.ppermute(shard, axis, [(i, (i + by) % length) for i in range(length)])  6.83 us
    all_to_all x1, waiting for transfers between devices, fetch_out_weight(): exchanged = lax.all_to_all(blocks, 'head', 0, 0)  6.18 us
    another operation x2, other arithmetic, local(): jnp.stack([local_kv, before, earlier]).reshape(3, span, 2 * width)  5.29 us
  transfers between devices with their start and end apart: 14, of which 6 were waited for; matrix products, arithmetic and copies ran while one was open for 36% of the time, Pallas kernels for 21%

profile of v9, /device:TPU:9, one launch (start us, length us, event | category | flops | bytes accessed | tf_op | source)
XLA Modules:
  0.0 168.1 jit_solution(440826005126256251)
XLA Ops:
  0.0 2.5 %reshape.53 = bf16[1,512,768]{2,1,0:T(8,128)(2,1)S(1)} reshape(bf16[1,512,2,384]{3,2,1,0:T(2,128)(2,1)} %param.18) | data formatting | bytes 1572864 | tf_op jit(solution)/shard_map/reshape | solution.py:191
  2.5 2.2 %collective-permute-start.4 = (bf16[1,512,768]{2,1,0:T(8,128)(2,1)S(1)}, bf16[1,512,768]{2,1,0:T(8,128)(2,1)}, u32[]{:S(2)}, u32[]{:S(2)}) collective-permute-start(bf16[1,512,768]{2,1,0:T(8,128)(2,1)S(1)} %reshape.53), channel_id=1, source_target_pairs={{0,24},{4,28},{8,0},{12,4},{16,8},{20,12},{24,16},{28,20},{1,25},{... | collective-permute-start | bytes 2359304 | tf_op jit(solution)/shard_map/ppermute | solution.py:14
  5.3 1.8 %dynamic-slice_bitcast_fusion.6 = (bf16[1,384,768]{2,1,0:T(8,128)(2,1)S(1)}, bf16[1,384,768]{2,1,0:T(8,128)(2,1)S(1)}, bf16[1,384,768]{2,1,0:T(8,128)(2,1)S(1)}, bf16[1,384,768]{2,1,0:T(8,128)(2,1)S(1)}) fusion(bf16[384,6144]{1,0:T(8,128)(2,1)} %param.19, s32[]{:T(128)S(6)} %select_n.112, s32[]{:T(128)S(6)} %select_n.114, s32[]{:T(128)S(6)} %select_n.113, ...), kind=kLoop, calls=%fused_computation.44 | loop fusion | bytes 4718608 | tf_op jit(solution)/shard_map/stack | solution.py:155
  7.0 1.7 %pad_maximum_fusion.1 = bf16[4,384,768]{2,1,0:T(8,128)(2,1)} fusion(bf16[1,384,768]{2,1,0:T(8,128)(2,1)S(1)} %get-tuple-element.22, bf16[1,384,768]{2,1,0:T(8,128)(2,1)S(1)} %get-tuple-element.20, bf16[1,384,768]{2,1,0:T(8,128)(2,1)S(1)} %get-tuple-element.21, bf16[1,384,768]{2,1,0:T(8,128)(2,1)S(1)} %get-tuple-element.19), kind=kLoop, calls=%fused_computation.17 | loop fusion | flops 3538944 | bytes 4718592 | tf_op jit(solution)/shard_map/stack | solution.py:155
  8.8 4.9 %all-to-all-start = ((bf16[4,384,768]{2,1,0:T(8,128)(2,1)}), bf16[4,384,768]{2,1,0:T(8,128)(2,1)}, u32[]{:S(2)}, u32[]{:S(2)}) async-start(bf16[4,384,768]{2,1,0:T(8,128)(2,1)} %pad_maximum_fusion.1), calls=%async_computation | async-start | bytes 4718592 | tf_op jit(solution)/shard_map/all_to_all | solution.py:159
  15.2 4.1 %fusion = f32[512]{0:T(512)S(1)} fusion(bf16[512,6144]{1,0:T(8,128)(2,1)} %param.10), kind=kLoop, calls=%fused_computation.2 | loop fusion | flops 9436672 | bytes 6293504 | tf_op jit(solution)/shard_map/reduce_sum | solution.py:200
  19.3 18.8 %fusion.5 = f32[512,3,384]{0,2,1:T(8,128)} fusion(bf16[6144,3,384]{2,0,1:T(8,128)(2,1)} %param.15, bf16[512,6144]{1,0:T(8,128)(2,1)} %param.10, f32[6144]{0:T(1024)S(1)} %bitcast.87, f32[6144]{0:T(1024)S(1)} %bitcast.88, f32[512]{0:T(512)S(1)} %add_rsqrt_fusion.2), kind=kOutput, calls=%fused_computation.7 | convolution fusion | flops 7263485952 | bytes 22857728 | tf_op jit(solution)/shard_map/td,dkh->tkh/dot_general | solution.py:202
  38.1 1.5 fusion.33
  40.8 1.4 copy.18
  47.0 2.2 %fusion.32 = (bf16[1,512,768]{2,1,0:T(8,128)(2,1)}, bf16[512,768]{1,0:T(8,128)(2,1)}) fusion(bf16[512,384]{1,0:T(8,128)(2,1)S(1)} %bitcast.82, bf16[512,384]{1,0:T(8,128)(2,1)} %fusion.15), kind=kLoop, calls=%fused_computation.95 | loop fusion | flops 1572864 | bytes 2359296 | tf_op jit(solution)/shard_map/stack | solution.py:222
  49.3 4.1 %collective-permute-start = (bf16[512,768]{1,0:T(8,128)(2,1)}, bf16[512,768]{1,0:T(8,128)(2,1)}, u32[]{:S(2)}, u32[]{:S(2)}) collective-permute-start(bf16[512,768]{1,0:T(8,128)(2,1)} %get-tuple-element.29), channel_id=1, source_target_pairs={{0,4},{4,8},{8,12},{12,16},{16,20},{20,24},{24,28},{28,0},{1,5},{5... | collective-permute-start | bytes 2359304 | tf_op jit(solution)/shard_map/ppermute | solution.py:14
  54.5 2.0 %pad_maximum_fusion.refs_4_.refs_5_ = bf16[4,512,768]{2,1,0:T(8,128)(2,1)S(1)} fusion(bf16[1,512,768]{2,1,0:T(8,128)(2,1)} %collective-permute-done.4, bf16[1,512,768]{2,1,0:T(8,128)(2,1)} %collective-permute-done.3, bf16[1,512,768]{2,1,0:T(8,128)(2,1)} %collective-permute-done.2, bf16[1,512,768]{2,1,0:T(8,128)(2,1)} %copy-done.6), kind=kLoop, calls=%fused_computation.11 | loop fusion | flops 4718592 | bytes 6291456 | tf_op jit(solution)/shard_map/concatenate | solution.py:193
  56.5 6.2 %all-to-all-done = bf16[4,384,768]{2,1,0:T(8,128)(2,1)} async-done(((bf16[4,384,768]{2,1,0:T(8,128)(2,1)}), bf16[4,384,768]{2,1,0:T(8,128)(2,1)}, u32[]{:S(2)}, u32[]{:S(2)}) %all-to-all-start) | async-done | bytes 2359328 | tf_op jit(solution)/shard_map/all_to_all | solution.py:159
  62.7 2.8 %dynamic-slice_bitcast_fusion = (bf16[384,768]{1,0:T(8,128)(2,1)}, bf16[384,768]{1,0:T(8,128)(2,1)}, bf16[384,768]{1,0:T(8,128)(2,1)}) fusion(bf16[4,384,768]{2,1,0:T(8,128)(2,1)} %all-to-all-done, s32[]{:T(128)S(6)} %select_n.121, s32[]{:T(128)S(6)} %select_n.119, s32[]{:T(128)S(6)} %select_n.117), kind=kLoop, calls=%fused_computation.38 | loop fusion | bytes 3538956 | tf_op jit(solution)/shard_map/jit(dynamic_index_in_dim)/squeeze | solution.py:161
  65.5 5.0 %collective-permute-done = bf16[512,768]{1,0:T(8,128)(2,1)} collective-permute-done((bf16[512,768]{1,0:T(8,128)(2,1)}, bf16[512,768]{1,0:T(8,128)(2,1)}, u32[]{:S(2)}, u32[]{:S(2)}) %collective-permute-start) | collective-permute-done | bytes 786464 | tf_op jit(solution)/shard_map/ppermute | solution.py:14
  70.5 9.7 %collective-permute-done.1 = bf16[512,768]{1,0:T(8,128)(2,1)} collective-permute-done((bf16[512,768]{1,0:T(8,128)(2,1)}, bf16[512,768]{1,0:T(8,128)(2,1)}, u32[]{:S(2)}, u32[]{:S(2)}) %collective-permute-start.1) | collective-permute-done | bytes 786464 | tf_op jit(solution)/shard_map/ppermute | solution.py:14
  83.1 1.7 %fusion.34 = (bf16[256,3,128]{0,2,1:T(8,128)(2,1)S(1)}, bf16[256,3,128]{0,2,1:T(8,128)(2,1)}) fusion(bf16[512,3,128]{0,2,1:T(8,128)(2,1)} %multiply_convert_fusion), kind=kLoop, calls=%fused_computation.97 | loop fusion | bytes 786432 | tf_op jit(solution)/shard_map/slice | solution.py:231
  84.8 1.8 %copy.22.refs_1_ = bf16[256,384]{1,0:T(8,128)(2,1)} copy(bf16[256,384]{0,1:T(8,128)(2,1)} %bitcast.84) | data formatting | bytes 393216 | tf_op jit(solution)/shard_map/slice | solution.py:231
  86.5 2.9 %pad_maximum_fusion.3 = bf16[3,384,768]{2,1,0:T(8,128)(2,1)} fusion(bf16[1,384,768]{2,1,0:T(8,128)(2,1)} %bitcast.79, bf16[1,384,768]{2,1,0:T(8,128)(2,1)} %bitcast.78, bf16[1,384,768]{2,1,0:T(8,128)(2,1)} %bitcast.77), kind=kLoop, calls=%fused_computation.19 | loop fusion | flops 1769472 | bytes 3538944 | tf_op jit(solution)/shard_map/stack | solution.py:236
  90.0 3.1 %pad_maximum_fusion.2.refs_2_.refs_3_ = bf16[3,512,768]{2,1,0:T(8,128)(2,1)} fusion(bf16[1,512,768]{2,1,0:T(8,128)(2,1)} %bitcast.23, bf16[1,512,768]{2,1,0:T(8,128)(2,1)} %bitcast.22, bf16[1,512,768]{2,1,0:T(8,128)(2,1)S(1)} %copy-done.7), kind=kLoop, calls=%fused_computation.18 | loop fusion | flops 2359296 | bytes 4718592 | tf_op jit(solution)/shard_map/stack | solution.py:222
  93.0 17.8 %shard_map.100 = bf16[256,384]{1,0:T(8,128)(2,1)} custom-call(s32[6]{0:T(128)} %compare_select_fusion.6.refs_0_, bf16[256,384]{1,0:T(8,128)(2,1)} %copy.22.refs_1_, bf16[3,512,768]{2,1,0:T(8,128)(2,1)} %pad_maximum_fusion.2.refs_2_.refs_3_, bf16[3,512,768]{2,1,0:T(8,128)(2,1)} %pad_maximum_fusion.2.refs_2_.refs_3_, bf16[4,512,768]{2,1,0:T(8,128)(2,1)} %copy-done.2, ...), custom_call_target="tpu_custom_call" | custom-call | flops 905969664 | bytes 3538944 | tf_op jit(solution)/shard_map/pallas_call | solution.py:138
  110.8 2.1 %collective-permute-start.8 = (bf16[256,384]{1,0:T(8,128)(2,1)}, bf16[256,384]{1,0:T(8,128)(2,1)S(1)}, u32[]{:S(2)}, u32[]{:S(2)}) collective-permute-start(bf16[256,384]{1,0:T(8,128)(2,1)} %shard_map.100), channel_id=1, source_target_pairs={{0,2},{1,3},{2,0},{3,1},{4,6},{5,7},{6,4},{7,5},{8,10},{9,11},{10,... | collective-permute-start | bytes 589832 | tf_op jit(solution)/shard_map/ppermute | solution.py:241
  113.8 18.0 %shard_map.101 = bf16[256,384]{1,0:T(8,128)(2,1)} custom-call(s32[6]{0:T(128)} %compare_select_fusion.6.refs_0_, bf16[256,384]{1,0:T(8,128)(2,1)} %copy.23.refs_1_, bf16[3,512,768]{2,1,0:T(8,128)(2,1)} %pad_maximum_fusion.2.refs_2_.refs_3_, bf16[3,512,768]{2,1,0:T(8,128)(2,1)} %pad_maximum_fusion.2.refs_2_.refs_3_, bf16[4,512,768]{2,1,0:T(8,128)(2,1)} %copy-done.2, ...), custom_call_target="tpu_custom_call" | custom-call | flops 905969664 | bytes 3538944 | tf_op jit(solution)/shard_map/pallas_call | solution.py:138
  131.7 2.4 %collective-permute-start.9 = (bf16[256,384]{1,0:T(8,128)(2,1)}, bf16[256,384]{1,0:T(8,128)(2,1)S(1)}, u32[]{:S(2)}, u32[]{:S(2)}) collective-permute-start(bf16[256,384]{1,0:T(8,128)(2,1)} %shard_map.101), channel_id=1, source_target_pairs={{0,2},{1,3},{2,0},{3,1},{4,6},{5,7},{6,4},{7,5},{8,10},{9,11},{10,... | collective-permute-start | bytes 589832 | tf_op jit(solution)/shard_map/ppermute | solution.py:241
  135.7 1.5 collective-permute-start.11
  137.1 15.3 %collective-permute-done.10 = bf16[256,384]{1,0:T(8,128)(2,1)S(1)} collective-permute-done((bf16[256,384]{1,0:T(8,128)(2,1)S(1)}, bf16[256,384]{1,0:T(8,128)(2,1)S(1)}, u32[]{:S(2)}, u32[]{:S(2)}) %collective-permute-start.10) | collective-permute-done | bytes 196640 | tf_op jit(solution)/shard_map/ppermute | solution.py:241
  152.5 2.6 %collective-permute-done.7 = bf16[256,384]{1,0:T(8,128)(2,1)S(1)} collective-permute-done((bf16[256,384]{1,0:T(8,128)(2,1)}, bf16[256,384]{1,0:T(8,128)(2,1)S(1)}, u32[]{:S(2)}, u32[]{:S(2)}) %collective-permute-start.7) | collective-permute-done | bytes 196640 | tf_op jit(solution)/shard_map/ppermute | solution.py:241
  155.1 1.5 collective-permute-done.11
  158.4 1.6 convolution_convert_fusion.2
  160.1 1.6 convolution_convert_fusion.3
  161.7 1.7 convert_add_fusion
  163.4 4.7 %fusion.12 = f32[512,1536]{1,0:T(8,128)} fusion(f32[512,768]{1,0:T(8,128)S(1)} %convert_add_fusion, f32[512,768]{1,0:T(8,128)S(1)} %convert_add_fusion.1, f32[1536]{0:T(1024)S(1)} %dynamic-slice_reduce_fusion, bf16[512,6144]{1,0:T(8,128)(2,1)} %param.10, s32[]{:T(128)S(6)} %select_n.103, pred[]{:T(512)S(6)} %eq.29, bf16[384,6144]{1,0:T(8,128)(2,1)} %param.19, ...), kind=kOutput, calls=%fused_computation.15 | convolution fusion | flops 611844096 | bytes 9444864 | tf_op jit(solution)/shard_map/dot_general | solution.py:249
  (78 shorter events, 16.7 us)
Async XLA Ops:
  0.0 14.2 %copy-start = (bf16[8,3,6144]{2,0,1:T(8,128)(2,1)S(1)}, bf16[8,3,6144]{2,0,1:T(8,128)(2,1)}, u32[]{:S(2)}) copy-start(bf16[8,3,6144]{2,0,1:T(8,128)(2,1)} %param.11) | copy-start | bytes 884740
  2.5 4.5 %copy-start.6 = (bf16[1,512,768]{2,1,0:T(8,128)(2,1)}, bf16[1,512,768]{2,1,0:T(8,128)(2,1)S(1)}, u32[]{:S(2)}) copy-start(bf16[1,512,768]{2,1,0:T(8,128)(2,1)S(1)} %reshape.53) | copy-start | bytes 2359300
  2.5 52.0 %collective-permute-start.4 = (bf16[1,512,768]{2,1,0:T(8,128)(2,1)S(1)}, bf16[1,512,768]{2,1,0:T(8,128)(2,1)}, u32[]{:S(2)}, u32[]{:S(2)}) collective-permute-start(bf16[1,512,768]{2,1,0:T(8,128)(2,1)S(1)} %reshape.53), channel_id=1, source_target_pairs={{0,24},{4,28},{8,0},{12,4},{16,8},{20,12},{24,16},{28,20},{1,25},{... | collective-permute-start | bytes 2359304 | tf_op jit(solution)/shard_map/ppermute | solution.py:14
  4.7 49.7 %collective-permute-start.3 = (bf16[1,512,768]{2,1,0:T(8,128)(2,1)S(1)}, bf16[1,512,768]{2,1,0:T(8,128)(2,1)}, u32[]{:S(2)}, u32[]{:S(2)}) collective-permute-start(bf16[1,512,768]{2,1,0:T(8,128)(2,1)S(1)} %reshape.53), channel_id=1, source_target_pairs={{0,16},{4,20},{8,24},{12,28},{16,0},{20,4},{24,8},{28,12},{1,17},{... | collective-permute-start | bytes 2359304 | tf_op jit(solution)/shard_map/ppermute | solution.py:14
  5.0 49.5 %collective-permute-start.2 = (bf16[1,512,768]{2,1,0:T(8,128)(2,1)S(1)}, bf16[1,512,768]{2,1,0:T(8,128)(2,1)}, u32[]{:S(2)}, u32[]{:S(2)}) collective-permute-start(bf16[1,512,768]{2,1,0:T(8,128)(2,1)S(1)} %reshape.53), channel_id=1, source_target_pairs={{0,8},{4,12},{8,16},{12,20},{16,24},{20,28},{24,0},{28,4},{1,9},{5... | collective-permute-start | bytes 2359304 | tf_op jit(solution)/shard_map/ppermute | solution.py:14
  8.8 4.9 %copy-start.12 = (s32[8]{0:T(128)S(1)}, s32[8]{0:T(128)}, u32[]{:S(2)}) copy-start(s32[8]{0:T(128)} %param.12) | copy-start | bytes 100
  8.8 53.9 %all-to-all-start = ((bf16[4,384,768]{2,1,0:T(8,128)(2,1)}), bf16[4,384,768]{2,1,0:T(8,128)(2,1)}, u32[]{:S(2)}, u32[]{:S(2)}) async-start(bf16[4,384,768]{2,1,0:T(8,128)(2,1)} %pad_maximum_fusion.1), calls=%async_computation | async-start | bytes 4718592 | tf_op jit(solution)/shard_map/all_to_all | solution.py:159
  40.8 3.9 %copy-start.10 = (f32[384]{0:T(512)S(1)}, f32[384]{0:T(512)}, u32[]{:S(2)}) copy-start(f32[384]{0:T(512)} %param.17) | copy-start | bytes 4612
  45.6 7.9 %copy-start.11 = (f32[384]{0:T(512)S(1)}, f32[384]{0:T(512)}, u32[]{:S(2)}) copy-start(f32[384]{0:T(512)} %param.16) | copy-start | bytes 4612
  49.3 21.2 %collective-permute-start = (bf16[512,768]{1,0:T(8,128)(2,1)}, bf16[512,768]{1,0:T(8,128)(2,1)}, u32[]{:S(2)}, u32[]{:S(2)}) collective-permute-start(bf16[512,768]{1,0:T(8,128)(2,1)} %get-tuple-element.29), channel_id=1, source_target_pairs={{0,4},{4,8},{8,12},{12,16},{16,20},{20,24},{24,28},{28,0},{1,5},{5... | collective-permute-start | bytes 2359304 | tf_op jit(solution)/shard_map/ppermute | solution.py:14
  53.4 26.8 %collective-permute-start.1 = (bf16[512,768]{1,0:T(8,128)(2,1)}, bf16[512,768]{1,0:T(8,128)(2,1)}, u32[]{:S(2)}, u32[]{:S(2)}) collective-permute-start(bf16[512,768]{1,0:T(8,128)(2,1)} %get-tuple-element.29), channel_id=1, source_target_pairs={{0,8},{4,12},{8,16},{12,20},{16,24},{20,28},{24,0},{28,4},{1,9},{5... | collective-permute-start | bytes 2359304 | tf_op jit(solution)/shard_map/ppermute | solution.py:14
  56.5 28.2 %copy-start.2 = (bf16[4,512,768]{2,1,0:T(8,128)(2,1)}, bf16[4,512,768]{2,1,0:T(8,128)(2,1)S(1)}, u32[]{:S(2)}) copy-start(bf16[4,512,768]{2,1,0:T(8,128)(2,1)S(1)} %pad_maximum_fusion.refs_4_.refs_5_) | copy-start | bytes 9437188
  80.2 12.9 %collective-permute-start.5 = (bf16[4,512,768]{2,1,0:T(8,128)(2,1)S(1)}, bf16[4,512,768]{2,1,0:T(8,128)(2,1)}, u32[]{:S(2)}, u32[]{:S(2)}) collective-permute-start(bf16[4,512,768]{2,1,0:T(8,128)(2,1)S(1)} %pad_maximum_fusion.refs_4_.refs_5_), channel_id=1, source_target_pairs={{0,4},{4,0},{8,12},{12,8},{16,20},{20,16},{24,28},{28,24},{1,5},{5... | collective-permute-start | bytes 9437192 | tf_op jit(solution)/shard_map/ppermute | solution.py:212
  86.5 3.4 %copy-start.7 = (bf16[1,512,768]{2,1,0:T(8,128)(2,1)S(1)}, bf16[1,512,768]{2,1,0:T(8,128)(2,1)}, u32[]{:S(2)}) copy-start(bf16[1,512,768]{2,1,0:T(8,128)(2,1)} %get-tuple-element.28) | copy-start | bytes 2359300
  89.5 69.0 %collective-permute-start.12 = (bf16[3,384,768]{2,1,0:T(8,128)(2,1)}, bf16[3,384,768]{2,1,0:T(8,128)(2,1)}, u32[]{:S(2)}, u32[]{:S(2)}) collective-permute-start(bf16[3,384,768]{2,1,0:T(8,128)(2,1)} %pad_maximum_fusion.3), channel_id=1, source_target_pairs={{0,4},{4,0},{8,12},{12,8},{16,20},{20,16},{24,28},{28,24},{1,5},{5... | collective-permute-start | bytes 5308424 | tf_op jit(solution)/shard_map/ppermute | solution.py:235
  110.8 23.6 %collective-permute-start.8 = (bf16[256,384]{1,0:T(8,128)(2,1)}, bf16[256,384]{1,0:T(8,128)(2,1)S(1)}, u32[]{:S(2)}, u32[]{:S(2)}) collective-permute-start(bf16[256,384]{1,0:T(8,128)(2,1)} %shard_map.100), channel_id=1, source_target_pairs={{0,2},{1,3},{2,0},{3,1},{4,6},{5,7},{6,4},{7,5},{8,10},{9,11},{10,... | collective-permute-start | bytes 589832 | tf_op jit(solution)/shard_map/ppermute | solution.py:241
  113.8 21.9 %collective-permute-start.6 = (bf16[256,384]{1,0:T(8,128)(2,1)}, bf16[256,384]{1,0:T(8,128)(2,1)S(1)}, u32[]{:S(2)}, u32[]{:S(2)}) collective-permute-start(bf16[256,384]{1,0:T(8,128)(2,1)} %shard_map.100), channel_id=1, source_target_pairs={{0,1},{1,2},{2,3},{3,0},{4,5},{5,6},{6,7},{7,4},{8,9},{9,10},{10,1... | collective-permute-start | bytes 589832 | tf_op jit(solution)/shard_map/ppermute | solution.py:241
  113.8 20.7 %copy-start.8 = (bf16[256,384]{1,0:T(8,128)(2,1)S(1)}, bf16[256,384]{1,0:T(8,128)(2,1)}, u32[]{:S(2)}) copy-start(bf16[256,384]{1,0:T(8,128)(2,1)} %shard_map.100) | copy-start | bytes 589828
  131.7 24.9 %copy-start.4 = (bf16[384,768]{1,0:T(8,128)(2,1)S(1)}, bf16[384,768]{1,0:T(8,128)(2,1)}, u32[]{:S(2)}) copy-start(bf16[384,768]{1,0:T(8,128)(2,1)} %get-tuple-element.17) | copy-start | bytes 1769476
  131.7 25.5 %copy-start.3 = (bf16[384,768]{1,0:T(8,128)(2,1)S(1)}, bf16[384,768]{1,0:T(8,128)(2,1)}, u32[]{:S(2)}) copy-start(bf16[384,768]{1,0:T(8,128)(2,1)} %get-tuple-element.16) | copy-start | bytes 1769476
  131.7 20.7 %collective-permute-start.9 = (bf16[256,384]{1,0:T(8,128)(2,1)}, bf16[256,384]{1,0:T(8,128)(2,1)S(1)}, u32[]{:S(2)}, u32[]{:S(2)}) collective-permute-start(bf16[256,384]{1,0:T(8,128)(2,1)} %shard_map.101), channel_id=1, source_target_pairs={{0,2},{1,3},{2,0},{3,1},{4,6},{5,7},{6,4},{7,5},{8,10},{9,11},{10,... | collective-permute-start | bytes 589832 | tf_op jit(solution)/shard_map/ppermute | solution.py:241
  134.1 20.9 %collective-permute-start.7 = (bf16[256,384]{1,0:T(8,128)(2,1)}, bf16[256,384]{1,0:T(8,128)(2,1)S(1)}, u32[]{:S(2)}, u32[]{:S(2)}) collective-permute-start(bf16[256,384]{1,0:T(8,128)(2,1)} %shard_map.101), channel_id=1, source_target_pairs={{0,1},{1,2},{2,3},{3,0},{4,5},{5,6},{6,7},{7,4},{8,9},{9,10},{10,1... | collective-permute-start | bytes 589832 | tf_op jit(solution)/shard_map/ppermute | solution.py:241
  134.4 18.0 %collective-permute-start.10 = (bf16[256,384]{1,0:T(8,128)(2,1)S(1)}, bf16[256,384]{1,0:T(8,128)(2,1)S(1)}, u32[]{:S(2)}, u32[]{:S(2)}) collective-permute-start(bf16[256,384]{1,0:T(8,128)(2,1)S(1)} %copy-done.8), channel_id=1, source_target_pairs={{0,3},{1,0},{2,1},{3,2},{4,7},{5,4},{6,5},{7,6},{8,11},{9,8},{10,9... | collective-permute-start | bytes 589832 | tf_op jit(solution)/shard_map/ppermute | solution.py:241
  135.7 21.0 %collective-permute-start.11 = (bf16[256,384]{1,0:T(8,128)(2,1)}, bf16[256,384]{1,0:T(8,128)(2,1)S(1)}, u32[]{:S(2)}, u32[]{:S(2)}) collective-permute-start(bf16[256,384]{1,0:T(8,128)(2,1)} %shard_map.101), channel_id=1, source_target_pairs={{0,3},{1,0},{2,1},{3,2},{4,7},{5,4},{6,5},{7,6},{8,11},{9,8},{10,9... | collective-permute-start | bytes 589832 | tf_op jit(solution)/shard_map/ppermute | solution.py:241
  152.4 5.4 %copy-start.5 = (bf16[384,768]{1,0:T(8,128)(2,1)S(1)}, bf16[384,768]{1,0:T(8,128)(2,1)}, u32[]{:S(2)}) copy-start(bf16[384,768]{1,0:T(8,128)(2,1)} %get-tuple-element.18) | copy-start | bytes 1769476
  161.7 1.7 %copy-start.9 = (bf16[256,384]{1,0:T(8,128)(2,1)S(1)}, bf16[256,384]{1,0:T(8,128)(2,1)}, u32[]{:S(2)}) copy-start(bf16[256,384]{1,0:T(8,128)(2,1)} %shard_map.101) | copy-start | bytes 589828
  163.4 4.7 %copy-start.1 = (bf16[8,3,6144]{2,0,1:T(8,128)(2,1)S(1)}, bf16[8,3,6144]{2,0,1:T(8,128)(2,1)}, u32[]{:S(2)}) copy-start(bf16[8,3,6144]{2,0,1:T(8,128)(2,1)} %param.11) | copy-start | bytes 884740

commit v10 on v9

--- a/solution.py
+++ b/solution.py
@@ -55,23 +55,25 @@
         acc_sc[...] = jnp.zeros(acc_sc.shape, jnp.float32)
 
     def body(k_ref, v_ref):
-        bias = bias_ref[...][:, None, :]
+        rows = span // blocks
         for h in range(heads):
             cols = slice(h * HD, (h + 1) * HD)
-            q = q_ref[:, cols]
             k = k_ref[:, cols]
-            s = lax.dot_general(q, k, (((1,), (1,)), ((), ())), preferred_element_type=jnp.float32)
-            s = (s * (1.0 / HD**0.5)).reshape(blocks, span // blocks, s.shape[1]) + bias
-            s = s.reshape(span, -1)
-            m_prev = m_sc[h]
-            m_new = jnp.maximum(m_prev, jnp.max(s, axis=1, keepdims=True))
-            factor = jnp.exp(m_prev - m_new)
-            p = jnp.exp(s - m_new)
-            l_sc[h] = l_sc[h] * factor + jnp.sum(p, axis=1, keepdims=True)
-            acc_sc[h] = acc_sc[h] * factor + jnp.dot(
-                p.astype(jnp.bfloat16), v_ref[:, cols], preferred_element_type=jnp.float32
-            )
-            m_sc[h] = m_new
+            v = v_ref[:, cols]
+            for a in range(blocks):
+                part = slice(a * rows, (a + 1) * rows)
+                q = q_ref[part, cols]
+                s = lax.dot_general(q, k, (((1,), (1,)), ((), ())), preferred_element_type=jnp.float32)
+                s = s * (1.0 / HD**0.5) + bias_ref[a : a + 1, :]
+                m_prev = m_sc[h, part]
+                m_new = jnp.maximum(m_prev, jnp.max(s, axis=1, keepdims=True))
+                factor = jnp.exp(m_prev - m_new)
+                p = jnp.exp(s - m_new)
+                l_sc[h, part] = l_sc[h, part] * factor + jnp.sum(p, axis=1, keepdims=True)
+                acc_sc[h, part] = acc_sc[h, part] * factor + jnp.dot(
+                    p.astype(jnp.bfloat16), v, preferred_element_type=jnp.float32
+                )
+                m_sc[h, part] = m_new
 
     @pl.when(step < n_local)
     def _():

time: 169 us -> 182 us (1.077)
  Pallas kernels: 35.8 us -> 48.9 us
    pallas_call x2, Pallas kernels: 35.8 us -> 48.9 us  [flash(): pl.pallas_call(kernel, grid_spec=grid_spec, out_shape=jax.ShapeDtypeStruc...]
  transfers between devices with their start and end apart: 14 -> 14, of which waited for: 6 -> 6; matrix products, arithmetic and copies ran while one was open for 36% -> 33% of each run, Pallas kernels for 21% -> 27%
where the time goes in v10:
time: 182 us; the launch traced here: 181 us
  Pallas kernels  48.9 us (27%)
  waiting for transfers between devices  40.2 us (22%)
  matrix products  30.9 us (17%)
  local copies, waits for them, and re-layouts  20.7 us (11%)
  other arithmetic  20.4 us (11%)
  starting transfers between devices  19.7 us (11%)
    pallas_call x2, Pallas kernels, flash(): pl.pallas_call(kernel, grid_spec=grid_spec, out_shape=jax.ShapeDtypeStruc...  48.9 us
    ppermute x6, waiting for transfers between devices, local(): lax.ppermute(part, 'head', [(i, (i + shift) % groups) for i in range(grou...  19.4 us
    dot_general x1, matrix products, local(): jnp.einsum('td,dkh->tkh', hidden, w_qkv, preferred_element_type=jnp.float32)  18.8 us
    ppermute x5, waiting for transfers between devices, from_behind(): lax.ppermute(shard, axis, [(i, (i + by) % length) for i in range(length)])  14.7 us
    ppermute x6, starting transfers between devices, local(): lax.ppermute(part, 'head', [(i, (i + shift) % groups) for i in range(grou...  7.43 us
    ppermute x5, starting transfers between devices, from_behind(): lax.ppermute(shard, axis, [(i, (i + by) % length) for i in range(length)])  6.83 us
    all_to_all x1, waiting for transfers between devices, fetch_out_weight(): exchanged = lax.all_to_all(blocks, 'head', 0, 0)  6.18 us
    another operation x2, other arithmetic, local(): jnp.stack([local_kv, before, earlier]).reshape(3, span, 2 * width)  5.29 us
  transfers between devices with their start and end apart: 14, of which 6 were waited for; matrix products, arithmetic and copies ran while one was open for 33% of the time, Pallas kernels for 27%

profile of v10, /device:TPU:9, one launch (start us, length us, event | category | flops | bytes accessed | tf_op | source)
XLA Modules:
  0.0 181.2 jit_solution(7500925156673589888)
XLA Ops:
  0.0 2.5 %reshape.53 = bf16[1,512,768]{2,1,0:T(8,128)(2,1)S(1)} reshape(bf16[1,512,2,384]{3,2,1,0:T(2,128)(2,1)} %param.18) | data formatting | bytes 1572864 | tf_op jit(solution)/shard_map/reshape | solution.py:193
  2.5 2.2 %collective-permute-start.4 = (bf16[1,512,768]{2,1,0:T(8,128)(2,1)S(1)}, bf16[1,512,768]{2,1,0:T(8,128)(2,1)}, u32[]{:S(2)}, u32[]{:S(2)}) collective-permute-start(bf16[1,512,768]{2,1,0:T(8,128)(2,1)S(1)} %reshape.53), channel_id=1, source_target_pairs={{0,24},{4,28},{8,0},{12,4},{16,8},{20,12},{24,16},{28,20},{1,25},{... | collective-permute-start | bytes 2359304 | tf_op jit(solution)/shard_map/ppermute | solution.py:14
  5.3 1.8 dynamic-slice_bitcast_fusion.6
  7.0 1.7 pad_maximum_fusion.1
  8.8 4.9 %all-to-all-start = ((bf16[4,384,768]{2,1,0:T(8,128)(2,1)}), bf16[4,384,768]{2,1,0:T(8,128)(2,1)}, u32[]{:S(2)}, u32[]{:S(2)}) async-start(bf16[4,384,768]{2,1,0:T(8,128)(2,1)} %pad_maximum_fusion.1), calls=%async_computation | async-start | bytes 4718592 | tf_op jit(solution)/shard_map/all_to_all | solution.py:161
  15.2 4.1 %fusion = f32[512]{0:T(512)S(1)} fusion(bf16[512,6144]{1,0:T(8,128)(2,1)} %param.10), kind=kLoop, calls=%fused_computation.2 | loop fusion | flops 9436672 | bytes 6293504 | tf_op jit(solution)/shard_map/reduce_sum | solution.py:202
  19.3 18.8 %fusion.5 = f32[512,3,384]{0,2,1:T(8,128)} fusion(bf16[6144,3,384]{2,0,1:T(8,128)(2,1)} %param.15, bf16[512,6144]{1,0:T(8,128)(2,1)} %param.10, f32[6144]{0:T(1024)S(1)} %bitcast.87, f32[6144]{0:T(1024)S(1)} %bitcast.88, f32[512]{0:T(512)S(1)} %add_rsqrt_fusion.2), kind=kOutput, calls=%fused_computation.7 | convolution fusion | flops 7263485952 | bytes 22857728 | tf_op jit(solution)/shard_map/td,dkh->tkh/dot_general | solution.py:204
  38.1 1.5 fusion.33
  40.8 1.4 copy.18
  47.0 2.2 %fusion.32 = (bf16[1,512,768]{2,1,0:T(8,128)(2,1)}, bf16[512,768]{1,0:T(8,128)(2,1)}) fusion(bf16[512,384]{1,0:T(8,128)(2,1)S(1)} %bitcast.82, bf16[512,384]{1,0:T(8,128)(2,1)} %fusion.15), kind=kLoop, calls=%fused_computation.95 | loop fusion | flops 1572864 | bytes 2359296 | tf_op jit(solution)/shard_map/stack | solution.py:224
  49.3 4.1 %collective-permute-start = (bf16[512,768]{1,0:T(8,128)(2,1)}, bf16[512,768]{1,0:T(8,128)(2,1)}, u32[]{:S(2)}, u32[]{:S(2)}) collective-permute-start(bf16[512,768]{1,0:T(8,128)(2,1)} %get-tuple-element.29), channel_id=1, source_target_pairs={{0,4},{4,8},{8,12},{12,16},{16,20},{20,24},{24,28},{28,0},{1,5},{5... | collective-permute-start | bytes 2359304 | tf_op jit(solution)/shard_map/ppermute | solution.py:14
  54.5 2.0 %pad_maximum_fusion.refs_4_.refs_5_ = bf16[4,512,768]{2,1,0:T(8,128)(2,1)S(1)} fusion(bf16[1,512,768]{2,1,0:T(8,128)(2,1)} %collective-permute-done.4, bf16[1,512,768]{2,1,0:T(8,128)(2,1)} %collective-permute-done.3, bf16[1,512,768]{2,1,0:T(8,128)(2,1)} %collective-permute-done.2, bf16[1,512,768]{2,1,0:T(8,128)(2,1)} %copy-done.6), kind=kLoop, calls=%fused_computation.11 | loop fusion | flops 4718592 | bytes 6291456 | tf_op jit(solution)/shard_map/concatenate | solution.py:195
  56.5 6.2 %all-to-all-done = bf16[4,384,768]{2,1,0:T(8,128)(2,1)} async-done(((bf16[4,384,768]{2,1,0:T(8,128)(2,1)}), bf16[4,384,768]{2,1,0:T(8,128)(2,1)}, u32[]{:S(2)}, u32[]{:S(2)}) %all-to-all-start) | async-done | bytes 2359328 | tf_op jit(solution)/shard_map/all_to_all | solution.py:161
  62.7 2.8 %dynamic-slice_bitcast_fusion = (bf16[384,768]{1,0:T(8,128)(2,1)}, bf16[384,768]{1,0:T(8,128)(2,1)}, bf16[384,768]{1,0:T(8,128)(2,1)}) fusion(bf16[4,384,768]{2,1,0:T(8,128)(2,1)} %all-to-all-done, s32[]{:T(128)S(6)} %select_n.121, s32[]{:T(128)S(6)} %select_n.119, s32[]{:T(128)S(6)} %select_n.117), kind=kLoop, calls=%fused_computation.38 | loop fusion | bytes 3538956 | tf_op jit(solution)/shard_map/jit(dynamic_index_in_dim)/squeeze | solution.py:163
  65.5 5.0 %collective-permute-done = bf16[512,768]{1,0:T(8,128)(2,1)} collective-permute-done((bf16[512,768]{1,0:T(8,128)(2,1)}, bf16[512,768]{1,0:T(8,128)(2,1)}, u32[]{:S(2)}, u32[]{:S(2)}) %collective-permute-start) | collective-permute-done | bytes 786464 | tf_op jit(solution)/shard_map/ppermute | solution.py:14
  70.5 9.7 %collective-permute-done.1 = bf16[512,768]{1,0:T(8,128)(2,1)} collective-permute-done((bf16[512,768]{1,0:T(8,128)(2,1)}, bf16[512,768]{1,0:T(8,128)(2,1)}, u32[]{:S(2)}, u32[]{:S(2)}) %collective-permute-start.1) | collective-permute-done | bytes 786464 | tf_op jit(solution)/shard_map/ppermute | solution.py:14
  83.1 1.7 fusion.34
  84.8 1.8 copy.22.refs_1_
  86.5 2.9 %pad_maximum_fusion.3 = bf16[3,384,768]{2,1,0:T(8,128)(2,1)} fusion(bf16[1,384,768]{2,1,0:T(8,128)(2,1)} %bitcast.79, bf16[1,384,768]{2,1,0:T(8,128)(2,1)} %bitcast.78, bf16[1,384,768]{2,1,0:T(8,128)(2,1)} %bitcast.77), kind=kLoop, calls=%fused_computation.19 | loop fusion | flops 1769472 | bytes 3538944 | tf_op jit(solution)/shard_map/stack | solution.py:238
  90.0 3.1 %pad_maximum_fusion.2.refs_2_.refs_3_ = bf16[3,512,768]{2,1,0:T(8,128)(2,1)} fusion(bf16[1,512,768]{2,1,0:T(8,128)(2,1)} %bitcast.23, bf16[1,512,768]{2,1,0:T(8,128)(2,1)} %bitcast.22, bf16[1,512,768]{2,1,0:T(8,128)(2,1)S(1)} %copy-done.7), kind=kLoop, calls=%fused_computation.18 | loop fusion | flops 2359296 | bytes 4718592 | tf_op jit(solution)/shard_map/stack | solution.py:224
  93.0 24.4 %shard_map.100 = bf16[256,384]{1,0:T(8,128)(2,1)} custom-call(s32[6]{0:T(128)} %compare_select_fusion.6.refs_0_, bf16[256,384]{1,0:T(8,128)(2,1)} %copy.22.refs_1_, bf16[3,512,768]{2,1,0:T(8,128)(2,1)} %pad_maximum_fusion.2.refs_2_.refs_3_, bf16[3,512,768]{2,1,0:T(8,128)(2,1)} %pad_maximum_fusion.2.refs_2_.refs_3_, bf16[4,512,768]{2,1,0:T(8,128)(2,1)} %copy-done.2, ...), custom_call_target="tpu_custom_call" | custom-call | flops 905969664 | bytes 3538944 | tf_op jit(solution)/shard_map/pallas_call | solution.py:140
  117.4 2.1 %collective-permute-start.8 = (bf16[256,384]{1,0:T(8,128)(2,1)}, bf16[256,384]{1,0:T(8,128)(2,1)S(1)}, u32[]{:S(2)}, u32[]{:S(2)}) collective-permute-start(bf16[256,384]{1,0:T(8,128)(2,1)} %shard_map.100), channel_id=1, source_target_pairs={{0,2},{1,3},{2,0},{3,1},{4,6},{5,7},{6,4},{7,5},{8,10},{9,11},{10,... | collective-permute-start | bytes 589832 | tf_op jit(solution)/shard_map/ppermute | solution.py:243
  120.3 24.5 %shard_map.101 = bf16[256,384]{1,0:T(8,128)(2,1)} custom-call(s32[6]{0:T(128)} %compare_select_fusion.6.refs_0_, bf16[256,384]{1,0:T(8,128)(2,1)} %copy.23.refs_1_, bf16[3,512,768]{2,1,0:T(8,128)(2,1)} %pad_maximum_fusion.2.refs_2_.refs_3_, bf16[3,512,768]{2,1,0:T(8,128)(2,1)} %pad_maximum_fusion.2.refs_2_.refs_3_, bf16[4,512,768]{2,1,0:T(8,128)(2,1)} %copy-done.2, ...), custom_call_target="tpu_custom_call" | custom-call | flops 905969664 | bytes 3538944 | tf_op jit(solution)/shard_map/pallas_call | solution.py:140
  144.9 2.4 %collective-permute-start.9 = (bf16[256,384]{1,0:T(8,128)(2,1)}, bf16[256,384]{1,0:T(8,128)(2,1)S(1)}, u32[]{:S(2)}, u32[]{:S(2)}) collective-permute-start(bf16[256,384]{1,0:T(8,128)(2,1)} %shard_map.101), channel_id=1, source_target_pairs={{0,2},{1,3},{2,0},{3,1},{4,6},{5,7},{6,4},{7,5},{8,10},{9,11},{10,... | collective-permute-start | bytes 589832 | tf_op jit(solution)/shard_map/ppermute | solution.py:243
  148.8 1.5 collective-permute-start.11
  150.3 15.3 %collective-permute-done.10 = bf16[256,384]{1,0:T(8,128)(2,1)S(1)} collective-permute-done((bf16[256,384]{1,0:T(8,128)(2,1)S(1)}, bf16[256,384]{1,0:T(8,128)(2,1)S(1)}, u32[]{:S(2)}, u32[]{:S(2)}) %collective-permute-start.10) | collective-permute-done | bytes 196640 | tf_op jit(solution)/shard_map/ppermute | solution.py:243
  165.7 2.6 %collective-permute-done.7 = bf16[256,384]{1,0:T(8,128)(2,1)S(1)} collective-permute-done((bf16[256,384]{1,0:T(8,128)(2,1)}, bf16[256,384]{1,0:T(8,128)(2,1)S(1)}, u32[]{:S(2)}, u32[]{:S(2)}) %collective-permute-start.7) | collective-permute-done | bytes 196640 | tf_op jit(solution)/shard_map/ppermute | solution.py:243
  168.3 1.5 collective-permute-done.11
  171.6 1.6 convolution_convert_fusion.2
  173.2 1.6 convolution_convert_fusion.3
  174.9 1.7 convert_add_fusion
  176.6 4.7 %fusion.12 = f32[512,1536]{1,0:T(8,128)} fusion(f32[512,768]{1,0:T(8,128)S(1)} %convert_add_fusion, f32[512,768]{1,0:T(8,128)S(1)} %convert_add_fusion.1, f32[1536]{0:T(1024)S(1)} %dynamic-slice_reduce_fusion, bf16[512,6144]{1,0:T(8,128)(2,1)} %param.10, s32[]{:T(128)S(6)} %select_n.103, pred[]{:T(512)S(6)} %eq.29, bf16[384,6144]{1,0:T(8,128)(2,1)} %param.19, ...), kind=kOutput, calls=%fused_computation.15 | convolution fusion | flops 611844096 | bytes 9444864 | tf_op jit(solution)/shard_map/dot_general | solution.py:251
  (78 shorter events, 16.7 us)
Async XLA Ops:
  0.0 14.2 %copy-start = (bf16[8,3,6144]{2,0,1:T(8,128)(2,1)S(1)}, bf16[8,3,6144]{2,0,1:T(8,128)(2,1)}, u32[]{:S(2)}) copy-start(bf16[8,3,6144]{2,0,1:T(8,128)(2,1)} %param.11) | copy-start | bytes 884740
  2.5 4.5 %copy-start.6 = (bf16[1,512,768]{2,1,0:T(8,128)(2,1)}, bf16[1,512,768]{2,1,0:T(8,128)(2,1)S(1)}, u32[]{:S(2)}) copy-start(bf16[1,512,768]{2,1,0:T(8,128)(2,1)S(1)} %reshape.53) | copy-start | bytes 2359300
  2.5 52.0 %collective-permute-start.4 = (bf16[1,512,768]{2,1,0:T(8,128)(2,1)S(1)}, bf16[1,512,768]{2,1,0:T(8,128)(2,1)}, u32[]{:S(2)}, u32[]{:S(2)}) collective-permute-start(bf16[1,512,768]{2,1,0:T(8,128)(2,1)S(1)} %reshape.53), channel_id=1, source_target_pairs={{0,24},{4,28},{8,0},{12,4},{16,8},{20,12},{24,16},{28,20},{1,25},{... | collective-permute-start | bytes 2359304 | tf_op jit(solution)/shard_map/ppermute | solution.py:14
  4.7 49.7 %collective-permute-start.3 = (bf16[1,512,768]{2,1,0:T(8,128)(2,1)S(1)}, bf16[1,512,768]{2,1,0:T(8,128)(2,1)}, u32[]{:S(2)}, u32[]{:S(2)}) collective-permute-start(bf16[1,512,768]{2,1,0:T(8,128)(2,1)S(1)} %reshape.53), channel_id=1, source_target_pairs={{0,16},{4,20},{8,24},{12,28},{16,0},{20,4},{24,8},{28,12},{1,17},{... | collective-permute-start | bytes 2359304 | tf_op jit(solution)/shard_map/ppermute | solution.py:14
  5.0 49.5 %collective-permute-start.2 = (bf16[1,512,768]{2,1,0:T(8,128)(2,1)S(1)}, bf16[1,512,768]{2,1,0:T(8,128)(2,1)}, u32[]{:S(2)}, u32[]{:S(2)}) collective-permute-start(bf16[1,512,768]{2,1,0:T(8,128)(2,1)S(1)} %reshape.53), channel_id=1, source_target_pairs={{0,8},{4,12},{8,16},{12,20},{16,24},{20,28},{24,0},{28,4},{1,9},{5... | collective-permute-start | bytes 2359304 | tf_op jit(solution)/shard_map/ppermute | solution.py:14
  8.8 4.9 %copy-start.12 = (s32[8]{0:T(128)S(1)}, s32[8]{0:T(128)}, u32[]{:S(2)}) copy-start(s32[8]{0:T(128)} %param.12) | copy-start | bytes 100
  8.8 53.9 %all-to-all-start = ((bf16[4,384,768]{2,1,0:T(8,128)(2,1)}), bf16[4,384,768]{2,1,0:T(8,128)(2,1)}, u32[]{:S(2)}, u32[]{:S(2)}) async-start(bf16[4,384,768]{2,1,0:T(8,128)(2,1)} %pad_maximum_fusion.1), calls=%async_computation | async-start | bytes 4718592 | tf_op jit(solution)/shard_map/all_to_all | solution.py:161
  40.8 3.9 %copy-start.10 = (f32[384]{0:T(512)S(1)}, f32[384]{0:T(512)}, u32[]{:S(2)}) copy-start(f32[384]{0:T(512)} %param.17) | copy-start | bytes 4612
  45.6 7.9 %copy-start.11 = (f32[384]{0:T(512)S(1)}, f32[384]{0:T(512)}, u32[]{:S(2)}) copy-start(f32[384]{0:T(512)} %param.16) | copy-start | bytes 4612
  49.3 21.2 %collective-permute-start = (bf16[512,768]{1,0:T(8,128)(2,1)}, bf16[512,768]{1,0:T(8,128)(2,1)}, u32[]{:S(2)}, u32[]{:S(2)}) collective-permute-start(bf16[512,768]{1,0:T(8,128)(2,1)} %get-tuple-element.29), channel_id=1, source_target_pairs={{0,4},{4,8},{8,12},{12,16},{16,20},{20,24},{24,28},{28,0},{1,5},{5... | collective-permute-start | bytes 2359304 | tf_op jit(solution)/shard_map/ppermute | solution.py:14
  53.4 26.8 %collective-permute-start.1 = (bf16[512,768]{1,0:T(8,128)(2,1)}, bf16[512,768]{1,0:T(8,128)(2,1)}, u32[]{:S(2)}, u32[]{:S(2)}) collective-permute-start(bf16[512,768]{1,0:T(8,128)(2,1)} %get-tuple-element.29), channel_id=1, source_target_pairs={{0,8},{4,12},{8,16},{12,20},{16,24},{20,28},{24,0},{28,4},{1,9},{5... | collective-permute-start | bytes 2359304 | tf_op jit(solution)/shard_map/ppermute | solution.py:14
  56.5 28.2 %copy-start.2 = (bf16[4,512,768]{2,1,0:T(8,128)(2,1)}, bf16[4,512,768]{2,1,0:T(8,128)(2,1)S(1)}, u32[]{:S(2)}) copy-start(bf16[4,512,768]{2,1,0:T(8,128)(2,1)S(1)} %pad_maximum_fusion.refs_4_.refs_5_) | copy-start | bytes 9437188
  80.2 12.9 %collective-permute-start.5 = (bf16[4,512,768]{2,1,0:T(8,128)(2,1)S(1)}, bf16[4,512,768]{2,1,0:T(8,128)(2,1)}, u32[]{:S(2)}, u32[]{:S(2)}) collective-permute-start(bf16[4,512,768]{2,1,0:T(8,128)(2,1)S(1)} %pad_maximum_fusion.refs_4_.refs_5_), channel_id=1, source_target_pairs={{0,4},{4,0},{8,12},{12,8},{16,20},{20,16},{24,28},{28,24},{1,5},{5... | collective-permute-start | bytes 9437192 | tf_op jit(solution)/shard_map/ppermute | solution.py:214
  86.5 3.4 %copy-start.7 = (bf16[1,512,768]{2,1,0:T(8,128)(2,1)S(1)}, bf16[1,512,768]{2,1,0:T(8,128)(2,1)}, u32[]{:S(2)}) copy-start(bf16[1,512,768]{2,1,0:T(8,128)(2,1)} %get-tuple-element.28) | copy-start | bytes 2359300
  89.5 82.1 %collective-permute-start.12 = (bf16[3,384,768]{2,1,0:T(8,128)(2,1)}, bf16[3,384,768]{2,1,0:T(8,128)(2,1)}, u32[]{:S(2)}, u32[]{:S(2)}) collective-permute-start(bf16[3,384,768]{2,1,0:T(8,128)(2,1)} %pad_maximum_fusion.3), channel_id=1, source_target_pairs={{0,4},{4,0},{8,12},{12,8},{16,20},{20,16},{24,28},{28,24},{1,5},{5... | collective-permute-start | bytes 5308424 | tf_op jit(solution)/shard_map/ppermute | solution.py:237
  117.4 30.2 %collective-permute-start.8 = (bf16[256,384]{1,0:T(8,128)(2,1)}, bf16[256,384]{1,0:T(8,128)(2,1)S(1)}, u32[]{:S(2)}, u32[]{:S(2)}) collective-permute-start(bf16[256,384]{1,0:T(8,128)(2,1)} %shard_map.100), channel_id=1, source_target_pairs={{0,2},{1,3},{2,0},{3,1},{4,6},{5,7},{6,4},{7,5},{8,10},{9,11},{10,... | collective-permute-start | bytes 589832 | tf_op jit(solution)/shard_map/ppermute | solution.py:243
  120.3 28.5 %collective-permute-start.6 = (bf16[256,384]{1,0:T(8,128)(2,1)}, bf16[256,384]{1,0:T(8,128)(2,1)S(1)}, u32[]{:S(2)}, u32[]{:S(2)}) collective-permute-start(bf16[256,384]{1,0:T(8,128)(2,1)} %shard_map.100), channel_id=1, source_target_pairs={{0,1},{1,2},{2,3},{3,0},{4,5},{5,6},{6,7},{7,4},{8,9},{9,10},{10,1... | collective-permute-start | bytes 589832 | tf_op jit(solution)/shard_map/ppermute | solution.py:243
  120.3 27.3 %copy-start.8 = (bf16[256,384]{1,0:T(8,128)(2,1)S(1)}, bf16[256,384]{1,0:T(8,128)(2,1)}, u32[]{:S(2)}) copy-start(bf16[256,384]{1,0:T(8,128)(2,1)} %shard_map.100) | copy-start | bytes 589828
  144.9 24.9 %copy-start.4 = (bf16[384,768]{1,0:T(8,128)(2,1)S(1)}, bf16[384,768]{1,0:T(8,128)(2,1)}, u32[]{:S(2)}) copy-start(bf16[384,768]{1,0:T(8,128)(2,1)} %get-tuple-element.17) | copy-start | bytes 1769476
  144.9 25.5 %copy-start.3 = (bf16[384,768]{1,0:T(8,128)(2,1)S(1)}, bf16[384,768]{1,0:T(8,128)(2,1)}, u32[]{:S(2)}) copy-start(bf16[384,768]{1,0:T(8,128)(2,1)} %get-tuple-element.16) | copy-start | bytes 1769476
  144.9 20.7 %collective-permute-start.9 = (bf16[256,384]{1,0:T(8,128)(2,1)}, bf16[256,384]{1,0:T(8,128)(2,1)S(1)}, u32[]{:S(2)}, u32[]{:S(2)}) collective-permute-start(bf16[256,384]{1,0:T(8,128)(2,1)} %shard_map.101), channel_id=1, source_target_pairs={{0,2},{1,3},{2,0},{3,1},{4,6},{5,7},{6,4},{7,5},{8,10},{9,11},{10,... | collective-permute-start | bytes 589832 | tf_op jit(solution)/shard_map/ppermute | solution.py:243
  147.3 20.9 %collective-permute-start.7 = (bf16[256,384]{1,0:T(8,128)(2,1)}, bf16[256,384]{1,0:T(8,128)(2,1)S(1)}, u32[]{:S(2)}, u32[]{:S(2)}) collective-permute-start(bf16[256,384]{1,0:T(8,128)(2,1)} %shard_map.101), channel_id=1, source_target_pairs={{0,1},{1,2},{2,3},{3,0},{4,5},{5,6},{6,7},{7,4},{8,9},{9,10},{10,1... | collective-permute-start | bytes 589832 | tf_op jit(solution)/shard_map/ppermute | solution.py:243
  147.6 18.0 %collective-permute-start.10 = (bf16[256,384]{1,0:T(8,128)(2,1)S(1)}, bf16[256,384]{1,0:T(8,128)(2,1)S(1)}, u32[]{:S(2)}, u32[]{:S(2)}) collective-permute-start(bf16[256,384]{1,0:T(8,128)(2,1)S(1)} %copy-done.8), channel_id=1, source_target_pairs={{0,3},{1,0},{2,1},{3,2},{4,7},{5,4},{6,5},{7,6},{8,11},{9,8},{10,9... | collective-permute-start | bytes 589832 | tf_op jit(solution)/shard_map/ppermute | solution.py:243
  148.8 21.0 %collective-permute-start.11 = (bf16[256,384]{1,0:T(8,128)(2,1)}, bf16[256,384]{1,0:T(8,128)(2,1)S(1)}, u32[]{:S(2)}, u32[]{:S(2)}) collective-permute-start(bf16[256,384]{1,0:T(8,128)(2,1)} %shard_map.101), channel_id=1, source_target_pairs={{0,3},{1,0},{2,1},{3,2},{4,7},{5,4},{6,5},{7,6},{8,11},{9,8},{10,9... | collective-permute-start | bytes 589832 | tf_op jit(solution)/shard_map/ppermute | solution.py:243
  165.6 5.4 %copy-start.5 = (bf16[384,768]{1,0:T(8,128)(2,1)S(1)}, bf16[384,768]{1,0:T(8,128)(2,1)}, u32[]{:S(2)}) copy-start(bf16[384,768]{1,0:T(8,128)(2,1)} %get-tuple-element.18) | copy-start | bytes 1769476
  174.9 1.7 copy-start.9
  176.6 4.7 %copy-start.1 = (bf16[8,3,6144]{2,0,1:T(8,128)(2,1)S(1)}, bf16[8,3,6144]{2,0,1:T(8,128)(2,1)}, u32[]{:S(2)}) copy-start(bf16[8,3,6144]{2,0,1:T(8,128)(2,1)} %param.11) | copy-start | bytes 884740

commit v11 on v9

--- a/solution.py
+++ b/solution.py
@@ -199,10 +199,11 @@
     inputs = activations.astype(jnp.float32)
     normed = inputs * lax.rsqrt(jnp.mean(inputs * inputs, axis=-1, keepdims=True) + 1e-06)
     hidden = (normed * (1.0 + modulation[1][None, :]) + modulation[0][None, :]).astype(jnp.bfloat16)
-    qkv = jnp.einsum("td,dkh->tkh", hidden, w_qkv, preferred_element_type=jnp.float32)
-    queries = head_norm(qkv[:, 0], q_gain, heads).astype(jnp.bfloat16)
-    keys = head_norm(qkv[:, 1], k_gain, heads).astype(jnp.bfloat16)
-    values = qkv[:, 2].astype(jnp.bfloat16)
+    width = heads * HD
+    qkv = jnp.einsum("td,dkh->kth", hidden, w_qkv, preferred_element_type=jnp.float32)
+    queries = head_norm(qkv[0], q_gain, heads).astype(jnp.bfloat16)
+    keys = head_norm(qkv[1], k_gain, heads).astype(jnp.bfloat16)
+    values = qkv[2].astype(jnp.bfloat16)
     local_kv = jnp.concatenate([keys.reshape(span, heads * HD), values], axis=1)
     before = from_behind(local_kv, "slot", 1)
     earlier = from_behind(local_kv, "slot", 2)

time: 169 us -> 162 us (0.959)
  matrix products: 30.9 us -> 25 us
    ppermute x5, waiting for transfers between devices: 14.7 us -> 8.12 us  [from_behind(): lax.ppermute(shard, axis, [(i, (i + by) % length) for i in range(length)])]
    all_to_all x1, waiting for transfers between devices: 6.18 us -> 12.4 us  [fetch_out_weight(): exchanged = lax.all_to_all(blocks, 'head', 0, 0)]
    dot_general x1, matrix products: 18.8 us -> 12.8 us  [local(): jnp.einsum('td,dkh->kth', hidden, w_qkv, preferred_element_type=jnp.float32)]
    slice x2 -> x1, local copies, waits for them, and re-layouts: 2.68 us -> 0.26 us  [local(): queries = head_norm(qkv[0], q_gain, heads).astype(jnp.bfloat16)]
  transfers between devices with their start and end apart: 14 -> 14, of which waited for: 6 -> 5; matrix products, arithmetic and copies ran while one was open for 36% -> 33% of each run, Pallas kernels for 21% -> 22%
where the time goes in v11:
time: 162 us
  waiting for transfers between devices  39.9 us (25%)
  Pallas kernels  35.7 us (22%)
  matrix products  25 us (15%)
  other arithmetic  21.2 us (13%)
  local copies, waits for them, and re-layouts  19.7 us (12%)
  starting transfers between devices  19.7 us (12%)
    pallas_call x2, Pallas kernels, flash(): pl.pallas_call(kernel, grid_spec=grid_spec, out_shape=jax.ShapeDtypeStruc...  35.7 us
    ppermute x6, waiting for transfers between devices, local(): lax.ppermute(part, 'head', [(i, (i + shift) % groups) for i in range(grou...  19.4 us
    dot_general x1, matrix products, local(): jnp.einsum('td,dkh->kth', hidden, w_qkv, preferred_element_type=jnp.float32)  12.8 us
    all_to_all x1, waiting for transfers between devices, fetch_out_weight(): exchanged = lax.all_to_all(blocks, 'head', 0, 0)  12.4 us
    ppermute x5, waiting for transfers between devices, from_behind(): lax.ppermute(shard, axis, [(i, (i + by) % length) for i in range(length)])  8.12 us
    ppermute x6, starting transfers between devices, local(): lax.ppermute(part, 'head', [(i, (i + shift) % groups) for i in range(grou...  7.43 us
    ppermute x5, starting transfers between devices, from_behind(): lax.ppermute(shard, axis, [(i, (i + by) % length) for i in range(length)])  6.83 us
    dot_general x3, matrix products, local(): jnp.dot(group_o, sibling[shift - 1], preferred_element_type=jnp.float32)  4.94 us
  transfers between devices with their start and end apart: 14, of which 5 were waited for; matrix products, arithmetic and copies ran while one was open for 33% of the time, Pallas kernels for 22%

profile of v11, /device:TPU:9, one launch (start us, length us, event | category | flops | bytes accessed | tf_op | source)
XLA Modules:
  0.0 161.6 jit_solution(10569848785781452921)
XLA Ops:
  0.0 2.5 %reshape.53 = bf16[1,512,768]{2,1,0:T(8,128)(2,1)S(1)} reshape(bf16[1,512,2,384]{3,2,1,0:T(2,128)(2,1)} %param.18) | data formatting | bytes 1572864 | tf_op jit(solution)/shard_map/reshape | solution.py:191
  2.5 2.2 %collective-permute-start.4 = (bf16[1,512,768]{2,1,0:T(8,128)(2,1)S(1)}, bf16[1,512,768]{2,1,0:T(8,128)(2,1)}, u32[]{:S(2)}, u32[]{:S(2)}) collective-permute-start(bf16[1,512,768]{2,1,0:T(8,128)(2,1)S(1)} %reshape.53), channel_id=1, source_target_pairs={{0,24},{4,28},{8,0},{12,4},{16,8},{20,12},{24,16},{28,20},{1,25},{... | collective-permute-start | bytes 2359304 | tf_op jit(solution)/shard_map/ppermute | solution.py:14
  5.3 1.8 %dynamic-slice_bitcast_fusion.6 = (bf16[1,384,768]{2,1,0:T(8,128)(2,1)S(1)}, bf16[1,384,768]{2,1,0:T(8,128)(2,1)S(1)}, bf16[1,384,768]{2,1,0:T(8,128)(2,1)S(1)}, bf16[1,384,768]{2,1,0:T(8,128)(2,1)S(1)}) fusion(bf16[384,6144]{1,0:T(8,128)(2,1)} %param.19, s32[]{:T(128)S(6)} %select_n.112, s32[]{:T(128)S(6)} %select_n.114, s32[]{:T(128)S(6)} %select_n.113, ...), kind=kLoop, calls=%fused_computation.47 | loop fusion | bytes 4718608 | tf_op jit(solution)/shard_map/stack | solution.py:155
  7.0 1.7 %pad_maximum_fusion.1 = bf16[4,384,768]{2,1,0:T(8,128)(2,1)} fusion(bf16[1,384,768]{2,1,0:T(8,128)(2,1)S(1)} %get-tuple-element.22, bf16[1,384,768]{2,1,0:T(8,128)(2,1)S(1)} %get-tuple-element.20, bf16[1,384,768]{2,1,0:T(8,128)(2,1)S(1)} %get-tuple-element.21, bf16[1,384,768]{2,1,0:T(8,128)(2,1)S(1)} %get-tuple-element.19), kind=kLoop, calls=%fused_computation.17 | loop fusion | flops 3538944 | bytes 4718592 | tf_op jit(solution)/shard_map/stack | solution.py:155
  8.8 4.9 %all-to-all-start = ((bf16[4,384,768]{2,1,0:T(8,128)(2,1)}), bf16[4,384,768]{2,1,0:T(8,128)(2,1)}, u32[]{:S(2)}, u32[]{:S(2)}) async-start(bf16[4,384,768]{2,1,0:T(8,128)(2,1)} %pad_maximum_fusion.1), calls=%async_computation | async-start | bytes 4718592 | tf_op jit(solution)/shard_map/all_to_all | solution.py:159
  15.2 4.1 %fusion = f32[512]{0:T(512)S(1)} fusion(bf16[512,6144]{1,0:T(8,128)(2,1)} %param.10), kind=kLoop, calls=%fused_computation.2 | loop fusion | flops 9436672 | bytes 6293504 | tf_op jit(solution)/shard_map/reduce_sum | solution.py:200
  19.3 12.8 %fusion.13 = f32[3,512,384]{2,1,0:T(8,128)S(1)} fusion(bf16[6144,3,384]{2,0,1:T(8,128)(2,1)} %param.15, bf16[512,6144]{1,0:T(8,128)(2,1)} %param.10, f32[6144]{0:T(1024)S(1)} %bitcast.89, f32[6144]{0:T(1024)S(1)} %bitcast.90, f32[512]{0:T(512)S(1)} %add_rsqrt_fusion.2), kind=kOutput, calls=%fused_computation.20 | convolution fusion | flops 7263485952 | bytes 22857728 | tf_op jit(solution)/shard_map/td,dkh->kth/dot_general | solution.py:203
  33.4 2.3 %copy.17 = f32[1,512,384]{1,2,0:T(8,128)} copy(f32[1,512,384]{2,1,0:T(8,128)} %get-tuple-element.26) | data formatting | bytes 1572864 | tf_op jit(solution)/shard_map/mul | solution.py:19
  37.9 2.3 %copy.18 = f32[512,384]{1,0:T(8,128)} copy(f32[512,384]{0,1:T(8,128)} %bitcast.84) | data formatting | bytes 1572864 | tf_op jit(solution)/shard_map/mul | solution.py:19
  41.5 1.2 fusion.36
  42.7 4.1 %collective-permute-start = (bf16[512,768]{1,0:T(8,128)(2,1)}, bf16[512,768]{1,0:T(8,128)(2,1)}, u32[]{:S(2)}, u32[]{:S(2)}) collective-permute-start(bf16[512,768]{1,0:T(8,128)(2,1)} %get-tuple-element.29), channel_id=1, source_target_pairs={{0,4},{4,8},{8,12},{12,16},{16,20},{20,24},{24,28},{28,0},{1,5},{5... | collective-permute-start | bytes 2359304 | tf_op jit(solution)/shard_map/ppermute | solution.py:14
  48.2 2.0 %pad_maximum_fusion.refs_4_.refs_5_ = bf16[4,512,768]{2,1,0:T(8,128)(2,1)S(1)} fusion(bf16[1,512,768]{2,1,0:T(8,128)(2,1)} %collective-permute-done.4, bf16[1,512,768]{2,1,0:T(8,128)(2,1)} %collective-permute-done.3, bf16[1,512,768]{2,1,0:T(8,128)(2,1)} %collective-permute-done.2, bf16[1,512,768]{2,1,0:T(8,128)(2,1)} %copy-done.6), kind=kLoop, calls=%fused_computation.11 | loop fusion | flops 4718592 | bytes 6291456 | tf_op jit(solution)/shard_map/concatenate | solution.py:193
  50.3 12.4 %all-to-all-done = bf16[4,384,768]{2,1,0:T(8,128)(2,1)} async-done(((bf16[4,384,768]{2,1,0:T(8,128)(2,1)}), bf16[4,384,768]{2,1,0:T(8,128)(2,1)}, u32[]{:S(2)}, u32[]{:S(2)}) %all-to-all-start) | async-done | bytes 2359328 | tf_op jit(solution)/shard_map/all_to_all | solution.py:159
  62.7 2.8 %dynamic-slice_bitcast_fusion = (bf16[384,768]{1,0:T(8,128)(2,1)}, bf16[384,768]{1,0:T(8,128)(2,1)}, bf16[384,768]{1,0:T(8,128)(2,1)}) fusion(bf16[4,384,768]{2,1,0:T(8,128)(2,1)} %all-to-all-done, s32[]{:T(128)S(6)} %select_n.121, s32[]{:T(128)S(6)} %select_n.119, s32[]{:T(128)S(6)} %select_n.117), kind=kLoop, calls=%fused_computation.41 | loop fusion | bytes 3538956 | tf_op jit(solution)/shard_map/jit(dynamic_index_in_dim)/squeeze | solution.py:161
  65.5 8.1 %collective-permute-done.1 = bf16[512,768]{1,0:T(8,128)(2,1)} collective-permute-done((bf16[512,768]{1,0:T(8,128)(2,1)}, bf16[512,768]{1,0:T(8,128)(2,1)}, u32[]{:S(2)}, u32[]{:S(2)}) %collective-permute-start.1) | collective-permute-done | bytes 786464 | tf_op jit(solution)/shard_map/ppermute | solution.py:14
  74.6 1.3 compare_select_fusion.6.refs_0_
  76.6 1.7 %fusion.37 = (bf16[256,3,128]{0,2,1:T(8,128)(2,1)S(1)}, bf16[256,3,128]{0,2,1:T(8,128)(2,1)}) fusion(bf16[512,3,128]{0,2,1:T(8,128)(2,1)} %multiply_convert_fusion), kind=kLoop, calls=%fused_computation.99 | loop fusion | bytes 786432 | tf_op jit(solution)/shard_map/slice | solution.py:232
  78.3 1.8 %copy.20.refs_1_ = bf16[256,384]{1,0:T(8,128)(2,1)} copy(bf16[256,384]{0,1:T(8,128)(2,1)} %bitcast.86) | data formatting | bytes 393216 | tf_op jit(solution)/shard_map/slice | solution.py:232
  80.0 2.9 %pad_maximum_fusion.3 = bf16[3,384,768]{2,1,0:T(8,128)(2,1)} fusion(bf16[1,384,768]{2,1,0:T(8,128)(2,1)} %bitcast.82, bf16[1,384,768]{2,1,0:T(8,128)(2,1)} %bitcast.81, bf16[1,384,768]{2,1,0:T(8,128)(2,1)} %bitcast.80), kind=kLoop, calls=%fused_computation.19 | loop fusion | flops 1769472 | bytes 3538944 | tf_op jit(solution)/shard_map/stack | solution.py:237
  83.5 3.1 %pad_maximum_fusion.2.refs_2_.refs_3_ = bf16[3,512,768]{2,1,0:T(8,128)(2,1)} fusion(bf16[1,512,768]{2,1,0:T(8,128)(2,1)} %bitcast.24, bf16[1,512,768]{2,1,0:T(8,128)(2,1)} %bitcast.23, bf16[1,512,768]{2,1,0:T(8,128)(2,1)S(1)} %copy-done.7), kind=kLoop, calls=%fused_computation.18 | loop fusion | flops 2359296 | bytes 4718592 | tf_op jit(solution)/shard_map/stack | solution.py:223
  86.5 17.8 %shard_map.100 = bf16[256,384]{1,0:T(8,128)(2,1)} custom-call(s32[6]{0:T(128)} %compare_select_fusion.6.refs_0_, bf16[256,384]{1,0:T(8,128)(2,1)} %copy.20.refs_1_, bf16[3,512,768]{2,1,0:T(8,128)(2,1)} %pad_maximum_fusion.2.refs_2_.refs_3_, bf16[3,512,768]{2,1,0:T(8,128)(2,1)} %pad_maximum_fusion.2.refs_2_.refs_3_, bf16[4,512,768]{2,1,0:T(8,128)(2,1)} %copy-done.2, ...), custom_call_target="tpu_custom_call" | custom-call | flops 905969664 | bytes 3538944 | tf_op jit(solution)/shard_map/pallas_call | solution.py:138
  104.3 2.1 %collective-permute-start.8 = (bf16[256,384]{1,0:T(8,128)(2,1)}, bf16[256,384]{1,0:T(8,128)(2,1)S(1)}, u32[]{:S(2)}, u32[]{:S(2)}) collective-permute-start(bf16[256,384]{1,0:T(8,128)(2,1)} %shard_map.100), channel_id=1, source_target_pairs={{0,2},{1,3},{2,0},{3,1},{4,6},{5,7},{6,4},{7,5},{8,10},{9,11},{10,... | collective-permute-start | bytes 589832 | tf_op jit(solution)/shard_map/ppermute | solution.py:242
  107.3 17.9 %shard_map.101 = bf16[256,384]{1,0:T(8,128)(2,1)} custom-call(s32[6]{0:T(128)} %compare_select_fusion.6.refs_0_, bf16[256,384]{1,0:T(8,128)(2,1)} %copy.21.refs_1_, bf16[3,512,768]{2,1,0:T(8,128)(2,1)} %pad_maximum_fusion.2.refs_2_.refs_3_, bf16[3,512,768]{2,1,0:T(8,128)(2,1)} %pad_maximum_fusion.2.refs_2_.refs_3_, bf16[4,512,768]{2,1,0:T(8,128)(2,1)} %copy-done.2, ...), custom_call_target="tpu_custom_call" | custom-call | flops 905969664 | bytes 3538944 | tf_op jit(solution)/shard_map/pallas_call | solution.py:138
  125.2 2.4 %collective-permute-start.9 = (bf16[256,384]{1,0:T(8,128)(2,1)}, bf16[256,384]{1,0:T(8,128)(2,1)S(1)}, u32[]{:S(2)}, u32[]{:S(2)}) collective-permute-start(bf16[256,384]{1,0:T(8,128)(2,1)} %shard_map.101), channel_id=1, source_target_pairs={{0,2},{1,3},{2,0},{3,1},{4,6},{5,7},{6,4},{7,5},{8,10},{9,11},{10,... | collective-permute-start | bytes 589832 | tf_op jit(solution)/shard_map/ppermute | solution.py:242
  129.2 1.4 collective-permute-start.11
  130.6 15.3 %collective-permute-done.10 = bf16[256,384]{1,0:T(8,128)(2,1)S(1)} collective-permute-done((bf16[256,384]{1,0:T(8,128)(2,1)S(1)}, bf16[256,384]{1,0:T(8,128)(2,1)S(1)}, u32[]{:S(2)}, u32[]{:S(2)}) %collective-permute-start.10) | collective-permute-done | bytes 196640 | tf_op jit(solution)/shard_map/ppermute | solution.py:242
  146.0 2.6 %collective-permute-done.7 = bf16[256,384]{1,0:T(8,128)(2,1)S(1)} collective-permute-done((bf16[256,384]{1,0:T(8,128)(2,1)}, bf16[256,384]{1,0:T(8,128)(2,1)S(1)}, u32[]{:S(2)}, u32[]{:S(2)}) %collective-permute-start.7) | collective-permute-done | bytes 196640 | tf_op jit(solution)/shard_map/ppermute | solution.py:242
  148.6 1.5 collective-permute-done.11
  151.9 1.6 %convolution_convert_fusion.2 = bf16[512,768]{1,0:T(8,128)(2,1)S(1)} fusion(bf16[512,384]{1,0:T(8,128)(2,1)S(1)} %constant_dynamic-update-slice_fusion.2, bf16[3,384,768]{2,1,0:T(8,128)(2,1)} %collective-permute-done.12), kind=kOutput, calls=%fused_computation.24 | convolution fusion | flops 302383104 | bytes 1769472 | tf_op jit(solution)/shard_map/dot_general | solution.py:258
  153.6 1.6 %convolution_convert_fusion.3 = bf16[512,768]{1,0:T(8,128)(2,1)S(1)} fusion(bf16[512,384]{1,0:T(8,128)(2,1)S(1)} %constant_dynamic-update-slice_fusion, bf16[3,384,768]{2,1,0:T(8,128)(2,1)} %collective-permute-done.12), kind=kOutput, calls=%fused_computation.25 | convolution fusion | flops 302383104 | bytes 1769472 | tf_op jit(solution)/shard_map/dot_general | solution.py:258
  155.2 1.7 %convert_add_fusion = f32[512,768]{1,0:T(8,128)S(1)} fusion(bf16[512,768]{1,0:T(8,128)(2,1)S(1)} %convolution_convert_fusion.2, bf16[512,768]{1,0:T(8,128)(2,1)S(1)} %convolution_convert_fusion.3, bf16[512,384]{1,0:T(8,128)(2,1)S(1)} %constant_dynamic-update-slice_fusion.4, bf16[3,384,768]{2,1,0:T(8,128)(2,1)} %collective-permute-done.12), kind=kOutput, calls=%fused_computation.21 | convolution fusion | flops 304349184 | bytes 4128768 | tf_op jit(solution)/shard_map/dot_general | solution.py:258
  156.9 4.7 %fusion.12 = f32[512,1536]{1,0:T(8,128)} fusion(f32[512,768]{1,0:T(8,128)S(1)} %convert_add_fusion, f32[512,768]{1,0:T(8,128)S(1)} %convert_add_fusion.1, f32[1536]{0:T(1024)S(1)} %dynamic-slice_reduce_fusion, bf16[512,6144]{1,0:T(8,128)(2,1)} %param.10, s32[]{:T(128)S(6)} %select_n.103, pred[]{:T(512)S(6)} %eq.29, bf16[384,6144]{1,0:T(8,128)(2,1)} %param.19, ...), kind=kOutput, calls=%fused_computation.15 | convolution fusion | flops 611844096 | bytes 9444864 | tf_op jit(solution)/shard_map/dot_general | solution.py:250
  (78 shorter events, 14.5 us)
Async XLA Ops:
  0.0 14.2 %copy-start = (bf16[8,3,6144]{2,0,1:T(8,128)(2,1)S(1)}, bf16[8,3,6144]{2,0,1:T(8,128)(2,1)}, u32[]{:S(2)}) copy-start(bf16[8,3,6144]{2,0,1:T(8,128)(2,1)} %param.11) | copy-start | bytes 884740
  2.5 4.5 %copy-start.6 = (bf16[1,512,768]{2,1,0:T(8,128)(2,1)}, bf16[1,512,768]{2,1,0:T(8,128)(2,1)S(1)}, u32[]{:S(2)}) copy-start(bf16[1,512,768]{2,1,0:T(8,128)(2,1)S(1)} %reshape.53) | copy-start | bytes 2359300
  2.5 45.7 %collective-permute-start.4 = (bf16[1,512,768]{2,1,0:T(8,128)(2,1)S(1)}, bf16[1,512,768]{2,1,0:T(8,128)(2,1)}, u32[]{:S(2)}, u32[]{:S(2)}) collective-permute-start(bf16[1,512,768]{2,1,0:T(8,128)(2,1)S(1)} %reshape.53), channel_id=1, source_target_pairs={{0,24},{4,28},{8,0},{12,4},{16,8},{20,12},{24,16},{28,20},{1,25},{... | collective-permute-start | bytes 2359304 | tf_op jit(solution)/shard_map/ppermute | solution.py:14
  4.7 43.5 %collective-permute-start.3 = (bf16[1,512,768]{2,1,0:T(8,128)(2,1)S(1)}, bf16[1,512,768]{2,1,0:T(8,128)(2,1)}, u32[]{:S(2)}, u32[]{:S(2)}) collective-permute-start(bf16[1,512,768]{2,1,0:T(8,128)(2,1)S(1)} %reshape.53), channel_id=1, source_target_pairs={{0,16},{4,20},{8,24},{12,28},{16,0},{20,4},{24,8},{28,12},{1,17},{... | collective-permute-start | bytes 2359304 | tf_op jit(solution)/shard_map/ppermute | solution.py:14
  5.0 43.2 %collective-permute-start.2 = (bf16[1,512,768]{2,1,0:T(8,128)(2,1)S(1)}, bf16[1,512,768]{2,1,0:T(8,128)(2,1)}, u32[]{:S(2)}, u32[]{:S(2)}) collective-permute-start(bf16[1,512,768]{2,1,0:T(8,128)(2,1)S(1)} %reshape.53), channel_id=1, source_target_pairs={{0,8},{4,12},{8,16},{12,20},{16,24},{20,28},{24,0},{28,4},{1,9},{5... | collective-permute-start | bytes 2359304 | tf_op jit(solution)/shard_map/ppermute | solution.py:14
  8.8 4.9 %copy-start.13 = (s32[8]{0:T(128)S(1)}, s32[8]{0:T(128)}, u32[]{:S(2)}) copy-start(s32[8]{0:T(128)} %param.12) | copy-start | bytes 100
  8.8 53.9 %all-to-all-start = ((bf16[4,384,768]{2,1,0:T(8,128)(2,1)}), bf16[4,384,768]{2,1,0:T(8,128)(2,1)}, u32[]{:S(2)}, u32[]{:S(2)}) async-start(bf16[4,384,768]{2,1,0:T(8,128)(2,1)} %pad_maximum_fusion.1), calls=%async_computation | async-start | bytes 4718592 | tf_op jit(solution)/shard_map/all_to_all | solution.py:159
  33.4 6.8 %copy-start.11 = (f32[384]{0:T(512)S(1)}, f32[384]{0:T(512)}, u32[]{:S(2)}) copy-start(f32[384]{0:T(512)} %param.17) | copy-start | bytes 4612
  41.5 5.3 %copy-start.8 = (f32[1,512,384]{2,1,0:T(8,128)S(1)}, f32[1,512,384]{2,1,0:T(8,128)}, u32[]{:S(2)}) copy-start(f32[1,512,384]{2,1,0:T(8,128)} %get-tuple-element.27) | copy-start | bytes 2359300
  41.5 5.8 %copy-start.12 = (f32[384]{0:T(512)S(1)}, f32[384]{0:T(512)}, u32[]{:S(2)}) copy-start(f32[384]{0:T(512)} %param.16) | copy-start | bytes 4612
  42.7 22.8 %collective-permute-start = (bf16[512,768]{1,0:T(8,128)(2,1)}, bf16[512,768]{1,0:T(8,128)(2,1)}, u32[]{:S(2)}, u32[]{:S(2)}) collective-permute-start(bf16[512,768]{1,0:T(8,128)(2,1)} %get-tuple-element.29), channel_id=1, source_target_pairs={{0,4},{4,8},{8,12},{12,16},{16,20},{20,24},{24,28},{28,0},{1,5},{5... | collective-permute-start | bytes 2359304 | tf_op jit(solution)/shard_map/ppermute | solution.py:14
  46.8 26.8 %collective-permute-start.1 = (bf16[512,768]{1,0:T(8,128)(2,1)}, bf16[512,768]{1,0:T(8,128)(2,1)}, u32[]{:S(2)}, u32[]{:S(2)}) collective-permute-start(bf16[512,768]{1,0:T(8,128)(2,1)} %get-tuple-element.29), channel_id=1, source_target_pairs={{0,8},{4,12},{8,16},{12,20},{16,24},{20,28},{24,0},{28,4},{1,9},{5... | collective-permute-start | bytes 2359304 | tf_op jit(solution)/shard_map/ppermute | solution.py:14
  50.3 28.0 %copy-start.2 = (bf16[4,512,768]{2,1,0:T(8,128)(2,1)}, bf16[4,512,768]{2,1,0:T(8,128)(2,1)S(1)}, u32[]{:S(2)}) copy-start(bf16[4,512,768]{2,1,0:T(8,128)(2,1)S(1)} %pad_maximum_fusion.refs_4_.refs_5_) | copy-start | bytes 9437188
  73.6 12.9 %collective-permute-start.5 = (bf16[4,512,768]{2,1,0:T(8,128)(2,1)S(1)}, bf16[4,512,768]{2,1,0:T(8,128)(2,1)}, u32[]{:S(2)}, u32[]{:S(2)}) collective-permute-start(bf16[4,512,768]{2,1,0:T(8,128)(2,1)S(1)} %pad_maximum_fusion.refs_4_.refs_5_), channel_id=1, source_target_pairs={{0,4},{4,0},{8,12},{12,8},{16,20},{20,16},{24,28},{28,24},{1,5},{5... | collective-permute-start | bytes 9437192 | tf_op jit(solution)/shard_map/ppermute | solution.py:213
  80.0 3.4 %copy-start.7 = (bf16[1,512,768]{2,1,0:T(8,128)(2,1)S(1)}, bf16[1,512,768]{2,1,0:T(8,128)(2,1)}, u32[]{:S(2)}) copy-start(bf16[1,512,768]{2,1,0:T(8,128)(2,1)} %get-tuple-element.28) | copy-start | bytes 2359300
  83.0 69.0 %collective-permute-start.12 = (bf16[3,384,768]{2,1,0:T(8,128)(2,1)}, bf16[3,384,768]{2,1,0:T(8,128)(2,1)}, u32[]{:S(2)}, u32[]{:S(2)}) collective-permute-start(bf16[3,384,768]{2,1,0:T(8,128)(2,1)} %pad_maximum_fusion.3), channel_id=1, source_target_pairs={{0,4},{4,0},{8,12},{12,8},{16,20},{20,16},{24,28},{28,24},{1,5},{5... | collective-permute-start | bytes 5308424 | tf_op jit(solution)/shard_map/ppermute | solution.py:236
  104.3 23.6 %collective-permute-start.8 = (bf16[256,384]{1,0:T(8,128)(2,1)}, bf16[256,384]{1,0:T(8,128)(2,1)S(1)}, u32[]{:S(2)}, u32[]{:S(2)}) collective-permute-start(bf16[256,384]{1,0:T(8,128)(2,1)} %shard_map.100), channel_id=1, source_target_pairs={{0,2},{1,3},{2,0},{3,1},{4,6},{5,7},{6,4},{7,5},{8,10},{9,11},{10,... | collective-permute-start | bytes 589832 | tf_op jit(solution)/shard_map/ppermute | solution.py:242
  107.3 21.9 %collective-permute-start.6 = (bf16[256,384]{1,0:T(8,128)(2,1)}, bf16[256,384]{1,0:T(8,128)(2,1)S(1)}, u32[]{:S(2)}, u32[]{:S(2)}) collective-permute-start(bf16[256,384]{1,0:T(8,128)(2,1)} %shard_map.100), channel_id=1, source_target_pairs={{0,1},{1,2},{2,3},{3,0},{4,5},{5,6},{6,7},{7,4},{8,9},{9,10},{10,1... | collective-permute-start | bytes 589832 | tf_op jit(solution)/shard_map/ppermute | solution.py:242
  107.3 20.7 %copy-start.9 = (bf16[256,384]{1,0:T(8,128)(2,1)S(1)}, bf16[256,384]{1,0:T(8,128)(2,1)}, u32[]{:S(2)}) copy-start(bf16[256,384]{1,0:T(8,128)(2,1)} %shard_map.100) | copy-start | bytes 589828
  125.2 24.9 %copy-start.4 = (bf16[384,768]{1,0:T(8,128)(2,1)S(1)}, bf16[384,768]{1,0:T(8,128)(2,1)}, u32[]{:S(2)}) copy-start(bf16[384,768]{1,0:T(8,128)(2,1)} %get-tuple-element.17) | copy-start | bytes 1769476
  125.2 25.5 %copy-start.3 = (bf16[384,768]{1,0:T(8,128)(2,1)S(1)}, bf16[384,768]{1,0:T(8,128)(2,1)}, u32[]{:S(2)}) copy-start(bf16[384,768]{1,0:T(8,128)(2,1)} %get-tuple-element.16) | copy-start | bytes 1769476
  125.2 20.7 %collective-permute-start.9 = (bf16[256,384]{1,0:T(8,128)(2,1)}, bf16[256,384]{1,0:T(8,128)(2,1)S(1)}, u32[]{:S(2)}, u32[]{:S(2)}) collective-permute-start(bf16[256,384]{1,0:T(8,128)(2,1)} %shard_map.101), channel_id=1, source_target_pairs={{0,2},{1,3},{2,0},{3,1},{4,6},{5,7},{6,4},{7,5},{8,10},{9,11},{10,... | collective-permute-start | bytes 589832 | tf_op jit(solution)/shard_map/ppermute | solution.py:242
  127.7 20.9 %collective-permute-start.7 = (bf16[256,384]{1,0:T(8,128)(2,1)}, bf16[256,384]{1,0:T(8,128)(2,1)S(1)}, u32[]{:S(2)}, u32[]{:S(2)}) collective-permute-start(bf16[256,384]{1,0:T(8,128)(2,1)} %shard_map.101), channel_id=1, source_target_pairs={{0,1},{1,2},{2,3},{3,0},{4,5},{5,6},{6,7},{7,4},{8,9},{9,10},{10,1... | collective-permute-start | bytes 589832 | tf_op jit(solution)/shard_map/ppermute | solution.py:242
  127.9 18.0 %collective-permute-start.10 = (bf16[256,384]{1,0:T(8,128)(2,1)S(1)}, bf16[256,384]{1,0:T(8,128)(2,1)S(1)}, u32[]{:S(2)}, u32[]{:S(2)}) collective-permute-start(bf16[256,384]{1,0:T(8,128)(2,1)S(1)} %copy-done.9), channel_id=1, source_target_pairs={{0,3},{1,0},{2,1},{3,2},{4,7},{5,4},{6,5},{7,6},{8,11},{9,8},{10,9... | collective-permute-start | bytes 589832 | tf_op jit(solution)/shard_map/ppermute | solution.py:242
  129.2 21.0 %collective-permute-start.11 = (bf16[256,384]{1,0:T(8,128)(2,1)}, bf16[256,384]{1,0:T(8,128)(2,1)S(1)}, u32[]{:S(2)}, u32[]{:S(2)}) collective-permute-start(bf16[256,384]{1,0:T(8,128)(2,1)} %shard_map.101), channel_id=1, source_target_pairs={{0,3},{1,0},{2,1},{3,2},{4,7},{5,4},{6,5},{7,6},{8,11},{9,8},{10,9... | collective-permute-start | bytes 589832 | tf_op jit(solution)/shard_map/ppermute | solution.py:242
  145.9 5.4 %copy-start.5 = (bf16[384,768]{1,0:T(8,128)(2,1)S(1)}, bf16[384,768]{1,0:T(8,128)(2,1)}, u32[]{:S(2)}) copy-start(bf16[384,768]{1,0:T(8,128)(2,1)} %get-tuple-element.18) | copy-start | bytes 1769476
  155.2 1.7 %copy-start.10 = (bf16[256,384]{1,0:T(8,128)(2,1)S(1)}, bf16[256,384]{1,0:T(8,128)(2,1)}, u32[]{:S(2)}) copy-start(bf16[256,384]{1,0:T(8,128)(2,1)} %shard_map.101) | copy-start | bytes 589828
  156.9 4.7 %copy-start.1 = (bf16[8,3,6144]{2,0,1:T(8,128)(2,1)S(1)}, bf16[8,3,6144]{2,0,1:T(8,128)(2,1)}, u32[]{:S(2)}) copy-start(bf16[8,3,6144]{2,0,1:T(8,128)(2,1)} %param.11) | copy-start | bytes 884740

commit v12 on v11

--- a/solution.py
+++ b/solution.py
@@ -225,23 +225,25 @@
     visible = jnp.transpose(visible.reshape(blocks_q, 3 + cache_len, blocks_q), (1, 0, 2))
     visible = jnp.repeat(visible, BLOCK, axis=2)
     bias = jnp.where(visible > 0, 0.0, -1e30).astype(jnp.float32)
-    rows = span // 2
+    chunks = 4
+    rows = span // chunks
     parts = rows // BLOCK
     queries = queries.reshape(span, width)
     mixed_parts = [
         flash(queries[p * rows : (p + 1) * rows], local_stack, same_core, other_core,
               bias[:, p * parts : (p + 1) * parts], own_cache, heads)
-        for p in range(2)
+        for p in range(chunks)
     ]
     sibling = lax.ppermute(
         jnp.stack(mine[1:]), "slot", [(i, i ^ 1) for i in range(slots)]
     )
 
+    exchanged_o = jnp.concatenate([
+        lax.all_to_all(jnp.broadcast_to(part[None], (groups,) + part.shape), "head", 0, 0)
+        for part in mixed_parts
+    ], axis=1)
     received = [
-        jnp.concatenate([
-            lax.ppermute(part, "head", [(i, (i + shift) % groups) for i in range(groups)])
-            for part in mixed_parts
-        ], axis=0)
+        lax.dynamic_index_in_dim(exchanged_o, (head - shift) % groups, 0, keepdims=False)
         for shift in range(1, groups)
     ]
     mixed = jnp.concatenate(mixed_parts, axis=0)

time: 162 us -> 206 us (1.27)
  the two profiles are of different devices: /device:TPU:9 before, /device:TPU:0 now
where the time goes in v12:
time: 206 us; the launch traced here: 204 us
  Pallas kernels  60.4 us (29%)
  starting transfers between devices  35.1 us (17%)
  local copies, waits for them, and re-layouts  30.7 us (15%)
  waiting for transfers between devices  28.8 us (14%)
  matrix products  28.3 us (14%)
  other arithmetic  20.4 us (10%)
    pallas_call x4, Pallas kernels, flash(): pl.pallas_call(kernel, grid_spec=grid_spec, out_shape=jax.ShapeDtypeStruc...  60.4 us
    all_to_all x4, starting transfers between devices, local(): lax.all_to_all(jnp.broadcast_to(part[None], (groups,) + part.shape), 'hea...  20.4 us
    all_to_all x1, waiting for transfers between devices, fetch_out_weight(): exchanged = lax.all_to_all(blocks, 'head', 0, 0)  19.4 us
    dot_general x1, matrix products, local(): jnp.einsum('td,dkh->kth', hidden, w_qkv, preferred_element_type=jnp.float32)  12.8 us
    all_to_all x4, waiting for transfers between devices, local(): lax.all_to_all(jnp.broadcast_to(part[None], (groups,) + part.shape), 'hea...  9.38 us
    broadcast_in_dim x4, local copies, waits for them, and re-layouts, local(): jnp.broadcast_to(part[None], (groups,) + part.shape)  6.69 us
    ppermute x5, starting transfers between devices, from_behind(): lax.ppermute(shard, axis, [(i, (i + by) % length) for i in range(length)])  6.57 us
    dot_general x3, matrix products, local(): jnp.dot(group_o, sibling[shift - 1], preferred_element_type=jnp.float32)  5.34 us
  transfers between devices with their start and end apart: 12, of which 2 were waited for; matrix products, arithmetic and copies ran while one was open for 30% of the time, Pallas kernels for 22%

profile of v12, /device:TPU:0, one launch (start us, length us, event | category | flops | bytes accessed | tf_op | source)
XLA Modules:
  0.0 204.2 jit_solution(4883884393685702285)
XLA Ops:
  0.0 2.5 %reshape.59 = bf16[1,512,768]{2,1,0:T(8,128)(2,1)S(1)} reshape(bf16[1,512,2,384]{3,2,1,0:T(2,128)(2,1)} %param.18) | data formatting | bytes 1572864 | tf_op jit(solution)/shard_map/reshape | solution.py:191
  2.5 3.0 %collective-permute-start.2 = (bf16[1,512,768]{2,1,0:T(8,128)(2,1)S(1)}, bf16[1,512,768]{2,1,0:T(8,128)(2,1)}, u32[]{:S(2)}, u32[]{:S(2)}) collective-permute-start(bf16[1,512,768]{2,1,0:T(8,128)(2,1)S(1)} %reshape.59), channel_id=1, source_target_pairs={{0,8},{4,12},{8,16},{12,20},{16,24},{20,28},{24,0},{28,4},{1,9},{5... | collective-permute-start | bytes 2359304 | tf_op jit(solution)/shard_map/ppermute | solution.py:14
  8.5 1.8 dynamic-slice_bitcast_fusion.6
  10.2 1.7 pad_maximum_fusion.1
  12.0 5.0 %all-to-all-start = ((bf16[4,384,768]{2,1,0:T(8,128)(2,1)}), bf16[4,384,768]{2,1,0:T(8,128)(2,1)}, u32[]{:S(2)}, u32[]{:S(2)}) async-start(bf16[4,384,768]{2,1,0:T(8,128)(2,1)} %pad_maximum_fusion.1), calls=%async_computation | async-start | bytes 4718592 | tf_op jit(solution)/shard_map/all_to_all | solution.py:159
  19.1 4.1 %fusion = f32[512]{0:T(512)S(1)} fusion(bf16[512,6144]{1,0:T(8,128)(2,1)} %param.10), kind=kLoop, calls=%fused_computation.2 | loop fusion | flops 9436672 | bytes 6293504 | tf_op jit(solution)/shard_map/reduce_sum | solution.py:200
  23.2 12.8 %fusion.13 = f32[3,512,384]{2,1,0:T(8,128)S(1)} fusion(bf16[6144,3,384]{2,0,1:T(8,128)(2,1)} %param.15, bf16[512,6144]{1,0:T(8,128)(2,1)} %param.10, f32[6144]{0:T(1024)S(1)} %bitcast.102, f32[6144]{0:T(1024)S(1)} %bitcast.103, f32[512]{0:T(512)S(1)} %add_rsqrt_fusion.2), kind=kOutput, calls=%fused_computation.20 | convolution fusion | flops 7263485952 | bytes 22857728 | tf_op jit(solution)/shard_map/td,dkh->kth/dot_general | solution.py:203
  37.2 2.3 %copy.17 = f32[1,512,384]{1,2,0:T(8,128)} copy(f32[1,512,384]{2,1,0:T(8,128)} %get-tuple-element.26) | data formatting | bytes 1572864 | tf_op jit(solution)/shard_map/mul | solution.py:19
  41.7 2.3 %copy.18 = f32[512,384]{1,0:T(8,128)} copy(f32[512,384]{0,1:T(8,128)} %bitcast.95) | data formatting | bytes 1572864 | tf_op jit(solution)/shard_map/mul | solution.py:19
  48.6 2.0 %pad_maximum_fusion.refs_4_.refs_5_ = bf16[4,512,768]{2,1,0:T(8,128)(2,1)S(1)} fusion(bf16[1,512,768]{2,1,0:T(8,128)(2,1)} %collective-permute-done.4, bf16[1,512,768]{2,1,0:T(8,128)(2,1)} %collective-permute-done.3, bf16[1,512,768]{2,1,0:T(8,128)(2,1)} %collective-permute-done.2, bf16[1,512,768]{2,1,0:T(8,128)(2,1)} %copy-done.6), kind=kLoop, calls=%fused_computation.11 | loop fusion | flops 4718592 | bytes 6291456 | tf_op jit(solution)/shard_map/concatenate | solution.py:193
  50.6 19.4 %all-to-all-done = bf16[4,384,768]{2,1,0:T(8,128)(2,1)} async-done(((bf16[4,384,768]{2,1,0:T(8,128)(2,1)}), bf16[4,384,768]{2,1,0:T(8,128)(2,1)}, u32[]{:S(2)}, u32[]{:S(2)}) %all-to-all-start) | async-done | bytes 2359328 | tf_op jit(solution)/shard_map/all_to_all | solution.py:159
  70.0 2.7 %dynamic-slice_bitcast_fusion = (bf16[384,768]{1,0:T(8,128)(2,1)}, bf16[384,768]{1,0:T(8,128)(2,1)}, bf16[384,768]{1,0:T(8,128)(2,1)}) fusion(bf16[4,384,768]{2,1,0:T(8,128)(2,1)} %all-to-all-done, s32[]{:T(128)S(6)} %select_n.131, s32[]{:T(128)S(6)} %select_n.129, s32[]{:T(128)S(6)} %select_n.127), kind=kLoop, calls=%fused_computation.41 | loop fusion | bytes 3538956 | tf_op jit(solution)/shard_map/jit(dynamic_index_in_dim)/squeeze | solution.py:161
  72.8 3.1 %collective-permute-start.5 = (bf16[4,512,768]{2,1,0:T(8,128)(2,1)S(1)}, bf16[4,512,768]{2,1,0:T(8,128)(2,1)}, u32[]{:S(2)}, u32[]{:S(2)}) collective-permute-start(bf16[4,512,768]{2,1,0:T(8,128)(2,1)S(1)} %pad_maximum_fusion.refs_4_.refs_5_), channel_id=1, source_target_pairs={{0,4},{4,0},{8,12},{12,8},{16,20},{20,16},{24,28},{28,24},{1,5},{5... | collective-permute-start | bytes 9437192 | tf_op jit(solution)/shard_map/ppermute | solution.py:213
  80.7 3.3 %pad_maximum_fusion.2.refs_2_.refs_3_ = bf16[3,512,768]{2,1,0:T(8,128)(2,1)} fusion(bf16[1,512,768]{2,1,0:T(8,128)(2,1)} %bitcast.24, bf16[1,512,768]{2,1,0:T(8,128)(2,1)} %bitcast.23, bf16[1,512,768]{2,1,0:T(8,128)(2,1)} %get-tuple-element.28), kind=kLoop, calls=%fused_computation.18 | loop fusion | flops 2359296 | bytes 4718592 | tf_op jit(solution)/shard_map/stack | solution.py:223
  83.9 15.1 %shard_map.102 = bf16[128,384]{1,0:T(8,128)(2,1)} custom-call(s32[6]{0:T(128)} %compare_select_fusion.6.refs_0_, bf16[128,384]{1,0:T(8,128)(2,1)} %copy.22.refs_1_, bf16[3,512,768]{2,1,0:T(8,128)(2,1)} %pad_maximum_fusion.2.refs_2_.refs_3_, bf16[3,512,768]{2,1,0:T(8,128)(2,1)} %pad_maximum_fusion.2.refs_2_.refs_3_, bf16[4,512,768]{2,1,0:T(8,128)(2,1)} %copy-done.2, ...), custom_call_target="tpu_custom_call" | custom-call | flops 226492416 | bytes 1769472 | tf_op jit(solution)/shard_map/pallas_call | solution.py:138
  99.0 1.7 broadcast_in_dim.23
  100.7 5.1 %all-to-all-start.3 = ((bf16[4,128,384]{2,1,0:T(8,128)(2,1)}), bf16[4,128,384]{2,1,0:T(8,128)(2,1)S(1)}, u32[]{:S(2)}, u32[]{:S(2)}) async-start(bf16[4,128,384]{2,1,0:T(8,128)(2,1)} %broadcast_in_dim.23), calls=%async_computation.3 | async-start | bytes 786432 | tf_op jit(solution)/shard_map/all_to_all | solution.py:242
  106.5 15.1 %shard_map.101 = bf16[128,384]{1,0:T(8,128)(2,1)} custom-call(s32[6]{0:T(128)} %compare_select_fusion.6.refs_0_, bf16[128,384]{1,0:T(8,128)(2,1)} %copy.21.refs_1_, bf16[3,512,768]{2,1,0:T(8,128)(2,1)} %pad_maximum_fusion.2.refs_2_.refs_3_, bf16[3,512,768]{2,1,0:T(8,128)(2,1)} %pad_maximum_fusion.2.refs_2_.refs_3_, bf16[4,512,768]{2,1,0:T(8,128)(2,1)} %copy-done.2, ...), custom_call_target="tpu_custom_call" | custom-call | flops 226492416 | bytes 1769472 | tf_op jit(solution)/shard_map/pallas_call | solution.py:138
  121.6 1.7 broadcast_in_dim.22
  123.3 5.1 %all-to-all-start.2 = ((bf16[4,128,384]{2,1,0:T(8,128)(2,1)}), bf16[4,128,384]{2,1,0:T(8,128)(2,1)S(1)}, u32[]{:S(2)}, u32[]{:S(2)}) async-start(bf16[4,128,384]{2,1,0:T(8,128)(2,1)} %broadcast_in_dim.22), calls=%async_computation.2 | async-start | bytes 786432 | tf_op jit(solution)/shard_map/all_to_all | solution.py:242
  129.1 15.2 %shard_map.100 = bf16[128,384]{1,0:T(8,128)(2,1)} custom-call(s32[6]{0:T(128)} %compare_select_fusion.6.refs_0_, bf16[128,384]{1,0:T(8,128)(2,1)} %copy.20.refs_1_, bf16[3,512,768]{2,1,0:T(8,128)(2,1)} %pad_maximum_fusion.2.refs_2_.refs_3_, bf16[3,512,768]{2,1,0:T(8,128)(2,1)} %pad_maximum_fusion.2.refs_2_.refs_3_, bf16[4,512,768]{2,1,0:T(8,128)(2,1)} %copy-done.2, ...), custom_call_target="tpu_custom_call" | custom-call | flops 226492416 | bytes 1769472 | tf_op jit(solution)/shard_map/pallas_call | solution.py:138
  144.3 1.7 broadcast_in_dim.21
  146.0 5.1 %all-to-all-start.1 = ((bf16[4,128,384]{2,1,0:T(8,128)(2,1)}), bf16[4,128,384]{2,1,0:T(8,128)(2,1)S(1)}, u32[]{:S(2)}, u32[]{:S(2)}) async-start(bf16[4,128,384]{2,1,0:T(8,128)(2,1)} %broadcast_in_dim.21), calls=%async_computation.1 | async-start | bytes 786432 | tf_op jit(solution)/shard_map/all_to_all | solution.py:242
  153.3 15.1 %shard_map.103 = bf16[128,384]{1,0:T(8,128)(2,1)} custom-call(s32[6]{0:T(128)} %compare_select_fusion.6.refs_0_, bf16[128,384]{1,0:T(8,128)(2,1)} %copy.23.refs_1_, bf16[3,512,768]{2,1,0:T(8,128)(2,1)} %pad_maximum_fusion.2.refs_2_.refs_3_, bf16[3,512,768]{2,1,0:T(8,128)(2,1)} %pad_maximum_fusion.2.refs_2_.refs_3_, bf16[4,512,768]{2,1,0:T(8,128)(2,1)} %copy-done.2, ...), custom_call_target="tpu_custom_call" | custom-call | flops 226492416 | bytes 1769472 | tf_op jit(solution)/shard_map/pallas_call | solution.py:138
  168.3 1.7 broadcast_in_dim.24
  170.0 5.1 %all-to-all-start.4 = ((bf16[4,128,384]{2,1,0:T(8,128)(2,1)}), bf16[4,128,384]{2,1,0:T(8,128)(2,1)}, u32[]{:S(2)}, u32[]{:S(2)}) async-start(bf16[4,128,384]{2,1,0:T(8,128)(2,1)} %broadcast_in_dim.24), calls=%async_computation.4 | async-start | bytes 786432 | tf_op jit(solution)/shard_map/all_to_all | solution.py:242
  178.2 9.4 %all-to-all-done.4 = bf16[4,128,384]{2,1,0:T(8,128)(2,1)} async-done(((bf16[4,128,384]{2,1,0:T(8,128)(2,1)}), bf16[4,128,384]{2,1,0:T(8,128)(2,1)}, u32[]{:S(2)}, u32[]{:S(2)}) %all-to-all-start.4) | async-done | bytes 393248 | tf_op jit(solution)/shard_map/all_to_all | solution.py:242
  187.6 1.8 constant_dynamic-update-slice_fusion
  194.1 1.8 convolution_convert_fusion.3
  195.8 1.8 convolution_convert_fusion.2
  197.6 1.8 convert_add_fusion
  199.5 4.7 %fusion.12 = f32[512,1536]{1,0:T(8,128)} fusion(f32[512,768]{1,0:T(8,128)S(1)} %convert_add_fusion, f32[512,768]{1,0:T(8,128)S(1)} %convert_add_fusion.1, f32[1536]{0:T(1024)S(1)} %dynamic-slice_reduce_fusion, bf16[512,6144]{1,0:T(8,128)(2,1)} %param.10, s32[]{:T(128)S(6)} %select_n.113, pred[]{:T(512)S(6)} %eq.32, bf16[384,6144]{1,0:T(8,128)(2,1)} %param.19, ...), kind=kOutput, calls=%fused_computation.15 | convolution fusion | flops 612630528 | bytes 9444864 | tf_op jit(solution)/shard_map/dot_general | solution.py:252
  (82 shorter events, 29.1 us)
Async XLA Ops:
  0.0 17.5 %copy-start = (bf16[8,3,6144]{2,0,1:T(8,128)(2,1)S(1)}, bf16[8,3,6144]{2,0,1:T(8,128)(2,1)}, u32[]{:S(2)}) copy-start(bf16[8,3,6144]{2,0,1:T(8,128)(2,1)} %param.11) | copy-start | bytes 884740
  2.5 7.7 %copy-start.6 = (bf16[1,512,768]{2,1,0:T(8,128)(2,1)}, bf16[1,512,768]{2,1,0:T(8,128)(2,1)S(1)}, u32[]{:S(2)}) copy-start(bf16[1,512,768]{2,1,0:T(8,128)(2,1)S(1)} %reshape.59) | copy-start | bytes 2359300
  2.5 46.0 %collective-permute-start.2 = (bf16[1,512,768]{2,1,0:T(8,128)(2,1)S(1)}, bf16[1,512,768]{2,1,0:T(8,128)(2,1)}, u32[]{:S(2)}, u32[]{:S(2)}) collective-permute-start(bf16[1,512,768]{2,1,0:T(8,128)(2,1)S(1)} %reshape.59), channel_id=1, source_target_pairs={{0,8},{4,12},{8,16},{12,20},{16,24},{20,28},{24,0},{28,4},{1,9},{5... | collective-permute-start | bytes 2359304 | tf_op jit(solution)/shard_map/ppermute | solution.py:14
  5.5 43.0 %collective-permute-start.3 = (bf16[1,512,768]{2,1,0:T(8,128)(2,1)S(1)}, bf16[1,512,768]{2,1,0:T(8,128)(2,1)}, u32[]{:S(2)}, u32[]{:S(2)}) collective-permute-start(bf16[1,512,768]{2,1,0:T(8,128)(2,1)S(1)} %reshape.59), channel_id=1, source_target_pairs={{0,16},{4,20},{8,24},{12,28},{16,0},{20,4},{24,8},{28,12},{1,17},{... | collective-permute-start | bytes 2359304 | tf_op jit(solution)/shard_map/ppermute | solution.py:14
  7.0 41.5 %collective-permute-start.4 = (bf16[1,512,768]{2,1,0:T(8,128)(2,1)S(1)}, bf16[1,512,768]{2,1,0:T(8,128)(2,1)}, u32[]{:S(2)}, u32[]{:S(2)}) collective-permute-start(bf16[1,512,768]{2,1,0:T(8,128)(2,1)S(1)} %reshape.59), channel_id=1, source_target_pairs={{0,24},{4,28},{8,0},{12,4},{16,8},{20,12},{24,16},{28,20},{1,25},{... | collective-permute-start | bytes 2359304 | tf_op jit(solution)/shard_map/ppermute | solution.py:14
  12.0 5.0 %copy-start.14 = (s32[8]{0:T(128)S(1)}, s32[8]{0:T(128)}, u32[]{:S(2)}) copy-start(s32[8]{0:T(128)} %param.12) | copy-start | bytes 100
  12.0 58.1 %all-to-all-start = ((bf16[4,384,768]{2,1,0:T(8,128)(2,1)}), bf16[4,384,768]{2,1,0:T(8,128)(2,1)}, u32[]{:S(2)}, u32[]{:S(2)}) async-start(bf16[4,384,768]{2,1,0:T(8,128)(2,1)} %pad_maximum_fusion.1), calls=%async_computation | async-start | bytes 4718592 | tf_op jit(solution)/shard_map/all_to_all | solution.py:159
  37.2 6.8 %copy-start.12 = (f32[384]{0:T(512)S(1)}, f32[384]{0:T(512)}, u32[]{:S(2)}) copy-start(f32[384]{0:T(512)} %param.17) | copy-start | bytes 4612
  45.3 1.9 copy-start.7
  45.3 2.3 %copy-start.13 = (f32[384]{0:T(512)S(1)}, f32[384]{0:T(512)}, u32[]{:S(2)}) copy-start(f32[384]{0:T(512)} %param.16) | copy-start | bytes 4612
  46.6 26.2 %collective-permute-start = (bf16[512,768]{1,0:T(8,128)(2,1)}, bf16[512,768]{1,0:T(8,128)(2,1)}, u32[]{:S(2)}, u32[]{:S(2)}) collective-permute-start(bf16[512,768]{1,0:T(8,128)(2,1)} %get-tuple-element.29), channel_id=1, source_target_pairs={{0,4},{4,8},{8,12},{12,16},{16,20},{20,24},{24,28},{28,0},{1,5},{5... | collective-permute-start | bytes 2359304 | tf_op jit(solution)/shard_map/ppermute | solution.py:14
  46.6 26.2 %collective-permute-start.1 = (bf16[512,768]{1,0:T(8,128)(2,1)}, bf16[512,768]{1,0:T(8,128)(2,1)}, u32[]{:S(2)}, u32[]{:S(2)}) collective-permute-start(bf16[512,768]{1,0:T(8,128)(2,1)} %get-tuple-element.29), channel_id=1, source_target_pairs={{0,8},{4,12},{8,16},{12,20},{16,24},{20,28},{24,0},{28,4},{1,9},{5... | collective-permute-start | bytes 2359304 | tf_op jit(solution)/shard_map/ppermute | solution.py:14
  50.6 29.3 %copy-start.2 = (bf16[4,512,768]{2,1,0:T(8,128)(2,1)}, bf16[4,512,768]{2,1,0:T(8,128)(2,1)S(1)}, u32[]{:S(2)}) copy-start(bf16[4,512,768]{2,1,0:T(8,128)(2,1)S(1)} %pad_maximum_fusion.refs_4_.refs_5_) | copy-start | bytes 9437188
  72.8 11.1 %collective-permute-start.5 = (bf16[4,512,768]{2,1,0:T(8,128)(2,1)S(1)}, bf16[4,512,768]{2,1,0:T(8,128)(2,1)}, u32[]{:S(2)}, u32[]{:S(2)}) collective-permute-start(bf16[4,512,768]{2,1,0:T(8,128)(2,1)S(1)} %pad_maximum_fusion.refs_4_.refs_5_), channel_id=1, source_target_pairs={{0,4},{4,0},{8,12},{12,8},{16,20},{20,16},{24,28},{28,24},{1,5},{5... | collective-permute-start | bytes 9437192 | tf_op jit(solution)/shard_map/ppermute | solution.py:213
  100.7 20.9 %all-to-all-start.3 = ((bf16[4,128,384]{2,1,0:T(8,128)(2,1)}), bf16[4,128,384]{2,1,0:T(8,128)(2,1)S(1)}, u32[]{:S(2)}, u32[]{:S(2)}) async-start(bf16[4,128,384]{2,1,0:T(8,128)(2,1)} %broadcast_in_dim.23), calls=%async_computation.3 | async-start | bytes 786432 | tf_op jit(solution)/shard_map/all_to_all | solution.py:242
  123.3 21.0 %all-to-all-start.2 = ((bf16[4,128,384]{2,1,0:T(8,128)(2,1)}), bf16[4,128,384]{2,1,0:T(8,128)(2,1)S(1)}, u32[]{:S(2)}, u32[]{:S(2)}) async-start(bf16[4,128,384]{2,1,0:T(8,128)(2,1)} %broadcast_in_dim.22), calls=%async_computation.2 | async-start | bytes 786432 | tf_op jit(solution)/shard_map/all_to_all | solution.py:242
  129.1 22.0 %copy-start.3 = (bf16[384,768]{1,0:T(8,128)(2,1)S(1)}, bf16[384,768]{1,0:T(8,128)(2,1)}, u32[]{:S(2)}) copy-start(bf16[384,768]{1,0:T(8,128)(2,1)} %get-tuple-element.18) | copy-start | bytes 1769476
  129.1 22.0 %copy-start.4 = (bf16[384,768]{1,0:T(8,128)(2,1)S(1)}, bf16[384,768]{1,0:T(8,128)(2,1)}, u32[]{:S(2)}) copy-start(bf16[384,768]{1,0:T(8,128)(2,1)} %get-tuple-element.17) | copy-start | bytes 1769476
  129.1 22.0 %copy-start.5 = (bf16[384,768]{1,0:T(8,128)(2,1)S(1)}, bf16[384,768]{1,0:T(8,128)(2,1)}, u32[]{:S(2)}) copy-start(bf16[384,768]{1,0:T(8,128)(2,1)} %get-tuple-element.16) | copy-start | bytes 1769476
  146.0 22.4 %all-to-all-start.1 = ((bf16[4,128,384]{2,1,0:T(8,128)(2,1)}), bf16[4,128,384]{2,1,0:T(8,128)(2,1)S(1)}, u32[]{:S(2)}, u32[]{:S(2)}) async-start(bf16[4,128,384]{2,1,0:T(8,128)(2,1)} %broadcast_in_dim.21), calls=%async_computation.1 | async-start | bytes 786432 | tf_op jit(solution)/shard_map/all_to_all | solution.py:242
  152.5 41.5 %collective-permute-start.6 = (bf16[3,384,768]{2,1,0:T(8,128)(2,1)}, bf16[3,384,768]{2,1,0:T(8,128)(2,1)}, u32[]{:S(2)}, u32[]{:S(2)}) collective-permute-start(bf16[3,384,768]{2,1,0:T(8,128)(2,1)} %pad_maximum_fusion.3), channel_id=1, source_target_pairs={{0,4},{4,0},{8,12},{12,8},{16,20},{20,16},{24,28},{28,24},{1,5},{5... | collective-permute-start | bytes 5308424 | tf_op jit(solution)/shard_map/ppermute | solution.py:237
  170.0 17.5 %all-to-all-start.4 = ((bf16[4,128,384]{2,1,0:T(8,128)(2,1)}), bf16[4,128,384]{2,1,0:T(8,128)(2,1)}, u32[]{:S(2)}, u32[]{:S(2)}) async-start(bf16[4,128,384]{2,1,0:T(8,128)(2,1)} %broadcast_in_dim.24), calls=%async_computation.4 | async-start | bytes 786432 | tf_op jit(solution)/shard_map/all_to_all | solution.py:242
  197.6 1.9 copy-start.8
  197.6 1.9 copy-start.9
  197.6 1.9 copy-start.10
  197.6 1.9 copy-start.11
  199.5 4.7 %copy-start.1 = (bf16[8,3,6144]{2,0,1:T(8,128)(2,1)S(1)}, bf16[8,3,6144]{2,0,1:T(8,128)(2,1)}, u32[]{:S(2)}) copy-start(bf16[8,3,6144]{2,0,1:T(8,128)(2,1)} %param.11) | copy-start | bytes 884740

commit v13 on v11

--- a/solution.py
+++ b/solution.py
@@ -205,12 +205,13 @@
     keys = head_norm(qkv[1], k_gain, heads).astype(jnp.bfloat16)
     values = qkv[2].astype(jnp.bfloat16)
     local_kv = jnp.concatenate([keys.reshape(span, heads * HD), values], axis=1)
+    local_kv, same_core = lax.optimization_barrier((local_kv, same_core))
+    other_core = lax.ppermute(same_core, "slot", [(i, i ^ 1) for i in range(slots)])
     before = from_behind(local_kv, "slot", 1)
     earlier = from_behind(local_kv, "slot", 2)
-    queries, before, earlier, same_core, mine = lax.optimization_barrier(
-        (queries, before, earlier, same_core, mine)
-    )
-    other_core = lax.ppermute(same_core, "slot", [(i, i ^ 1) for i in range(slots)])
+    queries, before, earlier, mine = lax.optimization_barrier(
+        (queries, before, earlier, mine)
+    )
     own_mask = lax.dynamic_index_in_dim(block_mask, slot, 0, keepdims=False)
     own_cache = lax.dynamic_index_in_dim(cache_index, slot, 0, keepdims=False)
     sibling_slot = jnp.bitwise_xor(slot, 1)

time: 162 us -> 166 us (1.025)
  other arithmetic: 21.2 us -> 23 us
    all_to_all x1, waiting for transfers between devices: 12.4 us -> 5.62 us  [fetch_out_weight(): exchanged = lax.all_to_all(blocks, 'head', 0, 0)]
    ppermute x5, waiting for transfers between devices: 8.12 us -> 14.7 us  [from_behind(): lax.ppermute(shard, axis, [(i, (i + by) % length) for i in range(length)])]
    ppermute x1, starting transfers between devices: 0.01 us -> 2.14 us  [local(): lax.ppermute(same_core, 'slot', [(i, i ^ 1) for i in range(slots)])]
    slice x1, local copies, waits for them, and re-layouts: 0.26 us -> 2.3 us  [local(): queries = head_norm(qkv[0], q_gain, heads).astype(jnp.bfloat16)]
    another operation x2 -> x1, other arithmetic: 4.3 us -> 3.05 us  [local(): jnp.stack([local_kv, before, earlier]).reshape(3, span, 2 * width)]
  transfers between devices with their start and end apart: 14 -> 14, of which waited for: 5 -> 6; matrix products, arithmetic and copies ran while one was open for 33% -> 35% of each run, Pallas kernels for 22% -> 22%
where the time goes in v13:
time: 166 us; the launch traced here: 164 us
  waiting for transfers between devices  39.3 us (24%)
  Pallas kernels  35.7 us (22%)
  matrix products  25 us (15%)
  other arithmetic  23 us (14%)
  local copies, waits for them, and re-layouts  20.7 us (12%)
  starting transfers between devices  19.8 us (12%)
    pallas_call x2, Pallas kernels, flash(): pl.pallas_call(kernel, grid_spec=grid_spec, out_shape=jax.ShapeDtypeStruc...  35.7 us
    ppermute x6, waiting for transfers between devices, local(): lax.ppermute(part, 'head', [(i, (i + shift) % groups) for i in range(grou...  19.1 us
    ppermute x5, waiting for transfers between devices, from_behind(): lax.ppermute(shard, axis, [(i, (i + by) % length) for i in range(length)])  14.7 us
    dot_general x1, matrix products, local(): jnp.einsum('td,dkh->kth', hidden, w_qkv, preferred_element_type=jnp.float32)  12.8 us
    ppermute x6, starting transfers between devices, local(): lax.ppermute(part, 'head', [(i, (i + shift) % groups) for i in range(grou...  7.18 us
    all_to_all x1, waiting for transfers between devices, fetch_out_weight(): exchanged = lax.all_to_all(blocks, 'head', 0, 0)  5.62 us
    ppermute x5, starting transfers between devices, from_behind(): lax.ppermute(shard, axis, [(i, (i + by) % length) for i in range(length)])  5.6 us
    dot_general x3, matrix products, local(): jnp.dot(group_o, sibling[shift - 1], preferred_element_type=jnp.float32)  4.93 us
  transfers between devices with their start and end apart: 14, of which 6 were waited for; matrix products, arithmetic and copies ran while one was open for 35% of the time, Pallas kernels for 22%

profile of v13, /device:TPU:9, one launch (start us, length us, event | category | flops | bytes accessed | tf_op | source)
XLA Modules:
  0.0 164.0 jit_solution(18162368924550331504)
XLA Ops:
  0.0 2.5 %reshape.53 = bf16[1,512,768]{2,1,0:T(8,128)(2,1)S(1)} reshape(bf16[1,512,2,384]{3,2,1,0:T(2,128)(2,1)} %param.18) | data formatting | bytes 1572864 | tf_op jit(solution)/shard_map/reshape | solution.py:191
  2.5 1.3 collective-permute-start
  6.2 1.8 %dynamic-slice_bitcast_fusion.6 = (bf16[1,384,768]{2,1,0:T(8,128)(2,1)S(1)}, bf16[1,384,768]{2,1,0:T(8,128)(2,1)S(1)}, bf16[1,384,768]{2,1,0:T(8,128)(2,1)S(1)}, bf16[1,384,768]{2,1,0:T(8,128)(2,1)S(1)}) fusion(bf16[384,6144]{1,0:T(8,128)(2,1)} %param.19, s32[]{:T(128)S(6)} %select_n.112, s32[]{:T(128)S(6)} %select_n.114, s32[]{:T(128)S(6)} %select_n.113, ...), kind=kLoop, calls=%fused_computation.47 | loop fusion | bytes 4718608 | tf_op jit(solution)/shard_map/stack | solution.py:155
  7.9 1.7 %pad_maximum_fusion.1 = bf16[4,384,768]{2,1,0:T(8,128)(2,1)} fusion(bf16[1,384,768]{2,1,0:T(8,128)(2,1)S(1)} %get-tuple-element.24, bf16[1,384,768]{2,1,0:T(8,128)(2,1)S(1)} %get-tuple-element.22, bf16[1,384,768]{2,1,0:T(8,128)(2,1)S(1)} %get-tuple-element.23, bf16[1,384,768]{2,1,0:T(8,128)(2,1)S(1)} %get-tuple-element.21), kind=kLoop, calls=%fused_computation.17 | loop fusion | flops 3538944 | bytes 4718592 | tf_op jit(solution)/shard_map/stack | solution.py:155
  9.6 4.9 %all-to-all-start = ((bf16[4,384,768]{2,1,0:T(8,128)(2,1)}), bf16[4,384,768]{2,1,0:T(8,128)(2,1)}, u32[]{:S(2)}, u32[]{:S(2)}) async-start(bf16[4,384,768]{2,1,0:T(8,128)(2,1)} %pad_maximum_fusion.1), calls=%async_computation | async-start | bytes 4718592 | tf_op jit(solution)/shard_map/all_to_all | solution.py:159
  16.1 4.1 %fusion = f32[512]{0:T(512)S(1)} fusion(bf16[512,6144]{1,0:T(8,128)(2,1)} %param.10), kind=kLoop, calls=%fused_computation.2 | loop fusion | flops 9436672 | bytes 6293504 | tf_op jit(solution)/shard_map/reduce_sum | solution.py:200
  20.2 12.8 %fusion.13 = f32[3,512,384]{2,1,0:T(8,128)S(1)} fusion(bf16[6144,3,384]{2,0,1:T(8,128)(2,1)} %param.15, bf16[512,6144]{1,0:T(8,128)(2,1)} %param.10, f32[6144]{0:T(1024)S(1)} %bitcast.89, f32[6144]{0:T(1024)S(1)} %bitcast.90, f32[512]{0:T(512)S(1)} %add_rsqrt_fusion.2), kind=kOutput, calls=%fused_computation.20 | convolution fusion | flops 7263485952 | bytes 22857728 | tf_op jit(solution)/shard_map/td,dkh->kth/dot_general | solution.py:203
  34.2 2.3 %copy.17 = f32[1,512,384]{1,2,0:T(8,128)} copy(f32[1,512,384]{2,1,0:T(8,128)} %get-tuple-element.28) | data formatting | bytes 1572864 | tf_op jit(solution)/shard_map/mul | solution.py:19
  38.8 2.3 %copy.18 = f32[512,384]{1,0:T(8,128)} copy(f32[512,384]{0,1:T(8,128)} %bitcast.84) | data formatting | bytes 1572864 | tf_op jit(solution)/shard_map/mul | solution.py:19
  41.2 1.3 fusion.18
  43.4 1.8 %pad_maximum_fusion.refs_4_.refs_5_ = bf16[4,512,768]{2,1,0:T(8,128)(2,1)S(1)} fusion(bf16[1,512,768]{2,1,0:T(8,128)(2,1)} %collective-permute-done.2, bf16[1,512,768]{2,1,0:T(8,128)(2,1)} %collective-permute-done.1, bf16[1,512,768]{2,1,0:T(8,128)(2,1)} %collective-permute-done, bf16[1,512,768]{2,1,0:T(8,128)(2,1)S(1)} %copy-done.8), kind=kLoop, calls=%fused_computation.11 | loop fusion | flops 4718592 | bytes 6291456 | tf_op jit(solution)/shard_map/concatenate | solution.py:193
  45.3 2.1 %collective-permute-start.5 = (bf16[4,512,768]{2,1,0:T(8,128)(2,1)S(1)}, bf16[4,512,768]{2,1,0:T(8,128)(2,1)}, u32[]{:S(2)}, u32[]{:S(2)}) collective-permute-start(bf16[4,512,768]{2,1,0:T(8,128)(2,1)S(1)} %pad_maximum_fusion.refs_4_.refs_5_), channel_id=1, source_target_pairs={{0,4},{4,0},{8,12},{12,8},{16,20},{20,16},{24,28},{28,24},{1,5},{5... | collective-permute-start | bytes 9437192 | tf_op jit(solution)/shard_map/ppermute | solution.py:209
  47.4 2.3 %copy.16 = f32[1,512,384]{1,2,0:T(8,128)} copy(f32[1,512,384]{2,1,0:T(8,128)} %get-tuple-element.29) | data formatting | bytes 1572864 | tf_op jit(solution)/shard_map/slice | solution.py:204
  53.9 1.3 compare_select_fusion.6.refs_0_
  55.9 2.1 %multiply_convert_fusion = bf16[512,3,128]{0,2,1:T(8,128)(2,1)} fusion(f32[512,3,128]{0,2,1:T(8,128)} %bitcast.78, f32[3,128]{1,0:T(4,128)S(1)} %bitcast.91, f32[512,3]{0,1:T(4,128)S(1)} %add_rsqrt_fusion.1), kind=kLoop, calls=%fused_computation.35 | loop fusion | flops 589824 | bytes 1187328 | tf_op jit(solution)/shard_map/convert_element_type | solution.py:204
  58.0 5.6 %all-to-all-done = bf16[4,384,768]{2,1,0:T(8,128)(2,1)} async-done(((bf16[4,384,768]{2,1,0:T(8,128)(2,1)}), bf16[4,384,768]{2,1,0:T(8,128)(2,1)}, u32[]{:S(2)}, u32[]{:S(2)}) %all-to-all-start) | async-done | bytes 2359328 | tf_op jit(solution)/shard_map/all_to_all | solution.py:159
  63.6 2.8 %dynamic-slice_bitcast_fusion = (bf16[384,768]{1,0:T(8,128)(2,1)}, bf16[384,768]{1,0:T(8,128)(2,1)}, bf16[384,768]{1,0:T(8,128)(2,1)}) fusion(bf16[4,384,768]{2,1,0:T(8,128)(2,1)} %all-to-all-done, s32[]{:T(128)S(6)} %select_n.121, s32[]{:T(128)S(6)} %select_n.119, s32[]{:T(128)S(6)} %select_n.117), kind=kLoop, calls=%fused_computation.41 | loop fusion | bytes 3538956 | tf_op jit(solution)/shard_map/jit(dynamic_index_in_dim)/squeeze | solution.py:161
  66.4 2.9 %collective-permute-done.3 = bf16[512,768]{1,0:T(8,128)(2,1)} collective-permute-done((bf16[512,768]{1,0:T(8,128)(2,1)}, bf16[512,768]{1,0:T(8,128)(2,1)}, u32[]{:S(2)}, u32[]{:S(2)}) %collective-permute-start.3) | collective-permute-done | bytes 786464 | tf_op jit(solution)/shard_map/ppermute | solution.py:14
  69.4 11.7 %collective-permute-done.4 = bf16[512,768]{1,0:T(8,128)(2,1)} collective-permute-done((bf16[512,768]{1,0:T(8,128)(2,1)}, bf16[512,768]{1,0:T(8,128)(2,1)}, u32[]{:S(2)}, u32[]{:S(2)}) %collective-permute-start.4) | collective-permute-done | bytes 786464 | tf_op jit(solution)/shard_map/ppermute | solution.py:14
  81.8 1.7 %copy.20.refs_1_ = bf16[256,384]{1,0:T(8,128)(2,1)} copy(bf16[256,384]{0,1:T(8,128)(2,1)} %bitcast.86) | data formatting | bytes 393216 | tf_op jit(solution)/shard_map/slice | solution.py:233
  83.5 2.9 %pad_maximum_fusion.3 = bf16[3,384,768]{2,1,0:T(8,128)(2,1)} fusion(bf16[1,384,768]{2,1,0:T(8,128)(2,1)} %bitcast.81, bf16[1,384,768]{2,1,0:T(8,128)(2,1)} %bitcast.79, bf16[1,384,768]{2,1,0:T(8,128)(2,1)} %bitcast.80), kind=kLoop, calls=%fused_computation.19 | loop fusion | flops 1769472 | bytes 3538944 | tf_op jit(solution)/shard_map/stack | solution.py:238
  86.4 3.1 %pad_maximum_fusion.2.refs_2_.refs_3_ = bf16[3,512,768]{2,1,0:T(8,128)(2,1)} fusion(bf16[1,512,768]{2,1,0:T(8,128)(2,1)} %bitcast.24, bf16[1,512,768]{2,1,0:T(8,128)(2,1)} %bitcast.23, bf16[1,512,768]{2,1,0:T(8,128)(2,1)S(1)} %bitcast.82), kind=kLoop, calls=%fused_computation.18 | loop fusion | flops 2359296 | bytes 4718592 | tf_op jit(solution)/shard_map/stack | solution.py:224
  89.5 17.8 %shard_map.100 = bf16[256,384]{1,0:T(8,128)(2,1)} custom-call(s32[6]{0:T(128)} %compare_select_fusion.6.refs_0_, bf16[256,384]{1,0:T(8,128)(2,1)} %copy.20.refs_1_, bf16[3,512,768]{2,1,0:T(8,128)(2,1)} %pad_maximum_fusion.2.refs_2_.refs_3_, bf16[3,512,768]{2,1,0:T(8,128)(2,1)} %pad_maximum_fusion.2.refs_2_.refs_3_, bf16[4,512,768]{2,1,0:T(8,128)(2,1)} %copy-done.2, ...), custom_call_target="tpu_custom_call" | custom-call | flops 905969664 | bytes 3538944 | tf_op jit(solution)/shard_map/pallas_call | solution.py:138
  110.2 17.9 %shard_map.101 = bf16[256,384]{1,0:T(8,128)(2,1)} custom-call(s32[6]{0:T(128)} %compare_select_fusion.6.refs_0_, bf16[256,384]{1,0:T(8,128)(2,1)} %copy.21.refs_1_, bf16[3,512,768]{2,1,0:T(8,128)(2,1)} %pad_maximum_fusion.2.refs_2_.refs_3_, bf16[3,512,768]{2,1,0:T(8,128)(2,1)} %pad_maximum_fusion.2.refs_2_.refs_3_, bf16[4,512,768]{2,1,0:T(8,128)(2,1)} %copy-done.2, ...), custom_call_target="tpu_custom_call" | custom-call | flops 905969664 | bytes 3538944 | tf_op jit(solution)/shard_map/pallas_call | solution.py:138
  128.8 3.0 %collective-permute-start.9 = (bf16[256,384]{1,0:T(8,128)(2,1)}, bf16[256,384]{1,0:T(8,128)(2,1)S(1)}, u32[]{:S(2)}, u32[]{:S(2)}) collective-permute-start(bf16[256,384]{1,0:T(8,128)(2,1)} %shard_map.101), channel_id=1, source_target_pairs={{0,2},{1,3},{2,0},{3,1},{4,6},{5,7},{6,4},{7,5},{8,10},{9,11},{10,... | collective-permute-start | bytes 589832 | tf_op jit(solution)/shard_map/ppermute | solution.py:243
  131.8 1.5 collective-permute-start.11
  133.4 15.0 %collective-permute-done.10 = bf16[256,384]{1,0:T(8,128)(2,1)S(1)} collective-permute-done((bf16[256,384]{1,0:T(8,128)(2,1)S(1)}, bf16[256,384]{1,0:T(8,128)(2,1)S(1)}, u32[]{:S(2)}, u32[]{:S(2)}) %collective-permute-start.10) | collective-permute-done | bytes 196640 | tf_op jit(solution)/shard_map/ppermute | solution.py:243
  149.6 3.0 %collective-permute-done.11 = bf16[256,384]{1,0:T(8,128)(2,1)S(1)} collective-permute-done((bf16[256,384]{1,0:T(8,128)(2,1)}, bf16[256,384]{1,0:T(8,128)(2,1)S(1)}, u32[]{:S(2)}, u32[]{:S(2)}) %collective-permute-start.11) | collective-permute-done | bytes 196640 | tf_op jit(solution)/shard_map/ppermute | solution.py:243
  154.3 1.6 convolution_convert_fusion.3
  156.0 1.6 convolution_convert_fusion.2
  157.6 1.7 %convert_add_fusion = f32[512,768]{1,0:T(8,128)S(1)} fusion(bf16[512,768]{1,0:T(8,128)(2,1)S(1)} %convolution_convert_fusion.2, bf16[512,768]{1,0:T(8,128)(2,1)S(1)} %convolution_convert_fusion.3, bf16[512,384]{1,0:T(8,128)(2,1)S(1)} %constant_dynamic-update-slice_fusion.4, bf16[3,384,768]{2,1,0:T(8,128)(2,1)} %collective-permute-done.12), kind=kOutput, calls=%fused_computation.21 | convolution fusion | flops 304349184 | bytes 4128768 | tf_op jit(solution)/shard_map/dot_general | solution.py:259
  159.3 4.7 %fusion.12 = f32[512,1536]{1,0:T(8,128)} fusion(f32[512,768]{1,0:T(8,128)S(1)} %convert_add_fusion, f32[512,768]{1,0:T(8,128)S(1)} %convert_add_fusion.1, f32[1536]{0:T(1024)S(1)} %dynamic-slice_reduce_fusion, bf16[512,6144]{1,0:T(8,128)(2,1)} %param.10, s32[]{:T(128)S(6)} %select_n.103, pred[]{:T(512)S(6)} %eq.29, bf16[384,6144]{1,0:T(8,128)(2,1)} %param.19, ...), kind=kOutput, calls=%fused_computation.15 | convolution fusion | flops 611844096 | bytes 9444864 | tf_op jit(solution)/shard_map/dot_general | solution.py:251
  (80 shorter events, 20.5 us)
Async XLA Ops:
  0.0 15.1 %copy-start = (bf16[8,3,6144]{2,0,1:T(8,128)(2,1)S(1)}, bf16[8,3,6144]{2,0,1:T(8,128)(2,1)}, u32[]{:S(2)}) copy-start(bf16[8,3,6144]{2,0,1:T(8,128)(2,1)} %param.11) | copy-start | bytes 884740
  2.5 5.4 %copy-start.7 = (bf16[1,512,768]{2,1,0:T(8,128)(2,1)}, bf16[1,512,768]{2,1,0:T(8,128)(2,1)S(1)}, u32[]{:S(2)}) copy-start(bf16[1,512,768]{2,1,0:T(8,128)(2,1)S(1)} %reshape.53) | copy-start | bytes 2359300
  2.5 40.9 %collective-permute-start = (bf16[1,512,768]{2,1,0:T(8,128)(2,1)S(1)}, bf16[1,512,768]{2,1,0:T(8,128)(2,1)}, u32[]{:S(2)}, u32[]{:S(2)}) collective-permute-start(bf16[1,512,768]{2,1,0:T(8,128)(2,1)S(1)} %reshape.53), channel_id=1, source_target_pairs={{0,8},{4,12},{8,16},{12,20},{16,24},{20,28},{24,0},{28,4},{1,9},{5... | collective-permute-start | bytes 2359304 | tf_op jit(solution)/shard_map/ppermute | solution.py:14
  3.8 39.6 %collective-permute-start.1 = (bf16[1,512,768]{2,1,0:T(8,128)(2,1)S(1)}, bf16[1,512,768]{2,1,0:T(8,128)(2,1)}, u32[]{:S(2)}, u32[]{:S(2)}) collective-permute-start(bf16[1,512,768]{2,1,0:T(8,128)(2,1)S(1)} %reshape.53), channel_id=1, source_target_pairs={{0,16},{4,20},{8,24},{12,28},{16,0},{20,4},{24,8},{28,12},{1,17},{... | collective-permute-start | bytes 2359304 | tf_op jit(solution)/shard_map/ppermute | solution.py:14
  5.0 38.4 %collective-permute-start.2 = (bf16[1,512,768]{2,1,0:T(8,128)(2,1)S(1)}, bf16[1,512,768]{2,1,0:T(8,128)(2,1)}, u32[]{:S(2)}, u32[]{:S(2)}) collective-permute-start(bf16[1,512,768]{2,1,0:T(8,128)(2,1)S(1)} %reshape.53), channel_id=1, source_target_pairs={{0,24},{4,28},{8,0},{12,4},{16,8},{20,12},{24,16},{28,20},{1,25},{... | collective-permute-start | bytes 2359304 | tf_op jit(solution)/shard_map/ppermute | solution.py:14
  9.6 4.9 %copy-start.14 = (s32[8]{0:T(128)S(1)}, s32[8]{0:T(128)}, u32[]{:S(2)}) copy-start(s32[8]{0:T(128)} %param.12) | copy-start | bytes 100
  9.6 53.9 %all-to-all-start = ((bf16[4,384,768]{2,1,0:T(8,128)(2,1)}), bf16[4,384,768]{2,1,0:T(8,128)(2,1)}, u32[]{:S(2)}, u32[]{:S(2)}) async-start(bf16[4,384,768]{2,1,0:T(8,128)(2,1)} %pad_maximum_fusion.1), calls=%async_computation | async-start | bytes 4718592 | tf_op jit(solution)/shard_map/all_to_all | solution.py:159
  36.6 4.6 %copy-start.12 = (f32[384]{0:T(512)S(1)}, f32[384]{0:T(512)}, u32[]{:S(2)}) copy-start(f32[384]{0:T(512)} %param.17) | copy-start | bytes 4612
  41.1 2.3 %copy-start.8 = (bf16[1,512,768]{2,1,0:T(8,128)(2,1)S(1)}, bf16[1,512,768]{2,1,0:T(8,128)(2,1)}, u32[]{:S(2)}) copy-start(bf16[1,512,768]{2,1,0:T(8,128)(2,1)} %copy-done.7) | copy-start | bytes 2359300
  45.2 21.2 %copy-start.2 = (bf16[4,512,768]{2,1,0:T(8,128)(2,1)}, bf16[4,512,768]{2,1,0:T(8,128)(2,1)S(1)}, u32[]{:S(2)}) copy-start(bf16[4,512,768]{2,1,0:T(8,128)(2,1)S(1)} %pad_maximum_fusion.refs_4_.refs_5_) | copy-start | bytes 9437188
  45.3 10.6 %copy-start.13 = (f32[384]{0:T(512)S(1)}, f32[384]{0:T(512)}, u32[]{:S(2)}) copy-start(f32[384]{0:T(512)} %param.16) | copy-start | bytes 4612
  45.3 44.2 %collective-permute-start.5 = (bf16[4,512,768]{2,1,0:T(8,128)(2,1)S(1)}, bf16[4,512,768]{2,1,0:T(8,128)(2,1)}, u32[]{:S(2)}, u32[]{:S(2)}) collective-permute-start(bf16[4,512,768]{2,1,0:T(8,128)(2,1)S(1)} %pad_maximum_fusion.refs_4_.refs_5_), channel_id=1, source_target_pairs={{0,4},{4,0},{8,12},{12,8},{16,20},{20,16},{24,28},{28,24},{1,5},{5... | collective-permute-start | bytes 9437192 | tf_op jit(solution)/shard_map/ppermute | solution.py:209
  51.6 17.7 %collective-permute-start.3 = (bf16[512,768]{1,0:T(8,128)(2,1)}, bf16[512,768]{1,0:T(8,128)(2,1)}, u32[]{:S(2)}, u32[]{:S(2)}) collective-permute-start(bf16[512,768]{1,0:T(8,128)(2,1)} %pad_maximum_fusion.4), channel_id=1, source_target_pairs={{0,4},{4,8},{8,12},{12,16},{16,20},{20,24},{24,28},{28,0},{1,5},{5... | collective-permute-start | bytes 2359304 | tf_op jit(solution)/shard_map/ppermute | solution.py:14
  52.5 28.6 %collective-permute-start.4 = (bf16[512,768]{1,0:T(8,128)(2,1)}, bf16[512,768]{1,0:T(8,128)(2,1)}, u32[]{:S(2)}, u32[]{:S(2)}) collective-permute-start(bf16[512,768]{1,0:T(8,128)(2,1)} %pad_maximum_fusion.4), channel_id=1, source_target_pairs={{0,8},{4,12},{8,16},{12,20},{16,24},{20,28},{24,0},{28,4},{1,9},{5... | collective-permute-start | bytes 2359304 | tf_op jit(solution)/shard_map/ppermute | solution.py:14
  63.6 17.5 %copy-start.9 = (bf16[512,3,128]{0,2,1:T(8,128)(2,1)S(1)}, bf16[512,3,128]{0,2,1:T(8,128)(2,1)}, u32[]{:S(2)}) copy-start(bf16[512,3,128]{0,2,1:T(8,128)(2,1)} %multiply_convert_fusion) | copy-start | bytes 1179652
  83.5 2.9 %copy-start.6 = (bf16[512,768]{1,0:T(8,128)(2,1)S(1)}, bf16[512,768]{1,0:T(8,128)(2,1)}, u32[]{:S(2)}) copy-start(bf16[512,768]{1,0:T(8,128)(2,1)} %pad_maximum_fusion.4) | copy-start | bytes 2359300
  86.4 67.9 %collective-permute-start.12 = (bf16[3,384,768]{2,1,0:T(8,128)(2,1)}, bf16[3,384,768]{2,1,0:T(8,128)(2,1)}, u32[]{:S(2)}, u32[]{:S(2)}) collective-permute-start(bf16[3,384,768]{2,1,0:T(8,128)(2,1)} %pad_maximum_fusion.3), channel_id=1, source_target_pairs={{0,4},{4,0},{8,12},{12,8},{16,20},{20,16},{24,28},{28,24},{1,5},{5... | collective-permute-start | bytes 5308424 | tf_op jit(solution)/shard_map/ppermute | solution.py:237
  107.3 24.5 %collective-permute-start.6 = (bf16[256,384]{1,0:T(8,128)(2,1)}, bf16[256,384]{1,0:T(8,128)(2,1)S(1)}, u32[]{:S(2)}, u32[]{:S(2)}) collective-permute-start(bf16[256,384]{1,0:T(8,128)(2,1)} %shard_map.100), channel_id=1, source_target_pairs={{0,1},{1,2},{2,3},{3,0},{4,5},{5,6},{6,7},{7,4},{8,9},{9,10},{10,1... | collective-permute-start | bytes 589832 | tf_op jit(solution)/shard_map/ppermute | solution.py:243
  109.3 22.5 %collective-permute-start.8 = (bf16[256,384]{1,0:T(8,128)(2,1)}, bf16[256,384]{1,0:T(8,128)(2,1)S(1)}, u32[]{:S(2)}, u32[]{:S(2)}) collective-permute-start(bf16[256,384]{1,0:T(8,128)(2,1)} %shard_map.100), channel_id=1, source_target_pairs={{0,2},{1,3},{2,0},{3,1},{4,6},{5,7},{6,4},{7,5},{8,10},{9,11},{10,... | collective-permute-start | bytes 589832 | tf_op jit(solution)/shard_map/ppermute | solution.py:243
  110.2 21.5 %copy-start.10 = (bf16[256,384]{1,0:T(8,128)(2,1)S(1)}, bf16[256,384]{1,0:T(8,128)(2,1)}, u32[]{:S(2)}) copy-start(bf16[256,384]{1,0:T(8,128)(2,1)} %shard_map.100) | copy-start | bytes 589828
  128.2 24.4 %copy-start.4 = (bf16[384,768]{1,0:T(8,128)(2,1)S(1)}, bf16[384,768]{1,0:T(8,128)(2,1)}, u32[]{:S(2)}) copy-start(bf16[384,768]{1,0:T(8,128)(2,1)} %get-tuple-element.18) | copy-start | bytes 1769476
  128.2 25.0 %copy-start.3 = (bf16[384,768]{1,0:T(8,128)(2,1)S(1)}, bf16[384,768]{1,0:T(8,128)(2,1)}, u32[]{:S(2)}) copy-start(bf16[384,768]{1,0:T(8,128)(2,1)} %get-tuple-element.19) | copy-start | bytes 1769476
  128.2 20.2 %collective-permute-start.7 = (bf16[256,384]{1,0:T(8,128)(2,1)}, bf16[256,384]{1,0:T(8,128)(2,1)S(1)}, u32[]{:S(2)}, u32[]{:S(2)}) collective-permute-start(bf16[256,384]{1,0:T(8,128)(2,1)} %shard_map.101), channel_id=1, source_target_pairs={{0,1},{1,2},{2,3},{3,0},{4,5},{5,6},{6,7},{7,4},{8,9},{9,10},{10,1... | collective-permute-start | bytes 589832 | tf_op jit(solution)/shard_map/ppermute | solution.py:243
  128.8 20.7 %collective-permute-start.9 = (bf16[256,384]{1,0:T(8,128)(2,1)}, bf16[256,384]{1,0:T(8,128)(2,1)S(1)}, u32[]{:S(2)}, u32[]{:S(2)}) collective-permute-start(bf16[256,384]{1,0:T(8,128)(2,1)} %shard_map.101), channel_id=1, source_target_pairs={{0,2},{1,3},{2,0},{3,1},{4,6},{5,7},{6,4},{7,5},{8,10},{9,11},{10,... | collective-permute-start | bytes 589832 | tf_op jit(solution)/shard_map/ppermute | solution.py:243
  131.8 16.5 %collective-permute-start.10 = (bf16[256,384]{1,0:T(8,128)(2,1)S(1)}, bf16[256,384]{1,0:T(8,128)(2,1)S(1)}, u32[]{:S(2)}, u32[]{:S(2)}) collective-permute-start(bf16[256,384]{1,0:T(8,128)(2,1)S(1)} %copy-done.10), channel_id=1, source_target_pairs={{0,3},{1,0},{2,1},{3,2},{4,7},{5,4},{6,5},{7,6},{8,11},{9,8},{10,9... | collective-permute-start | bytes 589832 | tf_op jit(solution)/shard_map/ppermute | solution.py:243
  131.8 20.7 %collective-permute-start.11 = (bf16[256,384]{1,0:T(8,128)(2,1)}, bf16[256,384]{1,0:T(8,128)(2,1)S(1)}, u32[]{:S(2)}, u32[]{:S(2)}) collective-permute-start(bf16[256,384]{1,0:T(8,128)(2,1)} %shard_map.101), channel_id=1, source_target_pairs={{0,3},{1,0},{2,1},{3,2},{4,7},{5,4},{6,5},{7,6},{8,11},{9,8},{10,9... | collective-permute-start | bytes 589832 | tf_op jit(solution)/shard_map/ppermute | solution.py:243
  148.3 5.4 %copy-start.5 = (bf16[384,768]{1,0:T(8,128)(2,1)S(1)}, bf16[384,768]{1,0:T(8,128)(2,1)}, u32[]{:S(2)}) copy-start(bf16[384,768]{1,0:T(8,128)(2,1)} %get-tuple-element.20) | copy-start | bytes 1769476
  157.6 1.7 %copy-start.11 = (bf16[256,384]{1,0:T(8,128)(2,1)S(1)}, bf16[256,384]{1,0:T(8,128)(2,1)}, u32[]{:S(2)}) copy-start(bf16[256,384]{1,0:T(8,128)(2,1)} %shard_map.101) | copy-start | bytes 589828
  159.3 4.7 %copy-start.1 = (bf16[8,3,6144]{2,0,1:T(8,128)(2,1)S(1)}, bf16[8,3,6144]{2,0,1:T(8,128)(2,1)}, u32[]{:S(2)}) copy-start(bf16[8,3,6144]{2,0,1:T(8,128)(2,1)} %param.11) | copy-start | bytes 884740

commit v14 on v11

--- a/solution.py
+++ b/solution.py
@@ -237,35 +237,35 @@
         jnp.stack(mine[1:]), "slot", [(i, i ^ 1) for i in range(slots)]
     )
 
-    received = [
-        jnp.concatenate([
-            lax.ppermute(part, "head", [(i, (i + shift) % groups) for i in range(groups)])
-            for part in mixed_parts
-        ], axis=0)
-        for shift in range(1, groups)
-    ]
-    mixed = jnp.concatenate(mixed_parts, axis=0)
     columns = own_full.shape[1]
-    half = columns // 2
-    attn = jnp.dot(mixed, own_full, preferred_element_type=jnp.float32).astype(jnp.bfloat16).astype(jnp.float32)
-    attn_mine = None
-    attn_sib = None
-    for shift in range(1, groups):
-        group_o = received[shift - 1]
-        part = jnp.dot(group_o, mine[shift], preferred_element_type=jnp.float32)
-        part = part.astype(jnp.bfloat16).astype(jnp.float32)
-        attn_mine = part if attn_mine is None else attn_mine + part
-        part = jnp.dot(group_o, sibling[shift - 1], preferred_element_type=jnp.float32)
-        part = part.astype(jnp.bfloat16).astype(jnp.float32)
-        attn_sib = part if attn_sib is None else attn_sib + part
-    other = jnp.concatenate([attn_mine, attn_sib], axis=1)
-    swapped = jnp.concatenate([attn_sib, attn_mine], axis=1)
-    attn = attn + jnp.where(core == 0, other, swapped)
-
     offset = head * columns
-    input_cols = lax.dynamic_slice_in_dim(activations, offset, columns, 1).astype(jnp.float32)
     gate_cols = lax.dynamic_slice_in_dim(modulation[2], offset, columns, 0)
-    return input_cols + gate_cols[None, :] * attn
+    results = []
+    for p, mixed_part in enumerate(mixed_parts):
+        received = [
+            lax.ppermute(mixed_part, "head", [(i, (i + shift) % groups) for i in range(groups)])
+            for shift in range(1, groups)
+        ]
+        attn = jnp.dot(mixed_part, own_full, preferred_element_type=jnp.float32)
+        attn = attn.astype(jnp.bfloat16).astype(jnp.float32)
+        attn_mine = None
+        attn_sib = None
+        for shift in range(1, groups):
+            group_o = received[shift - 1]
+            part = jnp.dot(group_o, mine[shift], preferred_element_type=jnp.float32)
+            part = part.astype(jnp.bfloat16).astype(jnp.float32)
+            attn_mine = part if attn_mine is None else attn_mine + part
+            part = jnp.dot(group_o, sibling[shift - 1], preferred_element_type=jnp.float32)
+            part = part.astype(jnp.bfloat16).astype(jnp.float32)
+            attn_sib = part if attn_sib is None else attn_sib + part
+        other = jnp.concatenate([attn_mine, attn_sib], axis=1)
+        swapped = jnp.concatenate([attn_sib, attn_mine], axis=1)
+        attn = attn + jnp.where(core == 0, other, swapped)
+        input_cols = lax.dynamic_slice(
+            activations, (p * rows, offset), (rows, columns)
+        ).astype(jnp.float32)
+        results.append(input_cols + gate_cols[None, :] * attn)
+    return jnp.concatenate(results, axis=0)
 
 
 def solution(mesh):

time: 162 us -> 167 us (1.031); the launches traced: 162 us -> 165 us
  matrix products: 25 us -> 28.8 us
    dot_general x3 -> x6, matrix products: 4.94 us -> 8.6 us  [local(): jnp.dot(group_o, sibling[shift - 1], preferred_element_type=jnp.float32)]
    concatenate x0 -> x1, other arithmetic: none -> 1.87 us  [local(): return jnp.concatenate(results, axis=0)]
    dot_general x1 -> x2, matrix products: 4.66 us -> 4.37 us  [local(): attn = jnp.dot(mixed_part, own_full, preferred_element_type=jnp.float32)]
  transfers between devices with their start and end apart: 14 -> 14, of which waited for: 5 -> 3; matrix products, arithmetic and copies ran while one was open for 33% -> 37% of each run, Pallas kernels for 22% -> 22%
where the time goes in v14:
time: 167 us; the launch traced here: 165 us
  waiting for transfers between devices  39.9 us (24%)
  Pallas kernels  35.7 us (21%)
  matrix products  28.8 us (17%)
  other arithmetic  21.8 us (13%)
  starting transfers between devices  19.5 us (12%)
  local copies, waits for them, and re-layouts  18.3 us (11%)
    pallas_call x2, Pallas kernels, flash(): pl.pallas_call(kernel, grid_spec=grid_spec, out_shape=jax.ShapeDtypeStruc...  35.7 us
    ppermute x6, waiting for transfers between devices, local(): lax.ppermute(mixed_part, 'head', [(i, (i + shift) % groups) for i in rang...  20.8 us
    dot_general x1, matrix products, local(): jnp.einsum('td,dkh->kth', hidden, w_qkv, preferred_element_type=jnp.float32)  12.8 us
    all_to_all x1, waiting for transfers between devices, fetch_out_weight(): exchanged = lax.all_to_all(blocks, 'head', 0, 0)  12.3 us
    dot_general x6, matrix products, local(): jnp.dot(group_o, sibling[shift - 1], preferred_element_type=jnp.float32)  8.6 us
    ppermute x5, starting transfers between devices, from_behind(): lax.ppermute(shard, axis, [(i, (i + by) % length) for i in range(length)])  6.86 us
    ppermute x5, waiting for transfers between devices, from_behind(): lax.ppermute(shard, axis, [(i, (i + by) % length) for i in range(length)])  6.85 us
    ppermute x6, starting transfers between devices, local(): lax.ppermute(mixed_part, 'head', [(i, (i + shift) % groups) for i in rang...  6.47 us
  transfers between devices with their start and end apart: 14, of which 3 were waited for; matrix products, arithmetic and copies ran while one was open for 37% of the time, Pallas kernels for 22%

profile of v14, /device:TPU:9, one launch (start us, length us, event | category | flops | bytes accessed | tf_op | source)
XLA Modules:
  0.0 164.7 jit_solution(17803993646209926322)
XLA Ops:
  0.0 2.5 %reshape.53 = bf16[1,512,768]{2,1,0:T(8,128)(2,1)S(1)} reshape(bf16[1,512,2,384]{3,2,1,0:T(2,128)(2,1)} %param.18) | data formatting | bytes 1572864 | tf_op jit(solution)/shard_map/reshape | solution.py:191
  2.5 2.2 %collective-permute-start.4 = (bf16[1,512,768]{2,1,0:T(8,128)(2,1)S(1)}, bf16[1,512,768]{2,1,0:T(8,128)(2,1)}, u32[]{:S(2)}, u32[]{:S(2)}) collective-permute-start(bf16[1,512,768]{2,1,0:T(8,128)(2,1)S(1)} %reshape.53), channel_id=1, source_target_pairs={{0,24},{4,28},{8,0},{12,4},{16,8},{20,12},{24,16},{28,20},{1,25},{... | collective-permute-start | bytes 2359304 | tf_op jit(solution)/shard_map/ppermute | solution.py:14
  5.3 1.8 %dynamic-slice_bitcast_fusion.6 = (bf16[1,384,768]{2,1,0:T(8,128)(2,1)S(1)}, bf16[1,384,768]{2,1,0:T(8,128)(2,1)S(1)}, bf16[1,384,768]{2,1,0:T(8,128)(2,1)S(1)}, bf16[1,384,768]{2,1,0:T(8,128)(2,1)S(1)}) fusion(bf16[384,6144]{1,0:T(8,128)(2,1)} %param.19, s32[]{:T(128)S(6)} %select_n.117, s32[]{:T(128)S(6)} %select_n.119, s32[]{:T(128)S(6)} %select_n.118, ...), kind=kLoop, calls=%fused_computation.80 | loop fusion | bytes 4718608 | tf_op jit(solution)/shard_map/stack | solution.py:155
  7.0 1.7 %pad_maximum_fusion.2 = bf16[4,384,768]{2,1,0:T(8,128)(2,1)} fusion(bf16[1,384,768]{2,1,0:T(8,128)(2,1)S(1)} %get-tuple-element.22, bf16[1,384,768]{2,1,0:T(8,128)(2,1)S(1)} %get-tuple-element.20, bf16[1,384,768]{2,1,0:T(8,128)(2,1)S(1)} %get-tuple-element.21, bf16[1,384,768]{2,1,0:T(8,128)(2,1)S(1)} %get-tuple-element.19), kind=kLoop, calls=%fused_computation.23 | loop fusion | flops 3538944 | bytes 4718592 | tf_op jit(solution)/shard_map/stack | solution.py:155
  8.8 4.8 %all-to-all-start = ((bf16[4,384,768]{2,1,0:T(8,128)(2,1)}), bf16[4,384,768]{2,1,0:T(8,128)(2,1)}, u32[]{:S(2)}, u32[]{:S(2)}) async-start(bf16[4,384,768]{2,1,0:T(8,128)(2,1)} %pad_maximum_fusion.2), calls=%async_computation | async-start | bytes 4718592 | tf_op jit(solution)/shard_map/all_to_all | solution.py:159
  13.5 4.1 %fusion = f32[512]{0:T(512)S(1)} fusion(bf16[512,6144]{1,0:T(8,128)(2,1)} %param.10), kind=kLoop, calls=%fused_computation.2 | loop fusion | flops 9436672 | bytes 6293504 | tf_op jit(solution)/shard_map/reduce_sum | solution.py:200
  19.2 12.8 %fusion.18 = f32[3,512,384]{2,1,0:T(8,128)S(1)} fusion(bf16[6144,3,384]{2,0,1:T(8,128)(2,1)} %param.15, bf16[512,6144]{1,0:T(8,128)(2,1)} %param.10, f32[6144]{0:T(1024)S(1)} %bitcast.103, f32[6144]{0:T(1024)S(1)} %bitcast.104, f32[512]{0:T(512)S(1)} %add_rsqrt_fusion.2), kind=kOutput, calls=%fused_computation.26 | convolution fusion | flops 7263485952 | bytes 22857728 | tf_op jit(solution)/shard_map/td,dkh->kth/dot_general | solution.py:203
  33.3 2.4 %copy.17 = f32[1,512,384]{1,2,0:T(8,128)} copy(f32[1,512,384]{2,1,0:T(8,128)} %get-tuple-element.26) | data formatting | bytes 1572864 | tf_op jit(solution)/shard_map/mul | solution.py:19
  37.8 2.4 %copy.18 = f32[512,384]{1,0:T(8,128)} copy(f32[512,384]{0,1:T(8,128)} %bitcast.98) | data formatting | bytes 1572864 | tf_op jit(solution)/shard_map/mul | solution.py:19
  42.8 2.1 %collective-permute-start.1 = (bf16[512,768]{1,0:T(8,128)(2,1)}, bf16[512,768]{1,0:T(8,128)(2,1)}, u32[]{:S(2)}, u32[]{:S(2)}) collective-permute-start(bf16[512,768]{1,0:T(8,128)(2,1)} %get-tuple-element.29), channel_id=1, source_target_pairs={{0,8},{4,12},{8,16},{12,20},{16,24},{20,28},{24,0},{28,4},{1,9},{5... | collective-permute-start | bytes 2359304 | tf_op jit(solution)/shard_map/ppermute | solution.py:14
  44.9 2.0 %collective-permute-start = (bf16[512,768]{1,0:T(8,128)(2,1)}, bf16[512,768]{1,0:T(8,128)(2,1)}, u32[]{:S(2)}, u32[]{:S(2)}) collective-permute-start(bf16[512,768]{1,0:T(8,128)(2,1)} %get-tuple-element.29), channel_id=1, source_target_pairs={{0,4},{4,8},{8,12},{12,16},{16,20},{20,24},{24,28},{28,0},{1,5},{5... | collective-permute-start | bytes 2359304 | tf_op jit(solution)/shard_map/ppermute | solution.py:14
  48.2 2.0 %pad_maximum_fusion.refs_4_.refs_5_ = bf16[4,512,768]{2,1,0:T(8,128)(2,1)S(1)} fusion(bf16[1,512,768]{2,1,0:T(8,128)(2,1)} %collective-permute-done.4, bf16[1,512,768]{2,1,0:T(8,128)(2,1)} %collective-permute-done.3, bf16[1,512,768]{2,1,0:T(8,128)(2,1)} %collective-permute-done.2, bf16[1,512,768]{2,1,0:T(8,128)(2,1)} %copy-done.9), kind=kLoop, calls=%fused_computation.11 | loop fusion | flops 4718592 | bytes 6291456 | tf_op jit(solution)/shard_map/concatenate | solution.py:193
  50.3 12.3 %all-to-all-done = bf16[4,384,768]{2,1,0:T(8,128)(2,1)} async-done(((bf16[4,384,768]{2,1,0:T(8,128)(2,1)}), bf16[4,384,768]{2,1,0:T(8,128)(2,1)}, u32[]{:S(2)}, u32[]{:S(2)}) %all-to-all-start) | async-done | bytes 2359328 | tf_op jit(solution)/shard_map/all_to_all | solution.py:159
  62.6 1.5 dynamic-slice_bitcast_fusion
  64.2 6.8 %collective-permute-done = bf16[512,768]{1,0:T(8,128)(2,1)} collective-permute-done((bf16[512,768]{1,0:T(8,128)(2,1)}, bf16[512,768]{1,0:T(8,128)(2,1)}, u32[]{:S(2)}, u32[]{:S(2)}) %collective-permute-start) | collective-permute-done | bytes 786464 | tf_op jit(solution)/shard_map/ppermute | solution.py:14
  72.4 1.5 pad_maximum_fusion.4
  76.9 1.7 %fusion.60 = (bf16[256,3,128]{0,2,1:T(8,128)(2,1)S(1)}, bf16[256,3,128]{0,2,1:T(8,128)(2,1)}) fusion(bf16[512,3,128]{0,2,1:T(8,128)(2,1)} %multiply_convert_fusion), kind=kLoop, calls=%fused_computation.123 | loop fusion | bytes 786432 | tf_op jit(solution)/shard_map/slice | solution.py:232
  78.6 1.7 %copy.21.refs_1_ = bf16[256,384]{1,0:T(8,128)(2,1)} copy(bf16[256,384]{0,1:T(8,128)(2,1)} %bitcast.100) | data formatting | bytes 393216 | tf_op jit(solution)/shard_map/slice | solution.py:232
  80.3 3.3 %pad_maximum_fusion.3.refs_2_.refs_3_ = bf16[3,512,768]{2,1,0:T(8,128)(2,1)} fusion(bf16[1,512,768]{2,1,0:T(8,128)(2,1)} %bitcast.24, bf16[1,512,768]{2,1,0:T(8,128)(2,1)} %bitcast.23, bf16[1,512,768]{2,1,0:T(8,128)(2,1)} %get-tuple-element.28), kind=kLoop, calls=%fused_computation.24 | loop fusion | flops 2359296 | bytes 4718592 | tf_op jit(solution)/shard_map/stack | solution.py:223
  83.6 17.8 %shard_map.101 = bf16[256,384]{1,0:T(8,128)(2,1)} custom-call(s32[6]{0:T(128)} %compare_select_fusion.6.refs_0_, bf16[256,384]{1,0:T(8,128)(2,1)} %copy.21.refs_1_, bf16[3,512,768]{2,1,0:T(8,128)(2,1)} %pad_maximum_fusion.3.refs_2_.refs_3_, bf16[3,512,768]{2,1,0:T(8,128)(2,1)} %pad_maximum_fusion.3.refs_2_.refs_3_, bf16[4,512,768]{2,1,0:T(8,128)(2,1)} %copy-done.2, ...), custom_call_target="tpu_custom_call" | custom-call | flops 905969664 | bytes 3538944 | tf_op jit(solution)/shard_map/pallas_call | solution.py:138
  101.4 2.1 %collective-permute-start.11 = (bf16[256,384]{1,0:T(8,128)(2,1)}, bf16[256,384]{1,0:T(8,128)(2,1)S(1)}, u32[]{:S(2)}, u32[]{:S(2)}) collective-permute-start(bf16[256,384]{1,0:T(8,128)(2,1)} %shard_map.101), channel_id=1, source_target_pairs={{0,2},{1,3},{2,0},{3,1},{4,6},{5,7},{6,4},{7,5},{8,10},{9,11},{10,... | collective-permute-start | bytes 589832 | tf_op jit(solution)/shard_map/ppermute | solution.py:246
  104.3 17.9 %shard_map.100 = bf16[256,384]{1,0:T(8,128)(2,1)} custom-call(s32[6]{0:T(128)} %compare_select_fusion.6.refs_0_, bf16[256,384]{1,0:T(8,128)(2,1)} %copy.20.refs_1_, bf16[3,512,768]{2,1,0:T(8,128)(2,1)} %pad_maximum_fusion.3.refs_2_.refs_3_, bf16[3,512,768]{2,1,0:T(8,128)(2,1)} %pad_maximum_fusion.3.refs_2_.refs_3_, bf16[4,512,768]{2,1,0:T(8,128)(2,1)} %copy-done.2, ...), custom_call_target="tpu_custom_call" | custom-call | flops 905969664 | bytes 3538944 | tf_op jit(solution)/shard_map/pallas_call | solution.py:138
  122.6 2.3 %collective-permute-start.6 = (bf16[256,384]{1,0:T(8,128)(2,1)}, bf16[256,384]{1,0:T(8,128)(2,1)S(1)}, u32[]{:S(2)}, u32[]{:S(2)}) collective-permute-start(bf16[256,384]{1,0:T(8,128)(2,1)} %shard_map.100), channel_id=1, source_target_pairs={{0,1},{1,2},{2,3},{3,0},{4,5},{5,6},{6,7},{7,4},{8,9},{9,10},{10,1... | collective-permute-start | bytes 589832 | tf_op jit(solution)/shard_map/ppermute | solution.py:246
  125.4 1.7 %collective-permute-start.10 = (bf16[256,384]{1,0:T(8,128)(2,1)S(1)}, bf16[256,384]{1,0:T(8,128)(2,1)S(1)}, u32[]{:S(2)}, u32[]{:S(2)}) collective-permute-start(bf16[256,384]{1,0:T(8,128)(2,1)S(1)} %copy-done.12), channel_id=1, source_target_pairs={{0,1},{1,2},{2,3},{3,0},{4,5},{5,6},{6,7},{7,4},{8,9},{9,10},{10,1... | collective-permute-start | bytes 589832 | tf_op jit(solution)/shard_map/ppermute | solution.py:246
  128.5 20.8 %collective-permute-done.12 = bf16[256,384]{1,0:T(8,128)(2,1)S(1)} collective-permute-done((bf16[256,384]{1,0:T(8,128)(2,1)S(1)}, bf16[256,384]{1,0:T(8,128)(2,1)S(1)}, u32[]{:S(2)}, u32[]{:S(2)}) %collective-permute-start.12) | collective-permute-done | bytes 196640 | tf_op jit(solution)/shard_map/ppermute | solution.py:246
  151.1 1.4 fusion.25
  152.9 2.2 %fusion.17 = f32[256,1536]{1,0:T(8,128)S(1)} fusion(bf16[256,384]{1,0:T(8,128)(2,1)S(1)} %copy-done.12, f32[256,768]{1,0:T(8,128)S(1)} %fusion.25, f32[256,768]{1,0:T(8,128)S(1)} %fusion.30, bf16[384,6144]{1,0:T(8,128)(2,1)} %param.19, s32[]{:T(128)S(6)} %select_n.108, bf16[512,6144]{1,0:T(8,128)(2,1)} %param.10, f32[1536]{0:T(1024)S(1)} %dynamic-slice_reduce_fusion, ...), kind=kOutput, calls=%fused_computation.22 | convolution fusion | flops 305528832 | bytes 5316096 | tf_op jit(solution)/shard_map/dot_general | solution.py:249
  155.5 1.4 fusion.32
  157.3 1.4 fusion.31
  159.1 1.5 fusion.35
  160.6 2.2 %fusion.13 = f32[256,1536]{1,0:T(8,128)S(1)} fusion(bf16[256,384]{1,0:T(8,128)(2,1)S(1)} %copy-done.11, f32[256,768]{1,0:T(8,128)S(1)} %fusion.35, f32[256,768]{1,0:T(8,128)S(1)} %fusion.40, bf16[384,6144]{1,0:T(8,128)(2,1)} %param.19, s32[]{:T(128)S(6)} %select_n.108, f32[1536]{0:T(1024)S(1)} %dynamic-slice_reduce_fusion, bf16[512,6144]{1,0:T(8,128)(2,1)} %param.10, ...), kind=kOutput, calls=%fused_computation.18 | convolution fusion | flops 305528832 | bytes 5316096 | tf_op jit(solution)/shard_map/dot_general | solution.py:249
  162.8 1.9 %pad_maximum_fusion.1 = f32[512,1536]{1,0:T(8,128)} fusion(f32[256,1536]{1,0:T(8,128)S(1)} %fusion.17, f32[256,1536]{1,0:T(8,128)S(1)} %fusion.13), kind=kLoop, calls=%fused_computation.12 | loop fusion | flops 786432 | bytes 6291456 | tf_op jit(solution)/shard_map/concatenate | solution.py:268
  (84 shorter events, 20.0 us)
Async XLA Ops:
  0.0 18.2 %copy-start = (bf16[8,3,6144]{2,0,1:T(8,128)(2,1)S(1)}, bf16[8,3,6144]{2,0,1:T(8,128)(2,1)}, u32[]{:S(2)}) copy-start(bf16[8,3,6144]{2,0,1:T(8,128)(2,1)} %param.11) | copy-start | bytes 884740
  2.5 4.5 %copy-start.9 = (bf16[1,512,768]{2,1,0:T(8,128)(2,1)}, bf16[1,512,768]{2,1,0:T(8,128)(2,1)S(1)}, u32[]{:S(2)}) copy-start(bf16[1,512,768]{2,1,0:T(8,128)(2,1)S(1)} %reshape.53) | copy-start | bytes 2359300
  2.5 45.7 %collective-permute-start.4 = (bf16[1,512,768]{2,1,0:T(8,128)(2,1)S(1)}, bf16[1,512,768]{2,1,0:T(8,128)(2,1)}, u32[]{:S(2)}, u32[]{:S(2)}) collective-permute-start(bf16[1,512,768]{2,1,0:T(8,128)(2,1)S(1)} %reshape.53), channel_id=1, source_target_pairs={{0,24},{4,28},{8,0},{12,4},{16,8},{20,12},{24,16},{28,20},{1,25},{... | collective-permute-start | bytes 2359304 | tf_op jit(solution)/shard_map/ppermute | solution.py:14
  4.7 43.5 %collective-permute-start.3 = (bf16[1,512,768]{2,1,0:T(8,128)(2,1)S(1)}, bf16[1,512,768]{2,1,0:T(8,128)(2,1)}, u32[]{:S(2)}, u32[]{:S(2)}) collective-permute-start(bf16[1,512,768]{2,1,0:T(8,128)(2,1)S(1)} %reshape.53), channel_id=1, source_target_pairs={{0,16},{4,20},{8,24},{12,28},{16,0},{20,4},{24,8},{28,12},{1,17},{... | collective-permute-start | bytes 2359304 | tf_op jit(solution)/shard_map/ppermute | solution.py:14
  5.0 43.3 %collective-permute-start.2 = (bf16[1,512,768]{2,1,0:T(8,128)(2,1)S(1)}, bf16[1,512,768]{2,1,0:T(8,128)(2,1)}, u32[]{:S(2)}, u32[]{:S(2)}) collective-permute-start(bf16[1,512,768]{2,1,0:T(8,128)(2,1)S(1)} %reshape.53), channel_id=1, source_target_pairs={{0,8},{4,12},{8,16},{12,20},{16,24},{20,28},{24,0},{28,4},{1,9},{5... | collective-permute-start | bytes 2359304 | tf_op jit(solution)/shard_map/ppermute | solution.py:14
  8.8 53.8 %all-to-all-start = ((bf16[4,384,768]{2,1,0:T(8,128)(2,1)}), bf16[4,384,768]{2,1,0:T(8,128)(2,1)}, u32[]{:S(2)}, u32[]{:S(2)}) async-start(bf16[4,384,768]{2,1,0:T(8,128)(2,1)} %pad_maximum_fusion.2), calls=%async_computation | async-start | bytes 4718592 | tf_op jit(solution)/shard_map/all_to_all | solution.py:159
  13.5 4.1 %copy-start.15 = (s32[8]{0:T(128)S(1)}, s32[8]{0:T(128)}, u32[]{:S(2)}) copy-start(s32[8]{0:T(128)} %param.12) | copy-start | bytes 100
  33.3 6.9 %copy-start.13 = (f32[384]{0:T(512)S(1)}, f32[384]{0:T(512)}, u32[]{:S(2)}) copy-start(f32[384]{0:T(512)} %param.17) | copy-start | bytes 4612
  41.5 5.4 %copy-start.10 = (f32[1,512,384]{2,1,0:T(8,128)S(1)}, f32[1,512,384]{2,1,0:T(8,128)}, u32[]{:S(2)}) copy-start(f32[1,512,384]{2,1,0:T(8,128)} %get-tuple-element.27) | copy-start | bytes 2359300
  41.5 5.9 %copy-start.14 = (f32[384]{0:T(512)S(1)}, f32[384]{0:T(512)}, u32[]{:S(2)}) copy-start(f32[384]{0:T(512)} %param.16) | copy-start | bytes 4612
  42.8 21.4 %collective-permute-start.1 = (bf16[512,768]{1,0:T(8,128)(2,1)}, bf16[512,768]{1,0:T(8,128)(2,1)}, u32[]{:S(2)}, u32[]{:S(2)}) collective-permute-start(bf16[512,768]{1,0:T(8,128)(2,1)} %get-tuple-element.29), channel_id=1, source_target_pairs={{0,8},{4,12},{8,16},{12,20},{16,24},{20,28},{24,0},{28,4},{1,9},{5... | collective-permute-start | bytes 2359304 | tf_op jit(solution)/shard_map/ppermute | solution.py:14
  44.9 26.1 %collective-permute-start = (bf16[512,768]{1,0:T(8,128)(2,1)}, bf16[512,768]{1,0:T(8,128)(2,1)}, u32[]{:S(2)}, u32[]{:S(2)}) collective-permute-start(bf16[512,768]{1,0:T(8,128)(2,1)} %get-tuple-element.29), channel_id=1, source_target_pairs={{0,4},{4,8},{8,12},{12,16},{16,20},{20,24},{24,28},{28,0},{1,5},{5... | collective-permute-start | bytes 2359304 | tf_op jit(solution)/shard_map/ppermute | solution.py:14
  50.3 23.6 %copy-start.2 = (bf16[4,512,768]{2,1,0:T(8,128)(2,1)}, bf16[4,512,768]{2,1,0:T(8,128)(2,1)S(1)}, u32[]{:S(2)}) copy-start(bf16[4,512,768]{2,1,0:T(8,128)(2,1)S(1)} %pad_maximum_fusion.refs_4_.refs_5_) | copy-start | bytes 9437188
  64.1 8.3 %copy-start.3 = (bf16[384,768]{1,0:T(8,128)(2,1)}, bf16[384,768]{1,0:T(8,128)(2,1)S(1)}, u32[]{:S(2)}) copy-start(bf16[384,768]{1,0:T(8,128)(2,1)S(1)} %get-tuple-element.18) | copy-start | bytes 1769476
  64.1 9.7 %copy-start.5 = (bf16[384,768]{1,0:T(8,128)(2,1)}, bf16[384,768]{1,0:T(8,128)(2,1)S(1)}, u32[]{:S(2)}) copy-start(bf16[384,768]{1,0:T(8,128)(2,1)S(1)} %get-tuple-element.17) | copy-start | bytes 1769476
  64.1 9.7 %copy-start.7 = (bf16[384,768]{1,0:T(8,128)(2,1)}, bf16[384,768]{1,0:T(8,128)(2,1)S(1)}, u32[]{:S(2)}) copy-start(bf16[384,768]{1,0:T(8,128)(2,1)S(1)} %get-tuple-element.16) | copy-start | bytes 1769476
  71.0 12.6 %collective-permute-start.5 = (bf16[4,512,768]{2,1,0:T(8,128)(2,1)S(1)}, bf16[4,512,768]{2,1,0:T(8,128)(2,1)}, u32[]{:S(2)}, u32[]{:S(2)}) collective-permute-start(bf16[4,512,768]{2,1,0:T(8,128)(2,1)S(1)} %pad_maximum_fusion.refs_4_.refs_5_), channel_id=1, source_target_pairs={{0,4},{4,0},{8,12},{12,8},{16,20},{20,16},{24,28},{28,24},{1,5},{5... | collective-permute-start | bytes 9437192 | tf_op jit(solution)/shard_map/ppermute | solution.py:213
  73.9 51.5 %collective-permute-start.9 = (bf16[3,384,768]{2,1,0:T(8,128)(2,1)}, bf16[3,384,768]{2,1,0:T(8,128)(2,1)}, u32[]{:S(2)}, u32[]{:S(2)}) collective-permute-start(bf16[3,384,768]{2,1,0:T(8,128)(2,1)} %pad_maximum_fusion.4), channel_id=1, source_target_pairs={{0,4},{4,0},{8,12},{12,8},{16,20},{20,16},{24,28},{28,24},{1,5},{5... | collective-permute-start | bytes 5308424 | tf_op jit(solution)/shard_map/ppermute | solution.py:236
  101.4 23.5 %collective-permute-start.11 = (bf16[256,384]{1,0:T(8,128)(2,1)}, bf16[256,384]{1,0:T(8,128)(2,1)S(1)}, u32[]{:S(2)}, u32[]{:S(2)}) collective-permute-start(bf16[256,384]{1,0:T(8,128)(2,1)} %shard_map.101), channel_id=1, source_target_pairs={{0,2},{1,3},{2,0},{3,1},{4,6},{5,7},{6,4},{7,5},{8,10},{9,11},{10,... | collective-permute-start | bytes 589832 | tf_op jit(solution)/shard_map/ppermute | solution.py:246
  104.3 20.6 %copy-start.12 = (bf16[256,384]{1,0:T(8,128)(2,1)S(1)}, bf16[256,384]{1,0:T(8,128)(2,1)}, u32[]{:S(2)}) copy-start(bf16[256,384]{1,0:T(8,128)(2,1)} %shard_map.101) | copy-start | bytes 589828
  104.3 20.7 %copy-start.6 = (bf16[384,768]{1,0:T(8,128)(2,1)S(1)}, bf16[384,768]{1,0:T(8,128)(2,1)}, u32[]{:S(2)}) copy-start(bf16[384,768]{1,0:T(8,128)(2,1)} %copy-done.5) | copy-start | bytes 1769476
  122.3 28.4 %copy-start.4 = (bf16[384,768]{1,0:T(8,128)(2,1)S(1)}, bf16[384,768]{1,0:T(8,128)(2,1)}, u32[]{:S(2)}) copy-start(bf16[384,768]{1,0:T(8,128)(2,1)} %copy-done.3) | copy-start | bytes 1769476
  122.3 34.6 %collective-permute-start.8 = (bf16[256,384]{1,0:T(8,128)(2,1)}, bf16[256,384]{1,0:T(8,128)(2,1)S(1)}, u32[]{:S(2)}, u32[]{:S(2)}) collective-permute-start(bf16[256,384]{1,0:T(8,128)(2,1)} %shard_map.100), channel_id=1, source_target_pairs={{0,3},{1,0},{2,1},{3,2},{4,7},{5,4},{6,5},{7,6},{8,11},{9,8},{10,9... | collective-permute-start | bytes 589832 | tf_op jit(solution)/shard_map/ppermute | solution.py:246
  122.6 32.5 %collective-permute-start.7 = (bf16[256,384]{1,0:T(8,128)(2,1)}, bf16[256,384]{1,0:T(8,128)(2,1)S(1)}, u32[]{:S(2)}, u32[]{:S(2)}) collective-permute-start(bf16[256,384]{1,0:T(8,128)(2,1)} %shard_map.100), channel_id=1, source_target_pairs={{0,2},{1,3},{2,0},{3,1},{4,6},{5,7},{6,4},{7,5},{8,10},{9,11},{10,... | collective-permute-start | bytes 589832 | tf_op jit(solution)/shard_map/ppermute | solution.py:246
  122.6 36.1 %collective-permute-start.6 = (bf16[256,384]{1,0:T(8,128)(2,1)}, bf16[256,384]{1,0:T(8,128)(2,1)S(1)}, u32[]{:S(2)}, u32[]{:S(2)}) collective-permute-start(bf16[256,384]{1,0:T(8,128)(2,1)} %shard_map.100), channel_id=1, source_target_pairs={{0,1},{1,2},{2,3},{3,0},{4,5},{5,6},{6,7},{7,4},{8,9},{9,10},{10,1... | collective-permute-start | bytes 589832 | tf_op jit(solution)/shard_map/ppermute | solution.py:246
  124.9 24.3 %collective-permute-start.12 = (bf16[256,384]{1,0:T(8,128)(2,1)S(1)}, bf16[256,384]{1,0:T(8,128)(2,1)S(1)}, u32[]{:S(2)}, u32[]{:S(2)}) collective-permute-start(bf16[256,384]{1,0:T(8,128)(2,1)S(1)} %copy-done.12), channel_id=1, source_target_pairs={{0,3},{1,0},{2,1},{3,2},{4,7},{5,4},{6,5},{7,6},{8,11},{9,8},{10,9... | collective-permute-start | bytes 589832 | tf_op jit(solution)/shard_map/ppermute | solution.py:246
  125.4 25.7 %collective-permute-start.10 = (bf16[256,384]{1,0:T(8,128)(2,1)S(1)}, bf16[256,384]{1,0:T(8,128)(2,1)S(1)}, u32[]{:S(2)}, u32[]{:S(2)}) collective-permute-start(bf16[256,384]{1,0:T(8,128)(2,1)S(1)} %copy-done.12), channel_id=1, source_target_pairs={{0,1},{1,2},{2,3},{3,0},{4,5},{5,6},{6,7},{7,4},{8,9},{9,10},{10,1... | collective-permute-start | bytes 589832 | tf_op jit(solution)/shard_map/ppermute | solution.py:246
  150.7 1.8 %copy-start.8 = (bf16[384,768]{1,0:T(8,128)(2,1)S(1)}, bf16[384,768]{1,0:T(8,128)(2,1)}, u32[]{:S(2)}) copy-start(bf16[384,768]{1,0:T(8,128)(2,1)} %copy-done.7) | copy-start | bytes 1769476
  159.1 1.5 copy-start.11
  160.6 4.1 %copy-start.1 = (bf16[8,3,6144]{2,0,1:T(8,128)(2,1)S(1)}, bf16[8,3,6144]{2,0,1:T(8,128)(2,1)}, u32[]{:S(2)}) copy-start(bf16[8,3,6144]{2,0,1:T(8,128)(2,1)} %param.11) | copy-start | bytes 884740

commit v15 on v11

--- a/solution.py
+++ b/solution.py
@@ -15,9 +15,13 @@
 
 
 def head_norm(values, gain, heads):
-    shaped = values.reshape(values.shape[0], heads, HD)
-    scaled = shaped * lax.rsqrt(jnp.mean(shaped * shaped, axis=-1, keepdims=True) + 1e-06)
-    return scaled * gain.reshape(heads, HD)
+    outs = []
+    for h in range(heads):
+        cols = slice(h * HD, (h + 1) * HD)
+        piece = values[:, cols]
+        scaled = piece * lax.rsqrt(jnp.mean(piece * piece, axis=-1, keepdims=True) + 1e-06)
+        outs.append(scaled * gain[cols][None, :])
+    return jnp.concatenate(outs, axis=1)
 
 
 def attend(state, queries, span_kv, visible_blocks):

time: 162 us -> 159 us (0.981)
  local copies, waits for them, and re-layouts: 19.7 us -> 12.1 us
  starting transfers between devices: 19.7 us -> 27.1 us
  other arithmetic: 21.2 us -> 18.5 us
    ppermute x1, starting transfers between devices: 0.01 us -> 7.93 us  [local(): lax.ppermute(same_core, 'slot', [(i, i ^ 1) for i in range(slots)])]
    ppermute x5, waiting for transfers between devices: 8.12 us -> 0.42 us  [from_behind(): lax.ppermute(shard, axis, [(i, (i + by) % length) for i in range(length)])]
    all_to_all x1, waiting for transfers between devices: 12.4 us -> 19.1 us  [fetch_out_weight(): exchanged = lax.all_to_all(blocks, 'head', 0, 0)]
    mul x3 -> x0, local copies, waits for them, and re-layouts: 5.6 us -> none  [the longest x2 3.28 us: head_norm(): shaped * lax.rsqrt(jnp.mean(shaped * shaped, axis=-1, keepdims=True) + 1e...]
    slice x3 -> x1, local copies, waits for them, and re-layouts: 4.3 us -> 0.79 us  [local(): queries[p * rows:(p + 1) * rows]]
    convert_element_type x2 -> x0, other arithmetic: 2.14 us -> none  [the longest x1 1.22 us: local(): keys = head_norm(qkv[1], k_gain, heads).astype(jnp.bfloat16)]
    unnamed x31 -> x35, local copies, waits for them, and re-layouts: 0.12 us -> 1.94 us
  transfers between devices with their start and end apart: 14 -> 14, of which waited for: 5 -> 5; matrix products, arithmetic and copies ran while one was open for 33% -> 26% of each run, Pallas kernels for 22% -> 23%
where the time goes in v15:
time: 159 us; the launch traced here: 158 us
  waiting for transfers between devices  39.2 us (25%)
  Pallas kernels  35.7 us (22%)
  starting transfers between devices  27.1 us (17%)
  matrix products  25 us (16%)
  other arithmetic  18.5 us (12%)
  local copies, waits for them, and re-layouts  12.1 us (8%)
    pallas_call x2, Pallas kernels, flash(): pl.pallas_call(kernel, grid_spec=grid_spec, out_shape=jax.ShapeDtypeStruc...  35.7 us
    ppermute x6, waiting for transfers between devices, local(): lax.ppermute(part, 'head', [(i, (i + shift) % groups) for i in range(grou...  19.6 us
    all_to_all x1, waiting for transfers between devices, fetch_out_weight(): exchanged = lax.all_to_all(blocks, 'head', 0, 0)  19.1 us
    dot_general x1, matrix products, local(): jnp.einsum('td,dkh->kth', hidden, w_qkv, preferred_element_type=jnp.float32)  12.8 us
    ppermute x1, starting transfers between devices, local(): lax.ppermute(same_core, 'slot', [(i, i ^ 1) for i in range(slots)])  7.93 us
    ppermute x6, starting transfers between devices, local(): lax.ppermute(part, 'head', [(i, (i + shift) % groups) for i in range(grou...  7.47 us
    ppermute x5, starting transfers between devices, from_behind(): lax.ppermute(shard, axis, [(i, (i + by) % length) for i in range(length)])  6.83 us
    dot_general x3, matrix products, local(): jnp.dot(group_o, sibling[shift - 1], preferred_element_type=jnp.float32)  4.93 us
  transfers between devices with their start and end apart: 14, of which 5 were waited for; matrix products, arithmetic and copies ran while one was open for 26% of the time, Pallas kernels for 23%

profile of v15, /device:TPU:9, one launch (start us, length us, event | category | flops | bytes accessed | tf_op | source)
XLA Modules:
  0.0 158.1 jit_solution(8848347581724777674)
XLA Ops:
  0.0 2.5 %reshape.80 = bf16[1,512,768]{2,1,0:T(8,128)(2,1)S(1)} reshape(bf16[1,512,2,384]{3,2,1,0:T(2,128)(2,1)} %param.18) | data formatting | bytes 1572864 | tf_op jit(solution)/shard_map/reshape | solution.py:195
  2.5 2.2 %collective-permute-start.4 = (bf16[1,512,768]{2,1,0:T(8,128)(2,1)S(1)}, bf16[1,512,768]{2,1,0:T(8,128)(2,1)S(1)}, u32[]{:S(2)}, u32[]{:S(2)}) collective-permute-start(bf16[1,512,768]{2,1,0:T(8,128)(2,1)S(1)} %reshape.80), channel_id=1, source_target_pairs={{0,24},{4,28},{8,0},{12,4},{16,8},{20,12},{24,16},{28,20},{1,25},{... | collective-permute-start | bytes 2359304 | tf_op jit(solution)/shard_map/ppermute | solution.py:14
  5.3 1.8 %dynamic-slice_bitcast_fusion.6 = (bf16[1,384,768]{2,1,0:T(8,128)(2,1)S(1)}, bf16[1,384,768]{2,1,0:T(8,128)(2,1)S(1)}, bf16[1,384,768]{2,1,0:T(8,128)(2,1)S(1)}, bf16[1,384,768]{2,1,0:T(8,128)(2,1)S(1)}) fusion(bf16[384,6144]{1,0:T(8,128)(2,1)} %param.19, s32[]{:T(128)S(6)} %select_n.112, s32[]{:T(128)S(6)} %select_n.114, s32[]{:T(128)S(6)} %select_n.113, ...), kind=kLoop, calls=%fused_computation.43 | loop fusion | bytes 4718608 | tf_op jit(solution)/shard_map/stack | solution.py:159
  7.0 1.7 %pad_maximum_fusion.1 = bf16[4,384,768]{2,1,0:T(8,128)(2,1)} fusion(bf16[1,384,768]{2,1,0:T(8,128)(2,1)S(1)} %get-tuple-element.28, bf16[1,384,768]{2,1,0:T(8,128)(2,1)S(1)} %get-tuple-element.26, bf16[1,384,768]{2,1,0:T(8,128)(2,1)S(1)} %get-tuple-element.27, bf16[1,384,768]{2,1,0:T(8,128)(2,1)S(1)} %get-tuple-element.25), kind=kLoop, calls=%fused_computation.17 | loop fusion | flops 3538944 | bytes 4718592 | tf_op jit(solution)/shard_map/stack | solution.py:159
  8.8 4.9 %all-to-all-start = ((bf16[4,384,768]{2,1,0:T(8,128)(2,1)}), bf16[4,384,768]{2,1,0:T(8,128)(2,1)}, u32[]{:S(2)}, u32[]{:S(2)}) async-start(bf16[4,384,768]{2,1,0:T(8,128)(2,1)} %pad_maximum_fusion.1), calls=%async_computation | async-start | bytes 4718592 | tf_op jit(solution)/shard_map/all_to_all | solution.py:163
  14.2 0.9 fusion.24
  15.2 4.1 %fusion = f32[512]{0:T(512)S(1)} fusion(bf16[512,6144]{1,0:T(8,128)(2,1)} %param.10), kind=kLoop, calls=%fused_computation.2 | loop fusion | flops 9436672 | bytes 6293504 | tf_op jit(solution)/shard_map/reduce_sum | solution.py:204
  19.3 12.8 %fusion.13 = f32[3,512,384]{2,1,0:T(8,128)S(1)} fusion(bf16[6144,3,384]{2,0,1:T(8,128)(2,1)} %param.15, bf16[512,6144]{1,0:T(8,128)(2,1)} %param.10, f32[6144]{0:T(1024)S(1)} %bitcast.75, f32[6144]{0:T(1024)S(1)} %bitcast.76, f32[512]{0:T(512)S(1)} %add_rsqrt_fusion.6), kind=kOutput, calls=%fused_computation.20 | convolution fusion | flops 7263485952 | bytes 22857728 | tf_op jit(solution)/shard_map/td,dkh->kth/dot_general | solution.py:207
  33.5 1.3 fusion.34
  34.8 4.1 %collective-permute-start = (bf16[512,768]{1,0:T(8,128)(2,1)}, bf16[512,768]{1,0:T(8,128)(2,1)}, u32[]{:S(2)}, u32[]{:S(2)}) collective-permute-start(bf16[512,768]{1,0:T(8,128)(2,1)} %get-tuple-element.35), channel_id=1, source_target_pairs={{0,4},{4,8},{8,12},{12,16},{16,20},{20,24},{24,28},{28,0},{1,5},{5... | collective-permute-start | bytes 2359304 | tf_op jit(solution)/shard_map/ppermute | solution.py:14
  39.7 0.9 copy-done.9
  40.6 0.9 copy-done.10
  41.5 2.0 %pad_maximum_fusion.refs_4_.refs_5_ = bf16[4,512,768]{2,1,0:T(8,128)(2,1)S(1)} fusion(bf16[1,512,768]{2,1,0:T(8,128)(2,1)} %copy-done.9, bf16[1,512,768]{2,1,0:T(8,128)(2,1)} %copy-done.10, bf16[1,512,768]{2,1,0:T(8,128)(2,1)} %collective-permute-done.2, bf16[1,512,768]{2,1,0:T(8,128)(2,1)} %copy-done.6), kind=kLoop, calls=%fused_computation.11 | loop fusion | flops 4718592 | bytes 6291456 | tf_op jit(solution)/shard_map/concatenate | solution.py:197
  43.6 19.1 %all-to-all-done = bf16[4,384,768]{2,1,0:T(8,128)(2,1)} async-done(((bf16[4,384,768]{2,1,0:T(8,128)(2,1)}), bf16[4,384,768]{2,1,0:T(8,128)(2,1)}, u32[]{:S(2)}, u32[]{:S(2)}) %all-to-all-start) | async-done | bytes 2359328 | tf_op jit(solution)/shard_map/all_to_all | solution.py:163
  62.7 2.7 %dynamic-slice_bitcast_fusion = (bf16[384,768]{1,0:T(8,128)(2,1)}, bf16[384,768]{1,0:T(8,128)(2,1)}, bf16[384,768]{1,0:T(8,128)(2,1)}) fusion(bf16[4,384,768]{2,1,0:T(8,128)(2,1)} %all-to-all-done, s32[]{:T(128)S(6)} %select_n.121, s32[]{:T(128)S(6)} %select_n.119, s32[]{:T(128)S(6)} %select_n.117), kind=kLoop, calls=%fused_computation.37 | loop fusion | bytes 3538956 | tf_op jit(solution)/shard_map/jit(dynamic_index_in_dim)/squeeze | solution.py:165
  65.8 7.9 %collective-permute-start.5 = (bf16[4,512,768]{2,1,0:T(8,128)(2,1)S(1)}, bf16[4,512,768]{2,1,0:T(8,128)(2,1)}, u32[]{:S(2)}, u32[]{:S(2)}) collective-permute-start(bf16[4,512,768]{2,1,0:T(8,128)(2,1)S(1)} %pad_maximum_fusion.refs_4_.refs_5_), channel_id=1, source_target_pairs={{0,4},{4,0},{8,12},{12,8},{16,20},{20,16},{24,28},{28,24},{1,5},{5... | collective-permute-start | bytes 9437192 | tf_op jit(solution)/shard_map/ppermute | solution.py:217
  74.7 1.4 compare_select_fusion.6.refs_0_
  76.8 2.8 %pad_maximum_fusion.3 = bf16[3,384,768]{2,1,0:T(8,128)(2,1)} fusion(bf16[1,384,768]{2,1,0:T(8,128)(2,1)} %bitcast.72, bf16[1,384,768]{2,1,0:T(8,128)(2,1)} %bitcast.71, bf16[1,384,768]{2,1,0:T(8,128)(2,1)} %bitcast.70), kind=kLoop, calls=%fused_computation.19 | loop fusion | flops 1769472 | bytes 3538944 | tf_op jit(solution)/shard_map/stack | solution.py:241
  79.6 3.1 %pad_maximum_fusion.2.refs_2_.refs_3_ = bf16[3,512,768]{2,1,0:T(8,128)(2,1)} fusion(bf16[1,512,768]{2,1,0:T(8,128)(2,1)} %bitcast.20, bf16[1,512,768]{2,1,0:T(8,128)(2,1)} %bitcast.19, bf16[1,512,768]{2,1,0:T(8,128)(2,1)S(1)} %copy-done.7), kind=kLoop, calls=%fused_computation.18 | loop fusion | flops 2359296 | bytes 4718592 | tf_op jit(solution)/shard_map/stack | solution.py:227
  83.6 17.8 %shard_map.100 = bf16[256,384]{1,0:T(8,128)(2,1)} custom-call(s32[6]{0:T(128)} %compare_select_fusion.6.refs_0_, bf16[256,384]{1,0:T(8,128)(2,1)} %get-tuple-element.43.refs_1_, bf16[3,512,768]{2,1,0:T(8,128)(2,1)} %pad_maximum_fusion.2.refs_2_.refs_3_, bf16[3,512,768]{2,1,0:T(8,128)(2,1)} %pad_maximum_fusion.2.refs_2_.refs_3_, ...), custom_call_target="tpu_custom_call" | custom-call | flops 905969664 | bytes 3538944 | tf_op jit(solution)/shard_map/pallas_call | solution.py:142
  101.4 2.3 %collective-permute-start.8 = (bf16[256,384]{1,0:T(8,128)(2,1)}, bf16[256,384]{1,0:T(8,128)(2,1)S(1)}, u32[]{:S(2)}, u32[]{:S(2)}) collective-permute-start(bf16[256,384]{1,0:T(8,128)(2,1)} %shard_map.100), channel_id=1, source_target_pairs={{0,2},{1,3},{2,0},{3,1},{4,6},{5,7},{6,4},{7,5},{8,10},{9,11},{10,... | collective-permute-start | bytes 589832 | tf_op jit(solution)/shard_map/ppermute | solution.py:246
  103.8 17.9 %shard_map.101 = bf16[256,384]{1,0:T(8,128)(2,1)} custom-call(s32[6]{0:T(128)} %compare_select_fusion.6.refs_0_, bf16[256,384]{1,0:T(8,128)(2,1)} %get-tuple-element.42.refs_1_, bf16[3,512,768]{2,1,0:T(8,128)(2,1)} %pad_maximum_fusion.2.refs_2_.refs_3_, bf16[3,512,768]{2,1,0:T(8,128)(2,1)} %pad_maximum_fusion.2.refs_2_.refs_3_, ...), custom_call_target="tpu_custom_call" | custom-call | flops 905969664 | bytes 3538944 | tf_op jit(solution)/shard_map/pallas_call | solution.py:142
  121.7 2.3 %collective-permute-start.9 = (bf16[256,384]{1,0:T(8,128)(2,1)}, bf16[256,384]{1,0:T(8,128)(2,1)S(1)}, u32[]{:S(2)}, u32[]{:S(2)}) collective-permute-start(bf16[256,384]{1,0:T(8,128)(2,1)} %shard_map.101), channel_id=1, source_target_pairs={{0,2},{1,3},{2,0},{3,1},{4,6},{5,7},{6,4},{7,5},{8,10},{9,11},{10,... | collective-permute-start | bytes 589832 | tf_op jit(solution)/shard_map/ppermute | solution.py:246
  124.4 1.1 collective-permute-start.10
  125.5 1.3 collective-permute-start.11
  126.9 15.5 %collective-permute-done.10 = bf16[256,384]{1,0:T(8,128)(2,1)S(1)} collective-permute-done((bf16[256,384]{1,0:T(8,128)(2,1)S(1)}, bf16[256,384]{1,0:T(8,128)(2,1)S(1)}, u32[]{:S(2)}, u32[]{:S(2)}) %collective-permute-start.10) | collective-permute-done | bytes 196640 | tf_op jit(solution)/shard_map/ppermute | solution.py:246
  142.5 2.3 %collective-permute-done.7 = bf16[256,384]{1,0:T(8,128)(2,1)S(1)} collective-permute-done((bf16[256,384]{1,0:T(8,128)(2,1)}, bf16[256,384]{1,0:T(8,128)(2,1)S(1)}, u32[]{:S(2)}, u32[]{:S(2)}) %collective-permute-start.7) | collective-permute-done | bytes 196640 | tf_op jit(solution)/shard_map/ppermute | solution.py:246
  144.9 1.8 %collective-permute-done.11 = bf16[256,384]{1,0:T(8,128)(2,1)S(1)} collective-permute-done((bf16[256,384]{1,0:T(8,128)(2,1)}, bf16[256,384]{1,0:T(8,128)(2,1)S(1)}, u32[]{:S(2)}, u32[]{:S(2)}) %collective-permute-start.11) | collective-permute-done | bytes 196640 | tf_op jit(solution)/shard_map/ppermute | solution.py:246
  148.4 1.6 %convolution_convert_fusion.2 = bf16[512,768]{1,0:T(8,128)(2,1)S(1)} fusion(bf16[512,384]{1,0:T(8,128)(2,1)S(1)} %constant_dynamic-update-slice_fusion.2, bf16[3,384,768]{2,1,0:T(8,128)(2,1)} %collective-permute-done.12), kind=kOutput, calls=%fused_computation.24 | convolution fusion | flops 302383104 | bytes 1769472 | tf_op jit(solution)/shard_map/dot_general | solution.py:262
  150.1 1.6 %convolution_convert_fusion.3 = bf16[512,768]{1,0:T(8,128)(2,1)S(1)} fusion(bf16[512,384]{1,0:T(8,128)(2,1)S(1)} %constant_dynamic-update-slice_fusion, bf16[3,384,768]{2,1,0:T(8,128)(2,1)} %collective-permute-done.12), kind=kOutput, calls=%fused_computation.25 | convolution fusion | flops 302383104 | bytes 1769472 | tf_op jit(solution)/shard_map/dot_general | solution.py:262
  151.7 1.7 %convert_add_fusion = f32[512,768]{1,0:T(8,128)S(1)} fusion(bf16[512,768]{1,0:T(8,128)(2,1)S(1)} %convolution_convert_fusion.2, bf16[512,768]{1,0:T(8,128)(2,1)S(1)} %convolution_convert_fusion.3, bf16[512,384]{1,0:T(8,128)(2,1)S(1)} %constant_dynamic-update-slice_fusion.4, bf16[3,384,768]{2,1,0:T(8,128)(2,1)} %collective-permute-done.12), kind=kOutput, calls=%fused_computation.21 | convolution fusion | flops 304349184 | bytes 4128768 | tf_op jit(solution)/shard_map/dot_general | solution.py:262
  153.4 4.7 %fusion.12 = f32[512,1536]{1,0:T(8,128)} fusion(f32[512,768]{1,0:T(8,128)S(1)} %convert_add_fusion, f32[512,768]{1,0:T(8,128)S(1)} %convert_add_fusion.1, f32[1536]{0:T(1024)S(1)} %dynamic-slice_reduce_fusion, bf16[512,6144]{1,0:T(8,128)(2,1)} %param.10, s32[]{:T(128)S(6)} %select_n.103, pred[]{:T(512)S(6)} %eq.29, bf16[384,6144]{1,0:T(8,128)(2,1)} %param.19, ...), kind=kOutput, calls=%fused_computation.15 | convolution fusion | flops 611844096 | bytes 9444864 | tf_op jit(solution)/shard_map/dot_general | solution.py:254
  (82 shorter events, 8.6 us)
Async XLA Ops:
  0.0 14.2 %copy-start = (bf16[8,3,6144]{2,0,1:T(8,128)(2,1)S(1)}, bf16[8,3,6144]{2,0,1:T(8,128)(2,1)}, u32[]{:S(2)}) copy-start(bf16[8,3,6144]{2,0,1:T(8,128)(2,1)} %param.11) | copy-start | bytes 884740
  2.5 4.5 %copy-start.6 = (bf16[1,512,768]{2,1,0:T(8,128)(2,1)}, bf16[1,512,768]{2,1,0:T(8,128)(2,1)S(1)}, u32[]{:S(2)}) copy-start(bf16[1,512,768]{2,1,0:T(8,128)(2,1)S(1)} %reshape.80) | copy-start | bytes 2359300
  2.5 37.2 %collective-permute-start.4 = (bf16[1,512,768]{2,1,0:T(8,128)(2,1)S(1)}, bf16[1,512,768]{2,1,0:T(8,128)(2,1)S(1)}, u32[]{:S(2)}, u32[]{:S(2)}) collective-permute-start(bf16[1,512,768]{2,1,0:T(8,128)(2,1)S(1)} %reshape.80), channel_id=1, source_target_pairs={{0,24},{4,28},{8,0},{12,4},{16,8},{20,12},{24,16},{28,20},{1,25},{... | collective-permute-start | bytes 2359304 | tf_op jit(solution)/shard_map/ppermute | solution.py:14
  4.7 35.0 %collective-permute-start.3 = (bf16[1,512,768]{2,1,0:T(8,128)(2,1)S(1)}, bf16[1,512,768]{2,1,0:T(8,128)(2,1)S(1)}, u32[]{:S(2)}, u32[]{:S(2)}) collective-permute-start(bf16[1,512,768]{2,1,0:T(8,128)(2,1)S(1)} %reshape.80), channel_id=1, source_target_pairs={{0,16},{4,20},{8,24},{12,28},{16,0},{20,4},{24,8},{28,12},{1,17},{... | collective-permute-start | bytes 2359304 | tf_op jit(solution)/shard_map/ppermute | solution.py:14
  5.0 36.6 %collective-permute-start.2 = (bf16[1,512,768]{2,1,0:T(8,128)(2,1)S(1)}, bf16[1,512,768]{2,1,0:T(8,128)(2,1)}, u32[]{:S(2)}, u32[]{:S(2)}) collective-permute-start(bf16[1,512,768]{2,1,0:T(8,128)(2,1)S(1)} %reshape.80), channel_id=1, source_target_pairs={{0,8},{4,12},{8,16},{12,20},{16,24},{20,28},{24,0},{28,4},{1,9},{5... | collective-permute-start | bytes 2359304 | tf_op jit(solution)/shard_map/ppermute | solution.py:14
  8.8 4.9 %copy-start.15 = (s32[8]{0:T(128)S(1)}, s32[8]{0:T(128)}, u32[]{:S(2)}) copy-start(s32[8]{0:T(128)} %param.12) | copy-start | bytes 100
  8.8 53.9 %all-to-all-start = ((bf16[4,384,768]{2,1,0:T(8,128)(2,1)}), bf16[4,384,768]{2,1,0:T(8,128)(2,1)}, u32[]{:S(2)}, u32[]{:S(2)}) async-start(bf16[4,384,768]{2,1,0:T(8,128)(2,1)} %pad_maximum_fusion.1), calls=%async_computation | async-start | bytes 4718592 | tf_op jit(solution)/shard_map/all_to_all | solution.py:163
  32.1 0.7 copy-start.13
  32.1 0.9 copy-start.14
  34.8 30.6 %collective-permute-start = (bf16[512,768]{1,0:T(8,128)(2,1)}, bf16[512,768]{1,0:T(8,128)(2,1)}, u32[]{:S(2)}, u32[]{:S(2)}) collective-permute-start(bf16[512,768]{1,0:T(8,128)(2,1)} %get-tuple-element.35), channel_id=1, source_target_pairs={{0,4},{4,8},{8,12},{12,16},{16,20},{20,24},{24,28},{28,0},{1,5},{5... | collective-permute-start | bytes 2359304 | tf_op jit(solution)/shard_map/ppermute | solution.py:14
  38.9 26.9 %collective-permute-start.1 = (bf16[512,768]{1,0:T(8,128)(2,1)}, bf16[512,768]{1,0:T(8,128)(2,1)}, u32[]{:S(2)}, u32[]{:S(2)}) collective-permute-start(bf16[512,768]{1,0:T(8,128)(2,1)} %get-tuple-element.35), channel_id=1, source_target_pairs={{0,8},{4,12},{8,16},{12,20},{16,24},{20,28},{24,0},{28,4},{1,9},{5... | collective-permute-start | bytes 2359304 | tf_op jit(solution)/shard_map/ppermute | solution.py:14
  39.7 0.9 copy-start.9
  40.6 0.9 copy-start.10
  43.6 36.0 %copy-start.2 = (bf16[4,512,768]{2,1,0:T(8,128)(2,1)}, bf16[4,512,768]{2,1,0:T(8,128)(2,1)S(1)}, u32[]{:S(2)}) copy-start(bf16[4,512,768]{2,1,0:T(8,128)(2,1)S(1)} %pad_maximum_fusion.refs_4_.refs_5_) | copy-start | bytes 9437188
  65.8 17.8 %collective-permute-start.5 = (bf16[4,512,768]{2,1,0:T(8,128)(2,1)S(1)}, bf16[4,512,768]{2,1,0:T(8,128)(2,1)}, u32[]{:S(2)}, u32[]{:S(2)}) collective-permute-start(bf16[4,512,768]{2,1,0:T(8,128)(2,1)S(1)} %pad_maximum_fusion.refs_4_.refs_5_), channel_id=1, source_target_pairs={{0,4},{4,0},{8,12},{12,8},{16,20},{20,16},{24,28},{28,24},{1,5},{5... | collective-permute-start | bytes 9437192 | tf_op jit(solution)/shard_map/ppermute | solution.py:217
  74.7 4.9 %copy-start.7 = (bf16[1,512,768]{2,1,0:T(8,128)(2,1)S(1)}, bf16[1,512,768]{2,1,0:T(8,128)(2,1)}, u32[]{:S(2)}) copy-start(bf16[1,512,768]{2,1,0:T(8,128)(2,1)} %get-tuple-element.34) | copy-start | bytes 2359300
  79.6 68.8 %collective-permute-start.12 = (bf16[3,384,768]{2,1,0:T(8,128)(2,1)}, bf16[3,384,768]{2,1,0:T(8,128)(2,1)}, u32[]{:S(2)}, u32[]{:S(2)}) collective-permute-start(bf16[3,384,768]{2,1,0:T(8,128)(2,1)} %pad_maximum_fusion.3), channel_id=1, source_target_pairs={{0,4},{4,0},{8,12},{12,8},{16,20},{20,16},{24,28},{28,24},{1,5},{5... | collective-permute-start | bytes 5308424 | tf_op jit(solution)/shard_map/ppermute | solution.py:240
  79.6 3.1 %copy-start.8 = (bf16[512,384]{1,0:T(8,128)(2,1)S(1)}, bf16[512,384]{1,0:T(8,128)(2,1)}, u32[]{:S(2)}) copy-start(bf16[512,384]{1,0:T(8,128)(2,1)} %pad_maximum_fusion.5) | copy-start | bytes 1179652
  101.4 23.0 %collective-permute-start.8 = (bf16[256,384]{1,0:T(8,128)(2,1)}, bf16[256,384]{1,0:T(8,128)(2,1)S(1)}, u32[]{:S(2)}, u32[]{:S(2)}) collective-permute-start(bf16[256,384]{1,0:T(8,128)(2,1)} %shard_map.100), channel_id=1, source_target_pairs={{0,2},{1,3},{2,0},{3,1},{4,6},{5,7},{6,4},{7,5},{8,10},{9,11},{10,... | collective-permute-start | bytes 589832 | tf_op jit(solution)/shard_map/ppermute | solution.py:246
  103.7 21.8 %collective-permute-start.6 = (bf16[256,384]{1,0:T(8,128)(2,1)}, bf16[256,384]{1,0:T(8,128)(2,1)S(1)}, u32[]{:S(2)}, u32[]{:S(2)}) collective-permute-start(bf16[256,384]{1,0:T(8,128)(2,1)} %shard_map.100), channel_id=1, source_target_pairs={{0,1},{1,2},{2,3},{3,0},{4,5},{5,6},{6,7},{7,4},{8,9},{9,10},{10,1... | collective-permute-start | bytes 589832 | tf_op jit(solution)/shard_map/ppermute | solution.py:246
  103.8 20.6 %copy-start.11 = (bf16[256,384]{1,0:T(8,128)(2,1)S(1)}, bf16[256,384]{1,0:T(8,128)(2,1)}, u32[]{:S(2)}) copy-start(bf16[256,384]{1,0:T(8,128)(2,1)} %shard_map.100) | copy-start | bytes 589828
  121.7 24.9 %copy-start.4 = (bf16[384,768]{1,0:T(8,128)(2,1)S(1)}, bf16[384,768]{1,0:T(8,128)(2,1)}, u32[]{:S(2)}) copy-start(bf16[384,768]{1,0:T(8,128)(2,1)} %get-tuple-element.17) | copy-start | bytes 1769476
  121.7 25.5 %copy-start.3 = (bf16[384,768]{1,0:T(8,128)(2,1)S(1)}, bf16[384,768]{1,0:T(8,128)(2,1)}, u32[]{:S(2)}) copy-start(bf16[384,768]{1,0:T(8,128)(2,1)} %get-tuple-element.16) | copy-start | bytes 1769476
  121.7 20.7 %collective-permute-start.9 = (bf16[256,384]{1,0:T(8,128)(2,1)}, bf16[256,384]{1,0:T(8,128)(2,1)S(1)}, u32[]{:S(2)}, u32[]{:S(2)}) collective-permute-start(bf16[256,384]{1,0:T(8,128)(2,1)} %shard_map.101), channel_id=1, source_target_pairs={{0,2},{1,3},{2,0},{3,1},{4,6},{5,7},{6,4},{7,5},{8,10},{9,11},{10,... | collective-permute-start | bytes 589832 | tf_op jit(solution)/shard_map/ppermute | solution.py:246
  124.0 20.8 %collective-permute-start.7 = (bf16[256,384]{1,0:T(8,128)(2,1)}, bf16[256,384]{1,0:T(8,128)(2,1)S(1)}, u32[]{:S(2)}, u32[]{:S(2)}) collective-permute-start(bf16[256,384]{1,0:T(8,128)(2,1)} %shard_map.101), channel_id=1, source_target_pairs={{0,1},{1,2},{2,3},{3,0},{4,5},{5,6},{6,7},{7,4},{8,9},{9,10},{10,1... | collective-permute-start | bytes 589832 | tf_op jit(solution)/shard_map/ppermute | solution.py:246
  124.4 18.0 %collective-permute-start.10 = (bf16[256,384]{1,0:T(8,128)(2,1)S(1)}, bf16[256,384]{1,0:T(8,128)(2,1)S(1)}, u32[]{:S(2)}, u32[]{:S(2)}) collective-permute-start(bf16[256,384]{1,0:T(8,128)(2,1)S(1)} %copy-done.11), channel_id=1, source_target_pairs={{0,3},{1,0},{2,1},{3,2},{4,7},{5,4},{6,5},{7,6},{8,11},{9,8},{10,9... | collective-permute-start | bytes 589832 | tf_op jit(solution)/shard_map/ppermute | solution.py:246
  125.5 21.1 %collective-permute-start.11 = (bf16[256,384]{1,0:T(8,128)(2,1)}, bf16[256,384]{1,0:T(8,128)(2,1)S(1)}, u32[]{:S(2)}, u32[]{:S(2)}) collective-permute-start(bf16[256,384]{1,0:T(8,128)(2,1)} %shard_map.101), channel_id=1, source_target_pairs={{0,3},{1,0},{2,1},{3,2},{4,7},{5,4},{6,5},{7,6},{8,11},{9,8},{10,9... | collective-permute-start | bytes 589832 | tf_op jit(solution)/shard_map/ppermute | solution.py:246
  142.4 5.4 %copy-start.5 = (bf16[384,768]{1,0:T(8,128)(2,1)S(1)}, bf16[384,768]{1,0:T(8,128)(2,1)}, u32[]{:S(2)}) copy-start(bf16[384,768]{1,0:T(8,128)(2,1)} %get-tuple-element.18) | copy-start | bytes 1769476
  151.7 1.7 %copy-start.12 = (bf16[256,384]{1,0:T(8,128)(2,1)S(1)}, bf16[256,384]{1,0:T(8,128)(2,1)}, u32[]{:S(2)}) copy-start(bf16[256,384]{1,0:T(8,128)(2,1)} %shard_map.101) | copy-start | bytes 589828
  153.4 4.7 %copy-start.1 = (bf16[8,3,6144]{2,0,1:T(8,128)(2,1)S(1)}, bf16[8,3,6144]{2,0,1:T(8,128)(2,1)}, u32[]{:S(2)}) copy-start(bf16[8,3,6144]{2,0,1:T(8,128)(2,1)} %param.11) | copy-start | bytes 884740

commit v16 on v15

--- a/solution.py
+++ b/solution.py
@@ -47,49 +47,57 @@
     return (new_high, totals, accum)
 
 
-def flash_kernel(chosen, q_ref, lk_ref, lv_ref, ak_ref, av_ref, bk_ref, bv_ref, bias_ref, o_ref, m_sc, l_sc, acc_sc, *, heads, n_local, half):
-    step = pl.program_id(0)
+def online_update(q_ref, k_ref, v_ref, bias_ref, m_sc, l_sc, acc_sc, heads):
     span = q_ref.shape[0]
     blocks = bias_ref.shape[0]
+    bias = bias_ref[...][:, None, :]
+    for h in range(heads):
+        cols = slice(h * HD, (h + 1) * HD)
+        q = q_ref[:, cols]
+        k = k_ref[:, cols]
+        s = lax.dot_general(q, k, (((1,), (1,)), ((), ())), preferred_element_type=jnp.float32)
+        s = (s * (1.0 / HD**0.5)).reshape(blocks, span // blocks, s.shape[1]) + bias
+        s = s.reshape(span, -1)
+        m_prev = m_sc[h]
+        m_new = jnp.maximum(m_prev, jnp.max(s, axis=1, keepdims=True))
+        factor = jnp.exp(m_prev - m_new)
+        p = jnp.exp(s - m_new)
+        l_sc[h] = l_sc[h] * factor + jnp.sum(p, axis=1, keepdims=True)
+        acc_sc[h] = acc_sc[h] * factor + jnp.dot(
+            p.astype(jnp.bfloat16), v_ref[:, cols], preferred_element_type=jnp.float32
+        )
+        m_sc[h] = m_new
+
+
+def local_kernel(q_ref, k_ref, v_ref, bias_ref, m_ref, l_ref, acc_ref, *, heads):
+    @pl.when(pl.program_id(0) == 0)
+    def _():
+        m_ref[...] = jnp.full(m_ref.shape, -1e30, jnp.float32)
+        l_ref[...] = jnp.zeros(l_ref.shape, jnp.float32)
+        acc_ref[...] = jnp.zeros(acc_ref.shape, jnp.float32)
+
+    online_update(q_ref, k_ref, v_ref, bias_ref, m_ref, l_ref, acc_ref, heads)
+
+
+def pool_kernel(chosen, q_ref, ak_ref, av_ref, bk_ref, bv_ref, bias_ref, m_in, l_in, acc_in,
+                o_ref, m_sc, l_sc, acc_sc, *, heads, half):
+    step = pl.program_id(0)
 
     @pl.when(step == 0)
     def _():
-        m_sc[...] = jnp.full(m_sc.shape, -1e30, jnp.float32)
-        l_sc[...] = jnp.zeros(l_sc.shape, jnp.float32)
-        acc_sc[...] = jnp.zeros(acc_sc.shape, jnp.float32)
-
-    def body(k_ref, v_ref):
-        bias = bias_ref[...][:, None, :]
-        for h in range(heads):
-            cols = slice(h * HD, (h + 1) * HD)
-            q = q_ref[:, cols]
-            k = k_ref[:, cols]
-            s = lax.dot_general(q, k, (((1,), (1,)), ((), ())), preferred_element_type=jnp.float32)
-            s = (s * (1.0 / HD**0.5)).reshape(blocks, span // blocks, s.shape[1]) + bias
-            s = s.reshape(span, -1)
-            m_prev = m_sc[h]
-            m_new = jnp.maximum(m_prev, jnp.max(s, axis=1, keepdims=True))
-            factor = jnp.exp(m_prev - m_new)
-            p = jnp.exp(s - m_new)
-            l_sc[h] = l_sc[h] * factor + jnp.sum(p, axis=1, keepdims=True)
-            acc_sc[h] = acc_sc[h] * factor + jnp.dot(
-                p.astype(jnp.bfloat16), v_ref[:, cols], preferred_element_type=jnp.float32
-            )
-            m_sc[h] = m_new
-
-    @pl.when(step < n_local)
-    def _():
-        body(lk_ref, lv_ref)
-
-    pos = chosen[jnp.maximum(step - n_local, 0)]
-
-    @pl.when((step >= n_local) & (pos < half))
-    def _():
-        body(ak_ref, av_ref)
-
-    @pl.when((step >= n_local) & (pos >= half))
-    def _():
-        body(bk_ref, bv_ref)
+        m_sc[...] = m_in[...]
+        l_sc[...] = l_in[...]
+        acc_sc[...] = acc_in[...]
+
+    pos = chosen[step]
+
+    @pl.when(pos < half)
+    def _():
+        online_update(q_ref, ak_ref, av_ref, bias_ref, m_sc, l_sc, acc_sc, heads)
+
+    @pl.when(pos >= half)
+    def _():
+        online_update(q_ref, bk_ref, bv_ref, bias_ref, m_sc, l_sc, acc_sc, heads)
 
     @pl.when(step == pl.num_programs(0) - 1)
     def _():
@@ -98,38 +106,65 @@
             o_ref[:, cols] = (acc_sc[h] / l_sc[h]).astype(o_ref.dtype)
 
 
-def flash(queries, local_stack, same_core, other_core, bias, chosen, heads):
+def flash_local(queries, local_stack, bias, heads):
     span, width = queries.shape
-    n_local = local_stack.shape[0]
-    half = same_core.shape[0]
-    steps = n_local + chosen.shape[0]
+    steps, keys_len = local_stack.shape[:2]
     blocks = bias.shape[1]
-
-    def local_map(kv):
-        return lambda j, c: (jnp.minimum(j, n_local - 1), 0, kv)
+    kv_block = (None, keys_len, width)
+    state = pl.BlockSpec((heads, span, 1), lambda j: (0, 0, 0))
+    kernel = lambda *refs: local_kernel(*refs, heads=heads)
+    return pl.pallas_call(
+        kernel,
+        grid=(steps,),
+        in_specs=[
+            pl.BlockSpec((span, width), lambda j: (0, 0)),
+            pl.BlockSpec(kv_block, lambda j: (j, 0, 0)),
+            pl.BlockSpec(kv_block, lambda j: (j, 0, 1)),
+            pl.BlockSpec((None, blocks, keys_len), lambda j: (j, 0, 0)),
+        ],
+        out_specs=[state, state, pl.BlockSpec((heads, span, HD), lambda j: (0, 0, 0))],
+        out_shape=[
+            jax.ShapeDtypeStruct((heads, span, 1), jnp.float32),
+            jax.ShapeDtypeStruct((heads, span, 1), jnp.float32),
+            jax.ShapeDtypeStruct((heads, span, HD), jnp.float32),
+        ],
+        compiler_params=pltpu.CompilerParams(dimension_semantics=("arbitrary",)),
+        cost_estimate=pl.CostEstimate(
+            flops=4 * steps * heads * span * keys_len * HD,
+            transcendentals=steps * heads * span * keys_len,
+            bytes_accessed=2 * steps * keys_len * width * 2,
+        ),
+    )(queries, local_stack, local_stack, bias)
+
+
+def flash_pool(queries, same_core, other_core, bias, chosen, state, heads):
+    span, width = queries.shape
+    half, keys_len = same_core.shape[:2]
+    steps = chosen.shape[0]
+    blocks = bias.shape[1]
+    kv_block = (None, keys_len, width)
 
     def pool_map(kv, upper):
         def index(j, c):
-            pos = c[jnp.maximum(j - n_local, 0)]
-            hit = (j >= n_local) & ((pos >= half) == upper)
-            return (jnp.where(hit, pos - upper * half, 0), 0, kv)
+            pos = c[j]
+            return (jnp.where((pos >= half) == upper, pos - upper * half, 0), 0, kv)
 
         return index
 
-    keys_len = local_stack.shape[1]
-    kv_block = (None, keys_len, width)
+    state_spec = pl.BlockSpec((heads, span, 1), lambda j, c: (0, 0, 0))
     grid_spec = pltpu.PrefetchScalarGridSpec(
         num_scalar_prefetch=1,
         grid=(steps,),
         in_specs=[
             pl.BlockSpec((span, width), lambda j, c: (0, 0)),
-            pl.BlockSpec(kv_block, local_map(0)),
-            pl.BlockSpec(kv_block, local_map(1)),
             pl.BlockSpec(kv_block, pool_map(0, False)),
             pl.BlockSpec(kv_block, pool_map(1, False)),
             pl.BlockSpec(kv_block, pool_map(0, True)),
             pl.BlockSpec(kv_block, pool_map(1, True)),
             pl.BlockSpec((None, blocks, keys_len), lambda j, c: (j, 0, 0)),
+            state_spec,
+            state_spec,
+            pl.BlockSpec((heads, span, HD), lambda j, c: (0, 0, 0)),
         ],
         out_specs=pl.BlockSpec((span, width), lambda j, c: (0, 0)),
         scratch_shapes=[
@@ -138,18 +173,18 @@
             pltpu.VMEM((heads, span, HD), jnp.float32),
         ],
     )
-    kernel = lambda *refs: flash_kernel(*refs, heads=heads, n_local=n_local, half=half)
+    kernel = lambda *refs: pool_kernel(*refs, heads=heads, half=half)
     return pl.pallas_call(
         kernel,
         grid_spec=grid_spec,
         out_shape=jax.ShapeDtypeStruct((span, width), jnp.bfloat16),
         compiler_params=pltpu.CompilerParams(dimension_semantics=("arbitrary",)),
         cost_estimate=pl.CostEstimate(
-            flops=4 * steps * heads * span * span * HD,
-            transcendentals=steps * heads * span * span,
-            bytes_accessed=2 * steps * span * width * 2,
+            flops=4 * steps * heads * span * keys_len * HD,
+            transcendentals=steps * heads * span * keys_len,
+            bytes_accessed=2 * steps * keys_len * width * 2,
         ),
-    )(chosen, queries, local_stack, local_stack, same_core, same_core, other_core, other_core, bias)
+    )(chosen, queries, same_core, same_core, other_core, other_core, bias, *state)
 
 
 def fetch_out_weight(w_out, head, core):
@@ -211,10 +246,7 @@
     local_kv = jnp.concatenate([keys.reshape(span, heads * HD), values], axis=1)
     before = from_behind(local_kv, "slot", 1)
     earlier = from_behind(local_kv, "slot", 2)
-    queries, before, earlier, same_core, mine = lax.optimization_barrier(
-        (queries, before, earlier, same_core, mine)
-    )
-    other_core = lax.ppermute(same_core, "slot", [(i, i ^ 1) for i in range(slots)])
+    queries, before, earlier = lax.optimization_barrier((queries, before, earlier))
     own_mask = lax.dynamic_index_in_dim(block_mask, slot, 0, keepdims=False)
     own_cache = lax.dynamic_index_in_dim(cache_index, slot, 0, keepdims=False)
     sibling_slot = jnp.bitwise_xor(slot, 1)
@@ -232,9 +264,17 @@
     rows = span // 2
     parts = rows // BLOCK
     queries = queries.reshape(span, width)
+    n_local = local_stack.shape[0]
+    states = [
+        flash_local(queries[p * rows : (p + 1) * rows], local_stack,
+                    bias[:n_local, p * parts : (p + 1) * parts], heads)
+        for p in range(2)
+    ]
+    states, same_core, mine = lax.optimization_barrier((states, same_core, mine))
+    other_core = lax.ppermute(same_core, "slot", [(i, i ^ 1) for i in range(slots)])
     mixed_parts = [
-        flash(queries[p * rows : (p + 1) * rows], local_stack, same_core, other_core,
-              bias[:, p * parts : (p + 1) * parts], own_cache, heads)
+        flash_pool(queries[p * rows : (p + 1) * rows], same_core, other_core,
+                   bias[n_local:, p * parts : (p + 1) * parts], own_cache, states[p], heads)
         for p in range(2)
     ]
     sibling = lax.ppermute(

time: 159 us -> 170 us (1.069)
  waiting for transfers between devices: 39.2 us -> 57.8 us
  starting transfers between devices: 27.1 us -> 18.8 us
  Pallas kernels: 35.7 us -> 39.2 us
  local copies, waits for them, and re-layouts: 12.1 us -> 10.1 us
    ppermute x5, waiting for transfers between devices: 0.42 us -> 38.2 us  [from_behind(): lax.ppermute(shard, axis, [(i, (i + by) % length) for i in range(length)])]
    all_to_all x1, waiting for transfers between devices: 19.1 us -> 0.01 us  [fetch_out_weight(): exchanged = lax.all_to_all(blocks, 'head', 0, 0)]
    ppermute x1, starting transfers between devices: 7.93 us -> 0.39 us  [local(): lax.ppermute(same_core, 'slot', [(i, i ^ 1) for i in range(slots)])]
    pallas_call x2 -> x4, Pallas kernels: 35.7 us -> 39.2 us  [the longest x2 25.5 us: flash_pool(): pl.pallas_call(kernel, grid_spec=grid_spec, out_shape=jax.ShapeDtypeStruc...]
    reshape x1, local copies, waits for them, and re-layouts: 2.49 us -> 0.5 us  [local(): pool_flat = pool_kv.reshape(1, pool_kv.shape[1], -1)]
    unnamed x35 -> x31, local copies, waits for them, and re-layouts: 1.94 us -> 0.13 us
  transfers between devices with their start and end apart: 14 -> 14, of which waited for: 5 -> 7; matrix products, arithmetic and copies ran while one was open for 26% -> 21% of each run, Pallas kernels for 23% -> 23%
where the time goes in v16:
time: 170 us; the launch traced here: 169 us
  waiting for transfers between devices  57.8 us (34%)
  Pallas kernels  39.2 us (23%)
  matrix products  25 us (15%)
  starting transfers between devices  18.8 us (11%)
  other arithmetic  17.3 us (10%)
  local copies, waits for them, and re-layouts  10.1 us (6%)
    ppermute x5, waiting for transfers between devices, from_behind(): lax.ppermute(shard, axis, [(i, (i + by) % length) for i in range(length)])  38.2 us
    pallas_call x2, Pallas kernels, flash_pool(): pl.pallas_call(kernel, grid_spec=grid_spec, out_shape=jax.ShapeDtypeStruc...  25.5 us
    ppermute x6, waiting for transfers between devices, local(): lax.ppermute(part, 'head', [(i, (i + shift) % groups) for i in range(grou...  19.1 us
    pallas_call x2, Pallas kernels, flash_local(): pl.pallas_call(kernel, grid=(steps,), in_specs=[pl.BlockSpec((span, width...  13.6 us
    dot_general x1, matrix products, local(): jnp.einsum('td,dkh->kth', hidden, w_qkv, preferred_element_type=jnp.float32)  12.8 us
    ppermute x6, starting transfers between devices, local(): lax.ppermute(part, 'head', [(i, (i + shift) % groups) for i in range(grou...  7.25 us
    ppermute x5, starting transfers between devices, from_behind(): lax.ppermute(shard, axis, [(i, (i + by) % length) for i in range(length)])  6.19 us
    dot_general x3, matrix products, local(): jnp.dot(group_o, sibling[shift - 1], preferred_element_type=jnp.float32)  4.93 us
  transfers between devices with their start and end apart: 14, of which 7 were waited for; matrix products, arithmetic and copies ran while one was open for 21% of the time, Pallas kernels for 23%

profile of v16, /device:TPU:9, one launch (start us, length us, event | category | flops | bytes accessed | tf_op | source)
XLA Modules:
  0.0 168.5 jit_solution(655372494053021957)
XLA Ops:
  0.0 1.8 %dynamic-slice_bitcast_fusion.6 = (bf16[1,384,768]{2,1,0:T(8,128)(2,1)S(1)}, bf16[1,384,768]{2,1,0:T(8,128)(2,1)S(1)}, bf16[1,384,768]{2,1,0:T(8,128)(2,1)S(1)}, bf16[1,384,768]{2,1,0:T(8,128)(2,1)S(1)}) fusion(bf16[384,6144]{1,0:T(8,128)(2,1)} %param.19, s32[]{:T(128)S(6)} %select_n.116, s32[]{:T(128)S(6)} %select_n.118, s32[]{:T(128)S(6)} %select_n.117, ...), kind=kLoop, calls=%fused_computation.43 | loop fusion | bytes 4718608 | tf_op jit(solution)/shard_map/stack | solution.py:194
  1.8 1.7 %pad_maximum_fusion.2 = bf16[4,384,768]{2,1,0:T(8,128)(2,1)} fusion(bf16[1,384,768]{2,1,0:T(8,128)(2,1)S(1)} %get-tuple-element.52, bf16[1,384,768]{2,1,0:T(8,128)(2,1)S(1)} %get-tuple-element.50, bf16[1,384,768]{2,1,0:T(8,128)(2,1)S(1)} %get-tuple-element.51, bf16[1,384,768]{2,1,0:T(8,128)(2,1)S(1)} %get-tuple-element.49), kind=kLoop, calls=%fused_computation.18 | loop fusion | flops 3538944 | bytes 4718592 | tf_op jit(solution)/shard_map/stack | solution.py:194
  3.5 4.9 %all-to-all-start = ((bf16[4,384,768]{2,1,0:T(8,128)(2,1)}), bf16[4,384,768]{2,1,0:T(8,128)(2,1)}, u32[]{:S(2)}, u32[]{:S(2)}) async-start(bf16[4,384,768]{2,1,0:T(8,128)(2,1)} %pad_maximum_fusion.2), calls=%async_computation | async-start | bytes 4718592 | tf_op jit(solution)/shard_map/all_to_all | solution.py:198
  10.0 4.1 %fusion = f32[512]{0:T(512)S(1)} fusion(bf16[512,6144]{1,0:T(8,128)(2,1)} %param.10), kind=kLoop, calls=%fused_computation.2 | loop fusion | flops 9436672 | bytes 6293504 | tf_op jit(solution)/shard_map/reduce_sum | solution.py:239
  14.1 12.8 %fusion.13 = f32[3,512,384]{2,1,0:T(8,128)S(1)} fusion(bf16[6144,3,384]{2,0,1:T(8,128)(2,1)} %param.15, bf16[512,6144]{1,0:T(8,128)(2,1)} %param.10, f32[6144]{0:T(1024)S(1)} %bitcast.75, f32[6144]{0:T(1024)S(1)} %bitcast.76, f32[512]{0:T(512)S(1)} %add_rsqrt_fusion.6), kind=kOutput, calls=%fused_computation.20 | convolution fusion | flops 7263485952 | bytes 22857728 | tf_op jit(solution)/shard_map/td,dkh->kth/dot_general | solution.py:242
  28.3 1.0 fusion.34
  29.3 2.3 %collective-permute-start = (bf16[512,768]{1,0:T(8,128)(2,1)}, bf16[512,768]{1,0:T(8,128)(2,1)}, u32[]{:S(2)}, u32[]{:S(2)}) collective-permute-start(bf16[512,768]{1,0:T(8,128)(2,1)} %get-tuple-element.59), channel_id=1, source_target_pairs={{0,4},{4,8},{8,12},{12,16},{16,20},{20,24},{24,28},{28,0},{1,5},{5... | collective-permute-start | bytes 2359304 | tf_op jit(solution)/shard_map/ppermute | solution.py:14
  31.6 1.2 collective-permute-start.1
  33.3 1.3 collective-permute-start.2
  34.8 1.2 collective-permute-start.4
  37.7 11.0 %collective-permute-done = bf16[512,768]{1,0:T(8,128)(2,1)} collective-permute-done((bf16[512,768]{1,0:T(8,128)(2,1)}, bf16[512,768]{1,0:T(8,128)(2,1)}, u32[]{:S(2)}, u32[]{:S(2)}) %collective-permute-start) | collective-permute-done | bytes 786464 | tf_op jit(solution)/shard_map/ppermute | solution.py:14
  48.7 18.7 %collective-permute-done.1 = bf16[512,768]{1,0:T(8,128)(2,1)} collective-permute-done((bf16[512,768]{1,0:T(8,128)(2,1)}, bf16[512,768]{1,0:T(8,128)(2,1)}, u32[]{:S(2)}, u32[]{:S(2)}) %collective-permute-start.1) | collective-permute-done | bytes 786464 | tf_op jit(solution)/shard_map/ppermute | solution.py:14
  67.4 3.0 %pad_maximum_fusion.1.refs_1_.refs_2_ = bf16[3,512,768]{2,1,0:T(8,128)(2,1)} fusion(bf16[1,512,768]{2,1,0:T(8,128)(2,1)} %bitcast.13, bf16[1,512,768]{2,1,0:T(8,128)(2,1)} %bitcast.12, bf16[1,512,768]{2,1,0:T(8,128)(2,1)S(1)} %get-tuple-element.58), kind=kLoop, calls=%fused_computation.17 | loop fusion | flops 2359296 | bytes 4718592 | tf_op jit(solution)/shard_map/stack | solution.py:259
  71.2 6.8 %shard_map.101 = (f32[3,256,1]{2,1,0:T(8,128)}, f32[3,256,1]{2,1,0:T(8,128)}, f32[3,256,128]{2,1,0:T(8,128)}) custom-call(bf16[256,384]{1,0:T(8,128)(2,1)} %get-tuple-element.66.refs_0_.refs_1_, bf16[3,512,768]{2,1,0:T(8,128)(2,1)} %pad_maximum_fusion.1.refs_1_.refs_2_, bf16[3,512,768]{2,1,0:T(8,128)(2,1)} %pad_maximum_fusion.1.refs_1_.refs_2_, ...), custom_call_target="tpu_custom_call" | custom-call | flops 603979776 | bytes 2359296 | tf_op jit(solution)/shard_map/pallas_call | solution.py:116
  78.0 6.8 %shard_map.100 = (f32[3,256,1]{2,1,0:T(8,128)}, f32[3,256,1]{2,1,0:T(8,128)}, f32[3,256,128]{2,1,0:T(8,128)}) custom-call(bf16[256,384]{1,0:T(8,128)(2,1)} %get-tuple-element.67.refs_0_.refs_1_, bf16[3,512,768]{2,1,0:T(8,128)(2,1)} %pad_maximum_fusion.1.refs_1_.refs_2_, bf16[3,512,768]{2,1,0:T(8,128)(2,1)} %pad_maximum_fusion.1.refs_1_.refs_2_, ...), custom_call_target="tpu_custom_call" | custom-call | flops 603979776 | bytes 2359296 | tf_op jit(solution)/shard_map/pallas_call | solution.py:116
  84.9 8.4 %collective-permute-done.3 = bf16[1,512,768]{2,1,0:T(8,128)(2,1)} collective-permute-done((bf16[1,512,768]{2,1,0:T(8,128)(2,1)S(1)}, bf16[1,512,768]{2,1,0:T(8,128)(2,1)}, u32[]{:S(2)}, u32[]{:S(2)}) %collective-permute-start.3) | collective-permute-done | bytes 786464 | tf_op jit(solution)/shard_map/ppermute | solution.py:14
  93.3 2.0 %pad_maximum_fusion.refs_2_.refs_3_ = bf16[4,512,768]{2,1,0:T(8,128)(2,1)S(1)} fusion(bf16[1,512,768]{2,1,0:T(8,128)(2,1)} %collective-permute-done.4, bf16[1,512,768]{2,1,0:T(8,128)(2,1)} %collective-permute-done.3, bf16[1,512,768]{2,1,0:T(8,128)(2,1)} %copy-done.7, bf16[1,512,768]{2,1,0:T(8,128)(2,1)} %copy-done.6), kind=kLoop, calls=%fused_computation.11 | loop fusion | flops 4718592 | bytes 6291456 | tf_op jit(solution)/shard_map/concatenate | solution.py:232
  95.4 3.8 %dynamic-slice_bitcast_fusion = (bf16[384,768]{1,0:T(8,128)(2,1)}, bf16[384,768]{1,0:T(8,128)(2,1)}, bf16[384,768]{1,0:T(8,128)(2,1)}) fusion(bf16[4,384,768]{2,1,0:T(8,128)(2,1)} %all-to-all-done, s32[]{:T(128)S(6)} %select_n.125, s32[]{:T(128)S(6)} %select_n.123, s32[]{:T(128)S(6)} %select_n.121), kind=kLoop, calls=%fused_computation.37 | loop fusion | bytes 3538956 | tf_op jit(solution)/shard_map/jit(dynamic_index_in_dim)/squeeze | solution.py:200
  99.6 1.2 compare_select_fusion.6.refs_0_
  101.5 2.9 %pad_maximum_fusion.3 = bf16[3,384,768]{2,1,0:T(8,128)(2,1)} fusion(bf16[1,384,768]{2,1,0:T(8,128)(2,1)} %bitcast.72, bf16[1,384,768]{2,1,0:T(8,128)(2,1)} %bitcast.70, bf16[1,384,768]{2,1,0:T(8,128)(2,1)} %bitcast.71), kind=kLoop, calls=%fused_computation.19 | loop fusion | flops 1769472 | bytes 3538944 | tf_op jit(solution)/shard_map/stack | solution.py:281
  105.0 12.7 %shard_map.102 = bf16[256,384]{1,0:T(8,128)(2,1)} custom-call(s32[6]{0:T(128)} %compare_select_fusion.6.refs_0_, bf16[256,384]{1,0:T(8,128)(2,1)} %get-tuple-element.67.refs_0_.refs_1_, bf16[4,512,768]{2,1,0:T(8,128)(2,1)} %copy-done.2, bf16[4,512,768]{2,1,0:T(8,128)(2,1)} %copy-done.2, bf16[4,512,768]{2,1,0:T(8,128)(2,1)} %collective-permute-done.5.refs_4_.refs_5_, ...), custom_call_target="tpu_custom_call" | custom-call | flops 1207959552 | bytes 4718592 | tf_op jit(solution)/shard_map/pallas_call | solution.py:177
  117.7 1.2 collective-permute-start.6
  119.9 12.8 %shard_map.103 = bf16[256,384]{1,0:T(8,128)(2,1)} custom-call(s32[6]{0:T(128)} %compare_select_fusion.6.refs_0_, bf16[256,384]{1,0:T(8,128)(2,1)} %get-tuple-element.66.refs_0_.refs_1_, bf16[4,512,768]{2,1,0:T(8,128)(2,1)} %copy-done.2, bf16[4,512,768]{2,1,0:T(8,128)(2,1)} %copy-done.2, bf16[4,512,768]{2,1,0:T(8,128)(2,1)} %collective-permute-done.5.refs_4_.refs_5_, ...), custom_call_target="tpu_custom_call" | custom-call | flops 1207959552 | bytes 4718592 | tf_op jit(solution)/shard_map/pallas_call | solution.py:177
  133.4 3.0 %collective-permute-start.9 = (bf16[256,384]{1,0:T(8,128)(2,1)}, bf16[256,384]{1,0:T(8,128)(2,1)S(1)}, u32[]{:S(2)}, u32[]{:S(2)}) collective-permute-start(bf16[256,384]{1,0:T(8,128)(2,1)} %shard_map.103), channel_id=1, source_target_pairs={{0,2},{1,3},{2,0},{3,1},{4,6},{5,7},{6,4},{7,5},{8,10},{9,11},{10,... | collective-permute-start | bytes 589832 | tf_op jit(solution)/shard_map/ppermute | solution.py:286
  136.4 1.5 collective-permute-start.11
  137.9 15.0 %collective-permute-done.10 = bf16[256,384]{1,0:T(8,128)(2,1)S(1)} collective-permute-done((bf16[256,384]{1,0:T(8,128)(2,1)S(1)}, bf16[256,384]{1,0:T(8,128)(2,1)S(1)}, u32[]{:S(2)}, u32[]{:S(2)}) %collective-permute-start.10) | collective-permute-done | bytes 196640 | tf_op jit(solution)/shard_map/ppermute | solution.py:286
  153.0 1.1 collective-permute-done.9
  154.1 3.0 %collective-permute-done.11 = bf16[256,384]{1,0:T(8,128)(2,1)S(1)} collective-permute-done((bf16[256,384]{1,0:T(8,128)(2,1)}, bf16[256,384]{1,0:T(8,128)(2,1)S(1)}, u32[]{:S(2)}, u32[]{:S(2)}) %collective-permute-start.11) | collective-permute-done | bytes 196640 | tf_op jit(solution)/shard_map/ppermute | solution.py:286
  158.9 1.6 convolution_convert_fusion.3
  160.5 1.6 convolution_convert_fusion.2
  162.2 1.7 convert_add_fusion
  163.9 4.7 %fusion.12 = f32[512,1536]{1,0:T(8,128)} fusion(f32[512,768]{1,0:T(8,128)S(1)} %convert_add_fusion, f32[512,768]{1,0:T(8,128)S(1)} %convert_add_fusion.1, f32[1536]{0:T(1024)S(1)} %dynamic-slice_reduce_fusion, bf16[512,6144]{1,0:T(8,128)(2,1)} %param.10, s32[]{:T(128)S(6)} %select_n.103, pred[]{:T(512)S(6)} %eq.29, bf16[384,6144]{1,0:T(8,128)(2,1)} %param.19, ...), kind=kOutput, calls=%fused_computation.15 | convolution fusion | flops 611844096 | bytes 9444864 | tf_op jit(solution)/shard_map/dot_general | solution.py:294
  (81 shorter events, 11.2 us)
Async XLA Ops:
  0.0 9.0 %copy-start = (bf16[8,3,6144]{2,0,1:T(8,128)(2,1)S(1)}, bf16[8,3,6144]{2,0,1:T(8,128)(2,1)}, u32[]{:S(2)}) copy-start(bf16[8,3,6144]{2,0,1:T(8,128)(2,1)} %param.11) | copy-start | bytes 884740
  3.5 4.9 %copy-start.13 = (s32[8]{0:T(128)S(1)}, s32[8]{0:T(128)}, u32[]{:S(2)}) copy-start(s32[8]{0:T(128)} %param.12) | copy-start | bytes 100
  3.5 91.8 %all-to-all-start = ((bf16[4,384,768]{2,1,0:T(8,128)(2,1)}), bf16[4,384,768]{2,1,0:T(8,128)(2,1)}, u32[]{:S(2)}, u32[]{:S(2)}) async-start(bf16[4,384,768]{2,1,0:T(8,128)(2,1)} %pad_maximum_fusion.2), calls=%async_computation | async-start | bytes 4718592 | tf_op jit(solution)/shard_map/all_to_all | solution.py:198
  26.9 0.7 copy-start.11
  26.9 0.7 copy-start.12
  27.8 5.0 %copy-start.8 = (bf16[1,512,2,384]{3,2,1,0:T(2,128)(2,1)S(1)}, bf16[1,512,2,384]{3,2,1,0:T(2,128)(2,1)}, u32[]{:S(2)}) copy-start(bf16[1,512,2,384]{3,2,1,0:T(2,128)(2,1)} %param.18) | copy-start | bytes 2359300
  29.3 19.5 %collective-permute-start = (bf16[512,768]{1,0:T(8,128)(2,1)}, bf16[512,768]{1,0:T(8,128)(2,1)}, u32[]{:S(2)}, u32[]{:S(2)}) collective-permute-start(bf16[512,768]{1,0:T(8,128)(2,1)} %get-tuple-element.59), channel_id=1, source_target_pairs={{0,4},{4,8},{8,12},{12,16},{16,20},{20,24},{24,28},{28,0},{1,5},{5... | collective-permute-start | bytes 2359304 | tf_op jit(solution)/shard_map/ppermute | solution.py:14
  31.6 35.8 %collective-permute-start.1 = (bf16[512,768]{1,0:T(8,128)(2,1)}, bf16[512,768]{1,0:T(8,128)(2,1)}, u32[]{:S(2)}, u32[]{:S(2)}) collective-permute-start(bf16[512,768]{1,0:T(8,128)(2,1)} %get-tuple-element.59), channel_id=1, source_target_pairs={{0,8},{4,12},{8,16},{12,20},{16,24},{20,28},{24,0},{28,4},{1,9},{5... | collective-permute-start | bytes 2359304 | tf_op jit(solution)/shard_map/ppermute | solution.py:14
  33.3 37.1 %copy-start.6 = (bf16[1,512,768]{2,1,0:T(8,128)(2,1)}, bf16[1,512,768]{2,1,0:T(8,128)(2,1)S(1)}, u32[]{:S(2)}) copy-start(bf16[1,512,768]{2,1,0:T(8,128)(2,1)S(1)} %reshape.80) | copy-start | bytes 2359300
  33.3 51.5 %collective-permute-start.2 = (bf16[1,512,768]{2,1,0:T(8,128)(2,1)S(1)}, bf16[1,512,768]{2,1,0:T(8,128)(2,1)S(1)}, u32[]{:S(2)}, u32[]{:S(2)}) collective-permute-start(bf16[1,512,768]{2,1,0:T(8,128)(2,1)S(1)} %reshape.80), channel_id=1, source_target_pairs={{0,8},{4,12},{8,16},{12,20},{16,24},{20,28},{24,0},{28,4},{1,9},{5... | collective-permute-start | bytes 2359304 | tf_op jit(solution)/shard_map/ppermute | solution.py:14
  34.6 58.7 %collective-permute-start.3 = (bf16[1,512,768]{2,1,0:T(8,128)(2,1)S(1)}, bf16[1,512,768]{2,1,0:T(8,128)(2,1)}, u32[]{:S(2)}, u32[]{:S(2)}) collective-permute-start(bf16[1,512,768]{2,1,0:T(8,128)(2,1)S(1)} %reshape.80), channel_id=1, source_target_pairs={{0,16},{4,20},{8,24},{12,28},{16,0},{20,4},{24,8},{28,12},{1,17},{... | collective-permute-start | bytes 2359304 | tf_op jit(solution)/shard_map/ppermute | solution.py:14
  34.8 58.5 %collective-permute-start.4 = (bf16[1,512,768]{2,1,0:T(8,128)(2,1)S(1)}, bf16[1,512,768]{2,1,0:T(8,128)(2,1)}, u32[]{:S(2)}, u32[]{:S(2)}) collective-permute-start(bf16[1,512,768]{2,1,0:T(8,128)(2,1)S(1)} %reshape.80), channel_id=1, source_target_pairs={{0,24},{4,28},{8,0},{12,4},{16,8},{20,12},{24,16},{28,20},{1,25},{... | collective-permute-start | bytes 2359304 | tf_op jit(solution)/shard_map/ppermute | solution.py:14
  84.9 8.4 %copy-start.7 = (bf16[1,512,768]{2,1,0:T(8,128)(2,1)}, bf16[1,512,768]{2,1,0:T(8,128)(2,1)S(1)}, u32[]{:S(2)}) copy-start(bf16[1,512,768]{2,1,0:T(8,128)(2,1)S(1)} %collective-permute-done.2) | copy-start | bytes 2359300
  95.4 9.0 %copy-start.2 = (bf16[4,512,768]{2,1,0:T(8,128)(2,1)}, bf16[4,512,768]{2,1,0:T(8,128)(2,1)S(1)}, u32[]{:S(2)}) copy-start(bf16[4,512,768]{2,1,0:T(8,128)(2,1)S(1)} %pad_maximum_fusion.refs_2_.refs_3_) | copy-start | bytes 9437188
  99.2 5.8 %collective-permute-start.5 = (bf16[4,512,768]{2,1,0:T(8,128)(2,1)S(1)}, bf16[4,512,768]{2,1,0:T(8,128)(2,1)}, u32[]{:S(2)}, u32[]{:S(2)}) collective-permute-start(bf16[4,512,768]{2,1,0:T(8,128)(2,1)S(1)} %pad_maximum_fusion.refs_2_.refs_3_), channel_id=1, source_target_pairs={{0,4},{4,0},{8,12},{12,8},{16,20},{20,16},{24,28},{28,24},{1,5},{5... | collective-permute-start | bytes 9437192 | tf_op jit(solution)/shard_map/ppermute | solution.py:274
  104.4 54.5 %collective-permute-start.12 = (bf16[3,384,768]{2,1,0:T(8,128)(2,1)}, bf16[3,384,768]{2,1,0:T(8,128)(2,1)}, u32[]{:S(2)}, u32[]{:S(2)}) collective-permute-start(bf16[3,384,768]{2,1,0:T(8,128)(2,1)} %pad_maximum_fusion.3), channel_id=1, source_target_pairs={{0,4},{4,0},{8,12},{12,8},{16,20},{20,16},{24,28},{28,24},{1,5},{5... | collective-permute-start | bytes 5308424 | tf_op jit(solution)/shard_map/ppermute | solution.py:280
  117.7 18.6 %collective-permute-start.6 = (bf16[256,384]{1,0:T(8,128)(2,1)}, bf16[256,384]{1,0:T(8,128)(2,1)S(1)}, u32[]{:S(2)}, u32[]{:S(2)}) collective-permute-start(bf16[256,384]{1,0:T(8,128)(2,1)} %shard_map.102), channel_id=1, source_target_pairs={{0,1},{1,2},{2,3},{3,0},{4,5},{5,6},{6,7},{7,4},{8,9},{9,10},{10,1... | collective-permute-start | bytes 589832 | tf_op jit(solution)/shard_map/ppermute | solution.py:286
  118.9 17.4 %collective-permute-start.8 = (bf16[256,384]{1,0:T(8,128)(2,1)}, bf16[256,384]{1,0:T(8,128)(2,1)S(1)}, u32[]{:S(2)}, u32[]{:S(2)}) collective-permute-start(bf16[256,384]{1,0:T(8,128)(2,1)} %shard_map.102), channel_id=1, source_target_pairs={{0,2},{1,3},{2,0},{3,1},{4,6},{5,7},{6,4},{7,5},{8,10},{9,11},{10,... | collective-permute-start | bytes 589832 | tf_op jit(solution)/shard_map/ppermute | solution.py:286
  119.9 16.4 %copy-start.9 = (bf16[256,384]{1,0:T(8,128)(2,1)S(1)}, bf16[256,384]{1,0:T(8,128)(2,1)}, u32[]{:S(2)}) copy-start(bf16[256,384]{1,0:T(8,128)(2,1)} %shard_map.102) | copy-start | bytes 589828
  132.7 24.4 %copy-start.4 = (bf16[384,768]{1,0:T(8,128)(2,1)S(1)}, bf16[384,768]{1,0:T(8,128)(2,1)}, u32[]{:S(2)}) copy-start(bf16[384,768]{1,0:T(8,128)(2,1)} %get-tuple-element.40) | copy-start | bytes 1769476
  132.7 25.0 %copy-start.3 = (bf16[384,768]{1,0:T(8,128)(2,1)S(1)}, bf16[384,768]{1,0:T(8,128)(2,1)}, u32[]{:S(2)}) copy-start(bf16[384,768]{1,0:T(8,128)(2,1)} %get-tuple-element.41) | copy-start | bytes 1769476
  132.8 20.2 %collective-permute-start.7 = (bf16[256,384]{1,0:T(8,128)(2,1)}, bf16[256,384]{1,0:T(8,128)(2,1)S(1)}, u32[]{:S(2)}, u32[]{:S(2)}) collective-permute-start(bf16[256,384]{1,0:T(8,128)(2,1)} %shard_map.103), channel_id=1, source_target_pairs={{0,1},{1,2},{2,3},{3,0},{4,5},{5,6},{6,7},{7,4},{8,9},{9,10},{10,1... | collective-permute-start | bytes 589832 | tf_op jit(solution)/shard_map/ppermute | solution.py:286
  133.4 20.7 %collective-permute-start.9 = (bf16[256,384]{1,0:T(8,128)(2,1)}, bf16[256,384]{1,0:T(8,128)(2,1)S(1)}, u32[]{:S(2)}, u32[]{:S(2)}) collective-permute-start(bf16[256,384]{1,0:T(8,128)(2,1)} %shard_map.103), channel_id=1, source_target_pairs={{0,2},{1,3},{2,0},{3,1},{4,6},{5,7},{6,4},{7,5},{8,10},{9,11},{10,... | collective-permute-start | bytes 589832 | tf_op jit(solution)/shard_map/ppermute | solution.py:286
  136.3 16.5 %collective-permute-start.10 = (bf16[256,384]{1,0:T(8,128)(2,1)S(1)}, bf16[256,384]{1,0:T(8,128)(2,1)S(1)}, u32[]{:S(2)}, u32[]{:S(2)}) collective-permute-start(bf16[256,384]{1,0:T(8,128)(2,1)S(1)} %copy-done.9), channel_id=1, source_target_pairs={{0,3},{1,0},{2,1},{3,2},{4,7},{5,4},{6,5},{7,6},{8,11},{9,8},{10,9... | collective-permute-start | bytes 589832 | tf_op jit(solution)/shard_map/ppermute | solution.py:286
  136.4 20.7 %collective-permute-start.11 = (bf16[256,384]{1,0:T(8,128)(2,1)}, bf16[256,384]{1,0:T(8,128)(2,1)S(1)}, u32[]{:S(2)}, u32[]{:S(2)}) collective-permute-start(bf16[256,384]{1,0:T(8,128)(2,1)} %shard_map.103), channel_id=1, source_target_pairs={{0,3},{1,0},{2,1},{3,2},{4,7},{5,4},{6,5},{7,6},{8,11},{9,8},{10,9... | collective-permute-start | bytes 589832 | tf_op jit(solution)/shard_map/ppermute | solution.py:286
  152.9 5.4 %copy-start.5 = (bf16[384,768]{1,0:T(8,128)(2,1)S(1)}, bf16[384,768]{1,0:T(8,128)(2,1)}, u32[]{:S(2)}) copy-start(bf16[384,768]{1,0:T(8,128)(2,1)} %get-tuple-element.42) | copy-start | bytes 1769476
  162.2 1.7 %copy-start.10 = (bf16[256,384]{1,0:T(8,128)(2,1)S(1)}, bf16[256,384]{1,0:T(8,128)(2,1)}, u32[]{:S(2)}) copy-start(bf16[256,384]{1,0:T(8,128)(2,1)} %shard_map.103) | copy-start | bytes 589828
  163.9 4.7 %copy-start.1 = (bf16[8,3,6144]{2,0,1:T(8,128)(2,1)S(1)}, bf16[8,3,6144]{2,0,1:T(8,128)(2,1)}, u32[]{:S(2)}) copy-start(bf16[8,3,6144]{2,0,1:T(8,128)(2,1)} %param.11) | copy-start | bytes 884740

commit v17 on v15

--- a/solution.py
+++ b/solution.py
@@ -47,16 +47,79 @@
     return (new_high, totals, accum)
 
 
-def flash_kernel(chosen, q_ref, lk_ref, lv_ref, ak_ref, av_ref, bk_ref, bv_ref, bias_ref, o_ref, m_sc, l_sc, acc_sc, *, heads, n_local, half):
+def online_update(q_ref, k_ref, v_ref, bias_ref, m_sc, l_sc, acc_sc, heads):
+    span = q_ref.shape[0]
+    blocks = bias_ref.shape[0]
+    bias = bias_ref[...][:, None, :]
+    for h in range(heads):
+        cols = slice(h * HD, (h + 1) * HD)
+        q = q_ref[:, cols]
+        k = k_ref[:, cols]
+        s = lax.dot_general(q, k, (((1,), (1,)), ((), ())), preferred_element_type=jnp.float32)
+        s = (s * (1.0 / HD**0.5)).reshape(blocks, span // blocks, s.shape[1]) + bias
+        s = s.reshape(span, -1)
+        m_prev = m_sc[h]
+        m_new = jnp.maximum(m_prev, jnp.max(s, axis=1, keepdims=True))
+        factor = jnp.exp(m_prev - m_new)
+        p = jnp.exp(s - m_new)
+        l_sc[h] = l_sc[h] * factor + jnp.sum(p, axis=1, keepdims=True)
+        acc_sc[h] = acc_sc[h] * factor + jnp.dot(
+            p.astype(jnp.bfloat16), v_ref[:, cols], preferred_element_type=jnp.float32
+        )
+        m_sc[h] = m_new
+
+
+def local_kernel(q_ref, k_ref, v_ref, bias_ref, m_ref, l_ref, acc_ref, *, heads):
+    @pl.when(pl.program_id(0) == 0)
+    def _():
+        m_ref[...] = jnp.full(m_ref.shape, -1e30, jnp.float32)
+        l_ref[...] = jnp.zeros(l_ref.shape, jnp.float32)
+        acc_ref[...] = jnp.zeros(acc_ref.shape, jnp.float32)
+
+    online_update(q_ref, k_ref, v_ref, bias_ref, m_ref, l_ref, acc_ref, heads)
+
+
+def flash_local(queries, local_stack, bias, heads):
+    span, width = queries.shape
+    steps, keys_len = local_stack.shape[:2]
+    blocks = bias.shape[1]
+    kv_block = (None, keys_len, width)
+    state = pl.BlockSpec((heads, span, 1), lambda j: (0, 0, 0))
+    kernel = lambda *refs: local_kernel(*refs, heads=heads)
+    return pl.pallas_call(
+        kernel,
+        grid=(steps,),
+        in_specs=[
+            pl.BlockSpec((span, width), lambda j: (0, 0)),
+            pl.BlockSpec(kv_block, lambda j: (j, 0, 0)),
+            pl.BlockSpec(kv_block, lambda j: (j, 0, 1)),
+            pl.BlockSpec((None, blocks, keys_len), lambda j: (j, 0, 0)),
+        ],
+        out_specs=[state, state, pl.BlockSpec((heads, span, HD), lambda j: (0, 0, 0))],
+        out_shape=[
+            jax.ShapeDtypeStruct((heads, span, 1), jnp.float32),
+            jax.ShapeDtypeStruct((heads, span, 1), jnp.float32),
+            jax.ShapeDtypeStruct((heads, span, HD), jnp.float32),
+        ],
+        compiler_params=pltpu.CompilerParams(dimension_semantics=("arbitrary",)),
+        cost_estimate=pl.CostEstimate(
+            flops=4 * steps * heads * span * keys_len * HD,
+            transcendentals=steps * heads * span * keys_len,
+            bytes_accessed=2 * steps * keys_len * width * 2,
+        ),
+    )(queries, local_stack, local_stack, bias)
+
+
+def flash_kernel(chosen, q_ref, lk_ref, lv_ref, ak_ref, av_ref, bk_ref, bv_ref, bias_ref, m_in, l_in, acc_in, o_ref, m_sc, l_sc, acc_sc, *, heads, n_local, half):
     step = pl.program_id(0)
     span = q_ref.shape[0]
     blocks = bias_ref.shape[0]
 
     @pl.when(step == 0)
     def _():
-        m_sc[...] = jnp.full(m_sc.shape, -1e30, jnp.float32)
-        l_sc[...] = jnp.zeros(l_sc.shape, jnp.float32)
-        acc_sc[...] = jnp.zeros(acc_sc.shape, jnp.float32)
+        m_sc[...] = m_in[...]
+        l_sc[...] = l_in[...]
+        acc_sc[...] = acc_in[...]
 
     def body(k_ref, v_ref):
         bias = bias_ref[...][:, None, :]
@@ -98,7 +161,7 @@
             o_ref[:, cols] = (acc_sc[h] / l_sc[h]).astype(o_ref.dtype)
 
 
-def flash(queries, local_stack, same_core, other_core, bias, chosen, heads):
+def flash(queries, local_stack, same_core, other_core, bias, chosen, state, heads):
     span, width = queries.shape
     n_local = local_stack.shape[0]
     half = same_core.shape[0]
@@ -130,6 +193,9 @@
             pl.BlockSpec(kv_block, pool_map(0, True)),
             pl.BlockSpec(kv_block, pool_map(1, True)),
             pl.BlockSpec((None, blocks, keys_len), lambda j, c: (j, 0, 0)),
+            pl.BlockSpec((heads, span, 1), lambda j, c: (0, 0, 0)),
+            pl.BlockSpec((heads, span, 1), lambda j, c: (0, 0, 0)),
+            pl.BlockSpec((heads, span, HD), lambda j, c: (0, 0, 0)),
         ],
         out_specs=pl.BlockSpec((span, width), lambda j, c: (0, 0)),
         scratch_shapes=[
@@ -149,7 +215,7 @@
             transcendentals=steps * heads * span * span,
             bytes_accessed=2 * steps * span * width * 2,
         ),
-    )(chosen, queries, local_stack, local_stack, same_core, same_core, other_core, other_core, bias)
+    )(chosen, queries, local_stack, local_stack, same_core, same_core, other_core, other_core, bias, *state)
 
 
 def fetch_out_weight(w_out, head, core):
@@ -211,8 +277,19 @@
     local_kv = jnp.concatenate([keys.reshape(span, heads * HD), values], axis=1)
     before = from_behind(local_kv, "slot", 1)
     earlier = from_behind(local_kv, "slot", 2)
-    queries, before, earlier, same_core, mine = lax.optimization_barrier(
-        (queries, before, earlier, same_core, mine)
+    rows = span // 2
+    parts = rows // BLOCK
+    width = heads * HD
+    own_mask = lax.dynamic_index_in_dim(block_mask, slot, 0, keepdims=False)
+    flat_queries = queries.reshape(span, width)
+    own_bias = jnp.zeros((1, blocks_q, span), jnp.float32)
+    states = [
+        flash_local(flat_queries[p * rows : (p + 1) * rows], local_kv.reshape(1, span, 2 * width),
+                    own_bias[:, p * parts : (p + 1) * parts], heads)
+        for p in range(2)
+    ]
+    states, queries, before, earlier, same_core, mine = lax.optimization_barrier(
+        (states, queries, before, earlier, same_core, mine)
     )
     other_core = lax.ppermute(same_core, "slot", [(i, i ^ 1) for i in range(slots)])
     own_mask = lax.dynamic_index_in_dim(block_mask, slot, 0, keepdims=False)
@@ -224,7 +301,7 @@
         slots // 2 + ((sibling_slot - own_cache) % slots) // 2,
     ).astype(jnp.int32)
     width = heads * HD
-    local_stack = jnp.stack([local_kv, before, earlier]).reshape(3, span, 2 * width)
+    local_stack = jnp.stack([before, earlier]).reshape(2, span, 2 * width)
     visible = jnp.concatenate([jnp.ones((blocks_q, blocks_q), jnp.int32), own_mask], axis=1)
     visible = jnp.transpose(visible.reshape(blocks_q, 3 + cache_len, blocks_q), (1, 0, 2))
     visible = jnp.repeat(visible, BLOCK, axis=2)
@@ -234,7 +311,7 @@
     queries = queries.reshape(span, width)
     mixed_parts = [
         flash(queries[p * rows : (p + 1) * rows], local_stack, same_core, other_core,
-              bias[:, p * parts : (p + 1) * parts], own_cache, heads)
+              bias[1:, p * parts : (p + 1) * parts], own_cache, states[p], heads)
         for p in range(2)
     ]
     sibling = lax.ppermute(

time: 159 us -> 156 us (0.981)
  waiting for transfers between devices: 39.2 us -> 30.6 us
  Pallas kernels: 35.7 us -> 40.7 us
  local copies, waits for them, and re-layouts: 12.1 us -> 14.2 us
    all_to_all x1, waiting for transfers between devices: 19.1 us -> 10.7 us  [fetch_out_weight(): exchanged = lax.all_to_all(blocks, 'head', 0, 0)]
    pallas_call x0 -> x2, Pallas kernels: none -> 7.14 us  [flash_local(): pl.pallas_call(kernel, grid=(steps,), in_specs=[pl.BlockSpec((span, width...]
    pallas_call x2, Pallas kernels: 35.7 us -> 33.5 us  [flash(): pl.pallas_call(kernel, grid_spec=grid_spec, out_shape=jax.ShapeDtypeStruc...]
    another operation x3 -> x2, other arithmetic: 4.92 us -> 3.23 us  [the longest x1 2.75 us: local(): local_stack = jnp.stack([before, earlier]).reshape(2, span, 2 * width)]
  transfers between devices with their start and end apart: 14 -> 14, of which waited for: 5 -> 5; matrix products, arithmetic and copies ran while one was open for 26% -> 27% of each run, Pallas kernels for 23% -> 26%
where the time goes in v17:
time: 156 us; the launch traced here: 155 us
  Pallas kernels  40.7 us (26%)
  waiting for transfers between devices  30.6 us (20%)
  starting transfers between devices  27.1 us (17%)
  matrix products  25 us (16%)
  other arithmetic  17.3 us (11%)
  local copies, waits for them, and re-layouts  14.2 us (9%)
    pallas_call x2, Pallas kernels, flash(): pl.pallas_call(kernel, grid_spec=grid_spec, out_shape=jax.ShapeDtypeStruc...  33.5 us
    ppermute x6, waiting for transfers between devices, local(): lax.ppermute(part, 'head', [(i, (i + shift) % groups) for i in range(grou...  19.6 us
    dot_general x1, matrix products, local(): jnp.einsum('td,dkh->kth', hidden, w_qkv, preferred_element_type=jnp.float32)  12.8 us
    all_to_all x1, waiting for transfers between devices, fetch_out_weight(): exchanged = lax.all_to_all(blocks, 'head', 0, 0)  10.7 us
    ppermute x1, starting transfers between devices, local(): lax.ppermute(same_core, 'slot', [(i, i ^ 1) for i in range(slots)])  7.92 us
    ppermute x6, starting transfers between devices, local(): lax.ppermute(part, 'head', [(i, (i + shift) % groups) for i in range(grou...  7.45 us
    pallas_call x2, Pallas kernels, flash_local(): pl.pallas_call(kernel, grid=(steps,), in_specs=[pl.BlockSpec((span, width...  7.14 us
    ppermute x5, starting transfers between devices, from_behind(): lax.ppermute(shard, axis, [(i, (i + by) % length) for i in range(length)])  6.83 us
  transfers between devices with their start and end apart: 14, of which 5 were waited for; matrix products, arithmetic and copies ran while one was open for 27% of the time, Pallas kernels for 26%

profile of v17, /device:TPU:9, one launch (start us, length us, event | category | flops | bytes accessed | tf_op | source)
XLA Modules:
  0.0 155.3 jit_solution(1511648856798397703)
XLA Ops:
  0.0 2.5 %reshape.85 = bf16[1,512,768]{2,1,0:T(8,128)(2,1)S(1)} reshape(bf16[1,512,2,384]{3,2,1,0:T(2,128)(2,1)} %param.18) | data formatting | bytes 1572864 | tf_op jit(solution)/shard_map/reshape | solution.py:261
  2.5 2.2 %collective-permute-start.4 = (bf16[1,512,768]{2,1,0:T(8,128)(2,1)S(1)}, bf16[1,512,768]{2,1,0:T(8,128)(2,1)S(1)}, u32[]{:S(2)}, u32[]{:S(2)}) collective-permute-start(bf16[1,512,768]{2,1,0:T(8,128)(2,1)S(1)} %reshape.85), channel_id=1, source_target_pairs={{0,24},{4,28},{8,0},{12,4},{16,8},{20,12},{24,16},{28,20},{1,25},{... | collective-permute-start | bytes 2359304 | tf_op jit(solution)/shard_map/ppermute | solution.py:14
  5.3 1.8 %dynamic-slice_bitcast_fusion.6 = (bf16[1,384,768]{2,1,0:T(8,128)(2,1)S(1)}, bf16[1,384,768]{2,1,0:T(8,128)(2,1)S(1)}, bf16[1,384,768]{2,1,0:T(8,128)(2,1)S(1)}, bf16[1,384,768]{2,1,0:T(8,128)(2,1)S(1)}) fusion(bf16[384,6144]{1,0:T(8,128)(2,1)} %param.19, s32[]{:T(128)S(6)} %select_n.112, s32[]{:T(128)S(6)} %select_n.114, s32[]{:T(128)S(6)} %select_n.113, ...), kind=kLoop, calls=%fused_computation.43 | loop fusion | bytes 4718608 | tf_op jit(solution)/shard_map/stack | solution.py:225
  7.0 1.7 %pad_maximum_fusion.1 = bf16[4,384,768]{2,1,0:T(8,128)(2,1)} fusion(bf16[1,384,768]{2,1,0:T(8,128)(2,1)S(1)} %get-tuple-element.52, bf16[1,384,768]{2,1,0:T(8,128)(2,1)S(1)} %get-tuple-element.50, bf16[1,384,768]{2,1,0:T(8,128)(2,1)S(1)} %get-tuple-element.51, bf16[1,384,768]{2,1,0:T(8,128)(2,1)S(1)} %get-tuple-element.49), kind=kLoop, calls=%fused_computation.17 | loop fusion | flops 3538944 | bytes 4718592 | tf_op jit(solution)/shard_map/stack | solution.py:225
  8.8 4.9 %all-to-all-start = ((bf16[4,384,768]{2,1,0:T(8,128)(2,1)}), bf16[4,384,768]{2,1,0:T(8,128)(2,1)}, u32[]{:S(2)}, u32[]{:S(2)}) async-start(bf16[4,384,768]{2,1,0:T(8,128)(2,1)} %pad_maximum_fusion.1), calls=%async_computation | async-start | bytes 4718592 | tf_op jit(solution)/shard_map/all_to_all | solution.py:229
  15.2 4.1 %fusion = f32[512]{0:T(512)S(1)} fusion(bf16[512,6144]{1,0:T(8,128)(2,1)} %param.10), kind=kLoop, calls=%fused_computation.2 | loop fusion | flops 9436672 | bytes 6293504 | tf_op jit(solution)/shard_map/reduce_sum | solution.py:270
  19.3 12.8 %fusion.13 = f32[3,512,384]{2,1,0:T(8,128)S(1)} fusion(bf16[6144,3,384]{2,0,1:T(8,128)(2,1)} %param.15, bf16[512,6144]{1,0:T(8,128)(2,1)} %param.10, f32[6144]{0:T(1024)S(1)} %bitcast.75, f32[6144]{0:T(1024)S(1)} %bitcast.76, f32[512]{0:T(512)S(1)} %add_rsqrt_fusion.6), kind=kOutput, calls=%fused_computation.19 | convolution fusion | flops 7263485952 | bytes 22857728 | tf_op jit(solution)/shard_map/td,dkh->kth/dot_general | solution.py:273
  33.5 1.2 pad_maximum_fusion.4
  34.8 4.1 %collective-permute-start = (bf16[512,768]{1,0:T(8,128)(2,1)}, bf16[512,768]{1,0:T(8,128)(2,1)}, u32[]{:S(2)}, u32[]{:S(2)}) collective-permute-start(bf16[512,768]{1,0:T(8,128)(2,1)} %get-tuple-element.58), channel_id=1, source_target_pairs={{0,4},{4,8},{8,12},{12,16},{16,20},{20,24},{24,28},{28,0},{1,5},{5... | collective-permute-start | bytes 2359304 | tf_op jit(solution)/shard_map/ppermute | solution.py:14
  41.1 3.6 %shard_map.100 = (f32[3,256,1]{2,1,0:T(8,128)}, f32[3,256,1]{2,1,0:T(8,128)}, f32[3,256,128]{2,1,0:T(8,128)}) custom-call(bf16[256,384]{1,0:T(8,128)(2,1)} %get-tuple-element.69.refs_0_, bf16[1,512,768]{2,1,0:T(8,128)(2,1)} %get-tuple-element.59.refs_1_.refs_2_, bf16[1,512,768]{2,1,0:T(8,128)(2,1)} %get-tuple-element.59.refs_1_.refs_2_, ...), custom_call_target="tpu_custom_call" | custom-call | flops 201326592 | bytes 786432 | tf_op jit(solution)/shard_map/pallas_call | solution.py:89
  44.6 3.6 %shard_map.101 = (f32[3,256,1]{2,1,0:T(8,128)}, f32[3,256,1]{2,1,0:T(8,128)}, f32[3,256,128]{2,1,0:T(8,128)}) custom-call(bf16[256,384]{1,0:T(8,128)(2,1)} %get-tuple-element.68.refs_0_, bf16[1,512,768]{2,1,0:T(8,128)(2,1)} %get-tuple-element.59.refs_1_.refs_2_, bf16[1,512,768]{2,1,0:T(8,128)(2,1)} %get-tuple-element.59.refs_1_.refs_2_, ...), custom_call_target="tpu_custom_call" | custom-call | flops 201326592 | bytes 786432 | tf_op jit(solution)/shard_map/pallas_call | solution.py:89
  49.1 0.9 copy-done.10
  50.0 2.0 %pad_maximum_fusion.refs_4_.refs_5_ = bf16[4,512,768]{2,1,0:T(8,128)(2,1)S(1)} fusion(bf16[1,512,768]{2,1,0:T(8,128)(2,1)} %copy-done.9, bf16[1,512,768]{2,1,0:T(8,128)(2,1)} %copy-done.10, bf16[1,512,768]{2,1,0:T(8,128)(2,1)} %collective-permute-done.2, bf16[1,512,768]{2,1,0:T(8,128)(2,1)} %copy-done.8), kind=kLoop, calls=%fused_computation.11 | loop fusion | flops 4718592 | bytes 6291456 | tf_op jit(solution)/shard_map/concatenate | solution.py:263
  52.1 10.7 %all-to-all-done = bf16[4,384,768]{2,1,0:T(8,128)(2,1)} async-done(((bf16[4,384,768]{2,1,0:T(8,128)(2,1)}), bf16[4,384,768]{2,1,0:T(8,128)(2,1)}, u32[]{:S(2)}, u32[]{:S(2)}) %all-to-all-start) | async-done | bytes 2359328 | tf_op jit(solution)/shard_map/all_to_all | solution.py:229
  62.7 2.7 %dynamic-slice_bitcast_fusion = (bf16[384,768]{1,0:T(8,128)(2,1)}, bf16[384,768]{1,0:T(8,128)(2,1)}, bf16[384,768]{1,0:T(8,128)(2,1)}) fusion(bf16[4,384,768]{2,1,0:T(8,128)(2,1)} %all-to-all-done, s32[]{:T(128)S(6)} %select_n.121, s32[]{:T(128)S(6)} %select_n.119, s32[]{:T(128)S(6)} %select_n.117), kind=kLoop, calls=%fused_computation.37 | loop fusion | bytes 3538956 | tf_op jit(solution)/shard_map/jit(dynamic_index_in_dim)/squeeze | solution.py:231
  65.7 7.9 %collective-permute-start.5 = (bf16[4,512,768]{2,1,0:T(8,128)(2,1)S(1)}, bf16[4,512,768]{2,1,0:T(8,128)(2,1)}, u32[]{:S(2)}, u32[]{:S(2)}) collective-permute-start(bf16[4,512,768]{2,1,0:T(8,128)(2,1)S(1)} %pad_maximum_fusion.refs_4_.refs_5_), channel_id=1, source_target_pairs={{0,4},{4,0},{8,12},{12,8},{16,20},{20,16},{24,28},{28,24},{1,5},{5... | collective-permute-start | bytes 9437192 | tf_op jit(solution)/shard_map/ppermute | solution.py:294
  74.7 1.3 compare_select_fusion.6.refs_0_
  76.6 2.9 %pad_maximum_fusion.2 = bf16[3,384,768]{2,1,0:T(8,128)(2,1)} fusion(bf16[1,384,768]{2,1,0:T(8,128)(2,1)} %bitcast.72, bf16[1,384,768]{2,1,0:T(8,128)(2,1)} %bitcast.71, bf16[1,384,768]{2,1,0:T(8,128)(2,1)} %bitcast.70), kind=kLoop, calls=%fused_computation.18 | loop fusion | flops 1769472 | bytes 3538944 | tf_op jit(solution)/shard_map/stack | solution.py:318
  79.5 2.7 %pad_maximum_fusion.3.refs_2_.refs_3_ = bf16[2,512,768]{2,1,0:T(8,128)(2,1)} fusion(bf16[1,512,768]{2,1,0:T(8,128)(2,1)} %bitcast.20, bf16[1,512,768]{2,1,0:T(8,128)(2,1)} %bitcast.19), kind=kLoop, calls=%fused_computation.20 | loop fusion | flops 786432 | bytes 3145728 | tf_op jit(solution)/shard_map/stack | solution.py:304
  83.1 16.7 %shard_map.102 = bf16[256,384]{1,0:T(8,128)(2,1)} custom-call(s32[6]{0:T(128)} %compare_select_fusion.6.refs_0_, bf16[256,384]{1,0:T(8,128)(2,1)} %get-tuple-element.67.refs_1_, bf16[2,512,768]{2,1,0:T(8,128)(2,1)} %pad_maximum_fusion.3.refs_2_.refs_3_, bf16[2,512,768]{2,1,0:T(8,128)(2,1)} %pad_maximum_fusion.3.refs_2_.refs_3_, ...), custom_call_target="tpu_custom_call" | custom-call | flops 805306368 | bytes 3145728 | tf_op jit(solution)/shard_map/pallas_call | solution.py:208
  99.7 2.3 %collective-permute-start.8 = (bf16[256,384]{1,0:T(8,128)(2,1)}, bf16[256,384]{1,0:T(8,128)(2,1)S(1)}, u32[]{:S(2)}, u32[]{:S(2)}) collective-permute-start(bf16[256,384]{1,0:T(8,128)(2,1)} %shard_map.102), channel_id=1, source_target_pairs={{0,2},{1,3},{2,0},{3,1},{4,6},{5,7},{6,4},{7,5},{8,10},{9,11},{10,... | collective-permute-start | bytes 589832 | tf_op jit(solution)/shard_map/ppermute | solution.py:323
  102.1 16.8 %shard_map.103 = bf16[256,384]{1,0:T(8,128)(2,1)} custom-call(s32[6]{0:T(128)} %compare_select_fusion.6.refs_0_, bf16[256,384]{1,0:T(8,128)(2,1)} %get-tuple-element.66.refs_1_, bf16[2,512,768]{2,1,0:T(8,128)(2,1)} %pad_maximum_fusion.3.refs_2_.refs_3_, bf16[2,512,768]{2,1,0:T(8,128)(2,1)} %pad_maximum_fusion.3.refs_2_.refs_3_, ...), custom_call_target="tpu_custom_call" | custom-call | flops 805306368 | bytes 3145728 | tf_op jit(solution)/shard_map/pallas_call | solution.py:208
  118.9 2.3 %collective-permute-start.9 = (bf16[256,384]{1,0:T(8,128)(2,1)}, bf16[256,384]{1,0:T(8,128)(2,1)S(1)}, u32[]{:S(2)}, u32[]{:S(2)}) collective-permute-start(bf16[256,384]{1,0:T(8,128)(2,1)} %shard_map.103), channel_id=1, source_target_pairs={{0,2},{1,3},{2,0},{3,1},{4,6},{5,7},{6,4},{7,5},{8,10},{9,11},{10,... | collective-permute-start | bytes 589832 | tf_op jit(solution)/shard_map/ppermute | solution.py:323
  121.7 1.1 collective-permute-start.10
  122.8 1.4 collective-permute-start.11
  124.1 15.5 %collective-permute-done.10 = bf16[256,384]{1,0:T(8,128)(2,1)S(1)} collective-permute-done((bf16[256,384]{1,0:T(8,128)(2,1)S(1)}, bf16[256,384]{1,0:T(8,128)(2,1)S(1)}, u32[]{:S(2)}, u32[]{:S(2)}) %collective-permute-start.10) | collective-permute-done | bytes 196640 | tf_op jit(solution)/shard_map/ppermute | solution.py:323
  139.7 2.4 %collective-permute-done.7 = bf16[256,384]{1,0:T(8,128)(2,1)S(1)} collective-permute-done((bf16[256,384]{1,0:T(8,128)(2,1)}, bf16[256,384]{1,0:T(8,128)(2,1)S(1)}, u32[]{:S(2)}, u32[]{:S(2)}) %collective-permute-start.7) | collective-permute-done | bytes 196640 | tf_op jit(solution)/shard_map/ppermute | solution.py:323
  142.1 1.7 %collective-permute-done.11 = bf16[256,384]{1,0:T(8,128)(2,1)S(1)} collective-permute-done((bf16[256,384]{1,0:T(8,128)(2,1)}, bf16[256,384]{1,0:T(8,128)(2,1)S(1)}, u32[]{:S(2)}, u32[]{:S(2)}) %collective-permute-start.11) | collective-permute-done | bytes 196640 | tf_op jit(solution)/shard_map/ppermute | solution.py:323
  145.6 1.6 %convolution_convert_fusion.2 = bf16[512,768]{1,0:T(8,128)(2,1)S(1)} fusion(bf16[512,384]{1,0:T(8,128)(2,1)S(1)} %constant_dynamic-update-slice_fusion.2, bf16[3,384,768]{2,1,0:T(8,128)(2,1)} %collective-permute-done.12), kind=kOutput, calls=%fused_computation.24 | convolution fusion | flops 302383104 | bytes 1769472 | tf_op jit(solution)/shard_map/dot_general | solution.py:339
  147.3 1.6 %convolution_convert_fusion.3 = bf16[512,768]{1,0:T(8,128)(2,1)S(1)} fusion(bf16[512,384]{1,0:T(8,128)(2,1)S(1)} %constant_dynamic-update-slice_fusion, bf16[3,384,768]{2,1,0:T(8,128)(2,1)} %collective-permute-done.12), kind=kOutput, calls=%fused_computation.25 | convolution fusion | flops 302383104 | bytes 1769472 | tf_op jit(solution)/shard_map/dot_general | solution.py:339
  148.9 1.7 %convert_add_fusion = f32[512,768]{1,0:T(8,128)S(1)} fusion(bf16[512,768]{1,0:T(8,128)(2,1)S(1)} %convolution_convert_fusion.2, bf16[512,768]{1,0:T(8,128)(2,1)S(1)} %convolution_convert_fusion.3, bf16[512,384]{1,0:T(8,128)(2,1)S(1)} %constant_dynamic-update-slice_fusion.4, bf16[3,384,768]{2,1,0:T(8,128)(2,1)} %collective-permute-done.12), kind=kOutput, calls=%fused_computation.21 | convolution fusion | flops 304349184 | bytes 4128768 | tf_op jit(solution)/shard_map/dot_general | solution.py:339
  150.6 4.7 %fusion.12 = f32[512,1536]{1,0:T(8,128)} fusion(f32[512,768]{1,0:T(8,128)S(1)} %convert_add_fusion, f32[512,768]{1,0:T(8,128)S(1)} %convert_add_fusion.1, f32[1536]{0:T(1024)S(1)} %dynamic-slice_reduce_fusion, bf16[512,6144]{1,0:T(8,128)(2,1)} %param.10, s32[]{:T(128)S(6)} %select_n.103, pred[]{:T(512)S(6)} %eq.29, bf16[384,6144]{1,0:T(8,128)(2,1)} %param.19, ...), kind=kOutput, calls=%fused_computation.15 | convolution fusion | flops 611844096 | bytes 9444864 | tf_op jit(solution)/shard_map/dot_general | solution.py:331
  (86 shorter events, 11.6 us)
Async XLA Ops:
  0.0 14.3 %copy-start = (bf16[8,3,6144]{2,0,1:T(8,128)(2,1)S(1)}, bf16[8,3,6144]{2,0,1:T(8,128)(2,1)}, u32[]{:S(2)}) copy-start(bf16[8,3,6144]{2,0,1:T(8,128)(2,1)} %param.11) | copy-start | bytes 884740
  2.5 4.5 %copy-start.8 = (bf16[1,512,768]{2,1,0:T(8,128)(2,1)}, bf16[1,512,768]{2,1,0:T(8,128)(2,1)S(1)}, u32[]{:S(2)}) copy-start(bf16[1,512,768]{2,1,0:T(8,128)(2,1)S(1)} %reshape.85) | copy-start | bytes 2359300
  2.5 45.7 %collective-permute-start.4 = (bf16[1,512,768]{2,1,0:T(8,128)(2,1)S(1)}, bf16[1,512,768]{2,1,0:T(8,128)(2,1)S(1)}, u32[]{:S(2)}, u32[]{:S(2)}) collective-permute-start(bf16[1,512,768]{2,1,0:T(8,128)(2,1)S(1)} %reshape.85), channel_id=1, source_target_pairs={{0,24},{4,28},{8,0},{12,4},{16,8},{20,12},{24,16},{28,20},{1,25},{... | collective-permute-start | bytes 2359304 | tf_op jit(solution)/shard_map/ppermute | solution.py:14
  4.7 43.5 %collective-permute-start.3 = (bf16[1,512,768]{2,1,0:T(8,128)(2,1)S(1)}, bf16[1,512,768]{2,1,0:T(8,128)(2,1)S(1)}, u32[]{:S(2)}, u32[]{:S(2)}) collective-permute-start(bf16[1,512,768]{2,1,0:T(8,128)(2,1)S(1)} %reshape.85), channel_id=1, source_target_pairs={{0,16},{4,20},{8,24},{12,28},{16,0},{20,4},{24,8},{28,12},{1,17},{... | collective-permute-start | bytes 2359304 | tf_op jit(solution)/shard_map/ppermute | solution.py:14
  5.0 45.0 %collective-permute-start.2 = (bf16[1,512,768]{2,1,0:T(8,128)(2,1)S(1)}, bf16[1,512,768]{2,1,0:T(8,128)(2,1)}, u32[]{:S(2)}, u32[]{:S(2)}) collective-permute-start(bf16[1,512,768]{2,1,0:T(8,128)(2,1)S(1)} %reshape.85), channel_id=1, source_target_pairs={{0,8},{4,12},{8,16},{12,20},{16,24},{20,28},{24,0},{28,4},{1,9},{5... | collective-permute-start | bytes 2359304 | tf_op jit(solution)/shard_map/ppermute | solution.py:14
  8.8 4.9 %copy-start.15 = (s32[8]{0:T(128)S(1)}, s32[8]{0:T(128)}, u32[]{:S(2)}) copy-start(s32[8]{0:T(128)} %param.12) | copy-start | bytes 100
  8.8 53.9 %all-to-all-start = ((bf16[4,384,768]{2,1,0:T(8,128)(2,1)}), bf16[4,384,768]{2,1,0:T(8,128)(2,1)}, u32[]{:S(2)}, u32[]{:S(2)}) async-start(bf16[4,384,768]{2,1,0:T(8,128)(2,1)} %pad_maximum_fusion.1), calls=%async_computation | async-start | bytes 4718592 | tf_op jit(solution)/shard_map/all_to_all | solution.py:229
  32.1 0.7 copy-start.13
  32.2 0.7 copy-start.14
  34.8 30.6 %collective-permute-start = (bf16[512,768]{1,0:T(8,128)(2,1)}, bf16[512,768]{1,0:T(8,128)(2,1)}, u32[]{:S(2)}, u32[]{:S(2)}) collective-permute-start(bf16[512,768]{1,0:T(8,128)(2,1)} %get-tuple-element.58), channel_id=1, source_target_pairs={{0,4},{4,8},{8,12},{12,16},{16,20},{20,24},{24,28},{28,0},{1,5},{5... | collective-permute-start | bytes 2359304 | tf_op jit(solution)/shard_map/ppermute | solution.py:14
  38.8 26.9 %collective-permute-start.1 = (bf16[512,768]{1,0:T(8,128)(2,1)}, bf16[512,768]{1,0:T(8,128)(2,1)}, u32[]{:S(2)}, u32[]{:S(2)}) collective-permute-start(bf16[512,768]{1,0:T(8,128)(2,1)} %get-tuple-element.58), channel_id=1, source_target_pairs={{0,8},{4,12},{8,16},{12,20},{16,24},{20,28},{24,0},{28,4},{1,9},{5... | collective-permute-start | bytes 2359304 | tf_op jit(solution)/shard_map/ppermute | solution.py:14
  38.9 0.8 copy-start.6
  48.2 0.9 copy-start.9
  49.1 0.9 copy-start.10
  52.0 27.4 %copy-start.2 = (bf16[4,512,768]{2,1,0:T(8,128)(2,1)}, bf16[4,512,768]{2,1,0:T(8,128)(2,1)S(1)}, u32[]{:S(2)}) copy-start(bf16[4,512,768]{2,1,0:T(8,128)(2,1)S(1)} %pad_maximum_fusion.refs_4_.refs_5_) | copy-start | bytes 9437188
  65.7 17.3 %collective-permute-start.5 = (bf16[4,512,768]{2,1,0:T(8,128)(2,1)S(1)}, bf16[4,512,768]{2,1,0:T(8,128)(2,1)}, u32[]{:S(2)}, u32[]{:S(2)}) collective-permute-start(bf16[4,512,768]{2,1,0:T(8,128)(2,1)S(1)} %pad_maximum_fusion.refs_4_.refs_5_), channel_id=1, source_target_pairs={{0,4},{4,0},{8,12},{12,8},{16,20},{20,16},{24,28},{28,24},{1,5},{5... | collective-permute-start | bytes 9437192 | tf_op jit(solution)/shard_map/ppermute | solution.py:294
  79.5 2.8 %copy-start.7 = (bf16[512,384]{1,0:T(8,128)(2,1)S(1)}, bf16[512,384]{1,0:T(8,128)(2,1)}, u32[]{:S(2)}) copy-start(bf16[512,384]{1,0:T(8,128)(2,1)} %copy-done.6) | copy-start | bytes 1179652
  79.5 66.2 %collective-permute-start.12 = (bf16[3,384,768]{2,1,0:T(8,128)(2,1)}, bf16[3,384,768]{2,1,0:T(8,128)(2,1)}, u32[]{:S(2)}, u32[]{:S(2)}) collective-permute-start(bf16[3,384,768]{2,1,0:T(8,128)(2,1)} %pad_maximum_fusion.2), channel_id=1, source_target_pairs={{0,4},{4,0},{8,12},{12,8},{16,20},{20,16},{24,28},{28,24},{1,5},{5... | collective-permute-start | bytes 5308424 | tf_op jit(solution)/shard_map/ppermute | solution.py:317
  99.7 21.9 %collective-permute-start.8 = (bf16[256,384]{1,0:T(8,128)(2,1)}, bf16[256,384]{1,0:T(8,128)(2,1)S(1)}, u32[]{:S(2)}, u32[]{:S(2)}) collective-permute-start(bf16[256,384]{1,0:T(8,128)(2,1)} %shard_map.102), channel_id=1, source_target_pairs={{0,2},{1,3},{2,0},{3,1},{4,6},{5,7},{6,4},{7,5},{8,10},{9,11},{10,... | collective-permute-start | bytes 589832 | tf_op jit(solution)/shard_map/ppermute | solution.py:323
  102.0 20.7 %collective-permute-start.6 = (bf16[256,384]{1,0:T(8,128)(2,1)}, bf16[256,384]{1,0:T(8,128)(2,1)S(1)}, u32[]{:S(2)}, u32[]{:S(2)}) collective-permute-start(bf16[256,384]{1,0:T(8,128)(2,1)} %shard_map.102), channel_id=1, source_target_pairs={{0,1},{1,2},{2,3},{3,0},{4,5},{5,6},{6,7},{7,4},{8,9},{9,10},{10,1... | collective-permute-start | bytes 589832 | tf_op jit(solution)/shard_map/ppermute | solution.py:323
  102.1 19.6 %copy-start.11 = (bf16[256,384]{1,0:T(8,128)(2,1)S(1)}, bf16[256,384]{1,0:T(8,128)(2,1)}, u32[]{:S(2)}) copy-start(bf16[256,384]{1,0:T(8,128)(2,1)} %shard_map.102) | copy-start | bytes 589828
  118.9 24.9 %copy-start.4 = (bf16[384,768]{1,0:T(8,128)(2,1)S(1)}, bf16[384,768]{1,0:T(8,128)(2,1)}, u32[]{:S(2)}) copy-start(bf16[384,768]{1,0:T(8,128)(2,1)} %get-tuple-element.41) | copy-start | bytes 1769476
  118.9 25.5 %copy-start.3 = (bf16[384,768]{1,0:T(8,128)(2,1)S(1)}, bf16[384,768]{1,0:T(8,128)(2,1)}, u32[]{:S(2)}) copy-start(bf16[384,768]{1,0:T(8,128)(2,1)} %get-tuple-element.40) | copy-start | bytes 1769476
  118.9 20.7 %collective-permute-start.9 = (bf16[256,384]{1,0:T(8,128)(2,1)}, bf16[256,384]{1,0:T(8,128)(2,1)S(1)}, u32[]{:S(2)}, u32[]{:S(2)}) collective-permute-start(bf16[256,384]{1,0:T(8,128)(2,1)} %shard_map.103), channel_id=1, source_target_pairs={{0,2},{1,3},{2,0},{3,1},{4,6},{5,7},{6,4},{7,5},{8,10},{9,11},{10,... | collective-permute-start | bytes 589832 | tf_op jit(solution)/shard_map/ppermute | solution.py:323
  121.3 20.8 %collective-permute-start.7 = (bf16[256,384]{1,0:T(8,128)(2,1)}, bf16[256,384]{1,0:T(8,128)(2,1)S(1)}, u32[]{:S(2)}, u32[]{:S(2)}) collective-permute-start(bf16[256,384]{1,0:T(8,128)(2,1)} %shard_map.103), channel_id=1, source_target_pairs={{0,1},{1,2},{2,3},{3,0},{4,5},{5,6},{6,7},{7,4},{8,9},{9,10},{10,1... | collective-permute-start | bytes 589832 | tf_op jit(solution)/shard_map/ppermute | solution.py:323
  121.7 18.0 %collective-permute-start.10 = (bf16[256,384]{1,0:T(8,128)(2,1)S(1)}, bf16[256,384]{1,0:T(8,128)(2,1)S(1)}, u32[]{:S(2)}, u32[]{:S(2)}) collective-permute-start(bf16[256,384]{1,0:T(8,128)(2,1)S(1)} %copy-done.11), channel_id=1, source_target_pairs={{0,3},{1,0},{2,1},{3,2},{4,7},{5,4},{6,5},{7,6},{8,11},{9,8},{10,9... | collective-permute-start | bytes 589832 | tf_op jit(solution)/shard_map/ppermute | solution.py:323
  122.8 21.1 %collective-permute-start.11 = (bf16[256,384]{1,0:T(8,128)(2,1)}, bf16[256,384]{1,0:T(8,128)(2,1)S(1)}, u32[]{:S(2)}, u32[]{:S(2)}) collective-permute-start(bf16[256,384]{1,0:T(8,128)(2,1)} %shard_map.103), channel_id=1, source_target_pairs={{0,3},{1,0},{2,1},{3,2},{4,7},{5,4},{6,5},{7,6},{8,11},{9,8},{10,9... | collective-permute-start | bytes 589832 | tf_op jit(solution)/shard_map/ppermute | solution.py:323
  139.7 5.4 %copy-start.5 = (bf16[384,768]{1,0:T(8,128)(2,1)S(1)}, bf16[384,768]{1,0:T(8,128)(2,1)}, u32[]{:S(2)}) copy-start(bf16[384,768]{1,0:T(8,128)(2,1)} %get-tuple-element.42) | copy-start | bytes 1769476
  148.9 1.7 %copy-start.12 = (bf16[256,384]{1,0:T(8,128)(2,1)S(1)}, bf16[256,384]{1,0:T(8,128)(2,1)}, u32[]{:S(2)}) copy-start(bf16[256,384]{1,0:T(8,128)(2,1)} %shard_map.103) | copy-start | bytes 589828
  150.6 4.7 %copy-start.1 = (bf16[8,3,6144]{2,0,1:T(8,128)(2,1)S(1)}, bf16[8,3,6144]{2,0,1:T(8,128)(2,1)}, u32[]{:S(2)}) copy-start(bf16[8,3,6144]{2,0,1:T(8,128)(2,1)} %param.11) | copy-start | bytes 884740

commit v18 on v17

--- a/solution.py
+++ b/solution.py
@@ -259,8 +259,12 @@
     own_full, mine = fetch_out_weight(w_out, head, core)
     slots = lax.axis_size("slot")
     pool_flat = pool_kv.reshape(1, pool_kv.shape[1], -1)
-    same_core = [pool_flat] + [from_behind(pool_flat, "slot", 2 * k) for k in range(1, slots // 2)]
-    same_core = jnp.concatenate(same_core, axis=0)
+    same_core = pool_flat
+    bit = 2
+    while bit < slots:
+        partner = lax.ppermute(same_core, "slot", [(i, i ^ bit) for i in range(slots)])
+        same_core = jnp.concatenate([same_core, partner], axis=0)
+        bit *= 2
 
     onehot = (jnp.arange(mod_table.shape[0], dtype=jnp.int32) == step_index[slot]).astype(
         jnp.float32
@@ -297,8 +301,8 @@
     sibling_slot = jnp.bitwise_xor(slot, 1)
     own_cache = jnp.where(
         own_cache % 2 == core,
-        ((slot - own_cache) % slots) // 2,
-        slots // 2 + ((sibling_slot - own_cache) % slots) // 2,
+        jnp.bitwise_xor(own_cache, slot) // 2,
+        slots // 2 + jnp.bitwise_xor(own_cache, sibling_slot) // 2,
     ).astype(jnp.int32)
     width = heads * HD
     local_stack = jnp.stack([before, earlier]).reshape(2, span, 2 * width)

time: 156 us -> 182 us (1.17)
  waiting for transfers between devices: 30.6 us -> 63.6 us
  starting transfers between devices: 27.1 us -> 20.5 us
    ppermute x0 -> x2, waiting for transfers between devices: none -> 44.2 us  [local(): lax.ppermute(same_core, 'slot', [(i, i ^ bit) for i in range(slots)])]
    all_to_all x1, waiting for transfers between devices: 10.7 us -> 0.01 us  [fetch_out_weight(): exchanged = lax.all_to_all(blocks, 'head', 0, 0)]
    ppermute x1, starting transfers between devices: 7.92 us -> 2.5 us  [local(): lax.ppermute(same_core, 'slot', [(i, i ^ 1) for i in range(slots)])]
    ppermute x5 -> x2, starting transfers between devices: 6.83 us -> 3.09 us  [from_behind(): lax.ppermute(shard, axis, [(i, (i + by) % length) for i in range(length)])]
    ppermute x0 -> x2, starting transfers between devices: none -> 2.58 us  [local(): lax.ppermute(same_core, 'slot', [(i, i ^ bit) for i in range(slots)])]
  transfers between devices with their start and end apart: 14 -> 13, of which waited for: 5 -> 4; matrix products, arithmetic and copies ran while one was open for 27% -> 24% of each run, Pallas kernels for 26% -> 22%
where the time goes in v18:
time: 182 us
  waiting for transfers between devices  63.6 us (35%)
  Pallas kernels  40.6 us (22%)
  matrix products  25 us (14%)
  starting transfers between devices  20.5 us (11%)
  other arithmetic  17.5 us (10%)
  local copies, waits for them, and re-layouts  13.9 us (8%)
    ppermute x2, waiting for transfers between devices, local(): lax.ppermute(same_core, 'slot', [(i, i ^ bit) for i in range(slots)])  44.2 us
    pallas_call x2, Pallas kernels, flash(): pl.pallas_call(kernel, grid_spec=grid_spec, out_shape=jax.ShapeDtypeStruc...  33.5 us
    ppermute x6, waiting for transfers between devices, local(): lax.ppermute(part, 'head', [(i, (i + shift) % groups) for i in range(grou...  19.4 us
    dot_general x1, matrix products, local(): jnp.einsum('td,dkh->kth', hidden, w_qkv, preferred_element_type=jnp.float32)  12.8 us
    ppermute x6, starting transfers between devices, local(): lax.ppermute(part, 'head', [(i, (i + shift) % groups) for i in range(grou...  7.43 us
    pallas_call x2, Pallas kernels, flash_local(): pl.pallas_call(kernel, grid=(steps,), in_specs=[pl.BlockSpec((span, width...  7.14 us
    dot_general x3, matrix products, local(): jnp.dot(group_o, sibling[shift - 1], preferred_element_type=jnp.float32)  4.93 us
    all_to_all x1, starting transfers between devices, fetch_out_weight(): exchanged = lax.all_to_all(blocks, 'head', 0, 0)  4.89 us
  transfers between devices with their start and end apart: 13, of which 4 were waited for; matrix products, arithmetic and copies ran while one was open for 24% of the time, Pallas kernels for 22%

profile of v18, /device:TPU:9, one launch (start us, length us, event | category | flops | bytes accessed | tf_op | source)
XLA Modules:
  0.0 181.5 jit_solution(13464830762924860271)
XLA Ops:
  0.0 2.5 %reshape.85 = bf16[1,512,768]{2,1,0:T(8,128)(2,1)S(1)} reshape(bf16[1,512,2,384]{3,2,1,0:T(2,128)(2,1)} %param.18) | data formatting | bytes 1572864 | tf_op jit(solution)/shard_map/reshape | solution.py:261
  2.5 1.3 collective-permute-start.2
  3.8 1.8 dynamic-slice_bitcast_fusion.6
  5.5 1.7 pad_maximum_fusion.1
  7.3 4.9 %all-to-all-start = ((bf16[4,384,768]{2,1,0:T(8,128)(2,1)}), bf16[4,384,768]{2,1,0:T(8,128)(2,1)}, u32[]{:S(2)}, u32[]{:S(2)}) async-start(bf16[4,384,768]{2,1,0:T(8,128)(2,1)} %pad_maximum_fusion.1), calls=%async_computation | async-start | bytes 4718592 | tf_op jit(solution)/shard_map/all_to_all | solution.py:229
  13.7 4.1 %fusion = f32[512]{0:T(512)S(1)} fusion(bf16[512,6144]{1,0:T(8,128)(2,1)} %param.10), kind=kLoop, calls=%fused_computation.2 | loop fusion | flops 9436672 | bytes 6293504 | tf_op jit(solution)/shard_map/reduce_sum | solution.py:274
  17.8 12.8 %fusion.13 = f32[3,512,384]{2,1,0:T(8,128)S(1)} fusion(bf16[6144,3,384]{2,0,1:T(8,128)(2,1)} %param.15, bf16[512,6144]{1,0:T(8,128)(2,1)} %param.10, f32[6144]{0:T(1024)S(1)} %bitcast.75, f32[6144]{0:T(1024)S(1)} %bitcast.76, f32[512]{0:T(512)S(1)} %add_rsqrt_fusion.6), kind=kOutput, calls=%fused_computation.19 | convolution fusion | flops 7263485952 | bytes 22857728 | tf_op jit(solution)/shard_map/td,dkh->kth/dot_general | solution.py:277
  31.8 1.3 collective-permute-start.3
  33.7 1.2 pad_maximum_fusion.5
  35.0 1.9 %collective-permute-start = (bf16[512,768]{1,0:T(8,128)(2,1)}, bf16[512,768]{1,0:T(8,128)(2,1)}, u32[]{:S(2)}, u32[]{:S(2)}) collective-permute-start(bf16[512,768]{1,0:T(8,128)(2,1)} %get-tuple-element.58), channel_id=1, source_target_pairs={{0,4},{4,8},{8,12},{12,16},{16,20},{20,24},{24,28},{28,0},{1,5},{5... | collective-permute-start | bytes 2359304 | tf_op jit(solution)/shard_map/ppermute | solution.py:14
  40.3 3.6 %shard_map.100 = (f32[3,256,1]{2,1,0:T(8,128)}, f32[3,256,1]{2,1,0:T(8,128)}, f32[3,256,128]{2,1,0:T(8,128)}) custom-call(bf16[256,384]{1,0:T(8,128)(2,1)} %get-tuple-element.69.refs_0_, bf16[1,512,768]{2,1,0:T(8,128)(2,1)} %get-tuple-element.59.refs_1_.refs_2_, bf16[1,512,768]{2,1,0:T(8,128)(2,1)} %get-tuple-element.59.refs_1_.refs_2_, ...), custom_call_target="tpu_custom_call" | custom-call | flops 201326592 | bytes 786432 | tf_op jit(solution)/shard_map/pallas_call | solution.py:89
  43.9 3.6 %shard_map.101 = (f32[3,256,1]{2,1,0:T(8,128)}, f32[3,256,1]{2,1,0:T(8,128)}, f32[3,256,128]{2,1,0:T(8,128)}) custom-call(bf16[256,384]{1,0:T(8,128)(2,1)} %get-tuple-element.68.refs_0_, bf16[1,512,768]{2,1,0:T(8,128)(2,1)} %get-tuple-element.59.refs_1_.refs_2_, bf16[1,512,768]{2,1,0:T(8,128)(2,1)} %get-tuple-element.59.refs_1_.refs_2_, ...), custom_call_target="tpu_custom_call" | custom-call | flops 201326592 | bytes 786432 | tf_op jit(solution)/shard_map/pallas_call | solution.py:89
  47.5 44.2 %collective-permute-done.3 = bf16[2,512,768]{2,1,0:T(8,128)(2,1)} collective-permute-done((bf16[2,512,768]{2,1,0:T(8,128)(2,1)S(1)}, bf16[2,512,768]{2,1,0:T(8,128)(2,1)}, u32[]{:S(2)}, u32[]{:S(2)}) %collective-permute-start.3) | collective-permute-done | bytes 1572896 | tf_op jit(solution)/shard_map/ppermute | solution.py:265
  91.7 2.1 %pad_maximum_fusion.refs_4_.refs_5_ = bf16[4,512,768]{2,1,0:T(8,128)(2,1)S(1)} fusion(bf16[2,512,768]{2,1,0:T(8,128)(2,1)} %collective-permute-done.3, bf16[1,512,768]{2,1,0:T(8,128)(2,1)} %copy-done.9, bf16[1,512,768]{2,1,0:T(8,128)(2,1)} %copy-done.3), kind=kLoop, calls=%fused_computation.11 | loop fusion | flops 3145728 | bytes 6291456 | tf_op jit(solution)/shard_map/concatenate | solution.py:266
  93.8 3.8 %dynamic-slice_bitcast_fusion = (bf16[384,768]{1,0:T(8,128)(2,1)}, bf16[384,768]{1,0:T(8,128)(2,1)}, bf16[384,768]{1,0:T(8,128)(2,1)}) fusion(bf16[4,384,768]{2,1,0:T(8,128)(2,1)} %all-to-all-done, s32[]{:T(128)S(6)} %select_n.111, s32[]{:T(128)S(6)} %select_n.109, s32[]{:T(128)S(6)} %select_n.107), kind=kLoop, calls=%fused_computation.38 | loop fusion | bytes 3538956 | tf_op jit(solution)/shard_map/jit(dynamic_index_in_dim)/squeeze | solution.py:231
  97.7 2.5 %collective-permute-start.4 = (bf16[4,512,768]{2,1,0:T(8,128)(2,1)S(1)}, bf16[4,512,768]{2,1,0:T(8,128)(2,1)}, u32[]{:S(2)}, u32[]{:S(2)}) collective-permute-start(bf16[4,512,768]{2,1,0:T(8,128)(2,1)S(1)} %pad_maximum_fusion.refs_4_.refs_5_), channel_id=1, source_target_pairs={{0,4},{4,0},{8,12},{12,8},{16,20},{20,16},{24,28},{28,24},{1,5},{5... | collective-permute-start | bytes 9437192 | tf_op jit(solution)/shard_map/ppermute | solution.py:298
  101.2 1.3 compare_select_fusion.2.refs_0_
  103.1 2.9 %pad_maximum_fusion.2 = bf16[3,384,768]{2,1,0:T(8,128)(2,1)} fusion(bf16[1,384,768]{2,1,0:T(8,128)(2,1)} %bitcast.72, bf16[1,384,768]{2,1,0:T(8,128)(2,1)} %bitcast.71, bf16[1,384,768]{2,1,0:T(8,128)(2,1)} %bitcast.70), kind=kLoop, calls=%fused_computation.18 | loop fusion | flops 1769472 | bytes 3538944 | tf_op jit(solution)/shard_map/stack | solution.py:322
  106.0 2.7 %pad_maximum_fusion.4.refs_2_.refs_3_ = bf16[2,512,768]{2,1,0:T(8,128)(2,1)} fusion(bf16[1,512,768]{2,1,0:T(8,128)(2,1)} %bitcast.20, bf16[1,512,768]{2,1,0:T(8,128)(2,1)} %bitcast.19), kind=kLoop, calls=%fused_computation.21 | loop fusion | flops 786432 | bytes 3145728 | tf_op jit(solution)/shard_map/stack | solution.py:308
  109.5 16.7 %shard_map.102 = bf16[256,384]{1,0:T(8,128)(2,1)} custom-call(s32[6]{0:T(128)} %compare_select_fusion.2.refs_0_, bf16[256,384]{1,0:T(8,128)(2,1)} %get-tuple-element.67.refs_1_, bf16[2,512,768]{2,1,0:T(8,128)(2,1)} %pad_maximum_fusion.4.refs_2_.refs_3_, bf16[2,512,768]{2,1,0:T(8,128)(2,1)} %pad_maximum_fusion.4.refs_2_.refs_3_, ...), custom_call_target="tpu_custom_call" | custom-call | flops 805306368 | bytes 3145728 | tf_op jit(solution)/shard_map/pallas_call | solution.py:208
  126.2 2.1 %collective-permute-start.7 = (bf16[256,384]{1,0:T(8,128)(2,1)}, bf16[256,384]{1,0:T(8,128)(2,1)S(1)}, u32[]{:S(2)}, u32[]{:S(2)}) collective-permute-start(bf16[256,384]{1,0:T(8,128)(2,1)} %shard_map.102), channel_id=1, source_target_pairs={{0,2},{1,3},{2,0},{3,1},{4,6},{5,7},{6,4},{7,5},{8,10},{9,11},{10,... | collective-permute-start | bytes 589832 | tf_op jit(solution)/shard_map/ppermute | solution.py:327
  128.3 16.8 %shard_map.103 = bf16[256,384]{1,0:T(8,128)(2,1)} custom-call(s32[6]{0:T(128)} %compare_select_fusion.2.refs_0_, bf16[256,384]{1,0:T(8,128)(2,1)} %get-tuple-element.66.refs_1_, bf16[2,512,768]{2,1,0:T(8,128)(2,1)} %pad_maximum_fusion.4.refs_2_.refs_3_, bf16[2,512,768]{2,1,0:T(8,128)(2,1)} %pad_maximum_fusion.4.refs_2_.refs_3_, ...), custom_call_target="tpu_custom_call" | custom-call | flops 805306368 | bytes 3145728 | tf_op jit(solution)/shard_map/pallas_call | solution.py:208
  145.2 2.4 %collective-permute-start.8 = (bf16[256,384]{1,0:T(8,128)(2,1)}, bf16[256,384]{1,0:T(8,128)(2,1)S(1)}, u32[]{:S(2)}, u32[]{:S(2)}) collective-permute-start(bf16[256,384]{1,0:T(8,128)(2,1)} %shard_map.103), channel_id=1, source_target_pairs={{0,2},{1,3},{2,0},{3,1},{4,6},{5,7},{6,4},{7,5},{8,10},{9,11},{10,... | collective-permute-start | bytes 589832 | tf_op jit(solution)/shard_map/ppermute | solution.py:327
  147.9 1.2 collective-permute-start.9
  149.1 1.5 collective-permute-start.10
  150.6 15.3 %collective-permute-done.9 = bf16[256,384]{1,0:T(8,128)(2,1)S(1)} collective-permute-done((bf16[256,384]{1,0:T(8,128)(2,1)S(1)}, bf16[256,384]{1,0:T(8,128)(2,1)S(1)}, u32[]{:S(2)}, u32[]{:S(2)}) %collective-permute-start.9) | collective-permute-done | bytes 196640 | tf_op jit(solution)/shard_map/ppermute | solution.py:327
  165.9 2.6 %collective-permute-done.6 = bf16[256,384]{1,0:T(8,128)(2,1)S(1)} collective-permute-done((bf16[256,384]{1,0:T(8,128)(2,1)}, bf16[256,384]{1,0:T(8,128)(2,1)S(1)}, u32[]{:S(2)}, u32[]{:S(2)}) %collective-permute-start.6) | collective-permute-done | bytes 196640 | tf_op jit(solution)/shard_map/ppermute | solution.py:327
  168.5 1.5 collective-permute-done.10
  171.9 1.6 convolution_convert_fusion.2
  173.5 1.6 convolution_convert_fusion.3
  175.1 1.7 convert_add_fusion
  176.8 4.7 %fusion.12 = f32[512,1536]{1,0:T(8,128)} fusion(f32[512,768]{1,0:T(8,128)S(1)} %convert_add_fusion, f32[512,768]{1,0:T(8,128)S(1)} %convert_add_fusion.1, f32[1536]{0:T(1024)S(1)} %dynamic-slice_reduce_fusion, bf16[512,6144]{1,0:T(8,128)(2,1)} %param.10, s32[]{:T(128)S(6)} %select_n.95, pred[]{:T(512)S(6)} %eq.27, bf16[384,6144]{1,0:T(8,128)(2,1)} %param.19, ...), kind=kOutput, calls=%fused_computation.15 | convolution fusion | flops 611844096 | bytes 9444864 | tf_op jit(solution)/shard_map/dot_general | solution.py:335
  (83 shorter events, 11.3 us)
Async XLA Ops:
  0.0 12.7 %copy-start = (bf16[8,3,6144]{2,0,1:T(8,128)(2,1)S(1)}, bf16[8,3,6144]{2,0,1:T(8,128)(2,1)}, u32[]{:S(2)}) copy-start(bf16[8,3,6144]{2,0,1:T(8,128)(2,1)} %param.11) | copy-start | bytes 884740
  2.5 29.2 %copy-start.3 = (bf16[1,512,768]{2,1,0:T(8,128)(2,1)}, bf16[1,512,768]{2,1,0:T(8,128)(2,1)S(1)}, u32[]{:S(2)}) copy-start(bf16[1,512,768]{2,1,0:T(8,128)(2,1)S(1)} %reshape.85) | copy-start | bytes 2359300
  2.5 29.1 %collective-permute-start.2 = (bf16[1,512,768]{2,1,0:T(8,128)(2,1)S(1)}, bf16[1,512,768]{2,1,0:T(8,128)(2,1)S(1)}, u32[]{:S(2)}, u32[]{:S(2)}) collective-permute-start(bf16[1,512,768]{2,1,0:T(8,128)(2,1)S(1)} %reshape.85), channel_id=1, source_target_pairs={{0,8},{4,12},{8,0},{12,4},{16,24},{20,28},{24,16},{28,20},{1,9},{5... | collective-permute-start | bytes 2359304 | tf_op jit(solution)/shard_map/ppermute | solution.py:265
  7.3 4.9 %copy-start.14 = (s32[8]{0:T(128)S(1)}, s32[8]{0:T(128)}, u32[]{:S(2)}) copy-start(s32[8]{0:T(128)} %param.12) | copy-start | bytes 100
  7.3 86.6 %all-to-all-start = ((bf16[4,384,768]{2,1,0:T(8,128)(2,1)}), bf16[4,384,768]{2,1,0:T(8,128)(2,1)}, u32[]{:S(2)}, u32[]{:S(2)}) async-start(bf16[4,384,768]{2,1,0:T(8,128)(2,1)} %pad_maximum_fusion.1), calls=%async_computation | async-start | bytes 4718592 | tf_op jit(solution)/shard_map/all_to_all | solution.py:229
  30.6 0.7 copy-start.12
  30.8 2.4 %copy-start.13 = (f32[384]{0:T(512)S(1)}, f32[384]{0:T(512)}, u32[]{:S(2)}) copy-start(f32[384]{0:T(512)} %param.16) | copy-start | bytes 4612
  31.7 2.0 %copy-start.9 = (bf16[1,512,768]{2,1,0:T(8,128)(2,1)}, bf16[1,512,768]{2,1,0:T(8,128)(2,1)S(1)}, u32[]{:S(2)}) copy-start(bf16[1,512,768]{2,1,0:T(8,128)(2,1)S(1)} %collective-permute-done.2) | copy-start | bytes 2359300
  31.8 59.8 %collective-permute-start.3 = (bf16[2,512,768]{2,1,0:T(8,128)(2,1)S(1)}, bf16[2,512,768]{2,1,0:T(8,128)(2,1)}, u32[]{:S(2)}, u32[]{:S(2)}) collective-permute-start(bf16[2,512,768]{2,1,0:T(8,128)(2,1)S(1)} %pad_maximum_fusion.3), channel_id=1, source_target_pairs={{0,16},{4,20},{8,24},{12,28},{16,0},{20,4},{24,8},{28,12},{1,17},{... | collective-permute-start | bytes 4718600 | tf_op jit(solution)/shard_map/ppermute | solution.py:265
  35.0 62.7 %collective-permute-start = (bf16[512,768]{1,0:T(8,128)(2,1)}, bf16[512,768]{1,0:T(8,128)(2,1)}, u32[]{:S(2)}, u32[]{:S(2)}) collective-permute-start(bf16[512,768]{1,0:T(8,128)(2,1)} %get-tuple-element.58), channel_id=1, source_target_pairs={{0,4},{4,8},{8,12},{12,16},{16,20},{20,24},{24,28},{28,0},{1,5},{5... | collective-permute-start | bytes 2359304 | tf_op jit(solution)/shard_map/ppermute | solution.py:14
  36.9 60.7 %collective-permute-start.1 = (bf16[512,768]{1,0:T(8,128)(2,1)}, bf16[512,768]{1,0:T(8,128)(2,1)}, u32[]{:S(2)}, u32[]{:S(2)}) collective-permute-start(bf16[512,768]{1,0:T(8,128)(2,1)} %get-tuple-element.58), channel_id=1, source_target_pairs={{0,8},{4,12},{8,16},{12,20},{16,24},{20,28},{24,0},{28,4},{1,9},{5... | collective-permute-start | bytes 2359304 | tf_op jit(solution)/shard_map/ppermute | solution.py:14
  38.1 0.8 copy-start.7
  93.8 12.2 %copy-start.2 = (bf16[4,512,768]{2,1,0:T(8,128)(2,1)}, bf16[4,512,768]{2,1,0:T(8,128)(2,1)S(1)}, u32[]{:S(2)}) copy-start(bf16[4,512,768]{2,1,0:T(8,128)(2,1)S(1)} %pad_maximum_fusion.refs_4_.refs_5_) | copy-start | bytes 9437188
  97.7 11.9 %collective-permute-start.4 = (bf16[4,512,768]{2,1,0:T(8,128)(2,1)S(1)}, bf16[4,512,768]{2,1,0:T(8,128)(2,1)}, u32[]{:S(2)}, u32[]{:S(2)}) collective-permute-start(bf16[4,512,768]{2,1,0:T(8,128)(2,1)S(1)} %pad_maximum_fusion.refs_4_.refs_5_), channel_id=1, source_target_pairs={{0,4},{4,0},{8,12},{12,8},{16,20},{20,16},{24,28},{28,24},{1,5},{5... | collective-permute-start | bytes 9437192 | tf_op jit(solution)/shard_map/ppermute | solution.py:298
  106.0 2.8 %copy-start.8 = (bf16[512,384]{1,0:T(8,128)(2,1)S(1)}, bf16[512,384]{1,0:T(8,128)(2,1)}, u32[]{:S(2)}) copy-start(bf16[512,384]{1,0:T(8,128)(2,1)} %copy-done.7) | copy-start | bytes 1179652
  106.0 65.9 %collective-permute-start.11 = (bf16[3,384,768]{2,1,0:T(8,128)(2,1)}, bf16[3,384,768]{2,1,0:T(8,128)(2,1)}, u32[]{:S(2)}, u32[]{:S(2)}) collective-permute-start(bf16[3,384,768]{2,1,0:T(8,128)(2,1)} %pad_maximum_fusion.2), channel_id=1, source_target_pairs={{0,4},{4,0},{8,12},{12,8},{16,20},{20,16},{24,28},{28,24},{1,5},{5... | collective-permute-start | bytes 5308424 | tf_op jit(solution)/shard_map/ppermute | solution.py:321
  126.2 21.7 %collective-permute-start.7 = (bf16[256,384]{1,0:T(8,128)(2,1)}, bf16[256,384]{1,0:T(8,128)(2,1)S(1)}, u32[]{:S(2)}, u32[]{:S(2)}) collective-permute-start(bf16[256,384]{1,0:T(8,128)(2,1)} %shard_map.102), channel_id=1, source_target_pairs={{0,2},{1,3},{2,0},{3,1},{4,6},{5,7},{6,4},{7,5},{8,10},{9,11},{10,... | collective-permute-start | bytes 589832 | tf_op jit(solution)/shard_map/ppermute | solution.py:327
  128.3 20.8 %collective-permute-start.5 = (bf16[256,384]{1,0:T(8,128)(2,1)}, bf16[256,384]{1,0:T(8,128)(2,1)S(1)}, u32[]{:S(2)}, u32[]{:S(2)}) collective-permute-start(bf16[256,384]{1,0:T(8,128)(2,1)} %shard_map.102), channel_id=1, source_target_pairs={{0,1},{1,2},{2,3},{3,0},{4,5},{5,6},{6,7},{7,4},{8,9},{9,10},{10,1... | collective-permute-start | bytes 589832 | tf_op jit(solution)/shard_map/ppermute | solution.py:327
  128.3 19.5 %copy-start.10 = (bf16[256,384]{1,0:T(8,128)(2,1)S(1)}, bf16[256,384]{1,0:T(8,128)(2,1)}, u32[]{:S(2)}) copy-start(bf16[256,384]{1,0:T(8,128)(2,1)} %shard_map.102) | copy-start | bytes 589828
  145.2 24.9 %copy-start.5 = (bf16[384,768]{1,0:T(8,128)(2,1)S(1)}, bf16[384,768]{1,0:T(8,128)(2,1)}, u32[]{:S(2)}) copy-start(bf16[384,768]{1,0:T(8,128)(2,1)} %get-tuple-element.41) | copy-start | bytes 1769476
  145.2 25.5 %copy-start.4 = (bf16[384,768]{1,0:T(8,128)(2,1)S(1)}, bf16[384,768]{1,0:T(8,128)(2,1)}, u32[]{:S(2)}) copy-start(bf16[384,768]{1,0:T(8,128)(2,1)} %get-tuple-element.40) | copy-start | bytes 1769476
  145.2 20.7 %collective-permute-start.8 = (bf16[256,384]{1,0:T(8,128)(2,1)}, bf16[256,384]{1,0:T(8,128)(2,1)S(1)}, u32[]{:S(2)}, u32[]{:S(2)}) collective-permute-start(bf16[256,384]{1,0:T(8,128)(2,1)} %shard_map.103), channel_id=1, source_target_pairs={{0,2},{1,3},{2,0},{3,1},{4,6},{5,7},{6,4},{7,5},{8,10},{9,11},{10,... | collective-permute-start | bytes 589832 | tf_op jit(solution)/shard_map/ppermute | solution.py:327
  147.6 20.9 %collective-permute-start.6 = (bf16[256,384]{1,0:T(8,128)(2,1)}, bf16[256,384]{1,0:T(8,128)(2,1)S(1)}, u32[]{:S(2)}, u32[]{:S(2)}) collective-permute-start(bf16[256,384]{1,0:T(8,128)(2,1)} %shard_map.103), channel_id=1, source_target_pairs={{0,1},{1,2},{2,3},{3,0},{4,5},{5,6},{6,7},{7,4},{8,9},{9,10},{10,1... | collective-permute-start | bytes 589832 | tf_op jit(solution)/shard_map/ppermute | solution.py:327
  147.9 18.0 %collective-permute-start.9 = (bf16[256,384]{1,0:T(8,128)(2,1)S(1)}, bf16[256,384]{1,0:T(8,128)(2,1)S(1)}, u32[]{:S(2)}, u32[]{:S(2)}) collective-permute-start(bf16[256,384]{1,0:T(8,128)(2,1)S(1)} %copy-done.10), channel_id=1, source_target_pairs={{0,3},{1,0},{2,1},{3,2},{4,7},{5,4},{6,5},{7,6},{8,11},{9,8},{10,9... | collective-permute-start | bytes 589832 | tf_op jit(solution)/shard_map/ppermute | solution.py:327
  149.1 21.0 %collective-permute-start.10 = (bf16[256,384]{1,0:T(8,128)(2,1)}, bf16[256,384]{1,0:T(8,128)(2,1)S(1)}, u32[]{:S(2)}, u32[]{:S(2)}) collective-permute-start(bf16[256,384]{1,0:T(8,128)(2,1)} %shard_map.103), channel_id=1, source_target_pairs={{0,3},{1,0},{2,1},{3,2},{4,7},{5,4},{6,5},{7,6},{8,11},{9,8},{10,9... | collective-permute-start | bytes 589832 | tf_op jit(solution)/shard_map/ppermute | solution.py:327
  165.9 5.4 %copy-start.6 = (bf16[384,768]{1,0:T(8,128)(2,1)S(1)}, bf16[384,768]{1,0:T(8,128)(2,1)}, u32[]{:S(2)}) copy-start(bf16[384,768]{1,0:T(8,128)(2,1)} %get-tuple-element.42) | copy-start | bytes 1769476
  175.1 1.7 copy-start.11
  176.8 4.7 %copy-start.1 = (bf16[8,3,6144]{2,0,1:T(8,128)(2,1)S(1)}, bf16[8,3,6144]{2,0,1:T(8,128)(2,1)}, u32[]{:S(2)}) copy-start(bf16[8,3,6144]{2,0,1:T(8,128)(2,1)} %param.11) | copy-start | bytes 884740

commit v19 on v17

--- a/solution.py
+++ b/solution.py
@@ -227,10 +227,7 @@
         for dest in range(groups)
     ])
     exchanged = lax.all_to_all(blocks, "head", 0, 0)
-    mine = [
-        lax.dynamic_index_in_dim(exchanged, (head - shift) % groups, 0, keepdims=False)
-        for shift in range(groups)
-    ]
+    mine = exchanged
     own_full = lax.dynamic_slice_in_dim(w_out, head * columns, columns, 1)
     return own_full, mine
 
@@ -315,7 +312,7 @@
         for p in range(2)
     ]
     sibling = lax.ppermute(
-        jnp.stack(mine[1:]), "slot", [(i, i ^ 1) for i in range(slots)]
+        mine, "slot", [(i, i ^ 1) for i in range(slots)]
     )
 
     received = [
@@ -333,10 +330,13 @@
     attn_sib = None
     for shift in range(1, groups):
         group_o = received[shift - 1]
-        part = jnp.dot(group_o, mine[shift], preferred_element_type=jnp.float32)
+        group = (head - shift) % groups
+        mine_block = lax.dynamic_index_in_dim(mine, group, 0, keepdims=False)
+        part = jnp.dot(group_o, mine_block, preferred_element_type=jnp.float32)
         part = part.astype(jnp.bfloat16).astype(jnp.float32)
         attn_mine = part if attn_mine is None else attn_mine + part
-        part = jnp.dot(group_o, sibling[shift - 1], preferred_element_type=jnp.float32)
+        sibling_block = lax.dynamic_index_in_dim(sibling, group, 0, keepdims=False)
+        part = jnp.dot(group_o, sibling_block, preferred_element_type=jnp.float32)
         part = part.astype(jnp.bfloat16).astype(jnp.float32)
         attn_sib = part if attn_sib is None else attn_sib + part
     other = jnp.concatenate([attn_mine, attn_sib], axis=1)

time: 156 us -> 154 us (0.987)
  starting transfers between devices: 27.1 us -> 23.3 us
  matrix products: 25 us -> 28.2 us
  other arithmetic: 17.3 us -> 14.4 us
  waiting for transfers between devices: 30.6 us -> 33.4 us
  local copies, waits for them, and re-layouts: 14.2 us -> 12.5 us
    ppermute x5, waiting for transfers between devices: 0.35 us -> 13.8 us  [from_behind(): lax.ppermute(shard, axis, [(i, (i + by) % length) for i in range(length)])]
    all_to_all x1, waiting for transfers between devices: 10.7 us -> 0.01 us  [fetch_out_weight(): exchanged = lax.all_to_all(blocks, 'head', 0, 0)]
    ppermute x1, starting transfers between devices: 7.92 us -> 4.11 us  [local(): lax.ppermute(same_core, 'slot', [(i, i ^ 1) for i in range(slots)])]
    dot_general x6, matrix products: 6.64 us -> 9.86 us  [the longest x3 4.95 us: local(): part = jnp.dot(group_o, sibling_block, preferred_element_type=jnp.float32)]
    another operation x2 -> x1, other arithmetic: 3.34 us -> 0.48 us  [the longest x1 2.86 us: local(): jnp.stack(mine[1:])]
    squeeze x1 -> x0, local copies, waits for them, and re-layouts: 2.69 us -> none  [fetch_out_weight(): lax.dynamic_index_in_dim(exchanged, (head - shift) % groups, 0, keepdims=...]
  transfers between devices with their start and end apart: 14 -> 14, of which waited for: 5 -> 5; matrix products, arithmetic and copies ran while one was open for 27% -> 27% of each run, Pallas kernels for 26% -> 27%
where the time goes in v19:
time: 154 us; the launch traced here: 153 us
  Pallas kernels  40.6 us (26%)
  waiting for transfers between devices  33.4 us (22%)
  matrix products  28.2 us (18%)
  starting transfers between devices  23.3 us (15%)
  other arithmetic  14.4 us (9%)
  local copies, waits for them, and re-layouts  12.5 us (8%)
    pallas_call x2, Pallas kernels, flash(): pl.pallas_call(kernel, grid_spec=grid_spec, out_shape=jax.ShapeDtypeStruc...  33.5 us
    ppermute x6, waiting for transfers between devices, local(): lax.ppermute(part, 'head', [(i, (i + shift) % groups) for i in range(grou...  19.6 us
    ppermute x5, waiting for transfers between devices, from_behind(): lax.ppermute(shard, axis, [(i, (i + by) % length) for i in range(length)])  13.8 us
    dot_general x1, matrix products, local(): jnp.einsum('td,dkh->kth', hidden, w_qkv, preferred_element_type=jnp.float32)  12.8 us
    ppermute x6, starting transfers between devices, local(): lax.ppermute(part, 'head', [(i, (i + shift) % groups) for i in range(grou...  7.38 us
    pallas_call x2, Pallas kernels, flash_local(): pl.pallas_call(kernel, grid=(steps,), in_specs=[pl.BlockSpec((span, width...  7.13 us
    ppermute x5, starting transfers between devices, from_behind(): lax.ppermute(shard, axis, [(i, (i + by) % length) for i in range(length)])  6.83 us
    dot_general x3, matrix products, local(): part = jnp.dot(group_o, sibling_block, preferred_element_type=jnp.float32)  4.95 us
  transfers between devices with their start and end apart: 14, of which 5 were waited for; matrix products, arithmetic and copies ran while one was open for 27% of the time, Pallas kernels for 27%

profile of v19, /device:TPU:9, one launch (start us, length us, event | category | flops | bytes accessed | tf_op | source)
XLA Modules:
  0.0 152.7 jit_solution(10669269283800060851)
XLA Ops:
  0.0 2.5 %reshape.85 = bf16[1,512,768]{2,1,0:T(8,128)(2,1)S(1)} reshape(bf16[1,512,2,384]{3,2,1,0:T(2,128)(2,1)} %param.18) | data formatting | bytes 1572864 | tf_op jit(solution)/shard_map/reshape | solution.py:258
  2.5 2.2 %collective-permute-start.4 = (bf16[1,512,768]{2,1,0:T(8,128)(2,1)S(1)}, bf16[1,512,768]{2,1,0:T(8,128)(2,1)S(1)}, u32[]{:S(2)}, u32[]{:S(2)}) collective-permute-start(bf16[1,512,768]{2,1,0:T(8,128)(2,1)S(1)} %reshape.85), channel_id=1, source_target_pairs={{0,24},{4,28},{8,0},{12,4},{16,8},{20,12},{24,16},{28,20},{1,25},{... | collective-permute-start | bytes 2359304 | tf_op jit(solution)/shard_map/ppermute | solution.py:14
  5.3 1.8 %dynamic-slice_bitcast_fusion.3 = (bf16[1,384,768]{2,1,0:T(8,128)(2,1)S(1)}, bf16[1,384,768]{2,1,0:T(8,128)(2,1)S(1)}, bf16[1,384,768]{2,1,0:T(8,128)(2,1)S(1)}, bf16[1,384,768]{2,1,0:T(8,128)(2,1)S(1)}) fusion(bf16[384,6144]{1,0:T(8,128)(2,1)} %param.19, s32[]{:T(128)S(6)} %select_n.112, s32[]{:T(128)S(6)} %select_n.114, s32[]{:T(128)S(6)} %select_n.113, ...), kind=kLoop, calls=%fused_computation.48 | loop fusion | bytes 4718608 | tf_op jit(solution)/shard_map/stack | solution.py:225
  7.0 1.7 %pad_maximum_fusion.1 = bf16[4,384,768]{2,1,0:T(8,128)(2,1)} fusion(bf16[1,384,768]{2,1,0:T(8,128)(2,1)S(1)} %get-tuple-element.48, bf16[1,384,768]{2,1,0:T(8,128)(2,1)S(1)} %get-tuple-element.46, bf16[1,384,768]{2,1,0:T(8,128)(2,1)S(1)} %get-tuple-element.47, bf16[1,384,768]{2,1,0:T(8,128)(2,1)S(1)} %get-tuple-element.45), kind=kLoop, calls=%fused_computation.17 | loop fusion | flops 3538944 | bytes 4718592 | tf_op jit(solution)/shard_map/stack | solution.py:225
  8.8 4.9 %all-to-all-start = ((bf16[4,384,768]{2,1,0:T(8,128)(2,1)}), bf16[4,384,768]{2,1,0:T(8,128)(2,1)}, u32[]{:S(2)}, u32[]{:S(2)}) async-start(bf16[4,384,768]{2,1,0:T(8,128)(2,1)} %pad_maximum_fusion.1), calls=%async_computation | async-start | bytes 4718592 | tf_op jit(solution)/shard_map/all_to_all | solution.py:229
  15.2 4.1 %fusion = f32[512]{0:T(512)S(1)} fusion(bf16[512,6144]{1,0:T(8,128)(2,1)} %param.10), kind=kLoop, calls=%fused_computation.2 | loop fusion | flops 9436672 | bytes 6293504 | tf_op jit(solution)/shard_map/reduce_sum | solution.py:267
  19.3 12.8 %fusion.13 = f32[3,512,384]{2,1,0:T(8,128)S(1)} fusion(bf16[6144,3,384]{2,0,1:T(8,128)(2,1)} %param.15, bf16[512,6144]{1,0:T(8,128)(2,1)} %param.10, f32[6144]{0:T(1024)S(1)} %bitcast.69, f32[6144]{0:T(1024)S(1)} %bitcast.70, f32[512]{0:T(512)S(1)} %add_rsqrt_fusion.6), kind=kOutput, calls=%fused_computation.18 | convolution fusion | flops 7263485952 | bytes 22857728 | tf_op jit(solution)/shard_map/td,dkh->kth/dot_general | solution.py:270
  34.8 4.1 %collective-permute-start = (bf16[512,768]{1,0:T(8,128)(2,1)}, bf16[512,768]{1,0:T(8,128)(2,1)}, u32[]{:S(2)}, u32[]{:S(2)}) collective-permute-start(bf16[512,768]{1,0:T(8,128)(2,1)} %get-tuple-element.51), channel_id=1, source_target_pairs={{0,4},{4,8},{8,12},{12,16},{16,20},{20,24},{24,28},{28,0},{1,5},{5... | collective-permute-start | bytes 2359304 | tf_op jit(solution)/shard_map/ppermute | solution.py:14
  41.0 3.6 %shard_map.100 = (f32[3,256,1]{2,1,0:T(8,128)}, f32[3,256,1]{2,1,0:T(8,128)}, f32[3,256,128]{2,1,0:T(8,128)}) custom-call(bf16[256,384]{1,0:T(8,128)(2,1)} %get-tuple-element.62.refs_0_, bf16[1,512,768]{2,1,0:T(8,128)(2,1)} %get-tuple-element.52.refs_1_.refs_2_, bf16[1,512,768]{2,1,0:T(8,128)(2,1)} %get-tuple-element.52.refs_1_.refs_2_, ...), custom_call_target="tpu_custom_call" | custom-call | flops 201326592 | bytes 786432 | tf_op jit(solution)/shard_map/pallas_call | solution.py:89
  44.6 3.6 %shard_map.101 = (f32[3,256,1]{2,1,0:T(8,128)}, f32[3,256,1]{2,1,0:T(8,128)}, f32[3,256,128]{2,1,0:T(8,128)}) custom-call(bf16[256,384]{1,0:T(8,128)(2,1)} %get-tuple-element.61.refs_0_, bf16[1,512,768]{2,1,0:T(8,128)(2,1)} %get-tuple-element.52.refs_1_.refs_2_, bf16[1,512,768]{2,1,0:T(8,128)(2,1)} %get-tuple-element.52.refs_1_.refs_2_, ...), custom_call_target="tpu_custom_call" | custom-call | flops 201326592 | bytes 786432 | tf_op jit(solution)/shard_map/pallas_call | solution.py:89
  49.9 2.0 %pad_maximum_fusion.refs_4_.refs_5_ = bf16[4,512,768]{2,1,0:T(8,128)(2,1)S(1)} fusion(bf16[1,512,768]{2,1,0:T(8,128)(2,1)} %copy-done.5, bf16[1,512,768]{2,1,0:T(8,128)(2,1)} %copy-done.6, bf16[1,512,768]{2,1,0:T(8,128)(2,1)} %collective-permute-done.2, bf16[1,512,768]{2,1,0:T(8,128)(2,1)} %copy-done.4), kind=kLoop, calls=%fused_computation.11 | loop fusion | flops 4718592 | bytes 6291456 | tf_op jit(solution)/shard_map/concatenate | solution.py:260
  52.0 4.0 %collective-permute-done = bf16[512,768]{1,0:T(8,128)(2,1)} collective-permute-done((bf16[512,768]{1,0:T(8,128)(2,1)}, bf16[512,768]{1,0:T(8,128)(2,1)}, u32[]{:S(2)}, u32[]{:S(2)}) %collective-permute-start) | collective-permute-done | bytes 786464 | tf_op jit(solution)/shard_map/ppermute | solution.py:14
  56.0 9.8 %collective-permute-done.1 = bf16[512,768]{1,0:T(8,128)(2,1)} collective-permute-done((bf16[512,768]{1,0:T(8,128)(2,1)}, bf16[512,768]{1,0:T(8,128)(2,1)}, u32[]{:S(2)}, u32[]{:S(2)}) %collective-permute-start.1) | collective-permute-done | bytes 786464 | tf_op jit(solution)/shard_map/ppermute | solution.py:14
  65.7 4.1 %collective-permute-start.5 = (bf16[4,512,768]{2,1,0:T(8,128)(2,1)S(1)}, bf16[4,512,768]{2,1,0:T(8,128)(2,1)}, u32[]{:S(2)}, u32[]{:S(2)}) collective-permute-start(bf16[4,512,768]{2,1,0:T(8,128)(2,1)S(1)} %pad_maximum_fusion.refs_4_.refs_5_), channel_id=1, source_target_pairs={{0,4},{4,0},{8,12},{12,8},{16,20},{20,16},{24,28},{28,24},{1,5},{5... | collective-permute-start | bytes 9437192 | tf_op jit(solution)/shard_map/ppermute | solution.py:291
  70.9 1.3 compare_select_fusion.6.refs_0_
  72.9 2.7 %pad_maximum_fusion.2.refs_2_.refs_3_ = bf16[2,512,768]{2,1,0:T(8,128)(2,1)} fusion(bf16[1,512,768]{2,1,0:T(8,128)(2,1)} %bitcast.17, bf16[1,512,768]{2,1,0:T(8,128)(2,1)} %bitcast.16), kind=kLoop, calls=%fused_computation.19 | loop fusion | flops 786432 | bytes 3145728 | tf_op jit(solution)/shard_map/stack | solution.py:301
  75.6 1.8 %fusion.53 = (bf16[256,384]{1,0:T(8,128)(2,1)}, bf16[256,384]{1,0:T(8,128)(2,1)}) fusion(bf16[512,384]{1,0:T(8,128)(2,1)} %copy-done.3), kind=kLoop, calls=%fused_computation.123 | loop fusion | bytes 786432 | tf_op jit(solution)/shard_map/slice | solution.py:310
  77.4 16.7 %shard_map.102 = bf16[256,384]{1,0:T(8,128)(2,1)} custom-call(s32[6]{0:T(128)} %compare_select_fusion.6.refs_0_, bf16[256,384]{1,0:T(8,128)(2,1)} %get-tuple-element.60.refs_1_, bf16[2,512,768]{2,1,0:T(8,128)(2,1)} %pad_maximum_fusion.2.refs_2_.refs_3_, bf16[2,512,768]{2,1,0:T(8,128)(2,1)} %pad_maximum_fusion.2.refs_2_.refs_3_, ...), custom_call_target="tpu_custom_call" | custom-call | flops 805306368 | bytes 3145728 | tf_op jit(solution)/shard_map/pallas_call | solution.py:208
  94.1 2.3 %collective-permute-start.8 = (bf16[256,384]{1,0:T(8,128)(2,1)}, bf16[256,384]{1,0:T(8,128)(2,1)S(1)}, u32[]{:S(2)}, u32[]{:S(2)}) collective-permute-start(bf16[256,384]{1,0:T(8,128)(2,1)} %shard_map.102), channel_id=1, source_target_pairs={{0,2},{1,3},{2,0},{3,1},{4,6},{5,7},{6,4},{7,5},{8,10},{9,11},{10,... | collective-permute-start | bytes 589832 | tf_op jit(solution)/shard_map/ppermute | solution.py:320
  96.4 16.8 %shard_map.103 = bf16[256,384]{1,0:T(8,128)(2,1)} custom-call(s32[6]{0:T(128)} %compare_select_fusion.6.refs_0_, bf16[256,384]{1,0:T(8,128)(2,1)} %get-tuple-element.59.refs_1_, bf16[2,512,768]{2,1,0:T(8,128)(2,1)} %pad_maximum_fusion.2.refs_2_.refs_3_, bf16[2,512,768]{2,1,0:T(8,128)(2,1)} %pad_maximum_fusion.2.refs_2_.refs_3_, ...), custom_call_target="tpu_custom_call" | custom-call | flops 805306368 | bytes 3145728 | tf_op jit(solution)/shard_map/pallas_call | solution.py:208
  113.2 2.3 %collective-permute-start.9 = (bf16[256,384]{1,0:T(8,128)(2,1)}, bf16[256,384]{1,0:T(8,128)(2,1)S(1)}, u32[]{:S(2)}, u32[]{:S(2)}) collective-permute-start(bf16[256,384]{1,0:T(8,128)(2,1)} %shard_map.103), channel_id=1, source_target_pairs={{0,2},{1,3},{2,0},{3,1},{4,6},{5,7},{6,4},{7,5},{8,10},{9,11},{10,... | collective-permute-start | bytes 589832 | tf_op jit(solution)/shard_map/ppermute | solution.py:320
  117.0 1.3 collective-permute-start.11
  118.4 15.5 %collective-permute-done.10 = bf16[256,384]{1,0:T(8,128)(2,1)S(1)} collective-permute-done((bf16[256,384]{1,0:T(8,128)(2,1)S(1)}, bf16[256,384]{1,0:T(8,128)(2,1)S(1)}, u32[]{:S(2)}, u32[]{:S(2)}) %collective-permute-start.10) | collective-permute-done | bytes 196640 | tf_op jit(solution)/shard_map/ppermute | solution.py:320
  133.9 2.4 %collective-permute-done.7 = bf16[256,384]{1,0:T(8,128)(2,1)S(1)} collective-permute-done((bf16[256,384]{1,0:T(8,128)(2,1)}, bf16[256,384]{1,0:T(8,128)(2,1)S(1)}, u32[]{:S(2)}, u32[]{:S(2)}) %collective-permute-start.7) | collective-permute-done | bytes 196640 | tf_op jit(solution)/shard_map/ppermute | solution.py:320
  136.3 1.7 %collective-permute-done.11 = bf16[256,384]{1,0:T(8,128)(2,1)S(1)} collective-permute-done((bf16[256,384]{1,0:T(8,128)(2,1)}, bf16[256,384]{1,0:T(8,128)(2,1)S(1)}, u32[]{:S(2)}, u32[]{:S(2)}) %collective-permute-start.11) | collective-permute-done | bytes 196640 | tf_op jit(solution)/shard_map/ppermute | solution.py:320
  138.1 1.6 %convolution_convert_fusion.5 = bf16[512,768]{1,0:T(8,128)(2,1)S(1)} fusion(bf16[512,384]{1,0:T(8,128)(2,1)S(1)} %constant_dynamic-update-slice_fusion.2, bf16[4,384,768]{2,1,0:T(8,128)(2,1)} %all-to-all-done, s32[]{:T(128)S(6)} %select_n.124), kind=kOutput, calls=%fused_computation.26 | convolution fusion | flops 302383104 | bytes 1769476 | tf_op jit(solution)/shard_map/dot_general | solution.py:335
  139.7 1.6 %convolution_convert_fusion.6 = bf16[512,768]{1,0:T(8,128)(2,1)S(1)} fusion(bf16[512,384]{1,0:T(8,128)(2,1)S(1)} %constant_dynamic-update-slice_fusion, bf16[4,384,768]{2,1,0:T(8,128)(2,1)} %all-to-all-done, s32[]{:T(128)S(6)} %select_n.122), kind=kOutput, calls=%fused_computation.27 | convolution fusion | flops 302383104 | bytes 1769476 | tf_op jit(solution)/shard_map/dot_general | solution.py:335
  141.4 1.6 %convert_add_fusion.1 = f32[512,768]{1,0:T(8,128)S(1)} fusion(bf16[512,768]{1,0:T(8,128)(2,1)S(1)} %convolution_convert_fusion.5, bf16[512,768]{1,0:T(8,128)(2,1)S(1)} %convolution_convert_fusion.6, bf16[512,384]{1,0:T(8,128)(2,1)S(1)} %constant_dynamic-update-slice_fusion.4, bf16[4,384,768]{2,1,0:T(8,128)(2,1)} %all-to-all-done, s32[]{:T(128)S(6)} %select_n.126), kind=kOutput, calls=%fused_computation.21 | convolution fusion | flops 304349184 | bytes 4128772 | tf_op jit(solution)/shard_map/dot_general | solution.py:335
  143.0 1.6 %convolution_convert_fusion.2 = bf16[512,768]{1,0:T(8,128)(2,1)S(1)} fusion(bf16[512,384]{1,0:T(8,128)(2,1)S(1)} %constant_dynamic-update-slice_fusion.2, bf16[4,384,768]{2,1,0:T(8,128)(2,1)} %collective-permute-done.12, s32[]{:T(128)S(6)} %select_n.124), kind=kOutput, calls=%fused_computation.23 | convolution fusion | flops 302383104 | bytes 1769476 | tf_op jit(solution)/shard_map/dot_general | solution.py:339
  144.7 1.6 %convolution_convert_fusion.3 = bf16[512,768]{1,0:T(8,128)(2,1)S(1)} fusion(bf16[512,384]{1,0:T(8,128)(2,1)S(1)} %constant_dynamic-update-slice_fusion, bf16[4,384,768]{2,1,0:T(8,128)(2,1)} %collective-permute-done.12, s32[]{:T(128)S(6)} %select_n.122), kind=kOutput, calls=%fused_computation.24 | convolution fusion | flops 302383104 | bytes 1769476 | tf_op jit(solution)/shard_map/dot_general | solution.py:339
  146.3 1.7 %convert_add_fusion = f32[512,768]{1,0:T(8,128)S(1)} fusion(bf16[512,768]{1,0:T(8,128)(2,1)S(1)} %convolution_convert_fusion.2, bf16[512,768]{1,0:T(8,128)(2,1)S(1)} %convolution_convert_fusion.3, bf16[512,384]{1,0:T(8,128)(2,1)S(1)} %constant_dynamic-update-slice_fusion.4, bf16[4,384,768]{2,1,0:T(8,128)(2,1)} %collective-permute-done.12, s32[]{:T(128)S(6)} %select_n.126), kind=kOutput, calls=%fused_computation.20 | convolution fusion | flops 304349184 | bytes 4128772 | tf_op jit(solution)/shard_map/dot_general | solution.py:339
  148.0 4.7 %fusion.12 = f32[512,1536]{1,0:T(8,128)} fusion(f32[512,768]{1,0:T(8,128)S(1)} %convert_add_fusion, f32[512,768]{1,0:T(8,128)S(1)} %convert_add_fusion.1, f32[1536]{0:T(1024)S(1)} %dynamic-slice_reduce_fusion, bf16[512,6144]{1,0:T(8,128)(2,1)} %param.10, s32[]{:T(128)S(6)} %select_n.103, pred[]{:T(512)S(6)} %eq.28, bf16[384,6144]{1,0:T(8,128)(2,1)} %param.19, ...), kind=kOutput, calls=%fused_computation.15 | convolution fusion | flops 611844096 | bytes 9444864 | tf_op jit(solution)/shard_map/dot_general | solution.py:328
  (76 shorter events, 11.9 us)
Async XLA Ops:
  0.0 14.2 %copy-start = (bf16[8,3,6144]{2,0,1:T(8,128)(2,1)S(1)}, bf16[8,3,6144]{2,0,1:T(8,128)(2,1)}, u32[]{:S(2)}) copy-start(bf16[8,3,6144]{2,0,1:T(8,128)(2,1)} %param.11) | copy-start | bytes 884740
  2.5 4.5 %copy-start.4 = (bf16[1,512,768]{2,1,0:T(8,128)(2,1)}, bf16[1,512,768]{2,1,0:T(8,128)(2,1)S(1)}, u32[]{:S(2)}) copy-start(bf16[1,512,768]{2,1,0:T(8,128)(2,1)S(1)} %reshape.85) | copy-start | bytes 2359300
  2.5 45.7 %collective-permute-start.4 = (bf16[1,512,768]{2,1,0:T(8,128)(2,1)S(1)}, bf16[1,512,768]{2,1,0:T(8,128)(2,1)S(1)}, u32[]{:S(2)}, u32[]{:S(2)}) collective-permute-start(bf16[1,512,768]{2,1,0:T(8,128)(2,1)S(1)} %reshape.85), channel_id=1, source_target_pairs={{0,24},{4,28},{8,0},{12,4},{16,8},{20,12},{24,16},{28,20},{1,25},{... | collective-permute-start | bytes 2359304 | tf_op jit(solution)/shard_map/ppermute | solution.py:14
  4.7 43.4 %collective-permute-start.3 = (bf16[1,512,768]{2,1,0:T(8,128)(2,1)S(1)}, bf16[1,512,768]{2,1,0:T(8,128)(2,1)S(1)}, u32[]{:S(2)}, u32[]{:S(2)}) collective-permute-start(bf16[1,512,768]{2,1,0:T(8,128)(2,1)S(1)} %reshape.85), channel_id=1, source_target_pairs={{0,16},{4,20},{8,24},{12,28},{16,0},{20,4},{24,8},{28,12},{1,17},{... | collective-permute-start | bytes 2359304 | tf_op jit(solution)/shard_map/ppermute | solution.py:14
  5.0 45.0 %collective-permute-start.2 = (bf16[1,512,768]{2,1,0:T(8,128)(2,1)S(1)}, bf16[1,512,768]{2,1,0:T(8,128)(2,1)}, u32[]{:S(2)}, u32[]{:S(2)}) collective-permute-start(bf16[1,512,768]{2,1,0:T(8,128)(2,1)S(1)} %reshape.85), channel_id=1, source_target_pairs={{0,8},{4,12},{8,16},{12,20},{16,24},{20,28},{24,0},{28,4},{1,9},{5... | collective-permute-start | bytes 2359304 | tf_op jit(solution)/shard_map/ppermute | solution.py:14
  8.8 4.9 %copy-start.11 = (s32[8]{0:T(128)S(1)}, s32[8]{0:T(128)}, u32[]{:S(2)}) copy-start(s32[8]{0:T(128)} %param.12) | copy-start | bytes 100
  8.8 57.0 %all-to-all-start = ((bf16[4,384,768]{2,1,0:T(8,128)(2,1)}), bf16[4,384,768]{2,1,0:T(8,128)(2,1)}, u32[]{:S(2)}, u32[]{:S(2)}) async-start(bf16[4,384,768]{2,1,0:T(8,128)(2,1)} %pad_maximum_fusion.1), calls=%async_computation | async-start | bytes 4718592 | tf_op jit(solution)/shard_map/all_to_all | solution.py:229
  32.1 0.7 copy-start.9
  32.2 0.7 copy-start.10
  34.8 21.2 %collective-permute-start = (bf16[512,768]{1,0:T(8,128)(2,1)}, bf16[512,768]{1,0:T(8,128)(2,1)}, u32[]{:S(2)}, u32[]{:S(2)}) collective-permute-start(bf16[512,768]{1,0:T(8,128)(2,1)} %get-tuple-element.51), channel_id=1, source_target_pairs={{0,4},{4,8},{8,12},{12,16},{16,20},{20,24},{24,28},{28,0},{1,5},{5... | collective-permute-start | bytes 2359304 | tf_op jit(solution)/shard_map/ppermute | solution.py:14
  38.8 26.9 %collective-permute-start.1 = (bf16[512,768]{1,0:T(8,128)(2,1)}, bf16[512,768]{1,0:T(8,128)(2,1)}, u32[]{:S(2)}, u32[]{:S(2)}) collective-permute-start(bf16[512,768]{1,0:T(8,128)(2,1)} %get-tuple-element.51), channel_id=1, source_target_pairs={{0,8},{4,12},{8,16},{12,20},{16,24},{20,28},{24,0},{28,4},{1,9},{5... | collective-permute-start | bytes 2359304 | tf_op jit(solution)/shard_map/ppermute | solution.py:14
  38.9 0.7 copy-start.3
  48.2 0.9 copy-start.5
  49.0 0.9 copy-start.6
  52.0 25.4 %copy-start.2 = (bf16[4,512,768]{2,1,0:T(8,128)(2,1)}, bf16[4,512,768]{2,1,0:T(8,128)(2,1)S(1)}, u32[]{:S(2)}) copy-start(bf16[4,512,768]{2,1,0:T(8,128)(2,1)S(1)} %pad_maximum_fusion.refs_4_.refs_5_) | copy-start | bytes 9437188
  65.7 11.7 %collective-permute-start.5 = (bf16[4,512,768]{2,1,0:T(8,128)(2,1)S(1)}, bf16[4,512,768]{2,1,0:T(8,128)(2,1)}, u32[]{:S(2)}, u32[]{:S(2)}) collective-permute-start(bf16[4,512,768]{2,1,0:T(8,128)(2,1)S(1)} %pad_maximum_fusion.refs_4_.refs_5_), channel_id=1, source_target_pairs={{0,4},{4,0},{8,12},{12,8},{16,20},{20,16},{24,28},{28,24},{1,5},{5... | collective-permute-start | bytes 9437192 | tf_op jit(solution)/shard_map/ppermute | solution.py:291
  72.2 70.9 %collective-permute-start.12 = (bf16[4,384,768]{2,1,0:T(8,128)(2,1)}, bf16[4,384,768]{2,1,0:T(8,128)(2,1)}, u32[]{:S(2)}, u32[]{:S(2)}) collective-permute-start(bf16[4,384,768]{2,1,0:T(8,128)(2,1)} %all-to-all-done), channel_id=1, source_target_pairs={{0,4},{4,0},{8,12},{12,8},{16,20},{20,16},{24,28},{28,24},{1,5},{5... | collective-permute-start | bytes 7077896 | tf_op jit(solution)/shard_map/ppermute | solution.py:314
  94.1 21.8 %collective-permute-start.8 = (bf16[256,384]{1,0:T(8,128)(2,1)}, bf16[256,384]{1,0:T(8,128)(2,1)S(1)}, u32[]{:S(2)}, u32[]{:S(2)}) collective-permute-start(bf16[256,384]{1,0:T(8,128)(2,1)} %shard_map.102), channel_id=1, source_target_pairs={{0,2},{1,3},{2,0},{3,1},{4,6},{5,7},{6,4},{7,5},{8,10},{9,11},{10,... | collective-permute-start | bytes 589832 | tf_op jit(solution)/shard_map/ppermute | solution.py:320
  96.4 20.6 %collective-permute-start.6 = (bf16[256,384]{1,0:T(8,128)(2,1)}, bf16[256,384]{1,0:T(8,128)(2,1)S(1)}, u32[]{:S(2)}, u32[]{:S(2)}) collective-permute-start(bf16[256,384]{1,0:T(8,128)(2,1)} %shard_map.102), channel_id=1, source_target_pairs={{0,1},{1,2},{2,3},{3,0},{4,5},{5,6},{6,7},{7,4},{8,9},{9,10},{10,1... | collective-permute-start | bytes 589832 | tf_op jit(solution)/shard_map/ppermute | solution.py:320
  96.4 19.5 %copy-start.7 = (bf16[256,384]{1,0:T(8,128)(2,1)S(1)}, bf16[256,384]{1,0:T(8,128)(2,1)}, u32[]{:S(2)}) copy-start(bf16[256,384]{1,0:T(8,128)(2,1)} %shard_map.102) | copy-start | bytes 589828
  113.2 20.6 %collective-permute-start.9 = (bf16[256,384]{1,0:T(8,128)(2,1)}, bf16[256,384]{1,0:T(8,128)(2,1)S(1)}, u32[]{:S(2)}, u32[]{:S(2)}) collective-permute-start(bf16[256,384]{1,0:T(8,128)(2,1)} %shard_map.103), channel_id=1, source_target_pairs={{0,2},{1,3},{2,0},{3,1},{4,6},{5,7},{6,4},{7,5},{8,10},{9,11},{10,... | collective-permute-start | bytes 589832 | tf_op jit(solution)/shard_map/ppermute | solution.py:320
  115.5 20.8 %collective-permute-start.7 = (bf16[256,384]{1,0:T(8,128)(2,1)}, bf16[256,384]{1,0:T(8,128)(2,1)S(1)}, u32[]{:S(2)}, u32[]{:S(2)}) collective-permute-start(bf16[256,384]{1,0:T(8,128)(2,1)} %shard_map.103), channel_id=1, source_target_pairs={{0,1},{1,2},{2,3},{3,0},{4,5},{5,6},{6,7},{7,4},{8,9},{9,10},{10,1... | collective-permute-start | bytes 589832 | tf_op jit(solution)/shard_map/ppermute | solution.py:320
  115.9 18.0 %collective-permute-start.10 = (bf16[256,384]{1,0:T(8,128)(2,1)S(1)}, bf16[256,384]{1,0:T(8,128)(2,1)S(1)}, u32[]{:S(2)}, u32[]{:S(2)}) collective-permute-start(bf16[256,384]{1,0:T(8,128)(2,1)S(1)} %copy-done.7), channel_id=1, source_target_pairs={{0,3},{1,0},{2,1},{3,2},{4,7},{5,4},{6,5},{7,6},{8,11},{9,8},{10,9... | collective-permute-start | bytes 589832 | tf_op jit(solution)/shard_map/ppermute | solution.py:320
  117.0 21.1 %collective-permute-start.11 = (bf16[256,384]{1,0:T(8,128)(2,1)}, bf16[256,384]{1,0:T(8,128)(2,1)S(1)}, u32[]{:S(2)}, u32[]{:S(2)}) collective-permute-start(bf16[256,384]{1,0:T(8,128)(2,1)} %shard_map.103), channel_id=1, source_target_pairs={{0,3},{1,0},{2,1},{3,2},{4,7},{5,4},{6,5},{7,6},{8,11},{9,8},{10,9... | collective-permute-start | bytes 589832 | tf_op jit(solution)/shard_map/ppermute | solution.py:320
  146.3 1.7 %copy-start.8 = (bf16[256,384]{1,0:T(8,128)(2,1)S(1)}, bf16[256,384]{1,0:T(8,128)(2,1)}, u32[]{:S(2)}) copy-start(bf16[256,384]{1,0:T(8,128)(2,1)} %shard_map.103) | copy-start | bytes 589828
  148.0 4.7 %copy-start.1 = (bf16[8,3,6144]{2,0,1:T(8,128)(2,1)S(1)}, bf16[8,3,6144]{2,0,1:T(8,128)(2,1)}, u32[]{:S(2)}) copy-start(bf16[8,3,6144]{2,0,1:T(8,128)(2,1)} %param.11) | copy-start | bytes 884740

commit v20 on v19

--- a/solution.py
+++ b/solution.py
@@ -110,7 +110,7 @@
     )(queries, local_stack, local_stack, bias)
 
 
-def flash_kernel(chosen, q_ref, lk_ref, lv_ref, ak_ref, av_ref, bk_ref, bv_ref, bias_ref, m_in, l_in, acc_in, o_ref, m_sc, l_sc, acc_sc, *, heads, n_local, half):
+def flash_kernel(chosen, q_ref, k1_ref, v1_ref, k2_ref, v2_ref, ak_ref, av_ref, bk_ref, bv_ref, bias_ref, m_in, l_in, acc_in, o_ref, m_sc, l_sc, acc_sc, *, heads, n_local, half):
     step = pl.program_id(0)
     span = q_ref.shape[0]
     blocks = bias_ref.shape[0]
@@ -140,9 +140,13 @@
             )
             m_sc[h] = m_new
 
-    @pl.when(step < n_local)
-    def _():
-        body(lk_ref, lv_ref)
+    @pl.when(step == 0)
+    def _():
+        body(k1_ref, v1_ref)
+
+    @pl.when(step == 1)
+    def _():
+        body(k2_ref, v2_ref)
 
     pos = chosen[jnp.maximum(step - n_local, 0)]
 
@@ -161,9 +165,9 @@
             o_ref[:, cols] = (acc_sc[h] / l_sc[h]).astype(o_ref.dtype)
 
 
-def flash(queries, local_stack, same_core, other_core, bias, chosen, state, heads):
+def flash(queries, before, earlier, same_core, other_core, bias, chosen, state, heads):
     span, width = queries.shape
-    n_local = local_stack.shape[0]
+    n_local = 2
     half = same_core.shape[0]
     steps = n_local + chosen.shape[0]
     blocks = bias.shape[1]
@@ -179,15 +183,17 @@
 
         return index
 
-    keys_len = local_stack.shape[1]
+    keys_len = before.shape[0]
     kv_block = (None, keys_len, width)
     grid_spec = pltpu.PrefetchScalarGridSpec(
         num_scalar_prefetch=1,
         grid=(steps,),
         in_specs=[
             pl.BlockSpec((span, width), lambda j, c: (0, 0)),
-            pl.BlockSpec(kv_block, local_map(0)),
-            pl.BlockSpec(kv_block, local_map(1)),
+            pl.BlockSpec((keys_len, width), lambda j, c: (0, 0)),
+            pl.BlockSpec((keys_len, width), lambda j, c: (0, 1)),
+            pl.BlockSpec((keys_len, width), lambda j, c: (0, 0)),
+            pl.BlockSpec((keys_len, width), lambda j, c: (0, 1)),
             pl.BlockSpec(kv_block, pool_map(0, False)),
             pl.BlockSpec(kv_block, pool_map(1, False)),
             pl.BlockSpec(kv_block, pool_map(0, True)),
@@ -215,7 +221,7 @@
             transcendentals=steps * heads * span * span,
             bytes_accessed=2 * steps * span * width * 2,
         ),
-    )(chosen, queries, local_stack, local_stack, same_core, same_core, other_core, other_core, bias, *state)
+    )(chosen, queries, before, before, earlier, earlier, same_core, same_core, other_core, other_core, bias, *state)
 
 
 def fetch_out_weight(w_out, head, core):
@@ -298,7 +304,6 @@
         slots // 2 + ((sibling_slot - own_cache) % slots) // 2,
     ).astype(jnp.int32)
     width = heads * HD
-    local_stack = jnp.stack([before, earlier]).reshape(2, span, 2 * width)
     visible = jnp.concatenate([jnp.ones((blocks_q, blocks_q), jnp.int32), own_mask], axis=1)
     visible = jnp.transpose(visible.reshape(blocks_q, 3 + cache_len, blocks_q), (1, 0, 2))
     visible = jnp.repeat(visible, BLOCK, axis=2)
@@ -307,7 +312,7 @@
     parts = rows // BLOCK
     queries = queries.reshape(span, width)
     mixed_parts = [
-        flash(queries[p * rows : (p + 1) * rows], local_stack, same_core, other_core,
+        flash(queries[p * rows : (p + 1) * rows], before, earlier, same_core, other_core,
               bias[1:, p * parts : (p + 1) * parts], own_cache, states[p], heads)
         for p in range(2)
     ]

time: 154 us -> 151 us (0.981)
  other arithmetic: 14.4 us -> 11.6 us
    another operation x2 -> x1, other arithmetic: 3.23 us -> 0.48 us  [the longest x1 2.75 us: local(): local_stack = jnp.stack([before, earlier]).reshape(2, span, 2 * width)]
  transfers between devices with their start and end apart: 14 -> 14, of which waited for: 5 -> 6; matrix products, arithmetic and copies ran while one was open for 27% -> 25% of each run, Pallas kernels for 27% -> 27%
where the time goes in v20:
time: 151 us; the launch traced here: 150 us
  Pallas kernels  40.5 us (27%)
  waiting for transfers between devices  34 us (23%)
  matrix products  28.2 us (19%)
  starting transfers between devices  23.3 us (15%)
  local copies, waits for them, and re-layouts  12.5 us (8%)
  other arithmetic  11.6 us (8%)
    pallas_call x2, Pallas kernels, flash(): pl.pallas_call(kernel, grid_spec=grid_spec, out_shape=jax.ShapeDtypeStruc...  33.3 us
    ppermute x6, waiting for transfers between devices, local(): lax.ppermute(part, 'head', [(i, (i + shift) % groups) for i in range(grou...  19.6 us
    ppermute x5, waiting for transfers between devices, from_behind(): lax.ppermute(shard, axis, [(i, (i + by) % length) for i in range(length)])  13.8 us
    dot_general x1, matrix products, local(): jnp.einsum('td,dkh->kth', hidden, w_qkv, preferred_element_type=jnp.float32)  12.8 us
    ppermute x6, starting transfers between devices, local(): lax.ppermute(part, 'head', [(i, (i + shift) % groups) for i in range(grou...  7.36 us
    pallas_call x2, Pallas kernels, flash_local(): pl.pallas_call(kernel, grid=(steps,), in_specs=[pl.BlockSpec((span, width...  7.12 us
    ppermute x5, starting transfers between devices, from_behind(): lax.ppermute(shard, axis, [(i, (i + by) % length) for i in range(length)])  6.83 us
    dot_general x3, matrix products, local(): part = jnp.dot(group_o, sibling_block, preferred_element_type=jnp.float32)  4.95 us
  transfers between devices with their start and end apart: 14, of which 6 were waited for; matrix products, arithmetic and copies ran while one was open for 25% of the time, Pallas kernels for 27%

profile of v20, /device:TPU:9, one launch (start us, length us, event | category | flops | bytes accessed | tf_op | source)
XLA Modules:
  0.0 150.4 jit_solution(14224962776761530551)
XLA Ops:
  0.0 2.5 %reshape.85 = bf16[1,512,768]{2,1,0:T(8,128)(2,1)S(1)} reshape(bf16[1,512,2,384]{3,2,1,0:T(2,128)(2,1)} %param.18) | data formatting | bytes 1572864 | tf_op jit(solution)/shard_map/reshape | solution.py:264
  2.5 2.2 %collective-permute-start.4 = (bf16[1,512,768]{2,1,0:T(8,128)(2,1)S(1)}, bf16[1,512,768]{2,1,0:T(8,128)(2,1)S(1)}, u32[]{:S(2)}, u32[]{:S(2)}) collective-permute-start(bf16[1,512,768]{2,1,0:T(8,128)(2,1)S(1)} %reshape.85), channel_id=1, source_target_pairs={{0,24},{4,28},{8,0},{12,4},{16,8},{20,12},{24,16},{28,20},{1,25},{... | collective-permute-start | bytes 2359304 | tf_op jit(solution)/shard_map/ppermute | solution.py:14
  5.3 1.8 %dynamic-slice_bitcast_fusion.3 = (bf16[1,384,768]{2,1,0:T(8,128)(2,1)S(1)}, bf16[1,384,768]{2,1,0:T(8,128)(2,1)S(1)}, bf16[1,384,768]{2,1,0:T(8,128)(2,1)S(1)}, bf16[1,384,768]{2,1,0:T(8,128)(2,1)S(1)}) fusion(bf16[384,6144]{1,0:T(8,128)(2,1)} %param.19, s32[]{:T(128)S(6)} %select_n.112, s32[]{:T(128)S(6)} %select_n.114, s32[]{:T(128)S(6)} %select_n.113, ...), kind=kLoop, calls=%fused_computation.47 | loop fusion | bytes 4718608 | tf_op jit(solution)/shard_map/stack | solution.py:231
  7.0 1.7 %pad_maximum_fusion.1 = bf16[4,384,768]{2,1,0:T(8,128)(2,1)} fusion(bf16[1,384,768]{2,1,0:T(8,128)(2,1)S(1)} %get-tuple-element.48, bf16[1,384,768]{2,1,0:T(8,128)(2,1)S(1)} %get-tuple-element.46, bf16[1,384,768]{2,1,0:T(8,128)(2,1)S(1)} %get-tuple-element.47, bf16[1,384,768]{2,1,0:T(8,128)(2,1)S(1)} %get-tuple-element.45), kind=kLoop, calls=%fused_computation.17 | loop fusion | flops 3538944 | bytes 4718592 | tf_op jit(solution)/shard_map/stack | solution.py:231
  8.8 4.9 %all-to-all-start = ((bf16[4,384,768]{2,1,0:T(8,128)(2,1)}), bf16[4,384,768]{2,1,0:T(8,128)(2,1)}, u32[]{:S(2)}, u32[]{:S(2)}) async-start(bf16[4,384,768]{2,1,0:T(8,128)(2,1)} %pad_maximum_fusion.1), calls=%async_computation | async-start | bytes 4718592 | tf_op jit(solution)/shard_map/all_to_all | solution.py:235
  15.2 4.1 %fusion = f32[512]{0:T(512)S(1)} fusion(bf16[512,6144]{1,0:T(8,128)(2,1)} %param.10), kind=kLoop, calls=%fused_computation.2 | loop fusion | flops 9436672 | bytes 6293504 | tf_op jit(solution)/shard_map/reduce_sum | solution.py:273
  19.3 12.8 %fusion.13 = f32[3,512,384]{2,1,0:T(8,128)S(1)} fusion(bf16[6144,3,384]{2,0,1:T(8,128)(2,1)} %param.15, bf16[512,6144]{1,0:T(8,128)(2,1)} %param.10, f32[6144]{0:T(1024)S(1)} %bitcast.67, f32[6144]{0:T(1024)S(1)} %bitcast.68, f32[512]{0:T(512)S(1)} %add_rsqrt_fusion.6), kind=kOutput, calls=%fused_computation.18 | convolution fusion | flops 7263485952 | bytes 22857728 | tf_op jit(solution)/shard_map/td,dkh->kth/dot_general | solution.py:276
  33.5 1.2 pad_maximum_fusion.2
  34.8 4.1 %collective-permute-start = (bf16[512,768]{1,0:T(8,128)(2,1)}, bf16[512,768]{1,0:T(8,128)(2,1)}, u32[]{:S(2)}, u32[]{:S(2)}) collective-permute-start(bf16[512,768]{1,0:T(8,128)(2,1)} %get-tuple-element.51), channel_id=1, source_target_pairs={{0,4},{4,8},{8,12},{12,16},{16,20},{20,24},{24,28},{28,0},{1,5},{5... | collective-permute-start | bytes 2359304 | tf_op jit(solution)/shard_map/ppermute | solution.py:14
  41.0 3.6 %shard_map.100 = (f32[3,256,1]{2,1,0:T(8,128)}, f32[3,256,1]{2,1,0:T(8,128)}, f32[3,256,128]{2,1,0:T(8,128)}) custom-call(bf16[256,384]{1,0:T(8,128)(2,1)} %get-tuple-element.62.refs_0_, bf16[1,512,768]{2,1,0:T(8,128)(2,1)} %get-tuple-element.52.refs_1_.refs_2_, bf16[1,512,768]{2,1,0:T(8,128)(2,1)} %get-tuple-element.52.refs_1_.refs_2_, ...), custom_call_target="tpu_custom_call" | custom-call | flops 201326592 | bytes 786432 | tf_op jit(solution)/shard_map/pallas_call | solution.py:89
  44.6 3.6 %shard_map.101 = (f32[3,256,1]{2,1,0:T(8,128)}, f32[3,256,1]{2,1,0:T(8,128)}, f32[3,256,128]{2,1,0:T(8,128)}) custom-call(bf16[256,384]{1,0:T(8,128)(2,1)} %get-tuple-element.61.refs_0_, bf16[1,512,768]{2,1,0:T(8,128)(2,1)} %get-tuple-element.52.refs_1_.refs_2_, bf16[1,512,768]{2,1,0:T(8,128)(2,1)} %get-tuple-element.52.refs_1_.refs_2_, ...), custom_call_target="tpu_custom_call" | custom-call | flops 201326592 | bytes 786432 | tf_op jit(solution)/shard_map/pallas_call | solution.py:89
  49.9 2.0 %pad_maximum_fusion.refs_6_.refs_7_ = bf16[4,512,768]{2,1,0:T(8,128)(2,1)S(1)} fusion(bf16[1,512,768]{2,1,0:T(8,128)(2,1)} %copy-done.5, bf16[1,512,768]{2,1,0:T(8,128)(2,1)} %copy-done.6, bf16[1,512,768]{2,1,0:T(8,128)(2,1)} %collective-permute-done.2, bf16[1,512,768]{2,1,0:T(8,128)(2,1)} %copy-done.4), kind=kLoop, calls=%fused_computation.11 | loop fusion | flops 4718592 | bytes 6291456 | tf_op jit(solution)/shard_map/concatenate | solution.py:266
  52.0 4.0 %collective-permute-done.refs_2_.refs_3_ = bf16[512,768]{1,0:T(8,128)(2,1)} collective-permute-done((bf16[512,768]{1,0:T(8,128)(2,1)}, bf16[512,768]{1,0:T(8,128)(2,1)}, u32[]{:S(2)}, u32[]{:S(2)}) %collective-permute-start) | collective-permute-done | bytes 786464 | tf_op jit(solution)/shard_map/ppermute | solution.py:14
  56.0 9.8 %collective-permute-done.1.refs_4_.refs_5_ = bf16[512,768]{1,0:T(8,128)(2,1)} collective-permute-done((bf16[512,768]{1,0:T(8,128)(2,1)}, bf16[512,768]{1,0:T(8,128)(2,1)}, u32[]{:S(2)}, u32[]{:S(2)}) %collective-permute-start.1) | collective-permute-done | bytes 786464 | tf_op jit(solution)/shard_map/ppermute | solution.py:14
  65.7 4.1 %collective-permute-start.5 = (bf16[4,512,768]{2,1,0:T(8,128)(2,1)S(1)}, bf16[4,512,768]{2,1,0:T(8,128)(2,1)}, u32[]{:S(2)}, u32[]{:S(2)}) collective-permute-start(bf16[4,512,768]{2,1,0:T(8,128)(2,1)S(1)} %pad_maximum_fusion.refs_6_.refs_7_), channel_id=1, source_target_pairs={{0,4},{4,0},{8,12},{12,8},{16,20},{20,16},{24,28},{28,24},{1,5},{5... | collective-permute-start | bytes 9437192 | tf_op jit(solution)/shard_map/ppermute | solution.py:297
  71.0 1.2 compare_select_fusion.6.refs_0_
  72.9 1.8 %fusion.53 = (bf16[256,384]{1,0:T(8,128)(2,1)}, bf16[256,384]{1,0:T(8,128)(2,1)}) fusion(bf16[512,384]{1,0:T(8,128)(2,1)} %copy-done.3), kind=kLoop, calls=%fused_computation.122 | loop fusion | bytes 786432 | tf_op jit(solution)/shard_map/slice | solution.py:315
  75.3 16.6 %shard_map.102 = bf16[256,384]{1,0:T(8,128)(2,1)} custom-call(s32[6]{0:T(128)} %compare_select_fusion.6.refs_0_, bf16[256,384]{1,0:T(8,128)(2,1)} %get-tuple-element.60.refs_1_, bf16[512,768]{1,0:T(8,128)(2,1)} %collective-permute-done.refs_2_.refs_3_, bf16[512,768]{1,0:T(8,128)(2,1)} %collective-permute-done.refs_2_.refs_3_, ...), custom_call_target="tpu_custom_call" | custom-call | flops 805306368 | bytes 3145728 | tf_op jit(solution)/shard_map/pallas_call | solution.py:214
  91.9 2.3 %collective-permute-start.8 = (bf16[256,384]{1,0:T(8,128)(2,1)}, bf16[256,384]{1,0:T(8,128)(2,1)S(1)}, u32[]{:S(2)}, u32[]{:S(2)}) collective-permute-start(bf16[256,384]{1,0:T(8,128)(2,1)} %shard_map.102), channel_id=1, source_target_pairs={{0,2},{1,3},{2,0},{3,1},{4,6},{5,7},{6,4},{7,5},{8,10},{9,11},{10,... | collective-permute-start | bytes 589832 | tf_op jit(solution)/shard_map/ppermute | solution.py:325
  94.2 16.8 %shard_map.103 = bf16[256,384]{1,0:T(8,128)(2,1)} custom-call(s32[6]{0:T(128)} %compare_select_fusion.6.refs_0_, bf16[256,384]{1,0:T(8,128)(2,1)} %get-tuple-element.59.refs_1_, bf16[512,768]{1,0:T(8,128)(2,1)} %collective-permute-done.refs_2_.refs_3_, bf16[512,768]{1,0:T(8,128)(2,1)} %collective-permute-done.refs_2_.refs_3_, ...), custom_call_target="tpu_custom_call" | custom-call | flops 805306368 | bytes 3145728 | tf_op jit(solution)/shard_map/pallas_call | solution.py:214
  111.0 2.2 %collective-permute-start.9 = (bf16[256,384]{1,0:T(8,128)(2,1)}, bf16[256,384]{1,0:T(8,128)(2,1)S(1)}, u32[]{:S(2)}, u32[]{:S(2)}) collective-permute-start(bf16[256,384]{1,0:T(8,128)(2,1)} %shard_map.103), channel_id=1, source_target_pairs={{0,2},{1,3},{2,0},{3,1},{4,6},{5,7},{6,4},{7,5},{8,10},{9,11},{10,... | collective-permute-start | bytes 589832 | tf_op jit(solution)/shard_map/ppermute | solution.py:325
  114.7 1.3 collective-permute-start.11
  116.1 15.5 %collective-permute-done.10 = bf16[256,384]{1,0:T(8,128)(2,1)S(1)} collective-permute-done((bf16[256,384]{1,0:T(8,128)(2,1)S(1)}, bf16[256,384]{1,0:T(8,128)(2,1)S(1)}, u32[]{:S(2)}, u32[]{:S(2)}) %collective-permute-start.10) | collective-permute-done | bytes 196640 | tf_op jit(solution)/shard_map/ppermute | solution.py:325
  131.7 2.5 %collective-permute-done.7 = bf16[256,384]{1,0:T(8,128)(2,1)S(1)} collective-permute-done((bf16[256,384]{1,0:T(8,128)(2,1)}, bf16[256,384]{1,0:T(8,128)(2,1)S(1)}, u32[]{:S(2)}, u32[]{:S(2)}) %collective-permute-start.7) | collective-permute-done | bytes 196640 | tf_op jit(solution)/shard_map/ppermute | solution.py:325
  134.2 1.6 %collective-permute-done.11 = bf16[256,384]{1,0:T(8,128)(2,1)S(1)} collective-permute-done((bf16[256,384]{1,0:T(8,128)(2,1)}, bf16[256,384]{1,0:T(8,128)(2,1)S(1)}, u32[]{:S(2)}, u32[]{:S(2)}) %collective-permute-start.11) | collective-permute-done | bytes 196640 | tf_op jit(solution)/shard_map/ppermute | solution.py:325
  135.8 1.6 %convolution_convert_fusion.5 = bf16[512,768]{1,0:T(8,128)(2,1)S(1)} fusion(bf16[512,384]{1,0:T(8,128)(2,1)S(1)} %constant_dynamic-update-slice_fusion.2, bf16[4,384,768]{2,1,0:T(8,128)(2,1)} %all-to-all-done, s32[]{:T(128)S(6)} %select_n.124), kind=kOutput, calls=%fused_computation.25 | convolution fusion | flops 302383104 | bytes 1769476 | tf_op jit(solution)/shard_map/dot_general | solution.py:340
  137.5 1.6 %convolution_convert_fusion.6 = bf16[512,768]{1,0:T(8,128)(2,1)S(1)} fusion(bf16[512,384]{1,0:T(8,128)(2,1)S(1)} %constant_dynamic-update-slice_fusion, bf16[4,384,768]{2,1,0:T(8,128)(2,1)} %all-to-all-done, s32[]{:T(128)S(6)} %select_n.122), kind=kOutput, calls=%fused_computation.26 | convolution fusion | flops 302383104 | bytes 1769476 | tf_op jit(solution)/shard_map/dot_general | solution.py:340
  139.1 1.6 %convert_add_fusion.1 = f32[512,768]{1,0:T(8,128)S(1)} fusion(bf16[512,768]{1,0:T(8,128)(2,1)S(1)} %convolution_convert_fusion.5, bf16[512,768]{1,0:T(8,128)(2,1)S(1)} %convolution_convert_fusion.6, bf16[512,384]{1,0:T(8,128)(2,1)S(1)} %constant_dynamic-update-slice_fusion.4, bf16[4,384,768]{2,1,0:T(8,128)(2,1)} %all-to-all-done, s32[]{:T(128)S(6)} %select_n.126), kind=kOutput, calls=%fused_computation.20 | convolution fusion | flops 304349184 | bytes 4128772 | tf_op jit(solution)/shard_map/dot_general | solution.py:340
  140.8 1.6 %convolution_convert_fusion.2 = bf16[512,768]{1,0:T(8,128)(2,1)S(1)} fusion(bf16[512,384]{1,0:T(8,128)(2,1)S(1)} %constant_dynamic-update-slice_fusion.2, bf16[4,384,768]{2,1,0:T(8,128)(2,1)} %collective-permute-done.12, s32[]{:T(128)S(6)} %select_n.124), kind=kOutput, calls=%fused_computation.22 | convolution fusion | flops 302383104 | bytes 1769476 | tf_op jit(solution)/shard_map/dot_general | solution.py:344
  142.4 1.6 %convolution_convert_fusion.3 = bf16[512,768]{1,0:T(8,128)(2,1)S(1)} fusion(bf16[512,384]{1,0:T(8,128)(2,1)S(1)} %constant_dynamic-update-slice_fusion, bf16[4,384,768]{2,1,0:T(8,128)(2,1)} %collective-permute-done.12, s32[]{:T(128)S(6)} %select_n.122), kind=kOutput, calls=%fused_computation.23 | convolution fusion | flops 302383104 | bytes 1769476 | tf_op jit(solution)/shard_map/dot_general | solution.py:344
  144.1 1.7 %convert_add_fusion = f32[512,768]{1,0:T(8,128)S(1)} fusion(bf16[512,768]{1,0:T(8,128)(2,1)S(1)} %convolution_convert_fusion.2, bf16[512,768]{1,0:T(8,128)(2,1)S(1)} %convolution_convert_fusion.3, bf16[512,384]{1,0:T(8,128)(2,1)S(1)} %constant_dynamic-update-slice_fusion.4, bf16[4,384,768]{2,1,0:T(8,128)(2,1)} %collective-permute-done.12, s32[]{:T(128)S(6)} %select_n.126), kind=kOutput, calls=%fused_computation.19 | convolution fusion | flops 304349184 | bytes 4128772 | tf_op jit(solution)/shard_map/dot_general | solution.py:344
  145.8 4.7 %fusion.12 = f32[512,1536]{1,0:T(8,128)} fusion(f32[512,768]{1,0:T(8,128)S(1)} %convert_add_fusion, f32[512,768]{1,0:T(8,128)S(1)} %convert_add_fusion.1, f32[1536]{0:T(1024)S(1)} %dynamic-slice_reduce_fusion, bf16[512,6144]{1,0:T(8,128)(2,1)} %param.10, s32[]{:T(128)S(6)} %select_n.103, pred[]{:T(512)S(6)} %eq.28, bf16[384,6144]{1,0:T(8,128)(2,1)} %param.19, ...), kind=kOutput, calls=%fused_computation.15 | convolution fusion | flops 611844096 | bytes 9444864 | tf_op jit(solution)/shard_map/dot_general | solution.py:333
  (75 shorter events, 11.3 us)
Async XLA Ops:
  0.0 14.2 %copy-start = (bf16[8,3,6144]{2,0,1:T(8,128)(2,1)S(1)}, bf16[8,3,6144]{2,0,1:T(8,128)(2,1)}, u32[]{:S(2)}) copy-start(bf16[8,3,6144]{2,0,1:T(8,128)(2,1)} %param.11) | copy-start | bytes 884740
  2.5 4.5 %copy-start.4 = (bf16[1,512,768]{2,1,0:T(8,128)(2,1)}, bf16[1,512,768]{2,1,0:T(8,128)(2,1)S(1)}, u32[]{:S(2)}) copy-start(bf16[1,512,768]{2,1,0:T(8,128)(2,1)S(1)} %reshape.85) | copy-start | bytes 2359300
  2.5 45.7 %collective-permute-start.4 = (bf16[1,512,768]{2,1,0:T(8,128)(2,1)S(1)}, bf16[1,512,768]{2,1,0:T(8,128)(2,1)S(1)}, u32[]{:S(2)}, u32[]{:S(2)}) collective-permute-start(bf16[1,512,768]{2,1,0:T(8,128)(2,1)S(1)} %reshape.85), channel_id=1, source_target_pairs={{0,24},{4,28},{8,0},{12,4},{16,8},{20,12},{24,16},{28,20},{1,25},{... | collective-permute-start | bytes 2359304 | tf_op jit(solution)/shard_map/ppermute | solution.py:14
  4.7 43.4 %collective-permute-start.3 = (bf16[1,512,768]{2,1,0:T(8,128)(2,1)S(1)}, bf16[1,512,768]{2,1,0:T(8,128)(2,1)S(1)}, u32[]{:S(2)}, u32[]{:S(2)}) collective-permute-start(bf16[1,512,768]{2,1,0:T(8,128)(2,1)S(1)} %reshape.85), channel_id=1, source_target_pairs={{0,16},{4,20},{8,24},{12,28},{16,0},{20,4},{24,8},{28,12},{1,17},{... | collective-permute-start | bytes 2359304 | tf_op jit(solution)/shard_map/ppermute | solution.py:14
  5.0 45.0 %collective-permute-start.2 = (bf16[1,512,768]{2,1,0:T(8,128)(2,1)S(1)}, bf16[1,512,768]{2,1,0:T(8,128)(2,1)}, u32[]{:S(2)}, u32[]{:S(2)}) collective-permute-start(bf16[1,512,768]{2,1,0:T(8,128)(2,1)S(1)} %reshape.85), channel_id=1, source_target_pairs={{0,8},{4,12},{8,16},{12,20},{16,24},{20,28},{24,0},{28,4},{1,9},{5... | collective-permute-start | bytes 2359304 | tf_op jit(solution)/shard_map/ppermute | solution.py:14
  8.8 4.9 %copy-start.11 = (s32[8]{0:T(128)S(1)}, s32[8]{0:T(128)}, u32[]{:S(2)}) copy-start(s32[8]{0:T(128)} %param.12) | copy-start | bytes 100
  8.8 57.0 %all-to-all-start = ((bf16[4,384,768]{2,1,0:T(8,128)(2,1)}), bf16[4,384,768]{2,1,0:T(8,128)(2,1)}, u32[]{:S(2)}, u32[]{:S(2)}) async-start(bf16[4,384,768]{2,1,0:T(8,128)(2,1)} %pad_maximum_fusion.1), calls=%async_computation | async-start | bytes 4718592 | tf_op jit(solution)/shard_map/all_to_all | solution.py:235
  32.1 0.7 copy-start.9
  32.2 0.7 copy-start.10
  34.8 21.2 %collective-permute-start = (bf16[512,768]{1,0:T(8,128)(2,1)}, bf16[512,768]{1,0:T(8,128)(2,1)}, u32[]{:S(2)}, u32[]{:S(2)}) collective-permute-start(bf16[512,768]{1,0:T(8,128)(2,1)} %get-tuple-element.51), channel_id=1, source_target_pairs={{0,4},{4,8},{8,12},{12,16},{16,20},{20,24},{24,28},{28,0},{1,5},{5... | collective-permute-start | bytes 2359304 | tf_op jit(solution)/shard_map/ppermute | solution.py:14
  38.8 26.9 %collective-permute-start.1 = (bf16[512,768]{1,0:T(8,128)(2,1)}, bf16[512,768]{1,0:T(8,128)(2,1)}, u32[]{:S(2)}, u32[]{:S(2)}) collective-permute-start(bf16[512,768]{1,0:T(8,128)(2,1)} %get-tuple-element.51), channel_id=1, source_target_pairs={{0,8},{4,12},{8,16},{12,20},{16,24},{20,28},{24,0},{28,4},{1,9},{5... | collective-permute-start | bytes 2359304 | tf_op jit(solution)/shard_map/ppermute | solution.py:14
  38.9 0.8 copy-start.3
  48.2 0.9 copy-start.5
  49.0 0.9 copy-start.6
  52.0 23.3 %copy-start.2 = (bf16[4,512,768]{2,1,0:T(8,128)(2,1)}, bf16[4,512,768]{2,1,0:T(8,128)(2,1)S(1)}, u32[]{:S(2)}) copy-start(bf16[4,512,768]{2,1,0:T(8,128)(2,1)S(1)} %pad_maximum_fusion.refs_6_.refs_7_) | copy-start | bytes 9437188
  65.7 9.5 %collective-permute-start.5 = (bf16[4,512,768]{2,1,0:T(8,128)(2,1)S(1)}, bf16[4,512,768]{2,1,0:T(8,128)(2,1)}, u32[]{:S(2)}, u32[]{:S(2)}) collective-permute-start(bf16[4,512,768]{2,1,0:T(8,128)(2,1)S(1)} %pad_maximum_fusion.refs_6_.refs_7_), channel_id=1, source_target_pairs={{0,4},{4,0},{8,12},{12,8},{16,20},{20,16},{24,28},{28,24},{1,5},{5... | collective-permute-start | bytes 9437192 | tf_op jit(solution)/shard_map/ppermute | solution.py:297
  70.9 69.9 %collective-permute-start.12 = (bf16[4,384,768]{2,1,0:T(8,128)(2,1)}, bf16[4,384,768]{2,1,0:T(8,128)(2,1)}, u32[]{:S(2)}, u32[]{:S(2)}) collective-permute-start(bf16[4,384,768]{2,1,0:T(8,128)(2,1)} %all-to-all-done), channel_id=1, source_target_pairs={{0,4},{4,0},{8,12},{12,8},{16,20},{20,16},{24,28},{28,24},{1,5},{5... | collective-permute-start | bytes 7077896 | tf_op jit(solution)/shard_map/ppermute | solution.py:319
  91.9 21.8 %collective-permute-start.8 = (bf16[256,384]{1,0:T(8,128)(2,1)}, bf16[256,384]{1,0:T(8,128)(2,1)S(1)}, u32[]{:S(2)}, u32[]{:S(2)}) collective-permute-start(bf16[256,384]{1,0:T(8,128)(2,1)} %shard_map.102), channel_id=1, source_target_pairs={{0,2},{1,3},{2,0},{3,1},{4,6},{5,7},{6,4},{7,5},{8,10},{9,11},{10,... | collective-permute-start | bytes 589832 | tf_op jit(solution)/shard_map/ppermute | solution.py:325
  94.2 20.5 %collective-permute-start.6 = (bf16[256,384]{1,0:T(8,128)(2,1)}, bf16[256,384]{1,0:T(8,128)(2,1)S(1)}, u32[]{:S(2)}, u32[]{:S(2)}) collective-permute-start(bf16[256,384]{1,0:T(8,128)(2,1)} %shard_map.102), channel_id=1, source_target_pairs={{0,1},{1,2},{2,3},{3,0},{4,5},{5,6},{6,7},{7,4},{8,9},{9,10},{10,1... | collective-permute-start | bytes 589832 | tf_op jit(solution)/shard_map/ppermute | solution.py:325
  94.2 19.4 %copy-start.7 = (bf16[256,384]{1,0:T(8,128)(2,1)S(1)}, bf16[256,384]{1,0:T(8,128)(2,1)}, u32[]{:S(2)}) copy-start(bf16[256,384]{1,0:T(8,128)(2,1)} %shard_map.102) | copy-start | bytes 589828
  111.0 20.6 %collective-permute-start.9 = (bf16[256,384]{1,0:T(8,128)(2,1)}, bf16[256,384]{1,0:T(8,128)(2,1)S(1)}, u32[]{:S(2)}, u32[]{:S(2)}) collective-permute-start(bf16[256,384]{1,0:T(8,128)(2,1)} %shard_map.103), channel_id=1, source_target_pairs={{0,2},{1,3},{2,0},{3,1},{4,6},{5,7},{6,4},{7,5},{8,10},{9,11},{10,... | collective-permute-start | bytes 589832 | tf_op jit(solution)/shard_map/ppermute | solution.py:325
  113.2 21.0 %collective-permute-start.7 = (bf16[256,384]{1,0:T(8,128)(2,1)}, bf16[256,384]{1,0:T(8,128)(2,1)S(1)}, u32[]{:S(2)}, u32[]{:S(2)}) collective-permute-start(bf16[256,384]{1,0:T(8,128)(2,1)} %shard_map.103), channel_id=1, source_target_pairs={{0,1},{1,2},{2,3},{3,0},{4,5},{5,6},{6,7},{7,4},{8,9},{9,10},{10,1... | collective-permute-start | bytes 589832 | tf_op jit(solution)/shard_map/ppermute | solution.py:325
  113.6 18.0 %collective-permute-start.10 = (bf16[256,384]{1,0:T(8,128)(2,1)S(1)}, bf16[256,384]{1,0:T(8,128)(2,1)S(1)}, u32[]{:S(2)}, u32[]{:S(2)}) collective-permute-start(bf16[256,384]{1,0:T(8,128)(2,1)S(1)} %copy-done.7), channel_id=1, source_target_pairs={{0,3},{1,0},{2,1},{3,2},{4,7},{5,4},{6,5},{7,6},{8,11},{9,8},{10,9... | collective-permute-start | bytes 589832 | tf_op jit(solution)/shard_map/ppermute | solution.py:325
  114.7 21.1 %collective-permute-start.11 = (bf16[256,384]{1,0:T(8,128)(2,1)}, bf16[256,384]{1,0:T(8,128)(2,1)S(1)}, u32[]{:S(2)}, u32[]{:S(2)}) collective-permute-start(bf16[256,384]{1,0:T(8,128)(2,1)} %shard_map.103), channel_id=1, source_target_pairs={{0,3},{1,0},{2,1},{3,2},{4,7},{5,4},{6,5},{7,6},{8,11},{9,8},{10,9... | collective-permute-start | bytes 589832 | tf_op jit(solution)/shard_map/ppermute | solution.py:325
  144.1 1.7 %copy-start.8 = (bf16[256,384]{1,0:T(8,128)(2,1)S(1)}, bf16[256,384]{1,0:T(8,128)(2,1)}, u32[]{:S(2)}) copy-start(bf16[256,384]{1,0:T(8,128)(2,1)} %shard_map.103) | copy-start | bytes 589828
  145.8 4.7 %copy-start.1 = (bf16[8,3,6144]{2,0,1:T(8,128)(2,1)S(1)}, bf16[8,3,6144]{2,0,1:T(8,128)(2,1)}, u32[]{:S(2)}) copy-start(bf16[8,3,6144]{2,0,1:T(8,128)(2,1)} %param.11) | copy-start | bytes 884740

commit v21 on v20

--- a/solution.py
+++ b/solution.py
@@ -110,7 +110,7 @@
     )(queries, local_stack, local_stack, bias)
 
 
-def flash_kernel(chosen, q_ref, k1_ref, v1_ref, k2_ref, v2_ref, ak_ref, av_ref, bk_ref, bv_ref, bias_ref, m_in, l_in, acc_in, o_ref, m_sc, l_sc, acc_sc, *, heads, n_local, half):
+def flash_kernel(chosen, q_ref, k1_ref, v1_ref, k2_ref, v2_ref, ak_ref, av_ref, ck_ref, cv_ref, bk_ref, bv_ref, bias_ref, m_in, l_in, acc_in, o_ref, m_sc, l_sc, acc_sc, *, heads, n_local, half):
     step = pl.program_id(0)
     span = q_ref.shape[0]
     blocks = bias_ref.shape[0]
@@ -154,7 +154,11 @@
     def _():
         body(ak_ref, av_ref)
 
-    @pl.when((step >= n_local) & (pos >= half))
+    @pl.when((step >= n_local) & (pos == half))
+    def _():
+        body(ck_ref, cv_ref)
+
+    @pl.when((step >= n_local) & (pos > half))
     def _():
         body(bk_ref, bv_ref)
 
@@ -165,7 +169,7 @@
             o_ref[:, cols] = (acc_sc[h] / l_sc[h]).astype(o_ref.dtype)
 
 
-def flash(queries, before, earlier, same_core, other_core, bias, chosen, state, heads):
+def flash(queries, before, earlier, same_core, sibling_own, other_core, bias, chosen, state, heads):
     span, width = queries.shape
     n_local = 2
     half = same_core.shape[0]
@@ -178,8 +182,11 @@
     def pool_map(kv, upper):
         def index(j, c):
             pos = c[jnp.maximum(j - n_local, 0)]
-            hit = (j >= n_local) & ((pos >= half) == upper)
-            return (jnp.where(hit, pos - upper * half, 0), 0, kv)
+            if upper:
+                hit = (j >= n_local) & (pos > half)
+                return (jnp.where(hit, pos - half - 1, 0), 0, kv)
+            hit = (j >= n_local) & (pos < half)
+            return (jnp.where(hit, pos, 0), 0, kv)
 
         return index
 
@@ -196,6 +203,8 @@
             pl.BlockSpec((keys_len, width), lambda j, c: (0, 1)),
             pl.BlockSpec(kv_block, pool_map(0, False)),
             pl.BlockSpec(kv_block, pool_map(1, False)),
+            pl.BlockSpec(kv_block, lambda j, c: (0, 0, 0)),
+            pl.BlockSpec(kv_block, lambda j, c: (0, 0, 1)),
             pl.BlockSpec(kv_block, pool_map(0, True)),
             pl.BlockSpec(kv_block, pool_map(1, True)),
             pl.BlockSpec((None, blocks, keys_len), lambda j, c: (j, 0, 0)),
@@ -221,7 +230,7 @@
             transcendentals=steps * heads * span * span,
             bytes_accessed=2 * steps * span * width * 2,
         ),
-    )(chosen, queries, before, before, earlier, earlier, same_core, same_core, other_core, other_core, bias, *state)
+    )(chosen, queries, before, before, earlier, earlier, same_core, same_core, sibling_own, sibling_own, other_core, other_core, bias, *state)
 
 
 def fetch_out_weight(w_out, head, core):
@@ -291,10 +300,11 @@
                     own_bias[:, p * parts : (p + 1) * parts], heads)
         for p in range(2)
     ]
-    states, queries, before, earlier, same_core, mine = lax.optimization_barrier(
-        (states, queries, before, earlier, same_core, mine)
-    )
-    other_core = lax.ppermute(same_core, "slot", [(i, i ^ 1) for i in range(slots)])
+    sibling_own = lax.ppermute(pool_flat, "slot", [(i, i ^ 1) for i in range(slots)])
+    states, queries, before, earlier, same_core, sibling_own, mine = lax.optimization_barrier(
+        (states, queries, before, earlier, same_core, sibling_own, mine)
+    )
+    other_core = lax.ppermute(same_core[1:], "slot", [(i, i ^ 1) for i in range(slots)])
     own_mask = lax.dynamic_index_in_dim(block_mask, slot, 0, keepdims=False)
     own_cache = lax.dynamic_index_in_dim(cache_index, slot, 0, keepdims=False)
     sibling_slot = jnp.bitwise_xor(slot, 1)
@@ -312,7 +322,7 @@
     parts = rows // BLOCK
     queries = queries.reshape(span, width)
     mixed_parts = [
-        flash(queries[p * rows : (p + 1) * rows], before, earlier, same_core, other_core,
+        flash(queries[p * rows : (p + 1) * rows], before, earlier, same_core, sibling_own, other_core,
               bias[1:, p * parts : (p + 1) * parts], own_cache, states[p], heads)
         for p in range(2)
     ]

time: 151 us -> 149 us (0.987)
  matrix products: 28.2 us -> 25 us
  starting transfers between devices: 23.3 us -> 20.6 us
  local copies, waits for them, and re-layouts: 12.5 us -> 14.4 us
    ppermute x1 -> x2, starting transfers between devices: 4.11 us -> 0.01 us  [the longest x1 0.01 us: local(): lax.ppermute(same_core[1:], 'slot', [(i, i ^ 1) for i in range(slots)])]
    dot_general x3, matrix products: 4.95 us -> 1.73 us  [local(): part = jnp.dot(group_o, sibling_block, preferred_element_type=jnp.float32)]
    slice x0 -> x1, local copies, waits for them, and re-layouts: none -> 1.6 us  [local(): same_core[1:]]
  transfers between devices with their start and end apart: 14 -> 15, of which waited for: 6 -> 5; matrix products, arithmetic and copies ran while one was open for 25% -> 25% of each run, Pallas kernels for 27% -> 28%
where the time goes in v21:
time: 149 us; the launch traced here: 148 us
  Pallas kernels  40.9 us (27%)
  waiting for transfers between devices  35.2 us (24%)
  matrix products  25 us (17%)
  starting transfers between devices  20.6 us (14%)
  local copies, waits for them, and re-layouts  14.4 us (10%)
  other arithmetic  11.7 us (8%)
    pallas_call x2, Pallas kernels, flash(): pl.pallas_call(kernel, grid_spec=grid_spec, out_shape=jax.ShapeDtypeStruc...  33.8 us
    ppermute x6, waiting for transfers between devices, local(): lax.ppermute(part, 'head', [(i, (i + shift) % groups) for i in range(grou...  20.1 us
    ppermute x5, waiting for transfers between devices, from_behind(): lax.ppermute(shard, axis, [(i, (i + by) % length) for i in range(length)])  15.1 us
    dot_general x1, matrix products, local(): jnp.einsum('td,dkh->kth', hidden, w_qkv, preferred_element_type=jnp.float32)  12.8 us
    ppermute x6, starting transfers between devices, local(): lax.ppermute(part, 'head', [(i, (i + shift) % groups) for i in range(grou...  8.14 us
    pallas_call x2, Pallas kernels, flash_local(): pl.pallas_call(kernel, grid=(steps,), in_specs=[pl.BlockSpec((span, width...  7.15 us
    ppermute x5, starting transfers between devices, from_behind(): lax.ppermute(shard, axis, [(i, (i + by) % length) for i in range(length)])  6.97 us
    dot_general x3, matrix products, local(): part = jnp.dot(group_o, mine_block, preferred_element_type=jnp.float32)  4.91 us
  transfers between devices with their start and end apart: 15, of which 5 were waited for; matrix products, arithmetic and copies ran while one was open for 25% of the time, Pallas kernels for 28%

profile of v21, /device:TPU:9, one launch (start us, length us, event | category | flops | bytes accessed | tf_op | source)
XLA Modules:
  0.0 148.1 jit_solution(5086269357715047546)
XLA Ops:
  0.0 3.2 %reshape.85 = bf16[1,512,768]{2,1,0:T(8,128)(2,1)} reshape(bf16[1,512,2,384]{3,2,1,0:T(2,128)(2,1)} %param.18) | data formatting | bytes 1572864 | tf_op jit(solution)/shard_map/reshape | solution.py:273
  3.2 1.2 collective-permute-start.2
  4.4 1.2 collective-permute-start.3
  5.7 1.2 collective-permute-start.4
  6.8 1.8 %dynamic-slice_bitcast_fusion.3 = (bf16[1,384,768]{2,1,0:T(8,128)(2,1)S(1)}, bf16[1,384,768]{2,1,0:T(8,128)(2,1)S(1)}, bf16[1,384,768]{2,1,0:T(8,128)(2,1)S(1)}, bf16[1,384,768]{2,1,0:T(8,128)(2,1)S(1)}) fusion(bf16[384,6144]{1,0:T(8,128)(2,1)} %param.19, s32[]{:T(128)S(6)} %select_n.112, s32[]{:T(128)S(6)} %select_n.114, s32[]{:T(128)S(6)} %select_n.113, ...), kind=kLoop, calls=%fused_computation.47 | loop fusion | bytes 4718608 | tf_op jit(solution)/shard_map/stack | solution.py:240
  8.6 1.7 %pad_maximum_fusion.1 = bf16[4,384,768]{2,1,0:T(8,128)(2,1)} fusion(bf16[1,384,768]{2,1,0:T(8,128)(2,1)S(1)} %get-tuple-element.50, bf16[1,384,768]{2,1,0:T(8,128)(2,1)S(1)} %get-tuple-element.48, bf16[1,384,768]{2,1,0:T(8,128)(2,1)S(1)} %get-tuple-element.49, bf16[1,384,768]{2,1,0:T(8,128)(2,1)S(1)} %get-tuple-element.47), kind=kLoop, calls=%fused_computation.17 | loop fusion | flops 3538944 | bytes 4718592 | tf_op jit(solution)/shard_map/stack | solution.py:240
  10.3 4.9 %all-to-all-start = ((bf16[4,384,768]{2,1,0:T(8,128)(2,1)}), bf16[4,384,768]{2,1,0:T(8,128)(2,1)}, u32[]{:S(2)}, u32[]{:S(2)}) async-start(bf16[4,384,768]{2,1,0:T(8,128)(2,1)} %pad_maximum_fusion.1), calls=%async_computation | async-start | bytes 4718592 | tf_op jit(solution)/shard_map/all_to_all | solution.py:244
  16.7 4.1 %fusion = f32[512]{0:T(512)S(1)} fusion(bf16[512,6144]{1,0:T(8,128)(2,1)} %param.10), kind=kLoop, calls=%fused_computation.2 | loop fusion | flops 9436672 | bytes 6293504 | tf_op jit(solution)/shard_map/reduce_sum | solution.py:282
  20.8 12.8 %fusion.13 = f32[3,512,384]{2,1,0:T(8,128)S(1)} fusion(bf16[6144,3,384]{2,0,1:T(8,128)(2,1)} %param.15, bf16[512,6144]{1,0:T(8,128)(2,1)} %param.10, f32[6144]{0:T(1024)S(1)} %bitcast.67, f32[6144]{0:T(1024)S(1)} %bitcast.68, f32[512]{0:T(512)S(1)} %add_rsqrt_fusion.6), kind=kOutput, calls=%fused_computation.18 | convolution fusion | flops 7263485952 | bytes 22857728 | tf_op jit(solution)/shard_map/td,dkh->kth/dot_general | solution.py:285
  35.0 1.2 pad_maximum_fusion.2
  36.3 2.3 %collective-permute-start = (bf16[512,768]{1,0:T(8,128)(2,1)}, bf16[512,768]{1,0:T(8,128)(2,1)}, u32[]{:S(2)}, u32[]{:S(2)}) collective-permute-start(bf16[512,768]{1,0:T(8,128)(2,1)} %get-tuple-element.53), channel_id=1, source_target_pairs={{0,4},{4,8},{8,12},{12,16},{16,20},{20,24},{24,28},{28,0},{1,5},{5... | collective-permute-start | bytes 2359304 | tf_op jit(solution)/shard_map/ppermute | solution.py:14
  38.6 1.1 collective-permute-start.1
  42.0 3.6 %shard_map.101 = (f32[3,256,1]{2,1,0:T(8,128)}, f32[3,256,1]{2,1,0:T(8,128)}, f32[3,256,128]{2,1,0:T(8,128)}) custom-call(bf16[256,384]{1,0:T(8,128)(2,1)} %get-tuple-element.63.refs_0_, bf16[1,512,768]{2,1,0:T(8,128)(2,1)} %get-tuple-element.54.refs_1_.refs_2_, bf16[1,512,768]{2,1,0:T(8,128)(2,1)} %get-tuple-element.54.refs_1_.refs_2_, ...), custom_call_target="tpu_custom_call" | custom-call | flops 201326592 | bytes 786432 | tf_op jit(solution)/shard_map/pallas_call | solution.py:89
  45.6 3.6 %shard_map.100 = (f32[3,256,1]{2,1,0:T(8,128)}, f32[3,256,1]{2,1,0:T(8,128)}, f32[3,256,128]{2,1,0:T(8,128)}) custom-call(bf16[256,384]{1,0:T(8,128)(2,1)} %get-tuple-element.64.refs_0_, bf16[1,512,768]{2,1,0:T(8,128)(2,1)} %get-tuple-element.54.refs_1_.refs_2_, bf16[1,512,768]{2,1,0:T(8,128)(2,1)} %get-tuple-element.54.refs_1_.refs_2_, ...), custom_call_target="tpu_custom_call" | custom-call | flops 201326592 | bytes 786432 | tf_op jit(solution)/shard_map/pallas_call | solution.py:89
  50.0 2.0 %pad_maximum_fusion.refs_6_.refs_7_ = bf16[4,512,768]{2,1,0:T(8,128)(2,1)S(1)} fusion(bf16[1,512,768]{2,1,0:T(8,128)(2,1)} %collective-permute-done.4, bf16[1,512,768]{2,1,0:T(8,128)(2,1)} %copy-done.5, bf16[1,512,768]{2,1,0:T(8,128)(2,1)} %copy-done.4, bf16[1,512,768]{2,1,0:T(8,128)(2,1)} %reshape.85), kind=kLoop, calls=%fused_computation.11 | loop fusion | flops 4718592 | bytes 6291456 | tf_op jit(solution)/shard_map/concatenate | solution.py:275
  52.1 3.6 %collective-permute-done.refs_2_.refs_3_ = bf16[512,768]{1,0:T(8,128)(2,1)} collective-permute-done((bf16[512,768]{1,0:T(8,128)(2,1)}, bf16[512,768]{1,0:T(8,128)(2,1)}, u32[]{:S(2)}, u32[]{:S(2)}) %collective-permute-start) | collective-permute-done | bytes 786464 | tf_op jit(solution)/shard_map/ppermute | solution.py:14
  55.7 11.5 %collective-permute-done.1.refs_4_.refs_5_ = bf16[512,768]{1,0:T(8,128)(2,1)} collective-permute-done((bf16[512,768]{1,0:T(8,128)(2,1)}, bf16[512,768]{1,0:T(8,128)(2,1)}, u32[]{:S(2)}, u32[]{:S(2)}) %collective-permute-start.1) | collective-permute-done | bytes 786464 | tf_op jit(solution)/shard_map/ppermute | solution.py:14
  67.2 1.6 %slice.97 = bf16[3,512,768]{2,1,0:T(8,128)(2,1)} slice(bf16[4,512,768]{2,1,0:T(8,128)(2,1)S(1)} %pad_maximum_fusion.refs_6_.refs_7_), slice={[1:4], [0:512], [0:768]} | slice | bytes 4718592 | tf_op jit(solution)/shard_map/slice | solution.py:307
  70.4 1.3 compare_select_fusion.6.refs_0_
  72.3 1.8 %fusion.53 = (bf16[256,384]{1,0:T(8,128)(2,1)}, bf16[256,384]{1,0:T(8,128)(2,1)}) fusion(bf16[512,384]{1,0:T(8,128)(2,1)} %copy-done.3), kind=kLoop, calls=%fused_computation.122 | loop fusion | bytes 786432 | tf_op jit(solution)/shard_map/slice | solution.py:325
  74.1 16.8 %shard_map.102 = bf16[256,384]{1,0:T(8,128)(2,1)} custom-call(s32[6]{0:T(128)} %compare_select_fusion.6.refs_0_, bf16[256,384]{1,0:T(8,128)(2,1)} %get-tuple-element.62.refs_1_, bf16[512,768]{1,0:T(8,128)(2,1)} %collective-permute-done.refs_2_.refs_3_, bf16[512,768]{1,0:T(8,128)(2,1)} %collective-permute-done.refs_2_.refs_3_, ...), custom_call_target="tpu_custom_call" | custom-call | flops 805306368 | bytes 3145728 | tf_op jit(solution)/shard_map/pallas_call | solution.py:223
  90.9 1.2 collective-permute-start.7
  92.1 3.3 %collective-permute-start.9 = (bf16[256,384]{1,0:T(8,128)(2,1)}, bf16[256,384]{1,0:T(8,128)(2,1)S(1)}, u32[]{:S(2)}, u32[]{:S(2)}) collective-permute-start(bf16[256,384]{1,0:T(8,128)(2,1)} %shard_map.102), channel_id=1, source_target_pairs={{0,2},{1,3},{2,0},{3,1},{4,6},{5,7},{6,4},{7,5},{8,10},{9,11},{10,... | collective-permute-start | bytes 589832 | tf_op jit(solution)/shard_map/ppermute | solution.py:335
  95.5 17.0 %shard_map.103 = bf16[256,384]{1,0:T(8,128)(2,1)} custom-call(s32[6]{0:T(128)} %compare_select_fusion.6.refs_0_, bf16[256,384]{1,0:T(8,128)(2,1)} %get-tuple-element.61.refs_1_, bf16[512,768]{1,0:T(8,128)(2,1)} %collective-permute-done.refs_2_.refs_3_, bf16[512,768]{1,0:T(8,128)(2,1)} %collective-permute-done.refs_2_.refs_3_, ...), custom_call_target="tpu_custom_call" | custom-call | flops 805306368 | bytes 3145728 | tf_op jit(solution)/shard_map/pallas_call | solution.py:223
  112.4 1.5 collective-permute-start.10
  114.0 2.1 %collective-permute-start.12 = (bf16[256,384]{1,0:T(8,128)(2,1)}, bf16[256,384]{1,0:T(8,128)(2,1)S(1)}, u32[]{:S(2)}, u32[]{:S(2)}) collective-permute-start(bf16[256,384]{1,0:T(8,128)(2,1)} %shard_map.103), channel_id=1, source_target_pairs={{0,3},{1,0},{2,1},{3,2},{4,7},{5,4},{6,5},{7,6},{8,11},{9,8},{10,9... | collective-permute-start | bytes 589832 | tf_op jit(solution)/shard_map/ppermute | solution.py:335
  116.2 16.0 %collective-permute-done.11 = bf16[256,384]{1,0:T(8,128)(2,1)S(1)} collective-permute-done((bf16[256,384]{1,0:T(8,128)(2,1)S(1)}, bf16[256,384]{1,0:T(8,128)(2,1)S(1)}, u32[]{:S(2)}, u32[]{:S(2)}) %collective-permute-start.11) | collective-permute-done | bytes 196640 | tf_op jit(solution)/shard_map/ppermute | solution.py:335
  133.1 3.3 %collective-permute-done.12 = bf16[256,384]{1,0:T(8,128)(2,1)S(1)} collective-permute-done((bf16[256,384]{1,0:T(8,128)(2,1)}, bf16[256,384]{1,0:T(8,128)(2,1)S(1)}, u32[]{:S(2)}, u32[]{:S(2)}) %collective-permute-start.12) | collective-permute-done | bytes 196640 | tf_op jit(solution)/shard_map/ppermute | solution.py:335
  136.5 1.6 %convolution_convert_fusion.6 = bf16[512,768]{1,0:T(8,128)(2,1)S(1)} fusion(bf16[512,384]{1,0:T(8,128)(2,1)S(1)} %constant_dynamic-update-slice_fusion, bf16[4,384,768]{2,1,0:T(8,128)(2,1)} %all-to-all-done, s32[]{:T(128)S(6)} %select_n.122), kind=kOutput, calls=%fused_computation.26 | convolution fusion | flops 302383104 | bytes 1769476 | tf_op jit(solution)/shard_map/dot_general | solution.py:350
  138.1 1.6 %convolution_convert_fusion.5 = bf16[512,768]{1,0:T(8,128)(2,1)S(1)} fusion(bf16[512,384]{1,0:T(8,128)(2,1)S(1)} %constant_dynamic-update-slice_fusion.2, bf16[4,384,768]{2,1,0:T(8,128)(2,1)} %all-to-all-done, s32[]{:T(128)S(6)} %select_n.124), kind=kOutput, calls=%fused_computation.25 | convolution fusion | flops 302383104 | bytes 1769476 | tf_op jit(solution)/shard_map/dot_general | solution.py:350
  139.7 1.6 %convert_add_fusion.1 = f32[512,768]{1,0:T(8,128)S(1)} fusion(bf16[512,768]{1,0:T(8,128)(2,1)S(1)} %convolution_convert_fusion.5, bf16[512,768]{1,0:T(8,128)(2,1)S(1)} %convolution_convert_fusion.6, bf16[512,384]{1,0:T(8,128)(2,1)S(1)} %constant_dynamic-update-slice_fusion.4, bf16[4,384,768]{2,1,0:T(8,128)(2,1)} %all-to-all-done, s32[]{:T(128)S(6)} %select_n.126), kind=kOutput, calls=%fused_computation.20 | convolution fusion | flops 304349184 | bytes 4128772 | tf_op jit(solution)/shard_map/dot_general | solution.py:350
  143.5 4.7 %fusion.12 = f32[512,1536]{1,0:T(8,128)} fusion(f32[512,768]{1,0:T(8,128)S(1)} %convert_add_fusion, f32[512,768]{1,0:T(8,128)S(1)} %convert_add_fusion.1, f32[1536]{0:T(1024)S(1)} %dynamic-slice_reduce_fusion, bf16[512,6144]{1,0:T(8,128)(2,1)} %param.10, s32[]{:T(128)S(6)} %select_n.103, pred[]{:T(512)S(6)} %eq.28, bf16[384,6144]{1,0:T(8,128)(2,1)} %param.19, ...), kind=kOutput, calls=%fused_computation.15 | convolution fusion | flops 611844096 | bytes 9444864 | tf_op jit(solution)/shard_map/dot_general | solution.py:343
  (76 shorter events, 11.3 us)
Async XLA Ops:
  0.0 15.8 %copy-start = (bf16[8,3,6144]{2,0,1:T(8,128)(2,1)S(1)}, bf16[8,3,6144]{2,0,1:T(8,128)(2,1)}, u32[]{:S(2)}) copy-start(bf16[8,3,6144]{2,0,1:T(8,128)(2,1)} %param.11) | copy-start | bytes 884740
  3.2 36.4 %collective-permute-start.2 = (bf16[1,512,768]{2,1,0:T(8,128)(2,1)}, bf16[1,512,768]{2,1,0:T(8,128)(2,1)S(1)}, u32[]{:S(2)}, u32[]{:S(2)}) collective-permute-start(bf16[1,512,768]{2,1,0:T(8,128)(2,1)} %reshape.85), channel_id=1, source_target_pairs={{0,8},{4,12},{8,16},{12,20},{16,24},{20,28},{24,0},{28,4},{1,9},{5... | collective-permute-start | bytes 2359304 | tf_op jit(solution)/shard_map/ppermute | solution.py:14
  4.4 44.7 %collective-permute-start.3 = (bf16[1,512,768]{2,1,0:T(8,128)(2,1)}, bf16[1,512,768]{2,1,0:T(8,128)(2,1)S(1)}, u32[]{:S(2)}, u32[]{:S(2)}) collective-permute-start(bf16[1,512,768]{2,1,0:T(8,128)(2,1)} %reshape.85), channel_id=1, source_target_pairs={{0,16},{4,20},{8,24},{12,28},{16,0},{20,4},{24,8},{28,12},{1,17},{... | collective-permute-start | bytes 2359304 | tf_op jit(solution)/shard_map/ppermute | solution.py:14
  5.7 44.4 %collective-permute-start.4 = (bf16[1,512,768]{2,1,0:T(8,128)(2,1)}, bf16[1,512,768]{2,1,0:T(8,128)(2,1)}, u32[]{:S(2)}, u32[]{:S(2)}) collective-permute-start(bf16[1,512,768]{2,1,0:T(8,128)(2,1)} %reshape.85), channel_id=1, source_target_pairs={{0,24},{4,28},{8,0},{12,4},{16,8},{20,12},{24,16},{28,20},{1,25},{... | collective-permute-start | bytes 2359304 | tf_op jit(solution)/shard_map/ppermute | solution.py:14
  10.3 4.9 %copy-start.10 = (s32[8]{0:T(128)S(1)}, s32[8]{0:T(128)}, u32[]{:S(2)}) copy-start(s32[8]{0:T(128)} %param.12) | copy-start | bytes 100
  10.3 56.9 %all-to-all-start = ((bf16[4,384,768]{2,1,0:T(8,128)(2,1)}), bf16[4,384,768]{2,1,0:T(8,128)(2,1)}, u32[]{:S(2)}, u32[]{:S(2)}) async-start(bf16[4,384,768]{2,1,0:T(8,128)(2,1)} %pad_maximum_fusion.1), calls=%async_computation | async-start | bytes 4718592 | tf_op jit(solution)/shard_map/all_to_all | solution.py:244
  33.7 0.7 copy-start.8
  33.7 0.8 copy-start.9
  36.3 19.4 %collective-permute-start = (bf16[512,768]{1,0:T(8,128)(2,1)}, bf16[512,768]{1,0:T(8,128)(2,1)}, u32[]{:S(2)}, u32[]{:S(2)}) collective-permute-start(bf16[512,768]{1,0:T(8,128)(2,1)} %get-tuple-element.53), channel_id=1, source_target_pairs={{0,4},{4,8},{8,12},{12,16},{16,20},{20,24},{24,28},{28,0},{1,5},{5... | collective-permute-start | bytes 2359304 | tf_op jit(solution)/shard_map/ppermute | solution.py:14
  38.6 28.6 %collective-permute-start.1 = (bf16[512,768]{1,0:T(8,128)(2,1)}, bf16[512,768]{1,0:T(8,128)(2,1)}, u32[]{:S(2)}, u32[]{:S(2)}) collective-permute-start(bf16[512,768]{1,0:T(8,128)(2,1)} %get-tuple-element.53), channel_id=1, source_target_pairs={{0,8},{4,12},{8,16},{12,20},{16,24},{20,28},{24,0},{28,4},{1,9},{5... | collective-permute-start | bytes 2359304 | tf_op jit(solution)/shard_map/ppermute | solution.py:14
  39.7 9.5 %copy-start.4 = (bf16[1,512,768]{2,1,0:T(8,128)(2,1)}, bf16[1,512,768]{2,1,0:T(8,128)(2,1)S(1)}, u32[]{:S(2)}) copy-start(bf16[1,512,768]{2,1,0:T(8,128)(2,1)S(1)} %collective-permute-done.2) | copy-start | bytes 2359300
  39.7 27.5 %collective-permute-start.5 = (bf16[1,512,768]{2,1,0:T(8,128)(2,1)}, bf16[1,512,768]{2,1,0:T(8,128)(2,1)}, u32[]{:S(2)}, u32[]{:S(2)}) collective-permute-start(bf16[1,512,768]{2,1,0:T(8,128)(2,1)} %reshape.85), channel_id=1, source_target_pairs={{0,4},{4,0},{8,12},{12,8},{16,20},{20,16},{24,28},{28,24},{1,5},{5... | collective-permute-start | bytes 2359304 | tf_op jit(solution)/shard_map/ppermute | solution.py:303
  39.7 0.9 copy-start.3
  49.1 0.9 copy-start.5
  52.1 16.7 %copy-start.2 = (bf16[4,512,768]{2,1,0:T(8,128)(2,1)}, bf16[4,512,768]{2,1,0:T(8,128)(2,1)S(1)}, u32[]{:S(2)}) copy-start(bf16[4,512,768]{2,1,0:T(8,128)(2,1)S(1)} %pad_maximum_fusion.refs_6_.refs_7_) | copy-start | bytes 9437188
  68.8 5.3 %collective-permute-start.6 = (bf16[3,512,768]{2,1,0:T(8,128)(2,1)}, bf16[3,512,768]{2,1,0:T(8,128)(2,1)}, u32[]{:S(2)}, u32[]{:S(2)}) collective-permute-start(bf16[3,512,768]{2,1,0:T(8,128)(2,1)} %slice.97), channel_id=1, source_target_pairs={{0,4},{4,0},{8,12},{12,8},{16,20},{20,16},{24,28},{28,24},{1,5},{5... | collective-permute-start | bytes 7077896 | tf_op jit(solution)/shard_map/ppermute | solution.py:307
  69.8 71.6 %collective-permute-start.13 = (bf16[4,384,768]{2,1,0:T(8,128)(2,1)}, bf16[4,384,768]{2,1,0:T(8,128)(2,1)S(1)}, u32[]{:S(2)}, u32[]{:S(2)}) collective-permute-start(bf16[4,384,768]{2,1,0:T(8,128)(2,1)} %all-to-all-done), channel_id=1, source_target_pairs={{0,4},{4,0},{8,12},{12,8},{16,20},{20,16},{24,28},{28,24},{1,5},{5... | collective-permute-start | bytes 7077896 | tf_op jit(solution)/shard_map/ppermute | solution.py:329
  90.9 23.0 %collective-permute-start.7 = (bf16[256,384]{1,0:T(8,128)(2,1)}, bf16[256,384]{1,0:T(8,128)(2,1)S(1)}, u32[]{:S(2)}, u32[]{:S(2)}) collective-permute-start(bf16[256,384]{1,0:T(8,128)(2,1)} %shard_map.102), channel_id=1, source_target_pairs={{0,1},{1,2},{2,3},{3,0},{4,5},{5,6},{6,7},{7,4},{8,9},{9,10},{10,1... | collective-permute-start | bytes 589832 | tf_op jit(solution)/shard_map/ppermute | solution.py:335
  92.1 21.9 %collective-permute-start.9 = (bf16[256,384]{1,0:T(8,128)(2,1)}, bf16[256,384]{1,0:T(8,128)(2,1)S(1)}, u32[]{:S(2)}, u32[]{:S(2)}) collective-permute-start(bf16[256,384]{1,0:T(8,128)(2,1)} %shard_map.102), channel_id=1, source_target_pairs={{0,2},{1,3},{2,0},{3,1},{4,6},{5,7},{6,4},{7,5},{8,10},{9,11},{10,... | collective-permute-start | bytes 589832 | tf_op jit(solution)/shard_map/ppermute | solution.py:335
  95.5 18.5 %copy-start.6 = (bf16[256,384]{1,0:T(8,128)(2,1)S(1)}, bf16[256,384]{1,0:T(8,128)(2,1)}, u32[]{:S(2)}) copy-start(bf16[256,384]{1,0:T(8,128)(2,1)} %shard_map.102) | copy-start | bytes 589828
  112.4 19.8 %collective-permute-start.8 = (bf16[256,384]{1,0:T(8,128)(2,1)}, bf16[256,384]{1,0:T(8,128)(2,1)S(1)}, u32[]{:S(2)}, u32[]{:S(2)}) collective-permute-start(bf16[256,384]{1,0:T(8,128)(2,1)} %shard_map.103), channel_id=1, source_target_pairs={{0,1},{1,2},{2,3},{3,0},{4,5},{5,6},{6,7},{7,4},{8,9},{9,10},{10,1... | collective-permute-start | bytes 589832 | tf_op jit(solution)/shard_map/ppermute | solution.py:335
  112.4 20.6 %collective-permute-start.10 = (bf16[256,384]{1,0:T(8,128)(2,1)}, bf16[256,384]{1,0:T(8,128)(2,1)S(1)}, u32[]{:S(2)}, u32[]{:S(2)}) collective-permute-start(bf16[256,384]{1,0:T(8,128)(2,1)} %shard_map.103), channel_id=1, source_target_pairs={{0,2},{1,3},{2,0},{3,1},{4,6},{5,7},{6,4},{7,5},{8,10},{9,11},{10,... | collective-permute-start | bytes 589832 | tf_op jit(solution)/shard_map/ppermute | solution.py:335
  113.9 18.3 %collective-permute-start.11 = (bf16[256,384]{1,0:T(8,128)(2,1)S(1)}, bf16[256,384]{1,0:T(8,128)(2,1)S(1)}, u32[]{:S(2)}, u32[]{:S(2)}) collective-permute-start(bf16[256,384]{1,0:T(8,128)(2,1)S(1)} %copy-done.6), channel_id=1, source_target_pairs={{0,3},{1,0},{2,1},{3,2},{4,7},{5,4},{6,5},{7,6},{8,11},{9,8},{10,9... | collective-permute-start | bytes 589832 | tf_op jit(solution)/shard_map/ppermute | solution.py:335
  114.0 22.4 %collective-permute-start.12 = (bf16[256,384]{1,0:T(8,128)(2,1)}, bf16[256,384]{1,0:T(8,128)(2,1)S(1)}, u32[]{:S(2)}, u32[]{:S(2)}) collective-permute-start(bf16[256,384]{1,0:T(8,128)(2,1)} %shard_map.103), channel_id=1, source_target_pairs={{0,3},{1,0},{2,1},{3,2},{4,7},{5,4},{6,5},{7,6},{8,11},{9,8},{10,9... | collective-permute-start | bytes 589832 | tf_op jit(solution)/shard_map/ppermute | solution.py:335
  142.6 0.9 copy-start.7
  143.5 4.7 %copy-start.1 = (bf16[8,3,6144]{2,0,1:T(8,128)(2,1)S(1)}, bf16[8,3,6144]{2,0,1:T(8,128)(2,1)}, u32[]{:S(2)}) copy-start(bf16[8,3,6144]{2,0,1:T(8,128)(2,1)} %param.11) | copy-start | bytes 884740

commit v22 on v21

--- a/solution.py
+++ b/solution.py
@@ -289,16 +289,15 @@
     local_kv = jnp.concatenate([keys.reshape(span, heads * HD), values], axis=1)
     before = from_behind(local_kv, "slot", 1)
     earlier = from_behind(local_kv, "slot", 2)
-    rows = span // 2
-    parts = rows // BLOCK
+    cuts = [(0, span - BLOCK), (span - BLOCK, span)]
     width = heads * HD
     own_mask = lax.dynamic_index_in_dim(block_mask, slot, 0, keepdims=False)
     flat_queries = queries.reshape(span, width)
     own_bias = jnp.zeros((1, blocks_q, span), jnp.float32)
     states = [
-        flash_local(flat_queries[p * rows : (p + 1) * rows], local_kv.reshape(1, span, 2 * width),
-                    own_bias[:, p * parts : (p + 1) * parts], heads)
-        for p in range(2)
+        flash_local(flat_queries[a:b], local_kv.reshape(1, span, 2 * width),
+                    own_bias[:, a // BLOCK : b // BLOCK], heads)
+        for a, b in cuts
     ]
     sibling_own = lax.ppermute(pool_flat, "slot", [(i, i ^ 1) for i in range(slots)])
     states, queries, before, earlier, same_core, sibling_own, mine = lax.optimization_barrier(
@@ -318,13 +317,12 @@
     visible = jnp.transpose(visible.reshape(blocks_q, 3 + cache_len, blocks_q), (1, 0, 2))
     visible = jnp.repeat(visible, BLOCK, axis=2)
     bias = jnp.where(visible > 0, 0.0, -1e30).astype(jnp.float32)
-    rows = span // 2
-    parts = rows // BLOCK
+    cuts = [(0, span - BLOCK), (span - BLOCK, span)]
     queries = queries.reshape(span, width)
     mixed_parts = [
-        flash(queries[p * rows : (p + 1) * rows], before, earlier, same_core, sibling_own, other_core,
-              bias[1:, p * parts : (p + 1) * parts], own_cache, states[p], heads)
-        for p in range(2)
+        flash(queries[a:b], before, earlier, same_core, sibling_own, other_core,
+              bias[1:, a // BLOCK : b // BLOCK], own_cache, states[p], heads)
+        for p, (a, b) in enumerate(cuts)
     ]
     sibling = lax.ppermute(
         mine, "slot", [(i, i ^ 1) for i in range(slots)]

time: 149 us -> 153 us (1.027); the launches traced: 148 us -> 150 us
  waiting for transfers between devices: 35.2 us -> 30.6 us
  Pallas kernels: 40.9 us -> 45.4 us
  local copies, waits for them, and re-layouts: 14.4 us -> 17 us
    ppermute x6, waiting for transfers between devices: 20.1 us -> 13.4 us  [local(): lax.ppermute(part, 'head', [(i, (i + shift) % groups) for i in range(grou...]
    pallas_call x2, Pallas kernels: 33.8 us -> 37.8 us  [flash(): pl.pallas_call(kernel, grid_spec=grid_spec, out_shape=jax.ShapeDtypeStruc...]
    slice x3 -> x8, local copies, waits for them, and re-layouts: 3.28 us -> 7.22 us  [the longest x2 3.27 us: local(): queries[a:b]]
    ppermute x1, waiting for transfers between devices: 0.01 us -> 3.09 us  [local(): lax.ppermute(same_core[1:], 'slot', [(i, i ^ 1) for i in range(slots)])]
  transfers between devices with their start and end apart: 15 -> 15, of which waited for: 5 -> 6; matrix products, arithmetic and copies ran while one was open for 25% -> 27% of each run, Pallas kernels for 28% -> 30%
where the time goes in v22:
time: 153 us; the launch traced here: 150 us
  Pallas kernels  45.4 us (30%)
  waiting for transfers between devices  30.6 us (20%)
  matrix products  25 us (16%)
  starting transfers between devices  20.3 us (13%)
  local copies, waits for them, and re-layouts  17 us (11%)
  other arithmetic  11.6 us (8%)
    pallas_call x2, Pallas kernels, flash(): pl.pallas_call(kernel, grid_spec=grid_spec, out_shape=jax.ShapeDtypeStruc...  37.8 us
    ppermute x5, waiting for transfers between devices, from_behind(): lax.ppermute(shard, axis, [(i, (i + by) % length) for i in range(length)])  14.1 us
    ppermute x6, waiting for transfers between devices, local(): lax.ppermute(part, 'head', [(i, (i + shift) % groups) for i in range(grou...  13.4 us
    dot_general x1, matrix products, local(): jnp.einsum('td,dkh->kth', hidden, w_qkv, preferred_element_type=jnp.float32)  12.8 us
    ppermute x6, starting transfers between devices, local(): lax.ppermute(part, 'head', [(i, (i + shift) % groups) for i in range(grou...  7.87 us
    pallas_call x2, Pallas kernels, flash_local(): pl.pallas_call(kernel, grid=(steps,), in_specs=[pl.BlockSpec((span, width...  7.59 us
    ppermute x5, starting transfers between devices, from_behind(): lax.ppermute(shard, axis, [(i, (i + by) % length) for i in range(length)])  6.98 us
    dot_general x3, matrix products, local(): part = jnp.dot(group_o, mine_block, preferred_element_type=jnp.float32)  4.91 us
  transfers between devices with their start and end apart: 15, of which 6 were waited for; matrix products, arithmetic and copies ran while one was open for 27% of the time, Pallas kernels for 30%

profile of v22, /device:TPU:9, one launch (start us, length us, event | category | flops | bytes accessed | tf_op | source)
XLA Modules:
  0.0 150.3 jit_solution(5602738634947161493)
XLA Ops:
  0.0 3.2 %reshape.85 = bf16[1,512,768]{2,1,0:T(8,128)(2,1)} reshape(bf16[1,512,2,384]{3,2,1,0:T(2,128)(2,1)} %param.18) | data formatting | bytes 1572864 | tf_op jit(solution)/shard_map/reshape | solution.py:273
  3.2 1.2 collective-permute-start.2
  4.4 1.2 collective-permute-start.3
  6.8 1.8 %dynamic-slice_bitcast_fusion.3 = (bf16[1,384,768]{2,1,0:T(8,128)(2,1)S(1)}, bf16[1,384,768]{2,1,0:T(8,128)(2,1)S(1)}, bf16[1,384,768]{2,1,0:T(8,128)(2,1)S(1)}, bf16[1,384,768]{2,1,0:T(8,128)(2,1)S(1)}) fusion(bf16[384,6144]{1,0:T(8,128)(2,1)} %param.19, s32[]{:T(128)S(6)} %select_n.112, s32[]{:T(128)S(6)} %select_n.114, s32[]{:T(128)S(6)} %select_n.113, ...), kind=kLoop, calls=%fused_computation.47 | loop fusion | bytes 4718608 | tf_op jit(solution)/shard_map/stack | solution.py:240
  8.6 1.7 %pad_maximum_fusion.1 = bf16[4,384,768]{2,1,0:T(8,128)(2,1)} fusion(bf16[1,384,768]{2,1,0:T(8,128)(2,1)S(1)} %get-tuple-element.50, bf16[1,384,768]{2,1,0:T(8,128)(2,1)S(1)} %get-tuple-element.48, bf16[1,384,768]{2,1,0:T(8,128)(2,1)S(1)} %get-tuple-element.49, bf16[1,384,768]{2,1,0:T(8,128)(2,1)S(1)} %get-tuple-element.47), kind=kLoop, calls=%fused_computation.17 | loop fusion | flops 3538944 | bytes 4718592 | tf_op jit(solution)/shard_map/stack | solution.py:240
  10.3 4.9 %all-to-all-start = ((bf16[4,384,768]{2,1,0:T(8,128)(2,1)}), bf16[4,384,768]{2,1,0:T(8,128)(2,1)}, u32[]{:S(2)}, u32[]{:S(2)}) async-start(bf16[4,384,768]{2,1,0:T(8,128)(2,1)} %pad_maximum_fusion.1), calls=%async_computation | async-start | bytes 4718592 | tf_op jit(solution)/shard_map/all_to_all | solution.py:244
  16.7 4.1 %fusion = f32[512]{0:T(512)S(1)} fusion(bf16[512,6144]{1,0:T(8,128)(2,1)} %param.10), kind=kLoop, calls=%fused_computation.2 | loop fusion | flops 9436672 | bytes 6293504 | tf_op jit(solution)/shard_map/reduce_sum | solution.py:282
  20.8 12.8 %fusion.13 = f32[3,512,384]{2,1,0:T(8,128)S(1)} fusion(bf16[6144,3,384]{2,0,1:T(8,128)(2,1)} %param.15, bf16[512,6144]{1,0:T(8,128)(2,1)} %param.10, f32[6144]{0:T(1024)S(1)} %bitcast.67, f32[6144]{0:T(1024)S(1)} %bitcast.68, f32[512]{0:T(512)S(1)} %add_rsqrt_fusion.6), kind=kOutput, calls=%fused_computation.18 | convolution fusion | flops 7263485952 | bytes 22857728 | tf_op jit(solution)/shard_map/td,dkh->kth/dot_general | solution.py:285
  35.0 1.2 pad_maximum_fusion.2
  36.3 2.3 %collective-permute-start = (bf16[512,768]{1,0:T(8,128)(2,1)}, bf16[512,768]{1,0:T(8,128)(2,1)}, u32[]{:S(2)}, u32[]{:S(2)}) collective-permute-start(bf16[512,768]{1,0:T(8,128)(2,1)} %get-tuple-element.53), channel_id=1, source_target_pairs={{0,4},{4,8},{8,12},{12,16},{16,20},{20,24},{24,28},{28,0},{1,5},{5... | collective-permute-start | bytes 2359304 | tf_op jit(solution)/shard_map/ppermute | solution.py:14
  42.0 3.1 %shard_map.101 = (f32[3,128,1]{2,1,0:T(8,128)}, f32[3,128,1]{2,1,0:T(8,128)}, f32[3,128,128]{2,1,0:T(8,128)}) custom-call(bf16[128,384]{1,0:T(8,128)(2,1)} %slice.122.refs_0_, bf16[1,512,768]{2,1,0:T(8,128)(2,1)} %get-tuple-element.54.refs_1_.refs_2_, bf16[1,512,768]{2,1,0:T(8,128)(2,1)} %get-tuple-element.54.refs_1_.refs_2_, f32[1,1,512]{2,1,0:T(1,128)} %slice.103.refs_3_), custom_call_target="tpu_custom_call" | custom-call | flops 100663296 | bytes 786432 | tf_op jit(solution)/shard_map/pallas_call | solution.py:89
  45.6 4.5 %shard_map.100 = (f32[3,384,1]{2,1,0:T(8,128)}, f32[3,384,1]{2,1,0:T(8,128)}, f32[3,384,128]{2,1,0:T(8,128)}) custom-call(bf16[384,384]{1,0:T(8,128)(2,1)} %slice.116.refs_0_, bf16[1,512,768]{2,1,0:T(8,128)(2,1)} %get-tuple-element.54.refs_1_.refs_2_, bf16[1,512,768]{2,1,0:T(8,128)(2,1)} %get-tuple-element.54.refs_1_.refs_2_, f32[1,3,512]{2,1,0:T(4,128)} %slice.101.refs_3_), custom_call_target="tpu_custom_call" | custom-call | flops 301989888 | bytes 786432 | tf_op jit(solution)/shard_map/pallas_call | solution.py:89
  51.0 2.0 %pad_maximum_fusion.refs_6_.refs_7_ = bf16[4,512,768]{2,1,0:T(8,128)(2,1)S(1)} fusion(bf16[1,512,768]{2,1,0:T(8,128)(2,1)} %collective-permute-done.4, bf16[1,512,768]{2,1,0:T(8,128)(2,1)} %copy-done.5, bf16[1,512,768]{2,1,0:T(8,128)(2,1)} %copy-done.4, bf16[1,512,768]{2,1,0:T(8,128)(2,1)} %reshape.85), kind=kLoop, calls=%fused_computation.11 | loop fusion | flops 4718592 | bytes 6291456 | tf_op jit(solution)/shard_map/concatenate | solution.py:275
  53.1 2.6 %collective-permute-done.refs_2_.refs_3_ = bf16[512,768]{1,0:T(8,128)(2,1)} collective-permute-done((bf16[512,768]{1,0:T(8,128)(2,1)}, bf16[512,768]{1,0:T(8,128)(2,1)}, u32[]{:S(2)}, u32[]{:S(2)}) %collective-permute-start) | collective-permute-done | bytes 786464 | tf_op jit(solution)/shard_map/ppermute | solution.py:14
  55.7 11.5 %collective-permute-done.1.refs_4_.refs_5_ = bf16[512,768]{1,0:T(8,128)(2,1)} collective-permute-done((bf16[512,768]{1,0:T(8,128)(2,1)}, bf16[512,768]{1,0:T(8,128)(2,1)}, u32[]{:S(2)}, u32[]{:S(2)}) %collective-permute-start.1) | collective-permute-done | bytes 786464 | tf_op jit(solution)/shard_map/ppermute | solution.py:14
  67.2 1.6 %slice.105 = bf16[3,512,768]{2,1,0:T(8,128)(2,1)} slice(bf16[4,512,768]{2,1,0:T(8,128)(2,1)S(1)} %pad_maximum_fusion.refs_6_.refs_7_), slice={[1:4], [0:512], [0:768]} | slice | bytes 4718592 | tf_op jit(solution)/shard_map/slice | solution.py:306
  70.9 1.2 compare_select_fusion.6.refs_0_
  72.2 1.7 %slice.104.refs_1_ = bf16[384,384]{1,0:T(8,128)(2,1)} slice(bf16[512,384]{1,0:T(8,128)(2,1)} %copy-done.3), slice={[0:384], [0:384]} | slice | bytes 589824 | tf_op jit(solution)/shard_map/slice | solution.py:323
  73.9 3.1 %collective-permute-done.6.refs_10_.refs_11_ = bf16[3,512,768]{2,1,0:T(8,128)(2,1)} collective-permute-done((bf16[3,512,768]{2,1,0:T(8,128)(2,1)}, bf16[3,512,768]{2,1,0:T(8,128)(2,1)}, u32[]{:S(2)}, u32[]{:S(2)}) %collective-permute-start.6) | collective-permute-done | bytes 2359328 | tf_op jit(solution)/shard_map/ppermute | solution.py:306
  77.0 23.4 %shard_map.102 = bf16[384,384]{1,0:T(8,128)(2,1)} custom-call(s32[6]{0:T(128)} %compare_select_fusion.6.refs_0_, bf16[384,384]{1,0:T(8,128)(2,1)} %slice.104.refs_1_, bf16[512,768]{1,0:T(8,128)(2,1)} %collective-permute-done.refs_2_.refs_3_, bf16[512,768]{1,0:T(8,128)(2,1)} %collective-permute-done.refs_2_.refs_3_, ...), custom_call_target="tpu_custom_call" | custom-call | flops 1811939328 | bytes 4718592 | tf_op jit(solution)/shard_map/pallas_call | solution.py:223
  101.5 3.4 %collective-permute-start.9 = (bf16[384,384]{1,0:T(8,128)(2,1)}, bf16[384,384]{1,0:T(8,128)(2,1)S(1)}, u32[]{:S(2)}, u32[]{:S(2)}) collective-permute-start(bf16[384,384]{1,0:T(8,128)(2,1)} %shard_map.102), channel_id=1, source_target_pairs={{0,2},{1,3},{2,0},{3,1},{4,6},{5,7},{6,4},{7,5},{8,10},{9,11},{10,... | collective-permute-start | bytes 884744 | tf_op jit(solution)/shard_map/ppermute | solution.py:333
  105.6 1.5 %slice.107.refs_1_ = bf16[128,384]{1,0:T(8,128)(2,1)} slice(bf16[512,384]{1,0:T(8,128)(2,1)} %copy-done.3), slice={[384:512], [0:384]} | slice | bytes 196608 | tf_op jit(solution)/shard_map/slice | solution.py:323
  107.1 14.5 %shard_map.103 = bf16[128,384]{1,0:T(8,128)(2,1)} custom-call(s32[6]{0:T(128)} %compare_select_fusion.6.refs_0_, bf16[128,384]{1,0:T(8,128)(2,1)} %slice.107.refs_1_, bf16[512,768]{1,0:T(8,128)(2,1)} %collective-permute-done.refs_2_.refs_3_, bf16[512,768]{1,0:T(8,128)(2,1)} %collective-permute-done.refs_2_.refs_3_, ...), custom_call_target="tpu_custom_call" | custom-call | flops 201326592 | bytes 1572864 | tf_op jit(solution)/shard_map/pallas_call | solution.py:223
  121.6 1.5 collective-permute-start.8
  123.1 1.8 %collective-permute-start.10 = (bf16[128,384]{1,0:T(8,128)(2,1)}, bf16[128,384]{1,0:T(8,128)(2,1)S(1)}, u32[]{:S(2)}, u32[]{:S(2)}) collective-permute-start(bf16[128,384]{1,0:T(8,128)(2,1)} %shard_map.103), channel_id=1, source_target_pairs={{0,2},{1,3},{2,0},{3,1},{4,6},{5,7},{6,4},{7,5},{8,10},{9,11},{10,... | collective-permute-start | bytes 294920 | tf_op jit(solution)/shard_map/ppermute | solution.py:333
  124.9 4.3 %collective-permute-done.9 = bf16[384,384]{1,0:T(8,128)(2,1)S(1)} collective-permute-done((bf16[384,384]{1,0:T(8,128)(2,1)}, bf16[384,384]{1,0:T(8,128)(2,1)S(1)}, u32[]{:S(2)}, u32[]{:S(2)}) %collective-permute-start.9) | collective-permute-done | bytes 294944 | tf_op jit(solution)/shard_map/ppermute | solution.py:333
  129.2 5.1 %collective-permute-done.11 = bf16[384,384]{1,0:T(8,128)(2,1)S(1)} collective-permute-done((bf16[384,384]{1,0:T(8,128)(2,1)}, bf16[384,384]{1,0:T(8,128)(2,1)S(1)}, u32[]{:S(2)}, u32[]{:S(2)}) %collective-permute-start.11) | collective-permute-done | bytes 294944 | tf_op jit(solution)/shard_map/ppermute | solution.py:333
  134.4 4.1 %collective-permute-done.12 = bf16[128,384]{1,0:T(8,128)(2,1)S(1)} collective-permute-done((bf16[128,384]{1,0:T(8,128)(2,1)}, bf16[128,384]{1,0:T(8,128)(2,1)S(1)}, u32[]{:S(2)}, u32[]{:S(2)}) %collective-permute-start.12) | collective-permute-done | bytes 98336 | tf_op jit(solution)/shard_map/ppermute | solution.py:333
  138.5 1.6 %convolution_convert_fusion.6 = bf16[512,768]{1,0:T(8,128)(2,1)S(1)} fusion(bf16[512,384]{1,0:T(8,128)(2,1)S(1)} %constant_dynamic-update-slice_fusion, bf16[4,384,768]{2,1,0:T(8,128)(2,1)} %all-to-all-done, s32[]{:T(128)S(6)} %select_n.122), kind=kOutput, calls=%fused_computation.26 | convolution fusion | flops 302383104 | bytes 1769476 | tf_op jit(solution)/shard_map/dot_general | solution.py:348
  140.2 1.6 %convolution_convert_fusion.5 = bf16[512,768]{1,0:T(8,128)(2,1)S(1)} fusion(bf16[512,384]{1,0:T(8,128)(2,1)S(1)} %constant_dynamic-update-slice_fusion.2, bf16[4,384,768]{2,1,0:T(8,128)(2,1)} %all-to-all-done, s32[]{:T(128)S(6)} %select_n.124), kind=kOutput, calls=%fused_computation.25 | convolution fusion | flops 302383104 | bytes 1769476 | tf_op jit(solution)/shard_map/dot_general | solution.py:348
  141.8 1.6 %convert_add_fusion.1 = f32[512,768]{1,0:T(8,128)S(1)} fusion(bf16[512,768]{1,0:T(8,128)(2,1)S(1)} %convolution_convert_fusion.5, bf16[512,768]{1,0:T(8,128)(2,1)S(1)} %convolution_convert_fusion.6, bf16[512,384]{1,0:T(8,128)(2,1)S(1)} %constant_dynamic-update-slice_fusion.4, bf16[4,384,768]{2,1,0:T(8,128)(2,1)} %all-to-all-done, s32[]{:T(128)S(6)} %select_n.126), kind=kOutput, calls=%fused_computation.20 | convolution fusion | flops 304349184 | bytes 4128772 | tf_op jit(solution)/shard_map/dot_general | solution.py:348
  145.6 4.7 %fusion.12 = f32[512,1536]{1,0:T(8,128)} fusion(f32[512,768]{1,0:T(8,128)S(1)} %convert_add_fusion, f32[512,768]{1,0:T(8,128)S(1)} %convert_add_fusion.1, f32[1536]{0:T(1024)S(1)} %dynamic-slice_reduce_fusion, bf16[512,6144]{1,0:T(8,128)(2,1)} %param.10, s32[]{:T(128)S(6)} %select_n.103, pred[]{:T(512)S(6)} %eq.28, bf16[384,6144]{1,0:T(8,128)(2,1)} %param.19, ...), kind=kOutput, calls=%fused_computation.15 | convolution fusion | flops 611844096 | bytes 9444864 | tf_op jit(solution)/shard_map/dot_general | solution.py:341
  (80 shorter events, 15.1 us)
Async XLA Ops:
  0.0 15.8 %copy-start = (bf16[8,3,6144]{2,0,1:T(8,128)(2,1)S(1)}, bf16[8,3,6144]{2,0,1:T(8,128)(2,1)}, u32[]{:S(2)}) copy-start(bf16[8,3,6144]{2,0,1:T(8,128)(2,1)} %param.11) | copy-start | bytes 884740
  3.2 36.4 %collective-permute-start.2 = (bf16[1,512,768]{2,1,0:T(8,128)(2,1)}, bf16[1,512,768]{2,1,0:T(8,128)(2,1)S(1)}, u32[]{:S(2)}, u32[]{:S(2)}) collective-permute-start(bf16[1,512,768]{2,1,0:T(8,128)(2,1)} %reshape.85), channel_id=1, source_target_pairs={{0,8},{4,12},{8,16},{12,20},{16,24},{20,28},{24,0},{28,4},{1,9},{5... | collective-permute-start | bytes 2359304 | tf_op jit(solution)/shard_map/ppermute | solution.py:14
  4.4 45.7 %collective-permute-start.3 = (bf16[1,512,768]{2,1,0:T(8,128)(2,1)}, bf16[1,512,768]{2,1,0:T(8,128)(2,1)S(1)}, u32[]{:S(2)}, u32[]{:S(2)}) collective-permute-start(bf16[1,512,768]{2,1,0:T(8,128)(2,1)} %reshape.85), channel_id=1, source_target_pairs={{0,16},{4,20},{8,24},{12,28},{16,0},{20,4},{24,8},{28,12},{1,17},{... | collective-permute-start | bytes 2359304 | tf_op jit(solution)/shard_map/ppermute | solution.py:14
  5.7 45.4 %collective-permute-start.4 = (bf16[1,512,768]{2,1,0:T(8,128)(2,1)}, bf16[1,512,768]{2,1,0:T(8,128)(2,1)}, u32[]{:S(2)}, u32[]{:S(2)}) collective-permute-start(bf16[1,512,768]{2,1,0:T(8,128)(2,1)} %reshape.85), channel_id=1, source_target_pairs={{0,24},{4,28},{8,0},{12,4},{16,8},{20,12},{24,16},{28,20},{1,25},{... | collective-permute-start | bytes 2359304 | tf_op jit(solution)/shard_map/ppermute | solution.py:14
  10.3 4.9 %copy-start.10 = (s32[8]{0:T(128)S(1)}, s32[8]{0:T(128)}, u32[]{:S(2)}) copy-start(s32[8]{0:T(128)} %param.12) | copy-start | bytes 100
  10.3 56.9 %all-to-all-start = ((bf16[4,384,768]{2,1,0:T(8,128)(2,1)}), bf16[4,384,768]{2,1,0:T(8,128)(2,1)}, u32[]{:S(2)}, u32[]{:S(2)}) async-start(bf16[4,384,768]{2,1,0:T(8,128)(2,1)} %pad_maximum_fusion.1), calls=%async_computation | async-start | bytes 4718592 | tf_op jit(solution)/shard_map/all_to_all | solution.py:244
  33.7 0.7 copy-start.8
  33.7 0.8 copy-start.9
  36.3 19.4 %collective-permute-start = (bf16[512,768]{1,0:T(8,128)(2,1)}, bf16[512,768]{1,0:T(8,128)(2,1)}, u32[]{:S(2)}, u32[]{:S(2)}) collective-permute-start(bf16[512,768]{1,0:T(8,128)(2,1)} %get-tuple-element.53), channel_id=1, source_target_pairs={{0,4},{4,8},{8,12},{12,16},{16,20},{20,24},{24,28},{28,0},{1,5},{5... | collective-permute-start | bytes 2359304 | tf_op jit(solution)/shard_map/ppermute | solution.py:14
  38.5 28.6 %collective-permute-start.1 = (bf16[512,768]{1,0:T(8,128)(2,1)}, bf16[512,768]{1,0:T(8,128)(2,1)}, u32[]{:S(2)}, u32[]{:S(2)}) collective-permute-start(bf16[512,768]{1,0:T(8,128)(2,1)} %get-tuple-element.53), channel_id=1, source_target_pairs={{0,8},{4,12},{8,16},{12,20},{16,24},{20,28},{24,0},{28,4},{1,9},{5... | collective-permute-start | bytes 2359304 | tf_op jit(solution)/shard_map/ppermute | solution.py:14
  39.6 10.5 %copy-start.4 = (bf16[1,512,768]{2,1,0:T(8,128)(2,1)}, bf16[1,512,768]{2,1,0:T(8,128)(2,1)S(1)}, u32[]{:S(2)}) copy-start(bf16[1,512,768]{2,1,0:T(8,128)(2,1)S(1)} %collective-permute-done.2) | copy-start | bytes 2359300
  39.7 27.5 %collective-permute-start.5 = (bf16[1,512,768]{2,1,0:T(8,128)(2,1)}, bf16[1,512,768]{2,1,0:T(8,128)(2,1)}, u32[]{:S(2)}, u32[]{:S(2)}) collective-permute-start(bf16[1,512,768]{2,1,0:T(8,128)(2,1)} %reshape.85), channel_id=1, source_target_pairs={{0,4},{4,0},{8,12},{12,8},{16,20},{20,16},{24,28},{28,24},{1,5},{5... | collective-permute-start | bytes 2359304 | tf_op jit(solution)/shard_map/ppermute | solution.py:302
  39.7 0.9 copy-start.3
  50.1 0.9 copy-start.5
  53.1 15.7 %copy-start.2 = (bf16[4,512,768]{2,1,0:T(8,128)(2,1)}, bf16[4,512,768]{2,1,0:T(8,128)(2,1)S(1)}, u32[]{:S(2)}) copy-start(bf16[4,512,768]{2,1,0:T(8,128)(2,1)S(1)} %pad_maximum_fusion.refs_6_.refs_7_) | copy-start | bytes 9437188
  68.8 8.2 %collective-permute-start.6 = (bf16[3,512,768]{2,1,0:T(8,128)(2,1)}, bf16[3,512,768]{2,1,0:T(8,128)(2,1)}, u32[]{:S(2)}, u32[]{:S(2)}) collective-permute-start(bf16[3,512,768]{2,1,0:T(8,128)(2,1)} %slice.105), channel_id=1, source_target_pairs={{0,4},{4,0},{8,12},{12,8},{16,20},{20,16},{24,28},{28,24},{1,5},{5... | collective-permute-start | bytes 7077896 | tf_op jit(solution)/shard_map/ppermute | solution.py:306
  68.8 74.7 %collective-permute-start.13 = (bf16[4,384,768]{2,1,0:T(8,128)(2,1)}, bf16[4,384,768]{2,1,0:T(8,128)(2,1)S(1)}, u32[]{:S(2)}, u32[]{:S(2)}) collective-permute-start(bf16[4,384,768]{2,1,0:T(8,128)(2,1)} %all-to-all-done), channel_id=1, source_target_pairs={{0,4},{4,0},{8,12},{12,8},{16,20},{20,16},{24,28},{28,24},{1,5},{5... | collective-permute-start | bytes 7077896 | tf_op jit(solution)/shard_map/ppermute | solution.py:327
  100.3 22.8 %collective-permute-start.7 = (bf16[384,384]{1,0:T(8,128)(2,1)}, bf16[384,384]{1,0:T(8,128)(2,1)S(1)}, u32[]{:S(2)}, u32[]{:S(2)}) collective-permute-start(bf16[384,384]{1,0:T(8,128)(2,1)} %shard_map.102), channel_id=1, source_target_pairs={{0,1},{1,2},{2,3},{3,0},{4,5},{5,6},{6,7},{7,4},{8,9},{9,10},{10,1... | collective-permute-start | bytes 884744 | tf_op jit(solution)/shard_map/ppermute | solution.py:333
  101.5 27.7 %collective-permute-start.9 = (bf16[384,384]{1,0:T(8,128)(2,1)}, bf16[384,384]{1,0:T(8,128)(2,1)S(1)}, u32[]{:S(2)}, u32[]{:S(2)}) collective-permute-start(bf16[384,384]{1,0:T(8,128)(2,1)} %shard_map.102), channel_id=1, source_target_pairs={{0,2},{1,3},{2,0},{3,1},{4,6},{5,7},{6,4},{7,5},{8,10},{9,11},{10,... | collective-permute-start | bytes 884744 | tf_op jit(solution)/shard_map/ppermute | solution.py:333
  104.9 29.4 %collective-permute-start.11 = (bf16[384,384]{1,0:T(8,128)(2,1)}, bf16[384,384]{1,0:T(8,128)(2,1)S(1)}, u32[]{:S(2)}, u32[]{:S(2)}) collective-permute-start(bf16[384,384]{1,0:T(8,128)(2,1)} %shard_map.102), channel_id=1, source_target_pairs={{0,3},{1,0},{2,1},{3,2},{4,7},{5,4},{6,5},{7,6},{8,11},{9,8},{10,9... | collective-permute-start | bytes 884744 | tf_op jit(solution)/shard_map/ppermute | solution.py:333
  121.6 12.7 %collective-permute-start.8 = (bf16[128,384]{1,0:T(8,128)(2,1)}, bf16[128,384]{1,0:T(8,128)(2,1)S(1)}, u32[]{:S(2)}, u32[]{:S(2)}) collective-permute-start(bf16[128,384]{1,0:T(8,128)(2,1)} %shard_map.103), channel_id=1, source_target_pairs={{0,1},{1,2},{2,3},{3,0},{4,5},{5,6},{6,7},{7,4},{8,9},{9,10},{10,1... | collective-permute-start | bytes 294920 | tf_op jit(solution)/shard_map/ppermute | solution.py:333
  123.1 11.3 %collective-permute-start.10 = (bf16[128,384]{1,0:T(8,128)(2,1)}, bf16[128,384]{1,0:T(8,128)(2,1)S(1)}, u32[]{:S(2)}, u32[]{:S(2)}) collective-permute-start(bf16[128,384]{1,0:T(8,128)(2,1)} %shard_map.103), channel_id=1, source_target_pairs={{0,2},{1,3},{2,0},{3,1},{4,6},{5,7},{6,4},{7,5},{8,10},{9,11},{10,... | collective-permute-start | bytes 294920 | tf_op jit(solution)/shard_map/ppermute | solution.py:333
  129.2 9.3 %collective-permute-start.12 = (bf16[128,384]{1,0:T(8,128)(2,1)}, bf16[128,384]{1,0:T(8,128)(2,1)S(1)}, u32[]{:S(2)}, u32[]{:S(2)}) collective-permute-start(bf16[128,384]{1,0:T(8,128)(2,1)} %shard_map.103), channel_id=1, source_target_pairs={{0,3},{1,0},{2,1},{3,2},{4,7},{5,4},{6,5},{7,6},{8,11},{9,8},{10,9... | collective-permute-start | bytes 294920 | tf_op jit(solution)/shard_map/ppermute | solution.py:333
  144.6 1.0 copy-start.6
  144.6 1.0 copy-start.7
  145.6 4.7 %copy-start.1 = (bf16[8,3,6144]{2,0,1:T(8,128)(2,1)S(1)}, bf16[8,3,6144]{2,0,1:T(8,128)(2,1)}, u32[]{:S(2)}) copy-start(bf16[8,3,6144]{2,0,1:T(8,128)(2,1)} %param.11) | copy-start | bytes 884740

commit v23 on v21

--- a/solution.py
+++ b/solution.py
@@ -110,7 +110,7 @@
     )(queries, local_stack, local_stack, bias)
 
 
-def flash_kernel(chosen, q_ref, k1_ref, v1_ref, k2_ref, v2_ref, ak_ref, av_ref, ck_ref, cv_ref, bk_ref, bv_ref, bias_ref, m_in, l_in, acc_in, o_ref, m_sc, l_sc, acc_sc, *, heads, n_local, half):
+def flash_kernel(chosen, q_ref, k1_ref, v1_ref, k2_ref, v2_ref, dk_ref, dv_ref, ak_ref, av_ref, ck_ref, cv_ref, bk_ref, bv_ref, bias_ref, m_in, l_in, acc_in, o_ref, m_sc, l_sc, acc_sc, *, heads, n_local, half):
     step = pl.program_id(0)
     span = q_ref.shape[0]
     blocks = bias_ref.shape[0]
@@ -150,7 +150,11 @@
 
     pos = chosen[jnp.maximum(step - n_local, 0)]
 
-    @pl.when((step >= n_local) & (pos < half))
+    @pl.when((step >= n_local) & (pos == 0))
+    def _():
+        body(dk_ref, dv_ref)
+
+    @pl.when((step >= n_local) & (pos > 0) & (pos < half))
     def _():
         body(ak_ref, av_ref)
 
@@ -169,10 +173,10 @@
             o_ref[:, cols] = (acc_sc[h] / l_sc[h]).astype(o_ref.dtype)
 
 
-def flash(queries, before, earlier, same_core, sibling_own, other_core, bias, chosen, state, heads):
+def flash(queries, before, earlier, own_pool, same_core, sibling_own, other_core, bias, chosen, state, heads):
     span, width = queries.shape
     n_local = 2
-    half = same_core.shape[0]
+    half = same_core.shape[0] + 1
     steps = n_local + chosen.shape[0]
     blocks = bias.shape[1]
 
@@ -185,8 +189,8 @@
             if upper:
                 hit = (j >= n_local) & (pos > half)
                 return (jnp.where(hit, pos - half - 1, 0), 0, kv)
-            hit = (j >= n_local) & (pos < half)
-            return (jnp.where(hit, pos, 0), 0, kv)
+            hit = (j >= n_local) & (pos > 0) & (pos < half)
+            return (jnp.where(hit, pos - 1, 0), 0, kv)
 
         return index
 
@@ -201,6 +205,8 @@
             pl.BlockSpec((keys_len, width), lambda j, c: (0, 1)),
             pl.BlockSpec((keys_len, width), lambda j, c: (0, 0)),
             pl.BlockSpec((keys_len, width), lambda j, c: (0, 1)),
+            pl.BlockSpec(kv_block, lambda j, c: (0, 0, 0)),
+            pl.BlockSpec(kv_block, lambda j, c: (0, 0, 1)),
             pl.BlockSpec(kv_block, pool_map(0, False)),
             pl.BlockSpec(kv_block, pool_map(1, False)),
             pl.BlockSpec(kv_block, lambda j, c: (0, 0, 0)),
@@ -230,7 +236,7 @@
             transcendentals=steps * heads * span * span,
             bytes_accessed=2 * steps * span * width * 2,
         ),
-    )(chosen, queries, before, before, earlier, earlier, same_core, same_core, sibling_own, sibling_own, other_core, other_core, bias, *state)
+    )(chosen, queries, before, before, earlier, earlier, own_pool, own_pool, same_core, same_core, sibling_own, sibling_own, other_core, other_core, bias, *state)
 
 
 def fetch_out_weight(w_out, head, core):
@@ -271,7 +277,7 @@
     own_full, mine = fetch_out_weight(w_out, head, core)
     slots = lax.axis_size("slot")
     pool_flat = pool_kv.reshape(1, pool_kv.shape[1], -1)
-    same_core = [pool_flat] + [from_behind(pool_flat, "slot", 2 * k) for k in range(1, slots // 2)]
+    same_core = [from_behind(pool_flat, "slot", 2 * k) for k in range(1, slots // 2)]
     same_core = jnp.concatenate(same_core, axis=0)
 
     onehot = (jnp.arange(mod_table.shape[0], dtype=jnp.int32) == step_index[slot]).astype(
@@ -304,7 +310,7 @@
     states, queries, before, earlier, same_core, sibling_own, mine = lax.optimization_barrier(
         (states, queries, before, earlier, same_core, sibling_own, mine)
     )
-    other_core = lax.ppermute(same_core[1:], "slot", [(i, i ^ 1) for i in range(slots)])
+    other_core = lax.ppermute(same_core, "slot", [(i, i ^ 1) for i in range(slots)])
     own_mask = lax.dynamic_index_in_dim(block_mask, slot, 0, keepdims=False)
     own_cache = lax.dynamic_index_in_dim(cache_index, slot, 0, keepdims=False)
     sibling_slot = jnp.bitwise_xor(slot, 1)
@@ -322,7 +328,7 @@
     parts = rows // BLOCK
     queries = queries.reshape(span, width)
     mixed_parts = [
-        flash(queries[p * rows : (p + 1) * rows], before, earlier, same_core, sibling_own, other_core,
+        flash(queries[p * rows : (p + 1) * rows], before, earlier, pool_flat, same_core, sibling_own, other_core,
               bias[1:, p * parts : (p + 1) * parts], own_cache, states[p], heads)
         for p in range(2)
     ]

time: 149 us -> 152 us (1.020)
  the two profiles are of different devices: /device:TPU:9 before, /device:TPU:0 now
where the time goes in v23:
time: 152 us; the launch traced here: 151 us
  Pallas kernels  41.8 us (28%)
  waiting for transfers between devices  35.8 us (24%)
  matrix products  28.2 us (19%)
  starting transfers between devices  22.1 us (15%)
  local copies, waits for them, and re-layouts  11.7 us (8%)
  other arithmetic  11.4 us (8%)
    pallas_call x2, Pallas kernels, flash(): pl.pallas_call(kernel, grid_spec=grid_spec, out_shape=jax.ShapeDtypeStruc...  34.6 us
    ppermute x5, waiting for transfers between devices, from_behind(): lax.ppermute(shard, axis, [(i, (i + by) % length) for i in range(length)])  19.1 us
    ppermute x6, waiting for transfers between devices, local(): lax.ppermute(part, 'head', [(i, (i + shift) % groups) for i in range(grou...  16.6 us
    dot_general x1, matrix products, local(): jnp.einsum('td,dkh->kth', hidden, w_qkv, preferred_element_type=jnp.float32)  12.8 us
    ppermute x6, starting transfers between devices, local(): lax.ppermute(part, 'head', [(i, (i + shift) % groups) for i in range(grou...  8.91 us
    ppermute x5, starting transfers between devices, from_behind(): lax.ppermute(shard, axis, [(i, (i + by) % length) for i in range(length)])  7.23 us
    pallas_call x2, Pallas kernels, flash_local(): pl.pallas_call(kernel, grid=(steps,), in_specs=[pl.BlockSpec((span, width...  7.16 us
    dot_general x3, matrix products, local(): part = jnp.dot(group_o, sibling_block, preferred_element_type=jnp.float32)  4.96 us
  transfers between devices with their start and end apart: 15, of which 3 were waited for; matrix products, arithmetic and copies ran while one was open for 25% of the time, Pallas kernels for 28%

profile of v23, /device:TPU:0, one launch (start us, length us, event | category | flops | bytes accessed | tf_op | source)
XLA Modules:
  0.0 151.4 jit_solution(83699257485511232)
XLA Ops:
  0.0 2.5 %reshape.85.refs_6_.refs_7_ = bf16[1,512,768]{2,1,0:T(8,128)(2,1)S(1)} reshape(bf16[1,512,2,384]{3,2,1,0:T(2,128)(2,1)} %param.18) | data formatting | bytes 1572864 | tf_op jit(solution)/shard_map/reshape | solution.py:279
  3.0 3.5 %collective-permute-start.4 = (bf16[1,512,768]{2,1,0:T(8,128)(2,1)S(1)}, bf16[1,512,768]{2,1,0:T(8,128)(2,1)S(1)}, u32[]{:S(2)}, u32[]{:S(2)}) collective-permute-start(bf16[1,512,768]{2,1,0:T(8,128)(2,1)S(1)} %reshape.85.refs_6_.refs_7_), channel_id=1, source_target_pairs={{0,24},{4,28},{8,0},{12,4},{16,8},{20,12},{24,16},{28,20},{1,25},{... | collective-permute-start | bytes 2359304 | tf_op jit(solution)/shard_map/ppermute | solution.py:14
  7.6 1.8 %dynamic-slice_bitcast_fusion.3 = (bf16[1,384,768]{2,1,0:T(8,128)(2,1)S(1)}, bf16[1,384,768]{2,1,0:T(8,128)(2,1)S(1)}, bf16[1,384,768]{2,1,0:T(8,128)(2,1)S(1)}, bf16[1,384,768]{2,1,0:T(8,128)(2,1)S(1)}) fusion(bf16[384,6144]{1,0:T(8,128)(2,1)} %param.19, s32[]{:T(128)S(6)} %select_n.112, s32[]{:T(128)S(6)} %select_n.114, s32[]{:T(128)S(6)} %select_n.113, ...), kind=kLoop, calls=%fused_computation.47 | loop fusion | bytes 4718608 | tf_op jit(solution)/shard_map/stack | solution.py:246
  9.4 1.7 %pad_maximum_fusion.1 = bf16[4,384,768]{2,1,0:T(8,128)(2,1)} fusion(bf16[1,384,768]{2,1,0:T(8,128)(2,1)S(1)} %get-tuple-element.50, bf16[1,384,768]{2,1,0:T(8,128)(2,1)S(1)} %get-tuple-element.48, bf16[1,384,768]{2,1,0:T(8,128)(2,1)S(1)} %get-tuple-element.49, bf16[1,384,768]{2,1,0:T(8,128)(2,1)S(1)} %get-tuple-element.47), kind=kLoop, calls=%fused_computation.17 | loop fusion | flops 3538944 | bytes 4718592 | tf_op jit(solution)/shard_map/stack | solution.py:246
  11.1 4.9 %all-to-all-start = ((bf16[4,384,768]{2,1,0:T(8,128)(2,1)}), bf16[4,384,768]{2,1,0:T(8,128)(2,1)}, u32[]{:S(2)}, u32[]{:S(2)}) async-start(bf16[4,384,768]{2,1,0:T(8,128)(2,1)} %pad_maximum_fusion.1), calls=%async_computation | async-start | bytes 4718592 | tf_op jit(solution)/shard_map/all_to_all | solution.py:250
  16.0 4.1 %fusion = f32[512]{0:T(512)S(1)} fusion(bf16[512,6144]{1,0:T(8,128)(2,1)} %param.10), kind=kLoop, calls=%fused_computation.2 | loop fusion | flops 9436672 | bytes 6293504 | tf_op jit(solution)/shard_map/reduce_sum | solution.py:288
  20.7 0.9 fusion.42
  21.7 12.8 %fusion.13 = f32[3,512,384]{2,1,0:T(8,128)S(1)} fusion(bf16[6144,3,384]{2,0,1:T(8,128)(2,1)} %param.15, bf16[512,6144]{1,0:T(8,128)(2,1)} %param.10, f32[6144]{0:T(1024)S(1)} %bitcast.67, f32[6144]{0:T(1024)S(1)} %bitcast.68, f32[512]{0:T(512)S(1)} %add_rsqrt_fusion.6), kind=kOutput, calls=%fused_computation.18 | convolution fusion | flops 7263485952 | bytes 22857728 | tf_op jit(solution)/shard_map/td,dkh->kth/dot_general | solution.py:291
  35.9 1.2 pad_maximum_fusion.2
  37.1 2.6 %collective-permute-start.1 = (bf16[512,768]{1,0:T(8,128)(2,1)}, bf16[512,768]{1,0:T(8,128)(2,1)}, u32[]{:S(2)}, u32[]{:S(2)}) collective-permute-start(bf16[512,768]{1,0:T(8,128)(2,1)} %get-tuple-element.53), channel_id=1, source_target_pairs={{0,8},{4,12},{8,16},{12,20},{16,24},{20,28},{24,0},{28,4},{1,9},{5... | collective-permute-start | bytes 2359304 | tf_op jit(solution)/shard_map/ppermute | solution.py:14
  42.0 3.6 %shard_map.101 = (f32[3,256,1]{2,1,0:T(8,128)}, f32[3,256,1]{2,1,0:T(8,128)}, f32[3,256,128]{2,1,0:T(8,128)}) custom-call(bf16[256,384]{1,0:T(8,128)(2,1)} %get-tuple-element.63.refs_0_, bf16[1,512,768]{2,1,0:T(8,128)(2,1)} %get-tuple-element.54.refs_1_.refs_2_, bf16[1,512,768]{2,1,0:T(8,128)(2,1)} %get-tuple-element.54.refs_1_.refs_2_, ...), custom_call_target="tpu_custom_call" | custom-call | flops 201326592 | bytes 786432 | tf_op jit(solution)/shard_map/pallas_call | solution.py:89
  45.5 3.6 %shard_map.100 = (f32[3,256,1]{2,1,0:T(8,128)}, f32[3,256,1]{2,1,0:T(8,128)}, f32[3,256,128]{2,1,0:T(8,128)}) custom-call(bf16[256,384]{1,0:T(8,128)(2,1)} %get-tuple-element.64.refs_0_, bf16[1,512,768]{2,1,0:T(8,128)(2,1)} %get-tuple-element.54.refs_1_.refs_2_, bf16[1,512,768]{2,1,0:T(8,128)(2,1)} %get-tuple-element.54.refs_1_.refs_2_, ...), custom_call_target="tpu_custom_call" | custom-call | flops 201326592 | bytes 786432 | tf_op jit(solution)/shard_map/pallas_call | solution.py:89
  49.1 19.1 %collective-permute-done.3 = bf16[1,512,768]{2,1,0:T(8,128)(2,1)S(1)} collective-permute-done((bf16[1,512,768]{2,1,0:T(8,128)(2,1)S(1)}, bf16[1,512,768]{2,1,0:T(8,128)(2,1)S(1)}, u32[]{:S(2)}, u32[]{:S(2)}) %collective-permute-start.3) | collective-permute-done | bytes 786464 | tf_op jit(solution)/shard_map/ppermute | solution.py:14
  68.3 0.9 copy-done.6
  69.2 1.9 %pad_maximum_fusion.refs_8_.refs_9_ = bf16[3,512,768]{2,1,0:T(8,128)(2,1)S(1)} fusion(bf16[1,512,768]{2,1,0:T(8,128)(2,1)} %copy-done.5, bf16[1,512,768]{2,1,0:T(8,128)(2,1)} %copy-done.6, bf16[1,512,768]{2,1,0:T(8,128)(2,1)} %collective-permute-done.2), kind=kLoop, calls=%fused_computation.16 | loop fusion | flops 2359296 | bytes 4718592 | tf_op jit(solution)/shard_map/concatenate | solution.py:281
  72.7 1.2 compare_select_fusion.6.refs_0_
  74.6 1.8 %fusion.53 = (bf16[256,384]{1,0:T(8,128)(2,1)}, bf16[256,384]{1,0:T(8,128)(2,1)}) fusion(bf16[512,384]{1,0:T(8,128)(2,1)} %copy-done.4), kind=kLoop, calls=%fused_computation.122 | loop fusion | bytes 786432 | tf_op jit(solution)/shard_map/slice | solution.py:331
  76.4 17.3 %shard_map.102 = bf16[256,384]{1,0:T(8,128)(2,1)} custom-call(s32[6]{0:T(128)} %compare_select_fusion.6.refs_0_, bf16[256,384]{1,0:T(8,128)(2,1)} %get-tuple-element.62.refs_1_, bf16[512,768]{1,0:T(8,128)(2,1)} %collective-permute-done.refs_2_.refs_3_, bf16[512,768]{1,0:T(8,128)(2,1)} %collective-permute-done.refs_2_.refs_3_, ...), custom_call_target="tpu_custom_call" | custom-call | flops 805306368 | bytes 3145728 | tf_op jit(solution)/shard_map/pallas_call | solution.py:229
  93.7 3.6 %collective-permute-start.11 = (bf16[256,384]{1,0:T(8,128)(2,1)}, bf16[256,384]{1,0:T(8,128)(2,1)S(1)}, u32[]{:S(2)}, u32[]{:S(2)}) collective-permute-start(bf16[256,384]{1,0:T(8,128)(2,1)} %shard_map.102), channel_id=1, source_target_pairs={{0,3},{1,0},{2,1},{3,2},{4,7},{5,4},{6,5},{7,6},{8,11},{9,8},{10,9... | collective-permute-start | bytes 589832 | tf_op jit(solution)/shard_map/ppermute | solution.py:341
  97.3 1.3 collective-permute-start.7
  98.6 17.3 %shard_map.103 = bf16[256,384]{1,0:T(8,128)(2,1)} custom-call(s32[6]{0:T(128)} %compare_select_fusion.6.refs_0_, bf16[256,384]{1,0:T(8,128)(2,1)} %get-tuple-element.61.refs_1_, bf16[512,768]{1,0:T(8,128)(2,1)} %collective-permute-done.refs_2_.refs_3_, bf16[512,768]{1,0:T(8,128)(2,1)} %collective-permute-done.refs_2_.refs_3_, ...), custom_call_target="tpu_custom_call" | custom-call | flops 805306368 | bytes 3145728 | tf_op jit(solution)/shard_map/pallas_call | solution.py:229
  115.9 2.8 %collective-permute-start.12 = (bf16[256,384]{1,0:T(8,128)(2,1)}, bf16[256,384]{1,0:T(8,128)(2,1)S(1)}, u32[]{:S(2)}, u32[]{:S(2)}) collective-permute-start(bf16[256,384]{1,0:T(8,128)(2,1)} %shard_map.103), channel_id=1, source_target_pairs={{0,3},{1,0},{2,1},{3,2},{4,7},{5,4},{6,5},{7,6},{8,11},{9,8},{10,9... | collective-permute-start | bytes 589832 | tf_op jit(solution)/shard_map/ppermute | solution.py:341
  118.8 1.1 collective-permute-start.10
  120.1 4.4 %collective-permute-done.12 = bf16[256,384]{1,0:T(8,128)(2,1)S(1)} collective-permute-done((bf16[256,384]{1,0:T(8,128)(2,1)}, bf16[256,384]{1,0:T(8,128)(2,1)S(1)}, u32[]{:S(2)}, u32[]{:S(2)}) %collective-permute-start.12) | collective-permute-done | bytes 196640 | tf_op jit(solution)/shard_map/ppermute | solution.py:341
  124.5 12.2 %collective-permute-done.10 = bf16[256,384]{1,0:T(8,128)(2,1)S(1)} collective-permute-done((bf16[256,384]{1,0:T(8,128)(2,1)}, bf16[256,384]{1,0:T(8,128)(2,1)S(1)}, u32[]{:S(2)}, u32[]{:S(2)}) %collective-permute-start.10) | collective-permute-done | bytes 196640 | tf_op jit(solution)/shard_map/ppermute | solution.py:341
  136.8 1.6 %convolution_convert_fusion.6 = bf16[512,768]{1,0:T(8,128)(2,1)S(1)} fusion(bf16[512,384]{1,0:T(8,128)(2,1)S(1)} %constant_dynamic-update-slice_fusion, bf16[4,384,768]{2,1,0:T(8,128)(2,1)} %all-to-all-done, s32[]{:T(128)S(6)} %select_n.122), kind=kOutput, calls=%fused_computation.26 | convolution fusion | flops 302383104 | bytes 1769476 | tf_op jit(solution)/shard_map/dot_general | solution.py:356
  138.5 1.6 %convolution_convert_fusion.5 = bf16[512,768]{1,0:T(8,128)(2,1)S(1)} fusion(bf16[512,384]{1,0:T(8,128)(2,1)S(1)} %constant_dynamic-update-slice_fusion.2, bf16[4,384,768]{2,1,0:T(8,128)(2,1)} %all-to-all-done, s32[]{:T(128)S(6)} %select_n.124), kind=kOutput, calls=%fused_computation.25 | convolution fusion | flops 302383104 | bytes 1769476 | tf_op jit(solution)/shard_map/dot_general | solution.py:356
  140.1 1.6 %convert_add_fusion.1 = f32[512,768]{1,0:T(8,128)S(1)} fusion(bf16[512,768]{1,0:T(8,128)(2,1)S(1)} %convolution_convert_fusion.5, bf16[512,768]{1,0:T(8,128)(2,1)S(1)} %convolution_convert_fusion.6, bf16[512,384]{1,0:T(8,128)(2,1)S(1)} %constant_dynamic-update-slice_fusion.4, bf16[4,384,768]{2,1,0:T(8,128)(2,1)} %all-to-all-done, s32[]{:T(128)S(6)} %select_n.126), kind=kOutput, calls=%fused_computation.20 | convolution fusion | flops 304349184 | bytes 4128772 | tf_op jit(solution)/shard_map/dot_general | solution.py:356
  141.7 1.6 %convolution_convert_fusion.2 = bf16[512,768]{1,0:T(8,128)(2,1)S(1)} fusion(bf16[512,384]{1,0:T(8,128)(2,1)S(1)} %constant_dynamic-update-slice_fusion.2, bf16[4,384,768]{2,1,0:T(8,128)(2,1)} %collective-permute-done.13, s32[]{:T(128)S(6)} %select_n.124), kind=kOutput, calls=%fused_computation.22 | convolution fusion | flops 302383104 | bytes 1769476 | tf_op jit(solution)/shard_map/dot_general | solution.py:360
  143.4 1.6 %convolution_convert_fusion.3 = bf16[512,768]{1,0:T(8,128)(2,1)S(1)} fusion(bf16[512,384]{1,0:T(8,128)(2,1)S(1)} %constant_dynamic-update-slice_fusion, bf16[4,384,768]{2,1,0:T(8,128)(2,1)} %collective-permute-done.13, s32[]{:T(128)S(6)} %select_n.122), kind=kOutput, calls=%fused_computation.23 | convolution fusion | flops 302383104 | bytes 1769476 | tf_op jit(solution)/shard_map/dot_general | solution.py:360
  145.1 1.7 %convert_add_fusion = f32[512,768]{1,0:T(8,128)S(1)} fusion(bf16[512,768]{1,0:T(8,128)(2,1)S(1)} %convolution_convert_fusion.2, bf16[512,768]{1,0:T(8,128)(2,1)S(1)} %convolution_convert_fusion.3, bf16[512,384]{1,0:T(8,128)(2,1)S(1)} %constant_dynamic-update-slice_fusion.4, bf16[4,384,768]{2,1,0:T(8,128)(2,1)} %collective-permute-done.13, s32[]{:T(128)S(6)} %select_n.126), kind=kOutput, calls=%fused_computation.19 | convolution fusion | flops 304349184 | bytes 4128772 | tf_op jit(solution)/shard_map/dot_general | solution.py:360
  146.8 4.7 %fusion.12 = f32[512,1536]{1,0:T(8,128)} fusion(f32[512,768]{1,0:T(8,128)S(1)} %convert_add_fusion, f32[512,768]{1,0:T(8,128)S(1)} %convert_add_fusion.1, f32[1536]{0:T(1024)S(1)} %dynamic-slice_reduce_fusion, bf16[512,6144]{1,0:T(8,128)(2,1)} %param.10, s32[]{:T(128)S(6)} %select_n.103, pred[]{:T(512)S(6)} %eq.28, bf16[384,6144]{1,0:T(8,128)(2,1)} %param.19, ...), kind=kOutput, calls=%fused_computation.14 | convolution fusion | flops 611844096 | bytes 9444864 | tf_op jit(solution)/shard_map/dot_general | solution.py:349
  (77 shorter events, 8.4 us)
Async XLA Ops:
  0.0 20.7 %copy-start = (bf16[8,3,6144]{2,0,1:T(8,128)(2,1)S(1)}, bf16[8,3,6144]{2,0,1:T(8,128)(2,1)}, u32[]{:S(2)}) copy-start(bf16[8,3,6144]{2,0,1:T(8,128)(2,1)} %param.11) | copy-start | bytes 884740
  2.5 6.9 %copy-start.3 = (bf16[1,512,768]{2,1,0:T(8,128)(2,1)}, bf16[1,512,768]{2,1,0:T(8,128)(2,1)S(1)}, u32[]{:S(2)}) copy-start(bf16[1,512,768]{2,1,0:T(8,128)(2,1)S(1)} %reshape.85.refs_6_.refs_7_) | copy-start | bytes 2359300
  2.5 68.5 %collective-permute-start.5 = (bf16[1,512,768]{2,1,0:T(8,128)(2,1)S(1)}, bf16[1,512,768]{2,1,0:T(8,128)(2,1)}, u32[]{:S(2)}, u32[]{:S(2)}) collective-permute-start(bf16[1,512,768]{2,1,0:T(8,128)(2,1)S(1)} %reshape.85.refs_6_.refs_7_), channel_id=1, source_target_pairs={{0,4},{4,0},{8,12},{12,8},{16,20},{20,16},{24,28},{28,24},{1,5},{5... | collective-permute-start | bytes 2359304 | tf_op jit(solution)/shard_map/ppermute | solution.py:309
  3.0 34.1 %collective-permute-start.4 = (bf16[1,512,768]{2,1,0:T(8,128)(2,1)S(1)}, bf16[1,512,768]{2,1,0:T(8,128)(2,1)S(1)}, u32[]{:S(2)}, u32[]{:S(2)}) collective-permute-start(bf16[1,512,768]{2,1,0:T(8,128)(2,1)S(1)} %reshape.85.refs_6_.refs_7_), channel_id=1, source_target_pairs={{0,24},{4,28},{8,0},{12,4},{16,8},{20,12},{24,16},{28,20},{1,25},{... | collective-permute-start | bytes 2359304 | tf_op jit(solution)/shard_map/ppermute | solution.py:14
  6.5 61.7 %collective-permute-start.3 = (bf16[1,512,768]{2,1,0:T(8,128)(2,1)S(1)}, bf16[1,512,768]{2,1,0:T(8,128)(2,1)S(1)}, u32[]{:S(2)}, u32[]{:S(2)}) collective-permute-start(bf16[1,512,768]{2,1,0:T(8,128)(2,1)S(1)} %reshape.85.refs_6_.refs_7_), channel_id=1, source_target_pairs={{0,16},{4,20},{8,24},{12,28},{16,0},{20,4},{24,8},{28,12},{1,17},{... | collective-permute-start | bytes 2359304 | tf_op jit(solution)/shard_map/ppermute | solution.py:14
  7.0 62.1 %collective-permute-start.2 = (bf16[1,512,768]{2,1,0:T(8,128)(2,1)S(1)}, bf16[1,512,768]{2,1,0:T(8,128)(2,1)}, u32[]{:S(2)}, u32[]{:S(2)}) collective-permute-start(bf16[1,512,768]{2,1,0:T(8,128)(2,1)S(1)} %reshape.85.refs_6_.refs_7_), channel_id=1, source_target_pairs={{0,8},{4,12},{8,16},{12,20},{16,24},{20,28},{24,0},{28,4},{1,9},{5... | collective-permute-start | bytes 2359304 | tf_op jit(solution)/shard_map/ppermute | solution.py:14
  11.1 60.0 %all-to-all-start = ((bf16[4,384,768]{2,1,0:T(8,128)(2,1)}), bf16[4,384,768]{2,1,0:T(8,128)(2,1)}, u32[]{:S(2)}, u32[]{:S(2)}) async-start(bf16[4,384,768]{2,1,0:T(8,128)(2,1)} %pad_maximum_fusion.1), calls=%async_computation | async-start | bytes 4718592 | tf_op jit(solution)/shard_map/all_to_all | solution.py:250
  16.0 4.1 %copy-start.11 = (s32[8]{0:T(128)S(1)}, s32[8]{0:T(128)}, u32[]{:S(2)}) copy-start(s32[8]{0:T(128)} %param.12) | copy-start | bytes 100
  34.5 0.7 copy-start.9
  34.5 0.8 copy-start.10
  37.1 33.9 %collective-permute-start = (bf16[512,768]{1,0:T(8,128)(2,1)}, bf16[512,768]{1,0:T(8,128)(2,1)}, u32[]{:S(2)}, u32[]{:S(2)}) collective-permute-start(bf16[512,768]{1,0:T(8,128)(2,1)} %get-tuple-element.53), channel_id=1, source_target_pairs={{0,4},{4,8},{8,12},{12,16},{16,20},{20,24},{24,28},{28,0},{1,5},{5... | collective-permute-start | bytes 2359304 | tf_op jit(solution)/shard_map/ppermute | solution.py:14
  37.1 12.0 %copy-start.5 = (bf16[1,512,768]{2,1,0:T(8,128)(2,1)}, bf16[1,512,768]{2,1,0:T(8,128)(2,1)S(1)}, u32[]{:S(2)}) copy-start(bf16[1,512,768]{2,1,0:T(8,128)(2,1)S(1)} %collective-permute-done.4) | copy-start | bytes 2359300
  37.1 33.9 %collective-permute-start.1 = (bf16[512,768]{1,0:T(8,128)(2,1)}, bf16[512,768]{1,0:T(8,128)(2,1)}, u32[]{:S(2)}, u32[]{:S(2)}) collective-permute-start(bf16[512,768]{1,0:T(8,128)(2,1)} %get-tuple-element.53), channel_id=1, source_target_pairs={{0,8},{4,12},{8,16},{12,20},{16,24},{20,28},{24,0},{28,4},{1,9},{5... | collective-permute-start | bytes 2359304 | tf_op jit(solution)/shard_map/ppermute | solution.py:14
  39.8 0.7 copy-start.4
  68.3 0.9 copy-start.6
  71.0 5.4 %copy-start.2 = (bf16[3,512,768]{2,1,0:T(8,128)(2,1)}, bf16[3,512,768]{2,1,0:T(8,128)(2,1)S(1)}, u32[]{:S(2)}) copy-start(bf16[3,512,768]{2,1,0:T(8,128)(2,1)S(1)} %pad_maximum_fusion.refs_8_.refs_9_) | copy-start | bytes 7077892
  71.1 5.3 %collective-permute-start.6 = (bf16[3,512,768]{2,1,0:T(8,128)(2,1)S(1)}, bf16[3,512,768]{2,1,0:T(8,128)(2,1)}, u32[]{:S(2)}, u32[]{:S(2)}) collective-permute-start(bf16[3,512,768]{2,1,0:T(8,128)(2,1)S(1)} %pad_maximum_fusion.refs_8_.refs_9_), channel_id=1, source_target_pairs={{0,4},{4,0},{8,12},{12,8},{16,20},{20,16},{24,28},{28,24},{1,5},{5... | collective-permute-start | bytes 7077896 | tf_op jit(solution)/shard_map/ppermute | solution.py:313
  72.2 69.5 %collective-permute-start.13 = (bf16[4,384,768]{2,1,0:T(8,128)(2,1)}, bf16[4,384,768]{2,1,0:T(8,128)(2,1)}, u32[]{:S(2)}, u32[]{:S(2)}) collective-permute-start(bf16[4,384,768]{2,1,0:T(8,128)(2,1)} %all-to-all-done), channel_id=1, source_target_pairs={{0,4},{4,0},{8,12},{12,8},{16,20},{20,16},{24,28},{28,24},{1,5},{5... | collective-permute-start | bytes 7077896 | tf_op jit(solution)/shard_map/ppermute | solution.py:335
  93.7 25.0 %collective-permute-start.11 = (bf16[256,384]{1,0:T(8,128)(2,1)}, bf16[256,384]{1,0:T(8,128)(2,1)S(1)}, u32[]{:S(2)}, u32[]{:S(2)}) collective-permute-start(bf16[256,384]{1,0:T(8,128)(2,1)} %shard_map.102), channel_id=1, source_target_pairs={{0,3},{1,0},{2,1},{3,2},{4,7},{5,4},{6,5},{7,6},{8,11},{9,8},{10,9... | collective-permute-start | bytes 589832 | tf_op jit(solution)/shard_map/ppermute | solution.py:341
  97.3 22.6 %collective-permute-start.9 = (bf16[256,384]{1,0:T(8,128)(2,1)}, bf16[256,384]{1,0:T(8,128)(2,1)S(1)}, u32[]{:S(2)}, u32[]{:S(2)}) collective-permute-start(bf16[256,384]{1,0:T(8,128)(2,1)} %shard_map.102), channel_id=1, source_target_pairs={{0,2},{1,3},{2,0},{3,1},{4,6},{5,7},{6,4},{7,5},{8,10},{9,11},{10,... | collective-permute-start | bytes 589832 | tf_op jit(solution)/shard_map/ppermute | solution.py:341
  97.3 22.7 %collective-permute-start.7 = (bf16[256,384]{1,0:T(8,128)(2,1)}, bf16[256,384]{1,0:T(8,128)(2,1)S(1)}, u32[]{:S(2)}, u32[]{:S(2)}) collective-permute-start(bf16[256,384]{1,0:T(8,128)(2,1)} %shard_map.102), channel_id=1, source_target_pairs={{0,1},{1,2},{2,3},{3,0},{4,5},{5,6},{6,7},{7,4},{8,9},{9,10},{10,1... | collective-permute-start | bytes 589832 | tf_op jit(solution)/shard_map/ppermute | solution.py:341
  115.9 8.5 %collective-permute-start.12 = (bf16[256,384]{1,0:T(8,128)(2,1)}, bf16[256,384]{1,0:T(8,128)(2,1)S(1)}, u32[]{:S(2)}, u32[]{:S(2)}) collective-permute-start(bf16[256,384]{1,0:T(8,128)(2,1)} %shard_map.103), channel_id=1, source_target_pairs={{0,3},{1,0},{2,1},{3,2},{4,7},{5,4},{6,5},{7,6},{8,11},{9,8},{10,9... | collective-permute-start | bytes 589832 | tf_op jit(solution)/shard_map/ppermute | solution.py:341
  118.8 18.0 %collective-permute-start.10 = (bf16[256,384]{1,0:T(8,128)(2,1)}, bf16[256,384]{1,0:T(8,128)(2,1)S(1)}, u32[]{:S(2)}, u32[]{:S(2)}) collective-permute-start(bf16[256,384]{1,0:T(8,128)(2,1)} %shard_map.103), channel_id=1, source_target_pairs={{0,2},{1,3},{2,0},{3,1},{4,6},{5,7},{6,4},{7,5},{8,10},{9,11},{10,... | collective-permute-start | bytes 589832 | tf_op jit(solution)/shard_map/ppermute | solution.py:341
  119.9 16.8 %collective-permute-start.8 = (bf16[256,384]{1,0:T(8,128)(2,1)}, bf16[256,384]{1,0:T(8,128)(2,1)S(1)}, u32[]{:S(2)}, u32[]{:S(2)}) collective-permute-start(bf16[256,384]{1,0:T(8,128)(2,1)} %shard_map.103), channel_id=1, source_target_pairs={{0,1},{1,2},{2,3},{3,0},{4,5},{5,6},{6,7},{7,4},{8,9},{9,10},{10,1... | collective-permute-start | bytes 589832 | tf_op jit(solution)/shard_map/ppermute | solution.py:341
  145.0 1.7 %copy-start.7 = (bf16[256,384]{1,0:T(8,128)(2,1)S(1)}, bf16[256,384]{1,0:T(8,128)(2,1)}, u32[]{:S(2)}) copy-start(bf16[256,384]{1,0:T(8,128)(2,1)} %shard_map.102) | copy-start | bytes 589828
  145.0 1.7 %copy-start.8 = (bf16[256,384]{1,0:T(8,128)(2,1)S(1)}, bf16[256,384]{1,0:T(8,128)(2,1)}, u32[]{:S(2)}) copy-start(bf16[256,384]{1,0:T(8,128)(2,1)} %shard_map.103) | copy-start | bytes 589828
  146.8 4.7 %copy-start.1 = (bf16[8,3,6144]{2,0,1:T(8,128)(2,1)S(1)}, bf16[8,3,6144]{2,0,1:T(8,128)(2,1)}, u32[]{:S(2)}) copy-start(bf16[8,3,6144]{2,0,1:T(8,128)(2,1)} %param.11) | copy-start | bytes 884740
